TPU v7x, 32 devices: a whole 2x2x4 slice. The times are simulated.
32 devices in a mesh: seq: 8 (over z, x), head: 4 (over y, core).
Axes of the slice: x: 2, y: 2, z: 4, core: 2. Of those that a mesh axis runs over, the one named last changes fastest.
Arguments:
- queries: bfloat16 [16, 8192, 128], P('head', 'seq'), may hold values from -16 to 16
- key_rows: bfloat16 [16, 8192, 128], P('head', 'seq'), may hold values from -16 to 16
- value_rows: bfloat16 [16, 8192, 128], P('head', 'seq'), may hold values from -6 to 6
- grad_out: bfloat16 [16, 8192, 128], P('head', 'seq'), may hold values from -6 to 6
- partner_pos: int32 [16, 2, 8], P('head'), may hold values from 0 to 7, each once within a row
Outputs:
- attended: bfloat16 [16, 8192, 128], P('head', 'seq')
- grad_queries: bfloat16 [16, 8192, 128], P('head', 'seq')
- grad_keys: bfloat16 [16, 8192, 128], P('head', 'seq')
- grad_values: bfloat16 [16, 8192, 128], P('head', 'seq')
Inputs may be any that keep to these rules, and one draw needn't show every extreme that they name: In head h, the block at place j of segment s takes the block at place partner_pos[h, s, j] of segment s as its partner; each row of 8 numbers is a permutation.
All inputs are finite; a program needn't handle non-finite values.
Results may differ from a plain program's by a relative error of at most 0.008.
Values may be sent and summed in bfloat16 or wider, within the bound.
No kernel may reach another device: no remote copies, remote signals or barrier semaphores. Data moves between devices by JAX's collectives and lax.ppermute only.
A program may use at most 128 MiB of HBM per device.

v0:
```python
import math

import jax
import jax.numpy as jnp
from jax import lax
from jax.sharding import PartitionSpec as P

BLK = 512
SEG_DEV = 4


def from_behind(value, axis, steps):
    count = lax.axis_size(axis)
    leading, last = (max(0, -steps), min(count, count - steps))
    return lax.ppermute(value, axis, [(source, source + steps) for source in range(leading, last)])


def passed_along(x, axis, by):
    size = lax.axis_size(axis)
    return lax.ppermute(x, axis, [(i, (i + by) % size) for i in range(size)])


def block_terms(query_rows, key_block, values, grad_rows, usable):
    scaling = 1.0 / math.sqrt(query_rows.shape[-1])
    scores = (
        jnp.einsum("cid,cjd->cij", query_rows, key_block, preferred_element_type=jnp.float32)
        * scaling
    )
    scores = jnp.where(usable[:, None, :], scores, -jnp.inf)
    highest = jnp.max(scores, axis=2, keepdims=True)
    weights = jnp.exp(scores - highest)
    shares = weights / jnp.sum(weights, axis=2, keepdims=True)
    shares_low = shares.astype(jnp.bfloat16)
    attended = jnp.einsum(
        "cij,cjd->cid", shares_low, values, preferred_element_type=jnp.float32
    ).astype(jnp.bfloat16)
    attended_wide = lax.optimization_barrier(attended).astype(jnp.float32)
    row_dot = jnp.sum(grad_rows.astype(jnp.float32) * attended_wide, axis=2, keepdims=True)
    grad_probs = jnp.einsum("cid,cjd->cij", grad_rows, values, preferred_element_type=jnp.float32)
    dscore = (shares * (grad_probs - row_dot)).astype(jnp.bfloat16)
    grad_query = (
        jnp.einsum("cij,cjd->cid", dscore, key_block, preferred_element_type=jnp.float32) * scaling
    ).astype(jnp.bfloat16)
    key_terms = (
        jnp.einsum("cij,cid->cjd", dscore, query_rows, preferred_element_type=jnp.float32) * scaling
    )
    value_terms = jnp.einsum(
        "cij,cid->cjd", shares_low, grad_rows, preferred_element_type=jnp.float32
    )
    return (attended, grad_query, jnp.stack([key_terms, value_terms], axis=0))


def pick_blocks(rows_head, index_head):
    return jnp.take(rows_head, index_head, axis=1)


def body(queries, key_rows, value_rows, grad_out, partner_pos):
    head_count, row_count, head_width = queries.shape
    blocks = row_count // BLK
    group_size = SEG_DEV
    seg_count = lax.axis_size("seq") // group_size
    device = lax.axis_index("seq")
    within = device // seg_count
    segment = device % seg_count
    pair_rows = jnp.stack([key_rows, value_rows], axis=1).reshape(
        head_count, 2, blocks, BLK, head_width
    )
    left_rows = from_behind(pair_rows[:, :, blocks - 1], "seq", 1)
    window = jnp.concatenate([left_rows[:, :, None], pair_rows[:, :, : blocks - 1]], axis=2)
    segment_row = lax.dynamic_index_in_dim(partner_pos, segment, axis=1, keepdims=False)
    my_partners = lax.dynamic_slice_in_dim(segment_row, within * blocks, blocks, axis=1)
    owner_pos = my_partners // blocks
    inner_pos = my_partners % blocks
    pieces = [pair_rows]
    for offset in range(1, group_size):
        pieces.append(passed_along(pair_rows, "seq", offset * seg_count))
    lookup = jnp.concatenate(pieces, axis=2)
    slot_index = (within - owner_pos) % group_size * blocks + inner_pos
    partner_rows = jax.vmap(pick_blocks)(lookup, slot_index)
    key_sets = jnp.concatenate([pair_rows, window, partner_rows], axis=3)
    block_ids = device * blocks + jnp.arange(blocks, dtype=jnp.int32)
    usable = (
        jnp.concatenate(
            [
                jnp.ones((blocks, BLK), jnp.int32),
                jnp.broadcast_to(block_ids[:, None], (blocks, BLK)),
                jnp.ones((blocks, BLK), jnp.int32),
            ],
            axis=1,
        )
        > 0
    )

    def per_head(pieces_in):
        query_rows, key_set, grad_rows = pieces_in
        return block_terms(query_rows, key_set[0], key_set[1], grad_rows, usable)

    attended, grad_query, term_rows = lax.map(
        per_head,
        (
            queries.reshape(head_count, blocks, BLK, head_width),
            key_sets,
            grad_out.reshape(head_count, blocks, BLK, head_width),
        ),
    )
    own_part = term_rows[:, :, :, :BLK]
    window_part = term_rows[:, :, :, BLK : 2 * BLK]
    partner_part = term_rows[:, :, :, 2 * BLK :]
    from_right = from_behind(window_part[:, :, 0], "seq", -1)
    window_back = jnp.concatenate([window_part[:, :, 1:], from_right[:, :, None]], axis=2)
    slot_total = group_size * blocks
    target_slot = (within - owner_pos) % group_size * blocks + inner_pos
    onehot = (target_slot[:, :, None] == jnp.arange(slot_total)[None, None, :]).astype(jnp.float32)
    buffer = jnp.einsum(
        "hcs,hxcid->hxsid",
        onehot,
        partner_part,
        precision=lax.Precision.HIGHEST,
        preferred_element_type=jnp.float32,
    )
    returned = buffer[:, :, :blocks]
    for offset in range(1, group_size):
        sent_part = buffer[:, :, offset * blocks : (offset + 1) * blocks]
        returned = returned + passed_along(sent_part, "seq", -offset * seg_count)
    grads_pair = (own_part + window_back + returned).astype(jnp.bfloat16)
    return (
        attended.reshape(head_count, row_count, head_width),
        grad_query.reshape(head_count, row_count, head_width),
        grads_pair[:, 0].reshape(head_count, row_count, head_width),
        grads_pair[:, 1].reshape(head_count, row_count, head_width),
    )


def solution(mesh):
    return jax.shard_map(
        body,
        mesh=mesh,
        in_specs=(
            P("head", "seq", None),
            P("head", "seq", None),
            P("head", "seq", None),
            P("head", "seq", None),
            P("head", None, None),
        ),
        out_specs=(
            P("head", "seq", None),
            P("head", "seq", None),
            P("head", "seq", None),
            P("head", "seq", None),
        ),
        check_vma=False,
    )
```

profile of v0, /device:TPU:10, one launch (start us, length us, event | category | flops | bytes accessed | tf_op | source)
XLA Modules:
  0.0 752.8 jit_solution(468083042225829427)
XLA Ops:
  0.7 3.2 pad_maximum_fusion.2
  12.7 128.5 %collective-permute-done.1 = bf16[4,2,2,512,128]{4,3,1,2,0:T(8,128)(2,1)} collective-permute-done((bf16[4,2,2,512,128]{4,3,1,2,0:T(8,128)(2,1)}, bf16[4,2,2,512,128]{4,3,1,2,0:T(8,128)(2,1)}, u32[]{:S(2)}, u32[]{:S(2)}) %collective-permute-start.1) | collective-permute-done | bytes 2097184 | tf_op jit(solution)/shard_map/ppermute | solution.py:20
  141.3 45.4 %collective-permute-done.2 = bf16[4,2,2,512,128]{4,3,1,2,0:T(8,128)(2,1)} collective-permute-done((bf16[4,2,2,512,128]{4,3,1,2,0:T(8,128)(2,1)}, bf16[4,2,2,512,128]{4,3,1,2,0:T(8,128)(2,1)}, u32[]{:S(2)}, u32[]{:S(2)}) %collective-permute-start.2) | collective-permute-done | bytes 2097184 | tf_op jit(solution)/shard_map/ppermute | solution.py:20
  187.3 6.6 pad_maximum_fusion
  193.9 5.6 gather_fusion
  201.4 6.5 collective-permute-done
  208.9 5.6 pad_maximum_fusion.1
  214.5 94.4 %while.14 = (s32[]{:T(128)}, bf16[4,2,512,128]{3,2,1,0:T(8,128)(2,1)}, bf16[4,2,512,128]{3,2,1,0:T(8,128)(2,1)}, f32[4,2,2,1536,128]{4,3,2,1,0:T(8,128)}, pred[2...) while((s32[]{:T(128)}, ...), condition=%wide.region_4.5_spmd, body=%wide.region_0.4_spmd.sunk | while | flops 2433745408 | bytes 71594176 | solution.py:98
  214.5 5.8 fusion.89
  220.3 3.7 fusion.90
  224.0 3.0 bitcast_dynamic-update-slice_fusion.2
  228.6 2.5 multiply_convert_fusion.2
  231.1 2.8 fusion.91
  238.1 5.8 fusion.89
  243.8 3.7 fusion.90
  247.6 3.0 bitcast_dynamic-update-slice_fusion.2
  254.7 2.8 fusion.91
  261.7 5.8 fusion.89
  267.4 3.7 fusion.90
  271.2 3.0 bitcast_dynamic-update-slice_fusion.2
  278.3 2.8 fusion.91
  285.3 5.8 fusion.89
  291.1 3.7 fusion.90
  294.8 3.0 bitcast_dynamic-update-slice_fusion.2
  299.4 2.5 multiply_convert_fusion.2
  301.9 2.8 fusion.91
  308.9 14.0 %convolution_bitcast_fusion.1 = f32[4,2,8,512,128]{4,2,3,1,0:T(8,128)S(1)} fusion(s32[4,2]{1,0:T(4,128)S(1)} %copy.33, f32[4,2,2,1536,128]{4,3,2,1,0:T(8,128)} %get-tuple-element.50), kind=kOutput, calls=%fused_computation.46 | convolution fusion | flops 100663360 | bytes 29360160 | tf_op jit(solution)/shard_map/hcs,hxcid->hxsid/dot_general | solution.py:114
  322.9 6.6 fusion.61
  333.3 5.2 collective-permute-start.4
  340.2 22.3 %copy.29 = f32[4,2,2,1536,128]{4,2,3,1,0:T(2,128)} copy(f32[4,2,2,1536,128]{4,3,2,1,0:T(8,128)} %get-tuple-element.50) | data formatting | bytes 25165824 | tf_op jit(solution)/shard_map/while | solution.py:98
  362.5 374.7 %collective-permute-done.4 = f32[4,2,512,128]{3,2,1,0:T(8,128)S(1)} collective-permute-done((f32[4,2,512,128]{3,2,1,0:T(8,128)S(1)}, f32[4,2,512,128]{3,2,1,0:T(8,128)S(1)}, u32[]{:S(2)}, u32[]{:S(2)}) %collective-permute-start.4) | collective-permute-done | bytes 2097184 | tf_op jit(solution)/shard_map/ppermute | solution.py:15
  739.2 9.9 %fusion.39 = bf16[4,2,2,512,128]{4,2,3,1,0:T(2,128)(2,1)S(1)} fusion(f32[4,2,2,512,128]{4,2,3,1,0:T(2,128)S(1)} %collective-permute-done.7, f32[4,2,2,512,128]{4,2,3,1,0:T(2,128)} %copy-done.6, f32[4,2,2,512,128]{4,2,3,1,0:T(2,128)S(1)} %collective-permute-done.5, f32[4,2,8,512,128]{4,2,3,1,0:T(8,128)S(1)} %convolution_bitcast_fusion.1, ...), kind=kLoop, calls=%fused_computation.54 | loop fusion | flops 7340032 | bytes 27262976 | tf_op jit(solution)/shard_map/convert_element_type | solution.py:125
  (87 shorter events, 51.5 us)
Async XLA Ops:
  0.6 11.4 %copy-start = (s32[4,2,8]{2,1,0:T(2,128)S(1)}, s32[4,2,8]{2,1,0:T(2,128)}, u32[]{:S(2)}) copy-start(s32[4,2,8]{2,1,0:T(2,128)} %param.11) | copy-start | bytes 772
  0.6 7.9 %copy-start.2 = (bf16[4,1024,128]{2,1,0:T(8,128)(2,1)S(1)}, bf16[4,1024,128]{2,1,0:T(8,128)(2,1)}, u32[]{:S(2)}) copy-start(bf16[4,1024,128]{2,1,0:T(8,128)(2,1)} %param.9) | copy-start | bytes 3145732
  0.7 7.9 %copy-start.3 = (bf16[4,1024,128]{2,1,0:T(8,128)(2,1)S(1)}, bf16[4,1024,128]{2,1,0:T(8,128)(2,1)}, u32[]{:S(2)}) copy-start(bf16[4,1024,128]{2,1,0:T(8,128)(2,1)} %param.8) | copy-start | bytes 3145732
  3.9 137.4 %collective-permute-start.1 = (bf16[4,2,2,512,128]{4,3,1,2,0:T(8,128)(2,1)}, bf16[4,2,2,512,128]{4,3,1,2,0:T(8,128)(2,1)}, u32[]{:S(2)}, u32[]{:S(2)}) collective-permute-start(bf16[4,2,2,512,128]{4,3,1,2,0:T(8,128)(2,1)} %pad_maximum_fusion.2), channel_id=1, source_target_pairs={{0,8},{4,12},{8,16},{12,20},{16,24},{20,28},{24,0},{28,4},{1,9},{5... | collective-permute-start | bytes 6291464 | tf_op jit(solution)/shard_map/ppermute | solution.py:20
  5.5 181.2 %collective-permute-start.2 = (bf16[4,2,2,512,128]{4,3,1,2,0:T(8,128)(2,1)}, bf16[4,2,2,512,128]{4,3,1,2,0:T(8,128)(2,1)}, u32[]{:S(2)}, u32[]{:S(2)}) collective-permute-start(bf16[4,2,2,512,128]{4,3,1,2,0:T(8,128)(2,1)} %pad_maximum_fusion.2), channel_id=1, source_target_pairs={{0,16},{4,20},{8,24},{12,28},{16,0},{20,4},{24,8},{28,12},{1,17},{... | collective-permute-start | bytes 6291464 | tf_op jit(solution)/shard_map/ppermute | solution.py:20
  6.7 180.6 %collective-permute-start.3 = (bf16[4,2,2,512,128]{4,3,1,2,0:T(8,128)(2,1)}, bf16[4,2,2,512,128]{4,3,1,2,0:T(8,128)(2,1)}, u32[]{:S(2)}, u32[]{:S(2)}) collective-permute-start(bf16[4,2,2,512,128]{4,3,1,2,0:T(8,128)(2,1)} %pad_maximum_fusion.2), channel_id=1, source_target_pairs={{0,24},{4,28},{8,0},{12,4},{16,8},{20,12},{24,16},{28,20},{1,25},{... | collective-permute-start | bytes 6291464 | tf_op jit(solution)/shard_map/ppermute | solution.py:20
  10.0 197.9 %collective-permute-start = (bf16[4,2,512,128]{3,2,1,0:T(8,128)(2,1)}, bf16[4,2,512,128]{3,2,1,0:T(8,128)(2,1)S(1)}, u32[]{:S(2)}, u32[]{:S(2)}) collective-permute-start(bf16[4,2,512,128]{3,2,1,0:T(8,128)(2,1)} %get-tuple-element.86), channel_id=1, source_target_pairs={{0,4},{4,8},{8,12},{12,16},{16,20},{20,24},{24,28},{1,5},{5,9},{9,... | collective-permute-start | bytes 3145736 | tf_op jit(solution)/shard_map/ppermute | solution.py:15
  199.5 9.5 %copy-start.5 = (bf16[4,2,1,512,128]{4,3,1,2,0:T(8,128)(2,1)S(1)}, bf16[4,2,1,512,128]{4,3,1,2,0:T(8,128)(2,1)}, u32[]{:S(2)}) copy-start(bf16[4,2,1,512,128]{4,3,1,2,0:T(8,128)(2,1)} %get-tuple-element.87) | copy-start | bytes 3145732
  208.0 1.0 copy-start.7
  208.9 5.6 copy-start.4
  220.3 8.3 %slice-start = ((s8[6291456]{0:T(1024)(128)(4,1)}), s8[4194304]{0:T(1024)(128)(4,1)S(1)}, s32[]{:S(2)}) async-start(s8[6291456]{0:T(1024)(128)(4,1)} %bitcast.150), calls=%async_computation | async-start | bytes 8388608 | tf_op jit(solution)/shard_map/while
  224.0 4.6 slice-start.1
  243.8 8.3 %slice-start = ((s8[6291456]{0:T(1024)(128)(4,1)}), s8[4194304]{0:T(1024)(128)(4,1)S(1)}, s32[]{:S(2)}) async-start(s8[6291456]{0:T(1024)(128)(4,1)} %bitcast.150), calls=%async_computation | async-start | bytes 8388608 | tf_op jit(solution)/shard_map/while
  247.6 4.6 slice-start.1
  267.4 8.3 %slice-start = ((s8[6291456]{0:T(1024)(128)(4,1)}), s8[4194304]{0:T(1024)(128)(4,1)S(1)}, s32[]{:S(2)}) async-start(s8[6291456]{0:T(1024)(128)(4,1)} %bitcast.150), calls=%async_computation | async-start | bytes 8388608 | tf_op jit(solution)/shard_map/while
  271.2 4.6 slice-start.1
  291.1 8.3 %slice-start = ((s8[6291456]{0:T(1024)(128)(4,1)}), s8[4194304]{0:T(1024)(128)(4,1)S(1)}, s32[]{:S(2)}) async-start(s8[6291456]{0:T(1024)(128)(4,1)} %bitcast.150), calls=%async_computation | async-start | bytes 8388608 | tf_op jit(solution)/shard_map/while
  294.8 4.6 slice-start.1
  329.5 407.8 %collective-permute-start.5 = (f32[4,2,2,512,128]{4,2,3,1,0:T(2,128)}, f32[4,2,2,512,128]{4,2,3,1,0:T(2,128)S(1)}, u32[]{:S(2)}, u32[]{:S(2)}) collective-permute-start(f32[4,2,2,512,128]{4,2,3,1,0:T(2,128)} %get-tuple-element.81), channel_id=1, source_target_pairs={{0,24},{4,28},{8,0},{12,4},{16,8},{20,12},{24,16},{28,20},{1,25},{... | collective-permute-start | bytes 12582920 | tf_op jit(solution)/shard_map/ppermute | solution.py:20
  329.5 407.8 %collective-permute-start.7 = (f32[4,2,2,512,128]{4,2,3,1,0:T(2,128)}, f32[4,2,2,512,128]{4,2,3,1,0:T(2,128)S(1)}, u32[]{:S(2)}, u32[]{:S(2)}) collective-permute-start(f32[4,2,2,512,128]{4,2,3,1,0:T(2,128)} %get-tuple-element.82), channel_id=1, source_target_pairs={{0,8},{4,12},{8,16},{12,20},{16,24},{20,28},{24,0},{28,4},{1,9},{5... | collective-permute-start | bytes 12582920 | tf_op jit(solution)/shard_map/ppermute | solution.py:20
  331.5 405.8 %collective-permute-start.6 = (f32[4,2,2,512,128]{4,2,3,1,0:T(2,128)}, f32[4,2,2,512,128]{4,2,3,1,0:T(2,128)S(1)}, u32[]{:S(2)}, u32[]{:S(2)}) collective-permute-start(f32[4,2,2,512,128]{4,2,3,1,0:T(2,128)} %get-tuple-element.83), channel_id=1, source_target_pairs={{0,16},{4,20},{8,24},{12,28},{16,0},{20,4},{24,8},{28,12},{1,17},{... | collective-permute-start | bytes 12582920 | tf_op jit(solution)/shard_map/ppermute | solution.py:20
  333.3 404.0 %collective-permute-start.4 = (f32[4,2,512,128]{3,2,1,0:T(8,128)S(1)}, f32[4,2,512,128]{3,2,1,0:T(8,128)S(1)}, u32[]{:S(2)}, u32[]{:S(2)}) collective-permute-start(f32[4,2,512,128]{3,2,1,0:T(8,128)S(1)} %slice_bitcast_fusion), channel_id=1, source_target_pairs={{4,0},{8,4},{12,8},{16,12},{20,16},{24,20},{28,24},{5,1},{9,5},{13... | collective-permute-start | bytes 6291464 | tf_op jit(solution)/shard_map/ppermute | solution.py:15
  737.3 2.0 copy-start.6
  739.2 13.6 %copy-start.1 = (s32[4,2,8]{2,1,0:T(2,128)S(1)}, s32[4,2,8]{2,1,0:T(2,128)}, u32[]{:S(2)}) copy-start(s32[4,2,8]{2,1,0:T(2,128)} %param.11) | copy-start | bytes 772
where the time goes:
time: 754 us; the launch traced here: 753 us
  waiting for transfers between devices  556 us (74%)
  matrix products  84.7 us (11%)
  other arithmetic  52.2 us (7%)
  local copies, waits for them, and re-layouts  45.3 us (6%)
  starting transfers between devices  13.7 us (2%)
    ppermute x2, waiting for transfers between devices, from_behind(): lax.ppermute(value, axis, [(source, source + steps) for source in range(l...  381 us
    ppermute x6, waiting for transfers between devices, passed_along(): return lax.ppermute(x, axis, [(i, (i + by) % size) for i in range(size)])  175 us
    sub x4, matrix products, block_terms(): weights = jnp.exp(scores - highest)  23 us
    while x1, local copies, waits for them, and re-layouts, body(): lax.map(per_head, (queries.reshape(head_count, blocks, BLK, head_width),...  22.3 us
  transfers between devices with their start and end apart: 8, of which 5 were waited for; matrix products, arithmetic and copies ran while one was open for 6% of the time, Pallas kernels for 0%

commit v1 on v0

v1 whole, which is shorter than its diff:
```python
import math

import jax
import jax.numpy as jnp
from jax import lax
from jax.sharding import PartitionSpec as P

BLK = 512


def group_pairs(nseg, group, shift):
    return [
        (seg + nseg * w, seg + nseg * ((w + shift) % group))
        for seg in range(nseg)
        for w in range(group)
    ]


def next_segment_pairs(nseg, group):
    return [
        (seg + nseg * w, (seg + 1) % nseg + nseg * w)
        for seg in range(nseg)
        for w in range(group)
    ]


def block_terms(query_rows, key_block, values, grad_rows, usable):
    scaling = 1.0 / math.sqrt(query_rows.shape[-1])
    scores = (
        jnp.einsum("cid,cjd->cij", query_rows, key_block, preferred_element_type=jnp.float32)
        * scaling
    )
    scores = jnp.where(usable[:, None, :], scores, -jnp.inf)
    highest = jnp.max(scores, axis=2, keepdims=True)
    weights = jnp.exp(scores - highest)
    shares = weights / jnp.sum(weights, axis=2, keepdims=True)
    shares_low = shares.astype(jnp.bfloat16)
    attended = jnp.einsum(
        "cij,cjd->cid", shares_low, values, preferred_element_type=jnp.float32
    ).astype(jnp.bfloat16)
    attended_wide = lax.optimization_barrier(attended).astype(jnp.float32)
    row_dot = jnp.sum(grad_rows.astype(jnp.float32) * attended_wide, axis=2, keepdims=True)
    grad_probs = jnp.einsum("cid,cjd->cij", grad_rows, values, preferred_element_type=jnp.float32)
    dscore = (shares * (grad_probs - row_dot)).astype(jnp.bfloat16)
    grad_query = (
        jnp.einsum("cij,cjd->cid", dscore, key_block, preferred_element_type=jnp.float32) * scaling
    ).astype(jnp.bfloat16)
    key_terms = (
        jnp.einsum("cij,cid->cjd", dscore, query_rows, preferred_element_type=jnp.float32) * scaling
    )
    value_terms = jnp.einsum(
        "cij,cid->cjd", shares_low, grad_rows, preferred_element_type=jnp.float32
    )
    return attended, grad_query, key_terms, value_terms


def interleave(even, odd):
    return jnp.stack([even, odd], axis=1).reshape((-1,) + even.shape[1:])


def body(queries, key_rows, value_rows, grad_out, partner_pos):
    heads, row_count, width = queries.shape
    blocks = row_count // BLK
    places = partner_pos.shape[2]
    group = places // blocks
    if heads != group:
        raise ValueError("heads mismatch")
    nseg = lax.axis_size("seq") // group
    device = lax.axis_index("seq")
    segment = device % nseg
    within = device // nseg

    data = jnp.stack(
        [
            queries.reshape(heads, blocks, BLK, width),
            grad_out.reshape(heads, blocks, BLK, width),
            key_rows.reshape(heads, blocks, BLK, width),
            value_rows.reshape(heads, blocks, BLK, width),
        ],
        axis=1,
    )
    received = [lax.dynamic_index_in_dim(data, within, axis=0, keepdims=False)]
    for shift in range(1, group):
        send = lax.dynamic_index_in_dim(data, (within + shift) % group, axis=0, keepdims=False)
        received.append(lax.ppermute(send, "seq", group_pairs(nseg, group, shift)))
    received = jnp.stack(received)
    order = (within - jnp.arange(group, dtype=jnp.int32)) % group
    local = jnp.take(received, order, axis=0)
    local = jnp.swapaxes(local, 0, 1).reshape(4, group * blocks, BLK, width)
    q_all, g_all, k_all, v_all = local[0], local[1], local[2], local[3]

    odd_kv = jnp.stack([k_all[1::2], v_all[1::2]], axis=1)
    odd_send = jnp.where(segment == nseg - 1, jnp.roll(odd_kv, 1, axis=0), odd_kv)
    window_kv = lax.ppermute(odd_send, "seq", next_segment_pairs(nseg, group))
    k_window = interleave(window_kv[:, 0], k_all[0::2])
    v_window = interleave(window_kv[:, 1], v_all[0::2])

    my_partners = lax.dynamic_index_in_dim(
        lax.dynamic_index_in_dim(partner_pos, within, axis=0, keepdims=False),
        segment,
        axis=0,
        keepdims=False,
    )
    k_partner = jnp.take(k_all, my_partners, axis=0)
    v_partner = jnp.take(v_all, my_partners, axis=0)
    key_sets = jnp.concatenate([k_all, k_window, k_partner], axis=1)
    value_sets = jnp.concatenate([v_all, v_window, v_partner], axis=1)

    place_ids = jnp.arange(places, dtype=jnp.int32)
    first_block = jnp.logical_and(segment == 0, place_ids == 0)
    usable = jnp.concatenate(
        [
            jnp.ones((places, BLK), jnp.bool_),
            jnp.broadcast_to(jnp.logical_not(first_block)[:, None], (places, BLK)),
            jnp.ones((places, BLK), jnp.bool_),
        ],
        axis=1,
    )
    attended, grad_query, key_terms, value_terms = block_terms(
        q_all, key_sets, value_sets, g_all, usable
    )
    terms = jnp.stack([key_terms, value_terms], axis=1)
    own_part = terms[:, :, :BLK]
    window_part = terms[:, :, BLK : 2 * BLK]
    partner_part = terms[:, :, 2 * BLK :]

    ret = window_part[0::2]
    ret = jnp.where(segment == 0, jnp.roll(ret, -1, axis=0), ret)
    back_pairs = [(b, a) for a, b in next_segment_pairs(nseg, group)]
    window_back = lax.ppermute(ret, "seq", back_pairs)
    window_sum = interleave(window_part[1::2], window_back)

    hits = my_partners[None, :] == place_ids[:, None]
    inverse = jnp.sum(jnp.where(hits, place_ids[None, :], 0), axis=1)
    partner_sum = jnp.take(partner_part, inverse, axis=0)
    grads = (own_part + window_sum + partner_sum).astype(jnp.bfloat16)

    outs = jnp.stack([attended, grad_query, grads[:, 0], grads[:, 1]], axis=1)
    outs = outs.reshape(group, blocks, 4, BLK, width)
    returned = [lax.dynamic_index_in_dim(outs, within, axis=0, keepdims=False)]
    for shift in range(1, group):
        send = lax.dynamic_index_in_dim(outs, (within - shift) % group, axis=0, keepdims=False)
        returned.append(lax.ppermute(send, "seq", group_pairs(nseg, group, group - shift)))
    returned = jnp.stack(returned)
    head_order = (jnp.arange(group, dtype=jnp.int32) - within) % group
    result = jnp.take(returned, head_order, axis=0)
    shape = (heads, row_count, width)
    return tuple(result[:, :, a].reshape(shape) for a in range(4))


def solution(mesh):
    return jax.shard_map(
        body,
        mesh=mesh,
        in_specs=(
            P("head", "seq", None),
            P("head", "seq", None),
            P("head", "seq", None),
            P("head", "seq", None),
            P("head", None, None),
        ),
        out_specs=(
            P("head", "seq", None),
            P("head", "seq", None),
            P("head", "seq", None),
            P("head", "seq", None),
        ),
        check_vma=False,
    )
```

time: 754 us -> 382 us (0.51)
  the two profiles are of different devices: /device:TPU:10 before, /device:TPU:14 now
where the time goes in v1:
time: 382 us; the launch traced here: 381 us
  waiting for transfers between devices  222 us (58%)
  matrix products  66.1 us (17%)
  other arithmetic  47.6 us (12%)
  local copies, waits for them, and re-layouts  34.2 us (9%)
  starting transfers between devices  10.8 us (3%)
    ppermute x3, waiting for transfers between devices, body(): lax.ppermute(send, 'seq', group_pairs(nseg, group, group - shift))  86.7 us
    ppermute x3, waiting for transfers between devices, body(): received.append(lax.ppermute(send, 'seq', group_pairs(nseg, group, shift)))  86.5 us
    ppermute x1, waiting for transfers between devices, body(): window_back = lax.ppermute(ret, 'seq', back_pairs)  32 us
    ppermute x1, waiting for transfers between devices, body(): window_kv = lax.ppermute(odd_send, 'seq', next_segment_pairs(nseg, group))  16.6 us
    convert_element_type x1, other arithmetic, block_terms(): shares_low = shares.astype(jnp.bfloat16)  13.6 us
    dot_general x1, matrix products, block_terms(): jnp.einsum('cid,cjd->cij', grad_rows, values, preferred_element_type=jnp....  13.4 us
    sub x1, matrix products, block_terms(): weights = jnp.exp(scores - highest)  13.3 us
    dot_general x1, matrix products, block_terms(): jnp.einsum('cij,cid->cjd', dscore, query_rows, preferred_element_type=jnp...  11.4 us
  transfers between devices with their start and end apart: 8, of which 7 were waited for; matrix products, arithmetic and copies ran while one was open for 6% of the time, Pallas kernels for 0%

profile of v1, /device:TPU:14, one launch (start us, length us, event | category | flops | bytes accessed | tf_op | source)
XLA Modules:
  0.0 381.4 jit_solution(9938106546838316308)
XLA Ops:
  0.7 2.5 pad_maximum_fusion.1
  5.0 2.6 collective-permute-start.1
  7.5 2.5 collective-permute-start
  10.6 65.2 %collective-permute-done.2 = bf16[4,2,512,128]{3,2,1,0:T(8,128)(2,1)} collective-permute-done((bf16[4,2,512,128]{3,2,1,0:T(8,128)(2,1)}, bf16[4,2,512,128]{3,2,1,0:T(8,128)(2,1)}, u32[]{:S(2)}, u32[]{:S(2)}) %collective-permute-start.2) | collective-permute-done | bytes 1048608 | tf_op jit(solution)/shard_map/ppermute | solution.py:85
  75.8 21.3 %collective-permute-done = bf16[4,2,512,128]{3,2,1,0:T(8,128)(2,1)} collective-permute-done((bf16[4,2,512,128]{3,2,1,0:T(8,128)(2,1)S(1)}, bf16[4,2,512,128]{3,2,1,0:T(8,128)(2,1)}, u32[]{:S(2)}, u32[]{:S(2)}) %collective-permute-start) | collective-permute-done | bytes 1048608 | tf_op jit(solution)/shard_map/ppermute | solution.py:85
  97.1 3.5 pad_maximum_fusion.2
  100.7 5.3 %gather_fusion = bf16[4,4,2,512,128]{4,3,2,1,0:T(8,128)(2,1)} fusion(bf16[4,4,2,512,128]{4,3,2,1,0:T(8,128)(2,1)} %pad_maximum_fusion.2, s32[1024]{0:T(1024)S(1)} %pad_clamp_fusion.3), kind=kCustom, calls=%fused_computation.2 | custom fusion | bytes 8388624 | tf_op jit(solution)/shard_map/jit(_take)/gather | solution.py:88
  106.0 2.7 select_bitcast_fusion
  114.2 1.6 gather_fusion.4
  115.9 1.6 gather_fusion.3
  117.5 3.2 broadcast_select_fusion.1
  120.7 16.6 %collective-permute-done.3 = bf16[4,2,512,128]{3,2,0,1:T(8,128)(2,1)} collective-permute-done((bf16[4,2,512,128]{3,2,0,1:T(8,128)(2,1)}, bf16[4,2,512,128]{3,2,0,1:T(8,128)(2,1)}, u32[]{:S(2)}, u32[]{:S(2)}) %collective-permute-start.3) | collective-permute-done | bytes 1048608 | tf_op jit(solution)/shard_map/ppermute | solution.py:94
  140.9 13.3 %fusion.34 = (f32[8,512]{1,0:T(8,128)S(1)}, f32[8,512,1536]{2,1,0:T(8,128)}) fusion(pred[8,1536]{1,0:T(8,128)(4,1)S(1)} %pad_add_fusion, bf16[8,512,128]{2,1,0:T(8,128)(2,1)} %bitcast.89, bf16[8,512,128]{2,1,0:T(8,128)(2,1)} %get-tuple-element.35, bf16[8,512,128]{2,1,0:T(8,128)(2,1)} %bitcast.92, bf16[8,512,128]{2,1,0:T(8,128)(2,1)S(1)} %bitcast.82), kind=kOutput, calls=%fused_computation.116 | convolution fusion | flops 1645217280 | bytes 29388800 | tf_op jit(solution)/shard_map/sub | solution.py:35
  154.2 13.6 %fusion.5 = bf16[8,512,1536]{2,1,0:T(8,128)(2,1)} fusion(f32[8,512,1536]{2,1,0:T(8,128)} %get-tuple-element.37, f32[8,512]{1,0:T(8,128)S(1)} %get-tuple-element.36), kind=kLoop, calls=%fused_computation.18 | loop fusion | flops 12582912 | bytes 37765120 | tf_op jit(solution)/shard_map/convert_element_type | solution.py:37
  167.8 11.2 %convolution_bitcast_fusion = f32[8,1,1536,128]{3,2,0,1:T(8,128)} fusion(bf16[8,512,1536]{2,1,0:T(8,128)(2,1)} %fusion.5, bf16[8,512,128]{2,1,0:T(8,128)(2,1)S(1)} %bitcast.78), kind=kOutput, calls=%fused_computation.20 | convolution fusion | flops 1610612736 | bytes 19922944 | tf_op jit(solution)/shard_map/cij,cid->cjd/dot_general | solution.py:51
  179.0 8.7 %convolution_convert_fusion = bf16[8,512,128]{2,1,0:T(8,128)(2,1)S(1)} fusion(bf16[8,512,1536]{2,1,0:T(8,128)(2,1)} %fusion.5, bf16[8,512,128]{2,1,0:T(8,128)(2,1)} %get-tuple-element.34, bf16[8,512,128]{2,1,0:T(8,128)(2,1)} %bitcast.94, bf16[8,512,128]{2,1,0:T(8,128)(2,1)S(1)} %bitcast.86), kind=kOutput, calls=%fused_computation.40 | convolution fusion | flops 1620574208 | bytes 16777216 | tf_op jit(solution)/shard_map/cij,cjd->cid/dot_general | solution.py:38
  189.3 13.4 %multiply_convert_fusion = bf16[8,512,1536]{2,1,0:T(8,128)(2,1)} fusion(bf16[8,512,128]{2,1,0:T(8,128)(2,1)S(1)} %bitcast.79, f32[8,512]{1,0:T(8,128)S(1)} %multiply_reduce_fusion, f32[8,512,1536]{2,1,0:T(8,128)} %get-tuple-element.37, f32[8,512]{1,0:T(8,128)S(1)} %get-tuple-element.36, bf16[8,512,128]{2,1,0:T(8,128)(2,1)S(1)} %copy-done.8, ...), kind=kOutput, calls=%fused_computation.6 | convolution fusion | flops 1645215744 | bytes 41975808 | tf_op jit(solution)/shard_map/cid,cjd->cij/dot_general | solution.py:43
  202.7 11.4 %multiply_bitcast_fusion = f32[8,1,1536,128]{3,2,0,1:T(8,128)} fusion(bf16[8,512,1536]{2,1,0:T(8,128)(2,1)} %multiply_convert_fusion, bf16[8,512,128]{2,1,0:T(8,128)(2,1)} %bitcast.90), kind=kOutput, calls=%fused_computation.19 | convolution fusion | flops 1612185600 | bytes 19922944 | tf_op jit(solution)/shard_map/cij,cid->cjd/dot_general | solution.py:49
  214.1 8.0 %pad_maximum_fusion = (f32[8,2,512,128]{3,2,0,1:T(8,128)}, f32[8,2,512,128]{3,2,0,1:T(8,128)}, f32[8,2,512,128]{3,2,0,1:T(8,128)S(1)}) fusion(f32[8,1,1536,128]{3,2,0,1:T(8,128)} %convolution_bitcast_fusion, f32[8,1,1536,128]{3,2,0,1:T(8,128)} %multiply_bitcast_fusion), kind=kLoop, calls=%fused_computation.23 | loop fusion | flops 3145728 | bytes 25165824 | tf_op jit(solution)/shard_map/stack | solution.py:122
  222.4 2.4 slice_bitcast_fusion
  225.5 5.1 %gather_fusion.1 = f32[8,2,512,128]{3,2,1,0:T(8,128)} fusion(f32[8,2,512,128]{3,2,0,1:T(8,128)} %get-tuple-element.7, s32[1024]{0:T(1024)S(1)} %pad_clamp_fusion.1), kind=kCustom, calls=%fused_computation.3 | custom fusion | bytes 8388640 | tf_op jit(solution)/shard_map/jit(_take)/gather | solution.py:135
  230.6 8.1 %multiply_convert_fusion.1 = bf16[8,512,128]{2,1,0:T(8,128)(2,1)S(1)} fusion(bf16[8,512,1536]{2,1,0:T(8,128)(2,1)} %multiply_convert_fusion, bf16[8,512,128]{2,1,0:T(8,128)(2,1)S(1)} %copy-done.7, bf16[8,512,128]{2,1,0:T(8,128)(2,1)S(1)} %bitcast.93, bf16[8,512,128]{2,1,0:T(8,128)(2,1)S(1)} %bitcast.83), kind=kOutput, calls=%fused_computation.38 | convolution fusion | flops 1621098496 | bytes 16777216 | tf_op jit(solution)/shard_map/cij,cjd->cid/dot_general | solution.py:46
  238.7 32.0 %collective-permute-done.4 = f32[4,2,512,128]{3,2,0,1:T(8,128)} collective-permute-done((f32[4,2,512,128]{3,2,0,1:T(8,128)}, f32[4,2,512,128]{3,2,0,1:T(8,128)}, u32[]{:S(2)}, u32[]{:S(2)}) %collective-permute-start.4) | collective-permute-done | bytes 2097184 | tf_op jit(solution)/shard_map/ppermute | solution.py:130
  270.7 2.0 pad_maximum_fusion.3
  273.1 1.8 copy-done
  278.3 2.6 collective-permute-start.7
  282.5 67.0 %collective-permute-done.7 = bf16[2,4,512,128]{3,2,1,0:T(8,128)(2,1)S(1)} collective-permute-done((bf16[2,4,512,128]{3,2,1,0:T(8,128)(2,1)S(1)}, bf16[2,4,512,128]{3,2,1,0:T(8,128)(2,1)S(1)}, u32[]{:S(2)}, u32[]{:S(2)}) %collective-permute-start.7) | collective-permute-done | bytes 1048608 | tf_op jit(solution)/shard_map/ppermute | solution.py:143
  349.5 18.6 %collective-permute-done.6 = bf16[2,4,512,128]{3,2,1,0:T(8,128)(2,1)S(1)} collective-permute-done((bf16[2,4,512,128]{3,2,1,0:T(8,128)(2,1)S(1)}, bf16[2,4,512,128]{3,2,1,0:T(8,128)(2,1)S(1)}, u32[]{:S(2)}, u32[]{:S(2)}) %collective-permute-start.6) | collective-permute-done | bytes 1048608 | tf_op jit(solution)/shard_map/ppermute | solution.py:143
  369.2 2.2 pad_maximum_fusion.5
  371.5 5.2 %gather_fusion.2 = bf16[4,2,4,512,128]{4,3,2,1,0:T(8,128)(2,1)} fusion(bf16[4,2,4,512,128]{4,3,2,1,0:T(8,128)(2,1)} %pad_maximum_fusion.5, s32[1024]{0:T(1024)S(1)} %pad_clamp_fusion), kind=kCustom, calls=%fused_computation.4 | custom fusion | bytes 8388624 | tf_op jit(solution)/shard_map/jit(_take)/gather | solution.py:146
  376.7 2.7 broadcast_select_fusion
  379.4 2.1 fusion.31
  (66 shorter events, 20.4 us)
Async XLA Ops:
  4.5 71.3 %collective-permute-start.2 = (bf16[4,2,512,128]{3,2,1,0:T(8,128)(2,1)}, bf16[4,2,512,128]{3,2,1,0:T(8,128)(2,1)}, u32[]{:S(2)}, u32[]{:S(2)}) collective-permute-start(bf16[4,2,512,128]{3,2,1,0:T(8,128)(2,1)} %get-tuple-element.25), channel_id=1, source_target_pairs={{0,24},{8,0},{16,8},{24,16},{4,28},{12,4},{20,12},{28,20},{1,25},{... | collective-permute-start | bytes 3145736 | tf_op jit(solution)/shard_map/ppermute | solution.py:85
  5.0 70.9 %collective-permute-start.1 = (bf16[4,2,512,128]{3,2,1,0:T(8,128)(2,1)S(1)}, bf16[4,2,512,128]{3,2,1,0:T(8,128)(2,1)}, u32[]{:S(2)}, u32[]{:S(2)}) collective-permute-start(bf16[4,2,512,128]{3,2,1,0:T(8,128)(2,1)S(1)} %get-tuple-element.26), channel_id=1, source_target_pairs={{0,16},{8,24},{16,0},{24,8},{4,20},{12,28},{20,4},{28,12},{1,17},{... | collective-permute-start | bytes 3145736 | tf_op jit(solution)/shard_map/ppermute | solution.py:85
  7.5 89.6 %collective-permute-start = (bf16[4,2,512,128]{3,2,1,0:T(8,128)(2,1)S(1)}, bf16[4,2,512,128]{3,2,1,0:T(8,128)(2,1)}, u32[]{:S(2)}, u32[]{:S(2)}) collective-permute-start(bf16[4,2,512,128]{3,2,1,0:T(8,128)(2,1)S(1)} %get-tuple-element.27), channel_id=1, source_target_pairs={{0,8},{8,16},{16,24},{24,0},{4,12},{12,20},{20,28},{28,4},{1,9},{9... | collective-permute-start | bytes 3145736 | tf_op jit(solution)/shard_map/ppermute | solution.py:85
  112.9 24.4 %collective-permute-start.3 = (bf16[4,2,512,128]{3,2,0,1:T(8,128)(2,1)}, bf16[4,2,512,128]{3,2,0,1:T(8,128)(2,1)}, u32[]{:S(2)}, u32[]{:S(2)}) collective-permute-start(bf16[4,2,512,128]{3,2,0,1:T(8,128)(2,1)} %fusion.11), channel_id=1, source_target_pairs={{0,4},{8,12},{16,20},{24,28},{4,0},{12,8},{20,16},{28,24},{1,5},{9... | collective-permute-start | bytes 3145736 | tf_op jit(solution)/shard_map/ppermute | solution.py:94
  117.5 21.0 %copy-start.6 = (bf16[4,1,512,128]{3,2,0,1:T(8,128)(2,1)S(1)}, bf16[4,1,512,128]{3,2,0,1:T(8,128)(2,1)}, u32[]{:S(2)}) copy-start(bf16[4,1,512,128]{3,2,0,1:T(8,128)(2,1)} %get-tuple-element.33) | copy-start | bytes 1572868
  120.7 19.0 %copy-start.5 = (bf16[4,1,512,128]{3,2,0,1:T(8,128)(2,1)S(1)}, bf16[4,1,512,128]{3,2,0,1:T(8,128)(2,1)}, u32[]{:S(2)}) copy-start(bf16[4,1,512,128]{3,2,0,1:T(8,128)(2,1)} %get-tuple-element.30) | copy-start | bytes 1572868
  179.0 10.3 %copy-start.8 = (bf16[8,512,128]{2,1,0:T(8,128)(2,1)S(1)}, bf16[8,512,128]{2,1,0:T(8,128)(2,1)}, u32[]{:S(2)}) copy-start(bf16[8,512,128]{2,1,0:T(8,128)(2,1)} %get-tuple-element.34) | copy-start | bytes 3145732
  179.0 10.3 %copy-start.10 = (bf16[4,2,512,128]{3,2,1,0:T(8,128)(2,1)S(1)}, bf16[4,2,512,128]{3,2,1,0:T(8,128)(2,1)}, u32[]{:S(2)}) copy-start(bf16[4,2,512,128]{3,2,1,0:T(8,128)(2,1)} %copy.25) | copy-start | bytes 3145732
  187.6 1.0 copy-start.3
  224.8 46.0 %collective-permute-start.4 = (f32[4,2,512,128]{3,2,0,1:T(8,128)}, f32[4,2,512,128]{3,2,0,1:T(8,128)}, u32[]{:S(2)}, u32[]{:S(2)}) collective-permute-start(f32[4,2,512,128]{3,2,0,1:T(8,128)} %get-tuple-element.19), channel_id=1, source_target_pairs={{4,0},{12,8},{20,16},{28,24},{0,4},{8,12},{16,20},{24,28},{5,1},{1... | collective-permute-start | bytes 6291464 | tf_op jit(solution)/shard_map/ppermute | solution.py:130
  225.5 5.1 %copy-start.7 = (bf16[8,512,128]{2,1,0:T(8,128)(2,1)S(1)}, bf16[8,512,128]{2,1,0:T(8,128)(2,1)}, u32[]{:S(2)}) copy-start(bf16[8,512,128]{2,1,0:T(8,128)(2,1)} %get-tuple-element.35) | copy-start | bytes 3145732
  225.5 5.1 %copy-start.9 = (bf16[4,2,512,128]{3,2,1,0:T(8,128)(2,1)S(1)}, bf16[4,2,512,128]{3,2,1,0:T(8,128)(2,1)}, u32[]{:S(2)}) copy-start(bf16[4,2,512,128]{3,2,1,0:T(8,128)(2,1)} %copy.24) | copy-start | bytes 3145732
  230.6 40.2 %copy-start.2 = (f32[4,1,2,512,128]{4,3,0,2,1:T(8,128)S(1)}, f32[4,1,2,512,128]{4,3,0,2,1:T(8,128)}, u32[]{:S(2)}) copy-start(f32[4,1,2,512,128]{4,3,0,2,1:T(8,128)} %get-tuple-element.18) | copy-start | bytes 6291460
  272.7 2.2 copy-start
  272.7 3.5 copy-start.1
  276.2 1.2 copy-start.4
  278.3 71.2 %collective-permute-start.7 = (bf16[2,4,512,128]{3,2,1,0:T(8,128)(2,1)S(1)}, bf16[2,4,512,128]{3,2,1,0:T(8,128)(2,1)S(1)}, u32[]{:S(2)}, u32[]{:S(2)}) collective-permute-start(bf16[2,4,512,128]{3,2,1,0:T(8,128)(2,1)S(1)} %get-tuple-element.15), channel_id=1, source_target_pairs={{0,8},{8,16},{16,24},{24,0},{4,12},{12,20},{20,28},{28,4},{1,9},{9... | collective-permute-start | bytes 3145736 | tf_op jit(solution)/shard_map/ppermute | solution.py:143
  280.9 87.2 %collective-permute-start.6 = (bf16[2,4,512,128]{3,2,1,0:T(8,128)(2,1)S(1)}, bf16[2,4,512,128]{3,2,1,0:T(8,128)(2,1)S(1)}, u32[]{:S(2)}, u32[]{:S(2)}) collective-permute-start(bf16[2,4,512,128]{3,2,1,0:T(8,128)(2,1)S(1)} %get-tuple-element.16), channel_id=1, source_target_pairs={{0,16},{8,24},{16,0},{24,8},{4,20},{12,28},{20,4},{28,12},{1,17},{... | collective-permute-start | bytes 3145736 | tf_op jit(solution)/shard_map/ppermute | solution.py:143
  282.1 87.2 %collective-permute-start.5 = (bf16[2,4,512,128]{3,2,1,0:T(8,128)(2,1)S(1)}, bf16[2,4,512,128]{3,2,1,0:T(8,128)(2,1)S(1)}, u32[]{:S(2)}, u32[]{:S(2)}) collective-permute-start(bf16[2,4,512,128]{3,2,1,0:T(8,128)(2,1)S(1)} %get-tuple-element.17), channel_id=1, source_target_pairs={{0,24},{8,0},{16,8},{24,16},{4,28},{12,4},{20,12},{28,20},{1,25},{... | collective-permute-start | bytes 3145736 | tf_op jit(solution)/shard_map/ppermute | solution.py:143
  371.5 5.2 %copy-start.11 = (pred[4]{0:T(512)(128)(4,1)S(1)}, pred[4]{0:T(512)(128)(4,1)}, u32[]{:S(2)}) copy-start(pred[4]{0:T(512)(128)(4,1)} %get-tuple-element.39) | copy-start | bytes 16

commit v2 on v1

--- a/solution.py
+++ b/solution.py
@@ -3,6 +3,8 @@
 import jax
 import jax.numpy as jnp
 from jax import lax
+from jax.experimental import pallas as pl
+from jax.experimental.pallas import tpu as pltpu
 from jax.sharding import PartitionSpec as P
 
 BLK = 512
@@ -54,6 +56,62 @@
     return attended, grad_query, key_terms, value_terms
 
 
+def attention_kernel(flag_ref, q_ref, g_ref, k_ref, v_ref, att_ref, dq_ref, kt_ref, vt_ref):
+    place = pl.program_id(0)
+    q = q_ref[0]
+    g = g_ref[0]
+    k = k_ref[0]
+    v = v_ref[0]
+    scaling = 1.0 / math.sqrt(q.shape[-1])
+    rows_by_rows = (((1,), (1,)), ((), ()))
+    cols_by_cols = (((0,), (0,)), ((), ()))
+    scores = lax.dot_general(q, k, rows_by_rows, preferred_element_type=jnp.float32) * scaling
+    col = lax.broadcasted_iota(jnp.int32, scores.shape, 1)
+    kill = jnp.where(place == 0, flag_ref[0], 0)
+    masked = jnp.logical_and(jnp.logical_and(col >= BLK, col < 2 * BLK), kill > 0)
+    scores = jnp.where(masked, -jnp.inf, scores)
+    highest = jnp.max(scores, axis=1, keepdims=True)
+    weights = jnp.exp(scores - highest)
+    shares = weights / jnp.sum(weights, axis=1, keepdims=True)
+    shares_low = shares.astype(jnp.bfloat16)
+    attended = jnp.dot(shares_low, v, preferred_element_type=jnp.float32).astype(jnp.bfloat16)
+    att_ref[0] = attended
+    row_dot = jnp.sum(g.astype(jnp.float32) * attended.astype(jnp.float32), axis=1, keepdims=True)
+    grad_probs = lax.dot_general(g, v, rows_by_rows, preferred_element_type=jnp.float32)
+    dscore = (shares * (grad_probs - row_dot)).astype(jnp.bfloat16)
+    dq_ref[0] = (jnp.dot(dscore, k, preferred_element_type=jnp.float32) * scaling).astype(jnp.bfloat16)
+    kt_ref[0] = lax.dot_general(dscore, q, cols_by_cols, preferred_element_type=jnp.float32) * scaling
+    vt_ref[0] = lax.dot_general(shares_low, g, cols_by_cols, preferred_element_type=jnp.float32)
+
+
+def fused_terms(q_all, g_all, key_sets, value_sets, first_masked):
+    places, rows, width = q_all.shape
+    keys = key_sets.shape[1]
+    row_spec = pl.BlockSpec((1, rows, width), lambda p, flag: (p, 0, 0))
+    key_spec = pl.BlockSpec((1, keys, width), lambda p, flag: (p, 0, 0))
+    flops = 12 * places * rows * keys * width
+    return pl.pallas_call(
+        attention_kernel,
+        grid_spec=pltpu.PrefetchScalarGridSpec(
+            num_scalar_prefetch=1,
+            grid=(places,),
+            in_specs=[row_spec, row_spec, key_spec, key_spec],
+            out_specs=[row_spec, row_spec, key_spec, key_spec],
+        ),
+        out_shape=[
+            jax.ShapeDtypeStruct((places, rows, width), jnp.bfloat16),
+            jax.ShapeDtypeStruct((places, rows, width), jnp.bfloat16),
+            jax.ShapeDtypeStruct((places, keys, width), jnp.float32),
+            jax.ShapeDtypeStruct((places, keys, width), jnp.float32),
+        ],
+        cost_estimate=pl.CostEstimate(
+            flops=flops,
+            transcendentals=places * rows * keys,
+            bytes_accessed=places * (rows * width * 8 + keys * width * 20),
+        ),
+    )(first_masked, q_all, g_all, key_sets, value_sets)
+
+
 def interleave(even, odd):
     return jnp.stack([even, odd], axis=1).reshape((-1,) + even.shape[1:])
 
@@ -107,17 +165,9 @@
     value_sets = jnp.concatenate([v_all, v_window, v_partner], axis=1)
 
     place_ids = jnp.arange(places, dtype=jnp.int32)
-    first_block = jnp.logical_and(segment == 0, place_ids == 0)
-    usable = jnp.concatenate(
-        [
-            jnp.ones((places, BLK), jnp.bool_),
-            jnp.broadcast_to(jnp.logical_not(first_block)[:, None], (places, BLK)),
-            jnp.ones((places, BLK), jnp.bool_),
-        ],
-        axis=1,
-    )
-    attended, grad_query, key_terms, value_terms = block_terms(
-        q_all, key_sets, value_sets, g_all, usable
+    first_masked = (segment == 0).astype(jnp.int32).reshape(1)
+    attended, grad_query, key_terms, value_terms = fused_terms(
+        q_all, g_all, key_sets, value_sets, first_masked
     )
     terms = jnp.stack([key_terms, value_terms], axis=1)
     own_part = terms[:, :, :BLK]

time: 382 us -> 340 us (0.89)
  the two profiles are of different devices: /device:TPU:14 before, /device:TPU:0 now
where the time goes in v2:
time: 340 us
  waiting for transfers between devices  232 us (68%)
  other arithmetic  34 us (10%)
  Pallas kernels  31.1 us (9%)
  local copies, waits for them, and re-layouts  30.8 us (9%)
  starting transfers between devices  11.5 us (3%)
    ppermute x3, waiting for transfers between devices, body(): received.append(lax.ppermute(send, 'seq', group_pairs(nseg, group, shift)))  89 us
    ppermute x3, waiting for transfers between devices, body(): lax.ppermute(send, 'seq', group_pairs(nseg, group, group - shift))  85.1 us
    ppermute x1, waiting for transfers between devices, body(): window_back = lax.ppermute(ret, 'seq', back_pairs)  39.3 us
    pallas_call x1, Pallas kernels, fused_terms(): pl.pallas_call(attention_kernel, grid_spec=pltpu.PrefetchScalarGridSpec(n...  31.1 us
    ppermute x1, waiting for transfers between devices, body(): window_kv = lax.ppermute(odd_send, 'seq', next_segment_pairs(nseg, group))  18.2 us
    another operation x1, other arithmetic, body(): terms = jnp.stack([key_terms, value_terms], axis=1)  8.01 us
  transfers between devices with their start and end apart: 8, of which 7 were waited for; matrix products, arithmetic and copies ran while one was open for 3% of the time, Pallas kernels for 0%

profile of v2, /device:TPU:0, one launch (start us, length us, event | category | flops | bytes accessed | tf_op | source)
XLA Modules:
  0.0 339.9 jit_solution(2473582158719999660)
XLA Ops:
  0.7 2.5 pad_maximum_fusion.1
  3.2 1.3 constant_dynamic-slice_fusion.2
  4.5 5.0 %collective-permute-start.2 = (bf16[4,2,512,128]{3,2,1,0:T(8,128)(2,1)}, bf16[4,2,512,128]{3,2,1,0:T(8,128)(2,1)}, u32[]{:S(2)}, u32[]{:S(2)}) collective-permute-start(bf16[4,2,512,128]{3,2,1,0:T(8,128)(2,1)} %get-tuple-element.33), channel_id=1, source_target_pairs={{0,24},{8,0},{16,8},{24,16},{4,28},{12,4},{20,12},{28,20},{1,25},{... | collective-permute-start | bytes 3145736 | tf_op jit(solution)/shard_map/ppermute | solution.py:143
  10.6 22.8 %collective-permute-done.2 = bf16[4,2,512,128]{3,2,1,0:T(8,128)(2,1)} collective-permute-done((bf16[4,2,512,128]{3,2,1,0:T(8,128)(2,1)}, bf16[4,2,512,128]{3,2,1,0:T(8,128)(2,1)}, u32[]{:S(2)}, u32[]{:S(2)}) %collective-permute-start.2) | collective-permute-done | bytes 1048608 | tf_op jit(solution)/shard_map/ppermute | solution.py:143
  33.4 23.5 %collective-permute-done = bf16[4,2,512,128]{3,2,1,0:T(8,128)(2,1)} collective-permute-done((bf16[4,2,512,128]{3,2,1,0:T(8,128)(2,1)S(1)}, bf16[4,2,512,128]{3,2,1,0:T(8,128)(2,1)}, u32[]{:S(2)}, u32[]{:S(2)}) %collective-permute-start) | collective-permute-done | bytes 1048608 | tf_op jit(solution)/shard_map/ppermute | solution.py:143
  56.9 42.7 %collective-permute-done.1 = bf16[4,2,512,128]{3,2,1,0:T(8,128)(2,1)} collective-permute-done((bf16[4,2,512,128]{3,2,1,0:T(8,128)(2,1)S(1)}, bf16[4,2,512,128]{3,2,1,0:T(8,128)(2,1)}, u32[]{:S(2)}, u32[]{:S(2)}) %collective-permute-start.1) | collective-permute-done | bytes 1048608 | tf_op jit(solution)/shard_map/ppermute | solution.py:143
  99.6 3.6 %pad_maximum_fusion.2 = bf16[4,4,2,512,128]{4,3,2,1,0:T(8,128)(2,1)} fusion(bf16[1,4,2,512,128]{4,3,2,1,0:T(8,128)(2,1)} %bitcast.10, bf16[1,4,2,512,128]{4,3,2,1,0:T(8,128)(2,1)} %bitcast.8, bf16[1,4,2,512,128]{4,3,2,1,0:T(8,128)(2,1)} %bitcast.6, bf16[1,4,2,512,128]{4,3,2,1,0:T(8,128)(2,1)S(1)} %get-tuple-element.32), kind=kLoop, calls=%fused_computation.13 | loop fusion | flops 6291456 | bytes 8388608 | tf_op jit(solution)/shard_map/stack | solution.py:144
  103.2 5.3 %gather_fusion = bf16[4,4,2,512,128]{4,3,2,1,0:T(8,128)(2,1)} fusion(bf16[4,4,2,512,128]{4,3,2,1,0:T(8,128)(2,1)} %pad_maximum_fusion.2, s32[1024]{0:T(1024)S(1)} %pad_clamp_fusion.3), kind=kCustom, calls=%fused_computation.2 | custom fusion | bytes 8388624 | tf_op jit(solution)/shard_map/jit(_take)/gather | solution.py:146
  108.4 2.7 select_bitcast_fusion
  111.1 1.6 fusion.17
  115.7 1.5 collective-permute-start.3
  118.6 1.7 gather_fusion.4
  120.3 1.5 broadcast_select_fusion.1
  121.8 18.2 %collective-permute-done.3 = bf16[4,2,512,128]{3,2,0,1:T(8,128)(2,1)} collective-permute-done((bf16[4,2,512,128]{3,2,0,1:T(8,128)(2,1)}, bf16[4,2,512,128]{3,2,0,1:T(8,128)(2,1)}, u32[]{:S(2)}, u32[]{:S(2)}) %collective-permute-start.3) | collective-permute-done | bytes 1048608 | tf_op jit(solution)/shard_map/ppermute | solution.py:152
  141.7 1.8 pad_maximum_fusion.7.v_ref
  143.5 1.7 pad_maximum_fusion.6.k_ref
  145.2 31.1 %shard_map.84 = (bf16[8,512,128]{2,1,0:T(8,128)(2,1)}, bf16[8,512,128]{2,1,0:T(8,128)(2,1)}, f32[8,1536,128]{2,1,0:T(8,128)}, f32[8,1536,128]{2,1,0:T(8,128)}) custom-call(s32[1]{0:T(128)} %bitcast.flag_ref, bf16[8,512,128]{2,1,0:T(8,128)(2,1)} %bitcast.86, bf16[8,512,128]{2,1,0:T(8,128)(2,1)} %bitcast.85, bf16[8,1536,128]{2,1,0:T(8,128)(2,1)} %pad_maximum_fusion.6.k_ref, ...), custom_call_target="tpu_custom_call" | custom-call | flops 9663676416 | bytes 35651584 | tf_op jit(solution)/shard_map/pallas_call | solution.py:93
  176.3 8.0 %pad_maximum_fusion = (f32[8,2,512,128]{3,2,0,1:T(8,128)}, f32[8,2,512,128]{3,2,0,1:T(8,128)}, f32[8,2,512,128]{3,2,0,1:T(8,128)S(1)}) fusion(f32[8,1,1536,128]{3,2,0,1:T(8,128)} %bitcast.76, f32[8,1,1536,128]{3,2,0,1:T(8,128)} %bitcast.75), kind=kLoop, calls=%fused_computation.11 | loop fusion | flops 3145728 | bytes 25165824 | tf_op jit(solution)/shard_map/stack | solution.py:172
  184.6 1.8 slice_bitcast_fusion
  186.4 1.5 collective-permute-start.4
  188.0 5.0 %gather_fusion.1 = f32[8,2,512,128]{3,2,1,0:T(8,128)} fusion(f32[8,2,512,128]{3,2,0,1:T(8,128)} %get-tuple-element.15, s32[1024]{0:T(1024)S(1)} %pad_clamp_fusion.1), kind=kCustom, calls=%fused_computation.3 | custom fusion | bytes 8388640 | tf_op jit(solution)/shard_map/jit(_take)/gather | solution.py:185
  192.9 39.3 %collective-permute-done.4 = f32[4,2,512,128]{3,2,0,1:T(8,128)} collective-permute-done((f32[4,2,512,128]{3,2,0,1:T(8,128)}, f32[4,2,512,128]{3,2,0,1:T(8,128)}, u32[]{:S(2)}, u32[]{:S(2)}) %collective-permute-start.4) | collective-permute-done | bytes 2097184 | tf_op jit(solution)/shard_map/ppermute | solution.py:180
  232.3 1.9 pad_maximum_fusion.3
  234.5 1.8 copy-done
  236.3 1.3 copy-done.1
  240.1 1.8 collective-permute-start.5
  242.6 22.9 %collective-permute-done.5 = bf16[2,4,512,128]{3,2,1,0:T(8,128)(2,1)S(1)} collective-permute-done((bf16[2,4,512,128]{3,2,1,0:T(8,128)(2,1)S(1)}, bf16[2,4,512,128]{3,2,1,0:T(8,128)(2,1)S(1)}, u32[]{:S(2)}, u32[]{:S(2)}) %collective-permute-start.5) | collective-permute-done | bytes 1048608 | tf_op jit(solution)/shard_map/ppermute | solution.py:193
  265.5 62.2 %collective-permute-done.6 = bf16[2,4,512,128]{3,2,1,0:T(8,128)(2,1)S(1)} collective-permute-done((bf16[2,4,512,128]{3,2,1,0:T(8,128)(2,1)S(1)}, bf16[2,4,512,128]{3,2,1,0:T(8,128)(2,1)S(1)}, u32[]{:S(2)}, u32[]{:S(2)}) %collective-permute-start.6) | collective-permute-done | bytes 1048608 | tf_op jit(solution)/shard_map/ppermute | solution.py:193
  327.7 2.2 pad_maximum_fusion.5
  329.9 5.3 %gather_fusion.2 = bf16[4,2,4,512,128]{4,3,2,1,0:T(8,128)(2,1)} fusion(bf16[4,2,4,512,128]{4,3,2,1,0:T(8,128)(2,1)} %pad_maximum_fusion.5, s32[1024]{0:T(1024)S(1)} %pad_clamp_fusion), kind=kCustom, calls=%fused_computation.4 | custom fusion | bytes 8388624 | tf_op jit(solution)/shard_map/jit(_take)/gather | solution.py:196
  335.2 2.7 broadcast_select_fusion
  337.8 2.1 fusion.16
  (45 shorter events, 10.9 us)
Async XLA Ops:
  4.5 28.9 %collective-permute-start.2 = (bf16[4,2,512,128]{3,2,1,0:T(8,128)(2,1)}, bf16[4,2,512,128]{3,2,1,0:T(8,128)(2,1)}, u32[]{:S(2)}, u32[]{:S(2)}) collective-permute-start(bf16[4,2,512,128]{3,2,1,0:T(8,128)(2,1)} %get-tuple-element.33), channel_id=1, source_target_pairs={{0,24},{8,0},{16,8},{24,16},{4,28},{12,4},{20,12},{28,20},{1,25},{... | collective-permute-start | bytes 3145736 | tf_op jit(solution)/shard_map/ppermute | solution.py:143
  9.6 47.4 %collective-permute-start = (bf16[4,2,512,128]{3,2,1,0:T(8,128)(2,1)S(1)}, bf16[4,2,512,128]{3,2,1,0:T(8,128)(2,1)}, u32[]{:S(2)}, u32[]{:S(2)}) collective-permute-start(bf16[4,2,512,128]{3,2,1,0:T(8,128)(2,1)S(1)} %get-tuple-element.35), channel_id=1, source_target_pairs={{0,8},{8,16},{16,24},{24,0},{4,12},{12,20},{20,28},{28,4},{1,9},{9... | collective-permute-start | bytes 3145736 | tf_op jit(solution)/shard_map/ppermute | solution.py:143
  9.6 90.0 %collective-permute-start.1 = (bf16[4,2,512,128]{3,2,1,0:T(8,128)(2,1)S(1)}, bf16[4,2,512,128]{3,2,1,0:T(8,128)(2,1)}, u32[]{:S(2)}, u32[]{:S(2)}) collective-permute-start(bf16[4,2,512,128]{3,2,1,0:T(8,128)(2,1)S(1)} %get-tuple-element.34), channel_id=1, source_target_pairs={{0,16},{8,24},{16,0},{24,8},{4,20},{12,28},{20,4},{28,12},{1,17},{... | collective-permute-start | bytes 3145736 | tf_op jit(solution)/shard_map/ppermute | solution.py:143
  115.7 24.3 %collective-permute-start.3 = (bf16[4,2,512,128]{3,2,0,1:T(8,128)(2,1)}, bf16[4,2,512,128]{3,2,0,1:T(8,128)(2,1)}, u32[]{:S(2)}, u32[]{:S(2)}) collective-permute-start(bf16[4,2,512,128]{3,2,0,1:T(8,128)(2,1)} %fusion.4), channel_id=1, source_target_pairs={{0,4},{8,12},{16,20},{24,28},{4,0},{12,8},{20,16},{28,24},{1,5},{9... | collective-permute-start | bytes 3145736 | tf_op jit(solution)/shard_map/ppermute | solution.py:152
  120.3 21.0 %copy-start.3 = (bf16[4,1,512,128]{3,2,0,1:T(8,128)(2,1)S(1)}, bf16[4,1,512,128]{3,2,0,1:T(8,128)(2,1)}, u32[]{:S(2)}) copy-start(bf16[4,1,512,128]{3,2,0,1:T(8,128)(2,1)} %get-tuple-element.38) | copy-start | bytes 1572868
  121.8 19.7 %copy-start.2 = (bf16[4,1,512,128]{3,2,0,1:T(8,128)(2,1)S(1)}, bf16[4,1,512,128]{3,2,0,1:T(8,128)(2,1)}, u32[]{:S(2)}) copy-start(bf16[4,1,512,128]{3,2,0,1:T(8,128)(2,1)} %get-tuple-element.41) | copy-start | bytes 1572868
  186.4 45.9 %collective-permute-start.4 = (f32[4,2,512,128]{3,2,0,1:T(8,128)}, f32[4,2,512,128]{3,2,0,1:T(8,128)}, u32[]{:S(2)}, u32[]{:S(2)}) collective-permute-start(f32[4,2,512,128]{3,2,0,1:T(8,128)} %get-tuple-element.27), channel_id=1, source_target_pairs={{4,0},{12,8},{20,16},{28,24},{0,4},{8,12},{16,20},{24,28},{5,1},{1... | collective-permute-start | bytes 6291464 | tf_op jit(solution)/shard_map/ppermute | solution.py:180
  234.1 2.2 copy-start
  234.2 3.5 %copy-start.1 = (f32[8,2,512,128]{3,2,0,1:T(8,128)S(1)}, f32[8,2,512,128]{3,2,0,1:T(8,128)}, u32[]{:S(2)}) copy-start(f32[8,2,512,128]{3,2,0,1:T(8,128)} %get-tuple-element.16) | copy-start | bytes 12582916
  237.6 1.2 copy-start.4
  237.6 1.5 copy-start.5
  240.1 25.5 %collective-permute-start.5 = (bf16[2,4,512,128]{3,2,1,0:T(8,128)(2,1)S(1)}, bf16[2,4,512,128]{3,2,1,0:T(8,128)(2,1)S(1)}, u32[]{:S(2)}, u32[]{:S(2)}) collective-permute-start(bf16[2,4,512,128]{3,2,1,0:T(8,128)(2,1)S(1)} %get-tuple-element.25), channel_id=1, source_target_pairs={{0,24},{8,0},{16,8},{24,16},{4,28},{12,4},{20,12},{28,20},{1,25},{... | collective-permute-start | bytes 3145736 | tf_op jit(solution)/shard_map/ppermute | solution.py:193
  241.9 85.8 %collective-permute-start.6 = (bf16[2,4,512,128]{3,2,1,0:T(8,128)(2,1)S(1)}, bf16[2,4,512,128]{3,2,1,0:T(8,128)(2,1)S(1)}, u32[]{:S(2)}, u32[]{:S(2)}) collective-permute-start(bf16[2,4,512,128]{3,2,1,0:T(8,128)(2,1)S(1)} %get-tuple-element.24), channel_id=1, source_target_pairs={{0,16},{8,24},{16,0},{24,8},{4,20},{12,28},{20,4},{28,12},{1,17},{... | collective-permute-start | bytes 3145736 | tf_op jit(solution)/shard_map/ppermute | solution.py:193
  241.9 85.8 %collective-permute-start.7 = (bf16[2,4,512,128]{3,2,1,0:T(8,128)(2,1)S(1)}, bf16[2,4,512,128]{3,2,1,0:T(8,128)(2,1)S(1)}, u32[]{:S(2)}, u32[]{:S(2)}) collective-permute-start(bf16[2,4,512,128]{3,2,1,0:T(8,128)(2,1)S(1)} %get-tuple-element.23), channel_id=1, source_target_pairs={{0,8},{8,16},{16,24},{24,0},{4,12},{12,20},{20,28},{28,4},{1,9},{9... | collective-permute-start | bytes 3145736 | tf_op jit(solution)/shard_map/ppermute | solution.py:193

commit v3 on v2

--- a/solution.py
+++ b/solution.py
@@ -116,42 +116,55 @@
     return jnp.stack([even, odd], axis=1).reshape((-1,) + even.shape[1:])
 
 
+def gather_group(x, within, nseg, group):
+    received = [lax.dynamic_index_in_dim(x, within, axis=0, keepdims=False)]
+    for shift in range(1, group):
+        send = lax.dynamic_index_in_dim(x, (within + shift) % group, axis=0, keepdims=False)
+        received.append(lax.ppermute(send, "seq", group_pairs(nseg, group, shift)))
+    order = (within - jnp.arange(group, dtype=jnp.int32)) % group
+    return jnp.take(jnp.stack(received), order, axis=0)
+
+
+def scatter_group(y, within, nseg, group):
+    returned = [lax.dynamic_index_in_dim(y, within, axis=0, keepdims=False)]
+    for shift in range(1, group):
+        send = lax.dynamic_index_in_dim(y, (within - shift) % group, axis=0, keepdims=False)
+        returned.append(lax.ppermute(send, "seq", group_pairs(nseg, group, group - shift)))
+    order = (jnp.arange(group, dtype=jnp.int32) - within) % group
+    return jnp.take(jnp.stack(returned), order, axis=0)
+
+
 def body(queries, key_rows, value_rows, grad_out, partner_pos):
     heads, row_count, width = queries.shape
     blocks = row_count // BLK
     places = partner_pos.shape[2]
     group = places // blocks
-    if heads != group:
-        raise ValueError("heads mismatch")
+    if heads != group or blocks != 2:
+        raise ValueError("layout mismatch")
     nseg = lax.axis_size("seq") // group
     device = lax.axis_index("seq")
     segment = device % nseg
     within = device // nseg
 
-    data = jnp.stack(
-        [
-            queries.reshape(heads, blocks, BLK, width),
-            grad_out.reshape(heads, blocks, BLK, width),
-            key_rows.reshape(heads, blocks, BLK, width),
-            value_rows.reshape(heads, blocks, BLK, width),
-        ],
-        axis=1,
-    )
-    received = [lax.dynamic_index_in_dim(data, within, axis=0, keepdims=False)]
-    for shift in range(1, group):
-        send = lax.dynamic_index_in_dim(data, (within + shift) % group, axis=0, keepdims=False)
-        received.append(lax.ppermute(send, "seq", group_pairs(nseg, group, shift)))
-    received = jnp.stack(received)
-    order = (within - jnp.arange(group, dtype=jnp.int32)) % group
-    local = jnp.take(received, order, axis=0)
-    local = jnp.swapaxes(local, 0, 1).reshape(4, group * blocks, BLK, width)
-    q_all, g_all, k_all, v_all = local[0], local[1], local[2], local[3]
+    def split(x):
+        return x.reshape(heads, blocks, BLK, width)
+
+    q4, g4, k4, v4 = split(queries), split(grad_out), split(key_rows), split(value_rows)
+    kv_local = gather_group(jnp.stack([k4, v4], axis=1), within, nseg, group)
+    k_all = kv_local[:, 0].reshape(places, BLK, width)
+    v_all = kv_local[:, 1].reshape(places, BLK, width)
+    kv_local, qd_odd = lax.optimization_barrier(
+        (kv_local, jnp.stack([q4[:, 1], g4[:, 1]], axis=1))
+    )
+    qd_odd = gather_group(qd_odd, within, nseg, group)
+    qd_odd, qd_even = lax.optimization_barrier(
+        (qd_odd, jnp.stack([q4[:, 0], g4[:, 0]], axis=1))
+    )
+    qd_even = gather_group(qd_even, within, nseg, group)
 
     odd_kv = jnp.stack([k_all[1::2], v_all[1::2]], axis=1)
     odd_send = jnp.where(segment == nseg - 1, jnp.roll(odd_kv, 1, axis=0), odd_kv)
     window_kv = lax.ppermute(odd_send, "seq", next_segment_pairs(nseg, group))
-    k_window = interleave(window_kv[:, 0], k_all[0::2])
-    v_window = interleave(window_kv[:, 1], v_all[0::2])
 
     my_partners = lax.dynamic_index_in_dim(
         lax.dynamic_index_in_dim(partner_pos, within, axis=0, keepdims=False),
@@ -161,15 +174,22 @@
     )
     k_partner = jnp.take(k_all, my_partners, axis=0)
     v_partner = jnp.take(v_all, my_partners, axis=0)
-    key_sets = jnp.concatenate([k_all, k_window, k_partner], axis=1)
-    value_sets = jnp.concatenate([v_all, v_window, v_partner], axis=1)
-
-    place_ids = jnp.arange(places, dtype=jnp.int32)
+
+    odd_keys = jnp.concatenate([k_all[1::2], k_all[0::2], k_partner[1::2]], axis=1)
+    odd_values = jnp.concatenate([v_all[1::2], v_all[0::2], v_partner[1::2]], axis=1)
+    att_odd, dq_odd, kt_odd, vt_odd = fused_terms(
+        qd_odd[:, 0], qd_odd[:, 1], odd_keys, odd_values, jnp.zeros((1,), jnp.int32)
+    )
+    sent_odd = scatter_group(jnp.stack([att_odd, dq_odd], axis=1), within, nseg, group)
+
+    even_keys = jnp.concatenate([k_all[0::2], window_kv[:, 0], k_partner[0::2]], axis=1)
+    even_values = jnp.concatenate([v_all[0::2], window_kv[:, 1], v_partner[0::2]], axis=1)
     first_masked = (segment == 0).astype(jnp.int32).reshape(1)
-    attended, grad_query, key_terms, value_terms = fused_terms(
-        q_all, g_all, key_sets, value_sets, first_masked
-    )
-    terms = jnp.stack([key_terms, value_terms], axis=1)
+    att_even, dq_even, kt_even, vt_even = fused_terms(
+        qd_even[:, 0], qd_even[:, 1], even_keys, even_values, first_masked
+    )
+
+    terms = interleave(jnp.stack([kt_even, vt_even], axis=1), jnp.stack([kt_odd, vt_odd], axis=1))
     own_part = terms[:, :, :BLK]
     window_part = terms[:, :, BLK : 2 * BLK]
     partner_part = terms[:, :, 2 * BLK :]
@@ -178,24 +198,32 @@
     ret = jnp.where(segment == 0, jnp.roll(ret, -1, axis=0), ret)
     back_pairs = [(b, a) for a, b in next_segment_pairs(nseg, group)]
     window_back = lax.ppermute(ret, "seq", back_pairs)
-    window_sum = interleave(window_part[1::2], window_back)
-
+
+    place_ids = jnp.arange(places, dtype=jnp.int32)
     hits = my_partners[None, :] == place_ids[:, None]
     inverse = jnp.sum(jnp.where(hits, place_ids[None, :], 0), axis=1)
     partner_sum = jnp.take(partner_part, inverse, axis=0)
-    grads = (own_part + window_sum + partner_sum).astype(jnp.bfloat16)
-
-    outs = jnp.stack([attended, grad_query, grads[:, 0], grads[:, 1]], axis=1)
-    outs = outs.reshape(group, blocks, 4, BLK, width)
-    returned = [lax.dynamic_index_in_dim(outs, within, axis=0, keepdims=False)]
-    for shift in range(1, group):
-        send = lax.dynamic_index_in_dim(outs, (within - shift) % group, axis=0, keepdims=False)
-        returned.append(lax.ppermute(send, "seq", group_pairs(nseg, group, group - shift)))
-    returned = jnp.stack(returned)
-    head_order = (jnp.arange(group, dtype=jnp.int32) - within) % group
-    result = jnp.take(returned, head_order, axis=0)
+    grads_even = (own_part[0::2] + window_part[1::2] + partner_sum[0::2]).astype(jnp.bfloat16)
+    sent_even = scatter_group(
+        jnp.stack([att_even, dq_even, grads_even[:, 0], grads_even[:, 1]], axis=1),
+        within,
+        nseg,
+        group,
+    )
+    grads_odd = (own_part[1::2] + window_back + partner_sum[1::2]).astype(jnp.bfloat16)
+    sent_last = scatter_group(grads_odd, within, nseg, group)
+
     shape = (heads, row_count, width)
-    return tuple(result[:, :, a].reshape(shape) for a in range(4))
+
+    def joined(even, odd):
+        return jnp.stack([even, odd], axis=1).reshape(shape)
+
+    return (
+        joined(sent_even[:, 0], sent_odd[:, 0]),
+        joined(sent_even[:, 1], sent_odd[:, 1]),
+        joined(sent_even[:, 2], sent_last[:, 0]),
+        joined(sent_even[:, 3], sent_last[:, 1]),
+    )
 
 
 def solution(mesh):

time: 340 us -> 337 us (level)
  waiting for transfers between devices: 232 us -> 128 us
  starting transfers between devices: 11.5 us -> 65.3 us
  other arithmetic: 34 us -> 55.9 us
  local copies, waits for them, and re-layouts: 30.8 us -> 51.7 us
    ppermute x6 -> x18, waiting for transfers between devices: 174 us -> 114 us  [the longest x9 58.6 us: scatter_group(): lax.ppermute(send, 'seq', group_pairs(nseg, group, group - shift))]
    ppermute x6 -> x18, starting transfers between devices: 8.55 us -> 62.4 us  [the longest x9 32.6 us: scatter_group(): lax.ppermute(send, 'seq', group_pairs(nseg, group, group - shift))]
    ppermute x1, waiting for transfers between devices: 39.3 us -> 14.7 us  [body(): window_back = lax.ppermute(ret, 'seq', back_pairs)]
    ppermute x1, waiting for transfers between devices: 18.2 us -> 0.01 us  [body(): window_kv = lax.ppermute(odd_send, 'seq', next_segment_pairs(nseg, group))]
    another operation x4 -> x3, other arithmetic: 3.85 us -> 20.4 us  [interleave(): return jnp.stack([even, odd], axis=1).reshape((-1,) + even.shape[1:])]
    slice x3 -> x9, local copies, waits for them, and re-layouts: 4.96 us -> 14.6 us  [the longest x1 9.08 us: body(): own_part = terms[:, :, :BLK]]
    another operation x4 -> x1, local copies, waits for them, and re-layouts: 1.33 us -> 10.4 us  [interleave(): return jnp.stack([even, odd], axis=1).reshape((-1,) + even.shape[1:])]
    select_n x1 -> x2, other arithmetic: 0.01 us -> 4.67 us  [body(): partner_sum = jnp.take(partner_part, inverse, axis=0)]
  transfers between devices with their start and end apart: 8 -> 20, of which waited for: 7 -> 12; matrix products, arithmetic and copies ran while one was open for 3% -> 8% of each run, Pallas kernels for 0% -> 0%
where the time goes in v3:
time: 337 us; the launch traced here: 336 us
  waiting for transfers between devices  128 us (38%)
  starting transfers between devices  65.3 us (19%)
  other arithmetic  55.9 us (17%)
  local copies, waits for them, and re-layouts  51.7 us (15%)
  Pallas kernels  33.3 us (10%)
    ppermute x9, waiting for transfers between devices, scatter_group(): lax.ppermute(send, 'seq', group_pairs(nseg, group, group - shift))  58.6 us
    ppermute x9, waiting for transfers between devices, gather_group(): received.append(lax.ppermute(send, 'seq', group_pairs(nseg, group, shift)))  55.2 us
    pallas_call x2, Pallas kernels, fused_terms(): pl.pallas_call(attention_kernel, grid_spec=pltpu.PrefetchScalarGridSpec(n...  33.3 us
    ppermute x9, starting transfers between devices, scatter_group(): lax.ppermute(send, 'seq', group_pairs(nseg, group, group - shift))  32.6 us
    ppermute x9, starting transfers between devices, gather_group(): received.append(lax.ppermute(send, 'seq', group_pairs(nseg, group, shift)))  29.7 us
    another operation x3, other arithmetic, interleave(): return jnp.stack([even, odd], axis=1).reshape((-1,) + even.shape[1:])  20.4 us
    ppermute x1, waiting for transfers between devices, body(): window_back = lax.ppermute(ret, 'seq', back_pairs)  14.7 us
    another operation x1, local copies, waits for them, and re-layouts, interleave(): return jnp.stack([even, odd], axis=1).reshape((-1,) + even.shape[1:])  10.4 us
  transfers between devices with their start and end apart: 20, of which 12 were waited for; matrix products, arithmetic and copies ran while one was open for 8% of the time, Pallas kernels for 0%

profile of v3, /device:TPU:0, one launch (start us, length us, event | category | flops | bytes accessed | tf_op | source)
XLA Modules:
  0.0 335.9 jit_solution(11963458433385205364)
XLA Ops:
  0.7 2.8 fusion.4
  3.5 3.0 collective-permute-start
  6.5 2.6 collective-permute-start.1
  14.2 7.5 %collective-permute-done = bf16[2,2,512,128]{3,2,1,0:T(8,128)(2,1)S(1)} collective-permute-done((bf16[2,2,512,128]{3,2,1,0:T(8,128)(2,1)}, bf16[2,2,512,128]{3,2,1,0:T(8,128)(2,1)S(1)}, u32[]{:S(2)}, u32[]{:S(2)}) %collective-permute-start) | collective-permute-done | bytes 524320 | tf_op jit(solution)/shard_map/ppermute | solution.py:123
  21.7 21.7 %collective-permute-done.1 = bf16[2,2,512,128]{3,2,1,0:T(8,128)(2,1)} collective-permute-done((bf16[2,2,512,128]{3,2,1,0:T(8,128)(2,1)}, bf16[2,2,512,128]{3,2,1,0:T(8,128)(2,1)}, u32[]{:S(2)}, u32[]{:S(2)}) %collective-permute-start.1) | collective-permute-done | bytes 524320 | tf_op jit(solution)/shard_map/ppermute | solution.py:123
  44.9 2.1 gather_fusion
  56.3 11.8 %collective-permute-start.3 = (bf16[2,512,128]{2,1,0:T(8,128)(2,1)S(1)}, bf16[2,512,128]{2,1,0:T(8,128)(2,1)S(1)}, u32[]{:S(2)}, u32[]{:S(2)}) collective-permute-start(bf16[2,512,128]{2,1,0:T(8,128)(2,1)S(1)} %get-tuple-element.88), channel_id=1, source_target_pairs={{0,8},{8,16},{16,24},{24,0},{4,12},{12,20},{20,28},{28,4},{1,9},{9... | collective-permute-start | bytes 786440 | tf_op jit(solution)/shard_map/ppermute | solution.py:123
  76.4 9.4 %collective-permute-done.4 = bf16[2,512,128]{2,1,0:T(8,128)(2,1)S(1)} collective-permute-done((bf16[2,512,128]{2,1,0:T(8,128)(2,1)S(1)}, bf16[2,512,128]{2,1,0:T(8,128)(2,1)S(1)}, u32[]{:S(2)}, u32[]{:S(2)}) %collective-permute-start.4) | collective-permute-done | bytes 262176 | tf_op jit(solution)/shard_map/ppermute | solution.py:123
  87.3 6.1 %collective-permute-start.6 = (bf16[2,512,128]{2,1,0:T(8,128)(2,1)S(1)}, bf16[2,512,128]{2,1,0:T(8,128)(2,1)S(1)}, u32[]{:S(2)}, u32[]{:S(2)}) collective-permute-start(bf16[2,512,128]{2,1,0:T(8,128)(2,1)S(1)} %get-tuple-element.74), channel_id=1, source_target_pairs={{0,8},{8,16},{16,24},{24,0},{4,12},{12,20},{20,28},{28,4},{1,9},{9... | collective-permute-start | bytes 786440 | tf_op jit(solution)/shard_map/ppermute | solution.py:123
  93.5 2.3 collective-permute-start.7
  96.9 5.6 %collective-permute-done.6 = bf16[2,512,128]{2,1,0:T(8,128)(2,1)S(1)} collective-permute-done((bf16[2,512,128]{2,1,0:T(8,128)(2,1)S(1)}, bf16[2,512,128]{2,1,0:T(8,128)(2,1)S(1)}, u32[]{:S(2)}, u32[]{:S(2)}) %collective-permute-start.6) | collective-permute-done | bytes 262176 | tf_op jit(solution)/shard_map/ppermute | solution.py:123
  102.6 10.0 %collective-permute-done.7 = bf16[2,512,128]{2,1,0:T(8,128)(2,1)S(1)} collective-permute-done((bf16[2,512,128]{2,1,0:T(8,128)(2,1)S(1)}, bf16[2,512,128]{2,1,0:T(8,128)(2,1)S(1)}, u32[]{:S(2)}, u32[]{:S(2)}) %collective-permute-start.7) | collective-permute-done | bytes 262176 | tf_op jit(solution)/shard_map/ppermute | solution.py:123
  116.1 2.0 pad_maximum_fusion.5
  120.0 16.7 %shard_map.84 = (bf16[4,512,128]{2,1,0:T(8,128)(2,1)}, bf16[4,512,128]{2,1,0:T(8,128)(2,1)}, f32[4,1536,128]{2,1,0:T(8,128)}, f32[4,1536,128]{2,1,0:T(8,128)}) custom-call(s32[1]{0:T(128)} %bitcast.flag_ref, bf16[4,512,128]{2,1,0:T(8,128)(2,1)} %get-tuple-element.70.q_ref, bf16[4,512,128]{2,1,0:T(8,128)(2,1)} %get-tuple-element.69.g_ref, ...), custom_call_target="tpu_custom_call" | custom-call | flops 4831838208 | bytes 17825792 | tf_op jit(solution)/shard_map/pallas_call | solution.py:93
  136.7 5.9 %maximum_bitcast_fusion = f32[4,1,2,1536,128]{4,3,0,2,1:T(8,128)} fusion(f32[4,1,1536,128]{3,2,0,1:T(8,128)} %bitcast.115, f32[4,1,1536,128]{3,2,0,1:T(8,128)} %bitcast.114), kind=kLoop, calls=%fused_computation.10 | loop fusion | flops 1572864 | bytes 12582912 | tf_op jit(solution)/shard_map/stack | solution.py:116
  142.6 16.6 %shard_map.85 = (bf16[4,512,128]{2,1,0:T(8,128)(2,1)}, bf16[4,512,128]{2,1,0:T(8,128)(2,1)}, f32[4,1536,128]{2,1,0:T(8,128)}, f32[4,1536,128]{2,1,0:T(8,128)}) custom-call(s32[1]{0:T(128)} %constant.255.clone.1.flag_ref, bf16[4,512,128]{2,1,0:T(8,128)(2,1)} %get-tuple-element.80.q_ref, bf16[4,512,128]{2,1,0:T(8,128)(2,1)} %get-tuple-element.79.g_ref, ...), custom_call_target="tpu_custom_call" | custom-call | flops 4831838208 | bytes 17825792 | tf_op jit(solution)/shard_map/pallas_call | solution.py:93
  159.2 6.1 %maximum_bitcast_fusion.1 = f32[4,1,2,1536,128]{4,3,0,2,1:T(8,128)} fusion(f32[4,1,1536,128]{3,2,0,1:T(8,128)} %bitcast.117, f32[4,1,1536,128]{3,2,0,1:T(8,128)} %bitcast.116), kind=kLoop, calls=%fused_computation.11 | loop fusion | flops 1572864 | bytes 12582912 | tf_op jit(solution)/shard_map/stack | solution.py:116
  165.4 8.3 %pad_maximum_fusion = f32[4,2,2,1536,128]{4,3,0,2,1:T(8,128)} fusion(f32[4,1,2,1536,128]{4,3,0,2,1:T(8,128)} %maximum_bitcast_fusion.1, f32[4,1,2,1536,128]{4,3,0,2,1:T(8,128)S(1)} %copy-done.1), kind=kLoop, calls=%fused_computation.9 | loop fusion | flops 3145728 | bytes 25165824 | tf_op jit(solution)/shard_map/stack | solution.py:116
  173.7 10.4 %copy.18 = f32[4,2,2,1536,128]{4,3,2,1,0:T(8,128)} copy(f32[4,2,2,1536,128]{4,3,0,2,1:T(8,128)} %pad_maximum_fusion) | data formatting | bytes 25165824 | tf_op jit(solution)/shard_map/stack | solution.py:116
  184.0 9.1 %fusion.26 = (f32[8,2,512,128]{3,2,1,0:T(8,128)}, f32[8,2,512,128]{3,2,1,0:T(8,128)}, f32[8,2,512,128]{3,2,1,0:T(8,128)S(1)}) fusion(f32[8,2,1536,128]{3,2,1,0:T(8,128)} %bitcast.109), kind=kLoop, calls=%fused_computation.143 | loop fusion | bytes 25165824 | tf_op jit(solution)/shard_map/slice | solution.py:193
  198.5 6.7 %collective-permute-start.13 = (bf16[2,512,128]{2,1,0:T(8,128)(2,1)S(1)}, bf16[2,512,128]{2,1,0:T(8,128)(2,1)S(1)}, u32[]{:S(2)}, u32[]{:S(2)}) collective-permute-start(bf16[2,512,128]{2,1,0:T(8,128)(2,1)S(1)} %get-tuple-element.76), channel_id=1, source_target_pairs={{0,24},{8,0},{16,8},{24,16},{4,28},{12,4},{20,12},{28,20},{1,25},{... | collective-permute-start | bytes 786440 | tf_op jit(solution)/shard_map/ppermute | solution.py:132
  206.1 5.0 %gather_fusion.1 = f32[8,2,512,128]{3,2,1,0:T(8,128)} fusion(f32[8,2,512,128]{3,2,1,0:T(8,128)} %get-tuple-element.31, s32[1024]{0:T(1024)S(1)} %pad_clamp_fusion.2), kind=kCustom, calls=%fused_computation.7 | custom fusion | bytes 8388640 | tf_op jit(solution)/shard_map/jit(_take)/gather | solution.py:205
  211.1 4.7 %broadcast_select_fusion = f32[8,2,512,128]{3,2,1,0:T(8,128)} fusion(f32[8,2,512,128]{3,2,1,0:T(8,128)} %gather_fusion.1, pred[8]{0:T(512)(128)(4,1)S(1)} %compare_and_fusion.2), kind=kLoop, calls=%fused_computation.26 | loop fusion | flops 1048576 | bytes 8388616 | tf_op jit(solution)/shard_map/jit(_take)/select_n | solution.py:205
  215.8 13.1 %collective-permute-done.14 = bf16[2,512,128]{2,1,0:T(8,128)(2,1)S(1)} collective-permute-done((bf16[2,512,128]{2,1,0:T(8,128)(2,1)S(1)}, bf16[2,512,128]{2,1,0:T(8,128)(2,1)S(1)}, u32[]{:S(2)}, u32[]{:S(2)}) %collective-permute-start.14) | collective-permute-done | bytes 262176 | tf_op jit(solution)/shard_map/ppermute | solution.py:132
  229.8 14.7 %collective-permute-done.16 = f32[4,2,512,128]{3,2,1,0:T(8,128)} collective-permute-done((f32[4,2,512,128]{3,2,1,0:T(8,128)}, f32[4,2,512,128]{3,2,1,0:T(8,128)}, u32[]{:S(2)}, u32[]{:S(2)}) %collective-permute-start.16) | collective-permute-done | bytes 2097184 | tf_op jit(solution)/shard_map/ppermute | solution.py:200
  244.5 5.4 %add_convert_fusion = (bf16[4,2,512,128]{3,2,1,0:T(8,128)(2,1)S(1)}, bf16[4,2,512,128]{3,2,1,0:T(8,128)(2,1)S(1)}) fusion(f32[8,2,512,128]{3,2,1,0:T(8,128)} %broadcast_select_fusion, f32[4,2,512,128]{3,2,1,0:T(8,128)} %collective-permute-done.16, f32[8,2,512,128]{3,2,1,0:T(8,128)} %get-tuple-element.30, f32[8,2,512,128]{3,2,1,0:T(8,128)} %copy-done), kind=kLoop, calls=%fused_computation.24 | loop fusion | flops 3145728 | bytes 14680064 | tf_op jit(solution)/shard_map/convert_element_type | solution.py:213
  250.0 6.4 %collective-permute-start.17 = (bf16[2,512,128]{2,1,0:T(8,128)(2,1)S(1)}, bf16[2,512,128]{2,1,0:T(8,128)(2,1)S(1)}, u32[]{:S(2)}, u32[]{:S(2)}) collective-permute-start(bf16[2,512,128]{2,1,0:T(8,128)(2,1)S(1)} %get-tuple-element.54), channel_id=1, source_target_pairs={{0,24},{8,0},{16,8},{24,16},{4,28},{12,4},{20,12},{28,20},{1,25},{... | collective-permute-start | bytes 786440 | tf_op jit(solution)/shard_map/ppermute | solution.py:132
  259.3 3.8 %collective-permute-start.10 = (bf16[4,512,128]{2,1,0:T(8,128)(2,1)}, bf16[4,512,128]{2,1,0:T(8,128)(2,1)}, u32[]{:S(2)}, u32[]{:S(2)}) collective-permute-start(bf16[4,512,128]{2,1,0:T(8,128)(2,1)} %get-tuple-element.42), channel_id=1, source_target_pairs={{0,24},{8,0},{16,8},{24,16},{4,28},{12,4},{20,12},{28,20},{1,25},{... | collective-permute-start | bytes 1572872 | tf_op jit(solution)/shard_map/ppermute | solution.py:132
  263.2 13.5 %collective-permute-start.12 = (bf16[4,512,128]{2,1,0:T(8,128)(2,1)}, bf16[4,512,128]{2,1,0:T(8,128)(2,1)}, u32[]{:S(2)}, u32[]{:S(2)}) collective-permute-start(bf16[4,512,128]{2,1,0:T(8,128)(2,1)} %get-tuple-element.40), channel_id=1, source_target_pairs={{0,8},{8,16},{16,24},{24,0},{4,12},{12,20},{20,28},{28,4},{1,9},{9... | collective-permute-start | bytes 1572872 | tf_op jit(solution)/shard_map/ppermute | solution.py:132
  276.7 5.1 %collective-permute-done.18 = bf16[2,512,128]{2,1,0:T(8,128)(2,1)S(1)} collective-permute-done((bf16[2,512,128]{2,1,0:T(8,128)(2,1)S(1)}, bf16[2,512,128]{2,1,0:T(8,128)(2,1)S(1)}, u32[]{:S(2)}, u32[]{:S(2)}) %collective-permute-start.18) | collective-permute-done | bytes 262176 | tf_op jit(solution)/shard_map/ppermute | solution.py:132
  285.8 39.1 %collective-permute-done.11 = bf16[4,512,128]{2,1,0:T(8,128)(2,1)} collective-permute-done((bf16[4,512,128]{2,1,0:T(8,128)(2,1)}, bf16[4,512,128]{2,1,0:T(8,128)(2,1)}, u32[]{:S(2)}, u32[]{:S(2)}) %collective-permute-start.11) | collective-permute-done | bytes 524320 | tf_op jit(solution)/shard_map/ppermute | solution.py:132
  326.6 2.1 gather_fusion.2
  (130 shorter events, 54.9 us)
Async XLA Ops:
  0.7 9.8 %copy-start.16 = (bf16[4,1024,128]{2,1,0:T(8,128)(2,1)S(1)}, bf16[4,1024,128]{2,1,0:T(8,128)(2,1)}, u32[]{:S(2)}) copy-start(bf16[4,1024,128]{2,1,0:T(8,128)(2,1)} %param.9) | copy-start | bytes 3145732
  3.5 18.2 %collective-permute-start = (bf16[2,2,512,128]{3,2,1,0:T(8,128)(2,1)}, bf16[2,2,512,128]{3,2,1,0:T(8,128)(2,1)S(1)}, u32[]{:S(2)}, u32[]{:S(2)}) collective-permute-start(bf16[2,2,512,128]{3,2,1,0:T(8,128)(2,1)} %get-tuple-element.46), channel_id=1, source_target_pairs={{0,8},{8,16},{16,24},{24,0},{4,12},{12,20},{20,28},{28,4},{1,9},{9... | collective-permute-start | bytes 1572872 | tf_op jit(solution)/shard_map/ppermute | solution.py:123
  6.5 36.9 %collective-permute-start.1 = (bf16[2,2,512,128]{3,2,1,0:T(8,128)(2,1)}, bf16[2,2,512,128]{3,2,1,0:T(8,128)(2,1)}, u32[]{:S(2)}, u32[]{:S(2)}) collective-permute-start(bf16[2,2,512,128]{3,2,1,0:T(8,128)(2,1)} %get-tuple-element.47), channel_id=1, source_target_pairs={{0,16},{8,24},{16,0},{24,8},{4,20},{12,28},{20,4},{28,12},{1,17},{... | collective-permute-start | bytes 1572872 | tf_op jit(solution)/shard_map/ppermute | solution.py:123
  9.1 34.3 %collective-permute-start.2 = (bf16[2,2,512,128]{3,2,1,0:T(8,128)(2,1)}, bf16[2,2,512,128]{3,2,1,0:T(8,128)(2,1)}, u32[]{:S(2)}, u32[]{:S(2)}) collective-permute-start(bf16[2,2,512,128]{3,2,1,0:T(8,128)(2,1)} %get-tuple-element.48), channel_id=1, source_target_pairs={{0,24},{8,0},{16,8},{24,16},{4,28},{12,4},{20,12},{28,20},{1,25},{... | collective-permute-start | bytes 1572872 | tf_op jit(solution)/shard_map/ppermute | solution.py:123
  54.9 15.6 %copy-start.4 = (bf16[3,2,512,128]{3,2,0,1:T(8,128)(2,1)S(1)}, bf16[3,2,512,128]{3,2,0,1:T(8,128)(2,1)}, u32[]{:S(2)}) copy-start(bf16[3,2,512,128]{3,2,0,1:T(8,128)(2,1)} %fusion.1) | copy-start | bytes 2359300
  56.3 16.8 %copy-start.2 = (bf16[8,512,128]{2,1,0:T(8,128)(2,1)S(1)}, bf16[8,512,128]{2,1,0:T(8,128)(2,1)}, u32[]{:S(2)}) copy-start(bf16[8,512,128]{2,1,0:T(8,128)(2,1)} %gather_fusion.5) | copy-start | bytes 3145732
  56.3 20.1 %collective-permute-start.3 = (bf16[2,512,128]{2,1,0:T(8,128)(2,1)S(1)}, bf16[2,512,128]{2,1,0:T(8,128)(2,1)S(1)}, u32[]{:S(2)}, u32[]{:S(2)}) collective-permute-start(bf16[2,512,128]{2,1,0:T(8,128)(2,1)S(1)} %get-tuple-element.88), channel_id=1, source_target_pairs={{0,8},{8,16},{16,24},{24,0},{4,12},{12,20},{20,28},{28,4},{1,9},{9... | collective-permute-start | bytes 786440 | tf_op jit(solution)/shard_map/ppermute | solution.py:123
  68.0 17.8 %collective-permute-start.4 = (bf16[2,512,128]{2,1,0:T(8,128)(2,1)S(1)}, bf16[2,512,128]{2,1,0:T(8,128)(2,1)S(1)}, u32[]{:S(2)}, u32[]{:S(2)}) collective-permute-start(bf16[2,512,128]{2,1,0:T(8,128)(2,1)S(1)} %get-tuple-element.87), channel_id=1, source_target_pairs={{0,16},{8,24},{16,0},{24,8},{4,20},{12,28},{20,4},{28,12},{1,17},{... | collective-permute-start | bytes 786440 | tf_op jit(solution)/shard_map/ppermute | solution.py:123
  69.6 16.2 %collective-permute-start.5 = (bf16[2,512,128]{2,1,0:T(8,128)(2,1)S(1)}, bf16[2,512,128]{2,1,0:T(8,128)(2,1)S(1)}, u32[]{:S(2)}, u32[]{:S(2)}) collective-permute-start(bf16[2,512,128]{2,1,0:T(8,128)(2,1)S(1)} %get-tuple-element.86), channel_id=1, source_target_pairs={{0,24},{8,0},{16,8},{24,16},{4,28},{12,4},{20,12},{28,20},{1,25},{... | collective-permute-start | bytes 786440 | tf_op jit(solution)/shard_map/ppermute | solution.py:123
  71.6 43.1 %collective-permute-start.9 = (bf16[4,2,512,128]{3,2,0,1:T(8,128)(2,1)}, bf16[4,2,512,128]{3,2,0,1:T(8,128)(2,1)}, u32[]{:S(2)}, u32[]{:S(2)}) collective-permute-start(bf16[4,2,512,128]{3,2,0,1:T(8,128)(2,1)} %fusion), channel_id=1, source_target_pairs={{0,4},{8,12},{16,20},{24,28},{4,0},{12,8},{20,16},{28,24},{1,5},{9... | collective-permute-start | bytes 3145736 | tf_op jit(solution)/shard_map/ppermute | solution.py:167
  87.3 15.2 %collective-permute-start.6 = (bf16[2,512,128]{2,1,0:T(8,128)(2,1)S(1)}, bf16[2,512,128]{2,1,0:T(8,128)(2,1)S(1)}, u32[]{:S(2)}, u32[]{:S(2)}) collective-permute-start(bf16[2,512,128]{2,1,0:T(8,128)(2,1)S(1)} %get-tuple-element.74), channel_id=1, source_target_pairs={{0,8},{8,16},{16,24},{24,0},{4,12},{12,20},{20,28},{28,4},{1,9},{9... | collective-permute-start | bytes 786440 | tf_op jit(solution)/shard_map/ppermute | solution.py:123
  93.5 19.1 %collective-permute-start.7 = (bf16[2,512,128]{2,1,0:T(8,128)(2,1)S(1)}, bf16[2,512,128]{2,1,0:T(8,128)(2,1)S(1)}, u32[]{:S(2)}, u32[]{:S(2)}) collective-permute-start(bf16[2,512,128]{2,1,0:T(8,128)(2,1)S(1)} %get-tuple-element.73), channel_id=1, source_target_pairs={{0,16},{8,24},{16,0},{24,8},{4,20},{12,28},{20,4},{28,12},{1,17},{... | collective-permute-start | bytes 786440 | tf_op jit(solution)/shard_map/ppermute | solution.py:123
  95.8 16.8 %collective-permute-start.8 = (bf16[2,512,128]{2,1,0:T(8,128)(2,1)S(1)}, bf16[2,512,128]{2,1,0:T(8,128)(2,1)S(1)}, u32[]{:S(2)}, u32[]{:S(2)}) collective-permute-start(bf16[2,512,128]{2,1,0:T(8,128)(2,1)S(1)} %get-tuple-element.72), channel_id=1, source_target_pairs={{0,24},{8,0},{16,8},{24,16},{4,28},{12,4},{20,12},{28,20},{1,25},{... | collective-permute-start | bytes 786440 | tf_op jit(solution)/shard_map/ppermute | solution.py:123
  113.6 2.4 copy-start.7
  113.6 2.4 copy-start.8
  113.7 2.4 copy-start.13
  159.2 6.1 %copy-start.1 = (f32[4,1,2,1536,128]{4,3,0,2,1:T(8,128)S(1)}, f32[4,1,2,1536,128]{4,3,0,2,1:T(8,128)}, u32[]{:S(2)}) copy-start(f32[4,1,2,1536,128]{4,3,0,2,1:T(8,128)} %maximum_bitcast_fusion) | copy-start | bytes 18874372
  195.1 3.3 copy-start.17
  195.1 3.3 copy-start.18
  196.7 47.8 %collective-permute-start.16 = (f32[4,2,512,128]{3,2,1,0:T(8,128)}, f32[4,2,512,128]{3,2,1,0:T(8,128)}, u32[]{:S(2)}, u32[]{:S(2)}) collective-permute-start(f32[4,2,512,128]{3,2,1,0:T(8,128)} %maximum_select_fusion), channel_id=1, source_target_pairs={{4,0},{12,8},{20,16},{28,24},{0,4},{8,12},{16,20},{24,28},{5,1},{1... | collective-permute-start | bytes 6291464 | tf_op jit(solution)/shard_map/ppermute | solution.py:200
  198.5 17.3 %collective-permute-start.13 = (bf16[2,512,128]{2,1,0:T(8,128)(2,1)S(1)}, bf16[2,512,128]{2,1,0:T(8,128)(2,1)S(1)}, u32[]{:S(2)}, u32[]{:S(2)}) collective-permute-start(bf16[2,512,128]{2,1,0:T(8,128)(2,1)S(1)} %get-tuple-element.76), channel_id=1, source_target_pairs={{0,24},{8,0},{16,8},{24,16},{4,28},{12,4},{20,12},{28,20},{1,25},{... | collective-permute-start | bytes 786440 | tf_op jit(solution)/shard_map/ppermute | solution.py:132
  205.3 23.6 %collective-permute-start.14 = (bf16[2,512,128]{2,1,0:T(8,128)(2,1)S(1)}, bf16[2,512,128]{2,1,0:T(8,128)(2,1)S(1)}, u32[]{:S(2)}, u32[]{:S(2)}) collective-permute-start(bf16[2,512,128]{2,1,0:T(8,128)(2,1)S(1)} %get-tuple-element.77), channel_id=1, source_target_pairs={{0,16},{8,24},{16,0},{24,8},{4,20},{12,28},{20,4},{28,12},{1,17},{... | collective-permute-start | bytes 786440 | tf_op jit(solution)/shard_map/ppermute | solution.py:132
  206.1 22.8 %collective-permute-start.15 = (bf16[2,512,128]{2,1,0:T(8,128)(2,1)S(1)}, bf16[2,512,128]{2,1,0:T(8,128)(2,1)S(1)}, u32[]{:S(2)}, u32[]{:S(2)}) collective-permute-start(bf16[2,512,128]{2,1,0:T(8,128)(2,1)S(1)} %get-tuple-element.78), channel_id=1, source_target_pairs={{0,8},{8,16},{16,24},{24,0},{4,12},{12,20},{20,28},{28,4},{1,9},{9... | collective-permute-start | bytes 786440 | tf_op jit(solution)/shard_map/ppermute | solution.py:132
  249.9 7.8 %copy-start.19 = (bf16[4,512,128]{2,1,0:T(8,128)(2,1)S(1)}, bf16[4,512,128]{2,1,0:T(8,128)(2,1)}, u32[]{:S(2)}) copy-start(bf16[4,512,128]{2,1,0:T(8,128)(2,1)} %get-tuple-element.19) | copy-start | bytes 1572868
  249.9 7.8 %copy-start.20 = (bf16[4,512,128]{2,1,0:T(8,128)(2,1)S(1)}, bf16[4,512,128]{2,1,0:T(8,128)(2,1)}, u32[]{:S(2)}) copy-start(bf16[4,512,128]{2,1,0:T(8,128)(2,1)} %get-tuple-element.20) | copy-start | bytes 1572868
  250.0 13.2 %collective-permute-start.17 = (bf16[2,512,128]{2,1,0:T(8,128)(2,1)S(1)}, bf16[2,512,128]{2,1,0:T(8,128)(2,1)S(1)}, u32[]{:S(2)}, u32[]{:S(2)}) collective-permute-start(bf16[2,512,128]{2,1,0:T(8,128)(2,1)S(1)} %get-tuple-element.54), channel_id=1, source_target_pairs={{0,24},{8,0},{16,8},{24,16},{4,28},{12,4},{20,12},{28,20},{1,25},{... | collective-permute-start | bytes 786440 | tf_op jit(solution)/shard_map/ppermute | solution.py:132
  256.4 25.4 %collective-permute-start.18 = (bf16[2,512,128]{2,1,0:T(8,128)(2,1)S(1)}, bf16[2,512,128]{2,1,0:T(8,128)(2,1)S(1)}, u32[]{:S(2)}, u32[]{:S(2)}) collective-permute-start(bf16[2,512,128]{2,1,0:T(8,128)(2,1)S(1)} %get-tuple-element.53), channel_id=1, source_target_pairs={{0,16},{8,24},{16,0},{24,8},{4,20},{12,28},{20,4},{28,12},{1,17},{... | collective-permute-start | bytes 786440 | tf_op jit(solution)/shard_map/ppermute | solution.py:132
  257.7 24.1 %collective-permute-start.19 = (bf16[2,512,128]{2,1,0:T(8,128)(2,1)S(1)}, bf16[2,512,128]{2,1,0:T(8,128)(2,1)S(1)}, u32[]{:S(2)}, u32[]{:S(2)}) collective-permute-start(bf16[2,512,128]{2,1,0:T(8,128)(2,1)S(1)} %get-tuple-element.52), channel_id=1, source_target_pairs={{0,8},{8,16},{16,24},{24,0},{4,12},{12,20},{20,28},{28,4},{1,9},{9... | collective-permute-start | bytes 786440 | tf_op jit(solution)/shard_map/ppermute | solution.py:132
  259.3 26.6 %collective-permute-start.10 = (bf16[4,512,128]{2,1,0:T(8,128)(2,1)}, bf16[4,512,128]{2,1,0:T(8,128)(2,1)}, u32[]{:S(2)}, u32[]{:S(2)}) collective-permute-start(bf16[4,512,128]{2,1,0:T(8,128)(2,1)} %get-tuple-element.42), channel_id=1, source_target_pairs={{0,24},{8,0},{16,8},{24,16},{4,28},{12,4},{20,12},{28,20},{1,25},{... | collective-permute-start | bytes 1572872 | tf_op jit(solution)/shard_map/ppermute | solution.py:132
  263.1 61.9 %collective-permute-start.11 = (bf16[4,512,128]{2,1,0:T(8,128)(2,1)}, bf16[4,512,128]{2,1,0:T(8,128)(2,1)}, u32[]{:S(2)}, u32[]{:S(2)}) collective-permute-start(bf16[4,512,128]{2,1,0:T(8,128)(2,1)} %get-tuple-element.41), channel_id=1, source_target_pairs={{0,16},{8,24},{16,0},{24,8},{4,20},{12,28},{20,4},{28,12},{1,17},{... | collective-permute-start | bytes 1572872 | tf_op jit(solution)/shard_map/ppermute | solution.py:132
  263.2 61.8 %collective-permute-start.12 = (bf16[4,512,128]{2,1,0:T(8,128)(2,1)}, bf16[4,512,128]{2,1,0:T(8,128)(2,1)}, u32[]{:S(2)}, u32[]{:S(2)}) collective-permute-start(bf16[4,512,128]{2,1,0:T(8,128)(2,1)} %get-tuple-element.40), channel_id=1, source_target_pairs={{0,8},{8,16},{16,24},{24,0},{4,12},{12,20},{20,28},{28,4},{1,9},{9... | collective-permute-start | bytes 1572872 | tf_op jit(solution)/shard_map/ppermute | solution.py:132
  282.9 42.0 %copy-start.15 = (bf16[1,4,512,128]{3,2,1,0:T(8,128)(2,1)S(1)}, bf16[1,4,512,128]{3,2,1,0:T(8,128)(2,1)}, u32[]{:S(2)}) copy-start(bf16[1,4,512,128]{3,2,1,0:T(8,128)(2,1)} %get-tuple-element.39) | copy-start | bytes 1572868
  (9 other events, 16.9 us)

commit v4 on v3

v4 whole, which is shorter than its diff:
```python
import math

import jax
import jax.numpy as jnp
from jax import lax
from jax.experimental import pallas as pl
from jax.experimental.pallas import tpu as pltpu
from jax.sharding import PartitionSpec as P

BLK = 512


def group_pairs(nseg, group, shift):
    return [
        (seg + nseg * w, seg + nseg * ((w + shift) % group))
        for seg in range(nseg)
        for w in range(group)
    ]


def next_segment_pairs(nseg, group):
    return [
        (seg + nseg * w, (seg + 1) % nseg + nseg * w)
        for seg in range(nseg)
        for w in range(group)
    ]


def block_terms(query_rows, key_block, values, grad_rows, usable):
    scaling = 1.0 / math.sqrt(query_rows.shape[-1])
    scores = (
        jnp.einsum("cid,cjd->cij", query_rows, key_block, preferred_element_type=jnp.float32)
        * scaling
    )
    scores = jnp.where(usable[:, None, :], scores, -jnp.inf)
    highest = jnp.max(scores, axis=2, keepdims=True)
    weights = jnp.exp(scores - highest)
    shares = weights / jnp.sum(weights, axis=2, keepdims=True)
    shares_low = shares.astype(jnp.bfloat16)
    attended = jnp.einsum(
        "cij,cjd->cid", shares_low, values, preferred_element_type=jnp.float32
    ).astype(jnp.bfloat16)
    attended_wide = lax.optimization_barrier(attended).astype(jnp.float32)
    row_dot = jnp.sum(grad_rows.astype(jnp.float32) * attended_wide, axis=2, keepdims=True)
    grad_probs = jnp.einsum("cid,cjd->cij", grad_rows, values, preferred_element_type=jnp.float32)
    dscore = (shares * (grad_probs - row_dot)).astype(jnp.bfloat16)
    grad_query = (
        jnp.einsum("cij,cjd->cid", dscore, key_block, preferred_element_type=jnp.float32) * scaling
    ).astype(jnp.bfloat16)
    key_terms = (
        jnp.einsum("cij,cid->cjd", dscore, query_rows, preferred_element_type=jnp.float32) * scaling
    )
    value_terms = jnp.einsum(
        "cij,cid->cjd", shares_low, grad_rows, preferred_element_type=jnp.float32
    )
    return attended, grad_query, key_terms, value_terms


def attention_kernel(index_ref, flag_ref, q_ref, g_ref, ko_ref, kw_ref, kp_ref, vo_ref, vw_ref, vp_ref, ad_ref, terms_ref):
    place = pl.program_id(0)
    q = q_ref[0]
    g = g_ref[0]
    keys = (ko_ref[0], kw_ref[0], kp_ref[0])
    values = (vo_ref[0], vw_ref[0], vp_ref[0])
    scaling = 1.0 / math.sqrt(q.shape[-1])
    rows_by_rows = (((1,), (1,)), ((), ()))
    cols_by_cols = (((0,), (0,)), ((), ()))
    scores = [
        lax.dot_general(q, k, rows_by_rows, preferred_element_type=jnp.float32) * scaling
        for k in keys
    ]
    kill = jnp.where(place == 0, flag_ref[0], 0)
    scores[1] = jnp.where(kill > 0, -jnp.inf, scores[1])
    highest = jnp.maximum(
        jnp.maximum(jnp.max(scores[0], axis=1, keepdims=True), jnp.max(scores[1], axis=1, keepdims=True)),
        jnp.max(scores[2], axis=1, keepdims=True),
    )
    weights = [jnp.exp(s - highest) for s in scores]
    total = (
        jnp.sum(weights[0], axis=1, keepdims=True)
        + jnp.sum(weights[1], axis=1, keepdims=True)
        + jnp.sum(weights[2], axis=1, keepdims=True)
    )
    shares = [w / total for w in weights]
    shares_low = [s.astype(jnp.bfloat16) for s in shares]
    attended_wide = jnp.dot(shares_low[0], values[0], preferred_element_type=jnp.float32)
    attended_wide = attended_wide + jnp.dot(shares_low[1], values[1], preferred_element_type=jnp.float32)
    attended_wide = attended_wide + jnp.dot(shares_low[2], values[2], preferred_element_type=jnp.float32)
    attended = attended_wide.astype(jnp.bfloat16)
    ad_ref[0, 0] = attended
    row_dot = jnp.sum(g.astype(jnp.float32) * attended.astype(jnp.float32), axis=1, keepdims=True)
    dq = None
    for part in range(3):
        grad_probs = lax.dot_general(g, values[part], rows_by_rows, preferred_element_type=jnp.float32)
        dscore = (shares[part] * (grad_probs - row_dot)).astype(jnp.bfloat16)
        term = jnp.dot(dscore, keys[part], preferred_element_type=jnp.float32)
        dq = term if dq is None else dq + term
        terms_ref[0, part, 0] = (
            lax.dot_general(dscore, q, cols_by_cols, preferred_element_type=jnp.float32) * scaling
        )
        terms_ref[0, part, 1] = lax.dot_general(
            shares_low[part], g, cols_by_cols, preferred_element_type=jnp.float32
        )
    ad_ref[0, 1] = (dq * scaling).astype(jnp.bfloat16)


def fused_terms(parity, q_rows, g_rows, k_all, v_all, k_window, v_window, partner_index, first_masked):
    places, rows, width = q_rows.shape
    row_spec = pl.BlockSpec((1, rows, width), lambda p, idx, flag: (p, 0, 0))
    own_spec = pl.BlockSpec((1, rows, width), lambda p, idx, flag: (2 * p + parity, 0, 0))
    partner_spec = pl.BlockSpec((1, rows, width), lambda p, idx, flag: (idx[p], 0, 0))
    if parity:
        window_spec = pl.BlockSpec((1, rows, width), lambda p, idx, flag: (2 * p, 0, 0))
    else:
        window_spec = row_spec
    flops = 36 * places * rows * rows * width
    return pl.pallas_call(
        attention_kernel,
        grid_spec=pltpu.PrefetchScalarGridSpec(
            num_scalar_prefetch=2,
            grid=(places,),
            in_specs=[row_spec, row_spec, own_spec, window_spec, partner_spec, own_spec, window_spec, partner_spec],
            out_specs=[
                pl.BlockSpec((1, 2, rows, width), lambda p, idx, flag: (p, 0, 0, 0)),
                pl.BlockSpec((1, 3, 2, rows, width), lambda p, idx, flag: (p, 0, 0, 0, 0)),
            ],
        ),
        out_shape=[
            jax.ShapeDtypeStruct((places, 2, rows, width), jnp.bfloat16),
            jax.ShapeDtypeStruct((places, 3, 2, rows, width), jnp.float32),
        ],
        cost_estimate=pl.CostEstimate(
            flops=flops,
            transcendentals=3 * places * rows * rows,
            bytes_accessed=places * rows * width * 60,
        ),
    )(partner_index, first_masked, q_rows, g_rows, k_all, k_window, k_all, v_all, v_window, v_all)


def interleave(even, odd):
    return jnp.stack([even, odd], axis=1).reshape((-1,) + even.shape[1:])


def pick(tree, index):
    return jax.tree.map(lambda x: lax.dynamic_index_in_dim(x, index, axis=0, keepdims=False), tree)


def gather_group(x, within, nseg, group):
    received = [pick(x, within)]
    for shift in range(1, group):
        received.append(lax.ppermute(pick(x, (within + shift) % group), "seq", group_pairs(nseg, group, shift)))
    order = (within - jnp.arange(group, dtype=jnp.int32)) % group
    return jax.tree.map(lambda *r: jnp.take(jnp.stack(r), order, axis=0), *received)


def scatter_group(y, within, nseg, group):
    returned = [pick(y, within)]
    for shift in range(1, group):
        returned.append(
            lax.ppermute(pick(y, (within - shift) % group), "seq", group_pairs(nseg, group, group - shift))
        )
    order = (jnp.arange(group, dtype=jnp.int32) - within) % group
    return jax.tree.map(lambda *r: jnp.take(jnp.stack(r), order, axis=0), *returned)


def body(queries, key_rows, value_rows, grad_out, partner_pos):
    heads, row_count, width = queries.shape
    blocks = row_count // BLK
    places = partner_pos.shape[2]
    group = places // blocks
    if heads != group or blocks != 2:
        raise ValueError("layout mismatch")
    nseg = lax.axis_size("seq") // group
    device = lax.axis_index("seq")
    segment = device % nseg
    within = device // nseg

    def split(x):
        return x.reshape(heads, blocks, BLK, width)

    q4, g4, k4, v4 = split(queries), split(grad_out), split(key_rows), split(value_rows)
    k_local, v_local = gather_group((k4, v4), within, nseg, group)
    k_all = k_local.reshape(places, BLK, width)
    v_all = v_local.reshape(places, BLK, width)
    k_all, v_all, q_odd_send, g_odd_send = lax.optimization_barrier((k_all, v_all, q4[:, 1], g4[:, 1]))
    q_odd, g_odd = gather_group((q_odd_send, g_odd_send), within, nseg, group)
    q_odd, g_odd, q_even_send, g_even_send = lax.optimization_barrier((q_odd, g_odd, q4[:, 0], g4[:, 0]))
    q_even, g_even = gather_group((q_even_send, g_even_send), within, nseg, group)

    odd_kv = jnp.stack([k_all[1::2], v_all[1::2]], axis=1)
    odd_send = jnp.where(segment == nseg - 1, jnp.roll(odd_kv, 1, axis=0), odd_kv)
    window_kv = lax.ppermute(odd_send, "seq", next_segment_pairs(nseg, group))

    my_partners = lax.dynamic_index_in_dim(
        lax.dynamic_index_in_dim(partner_pos, within, axis=0, keepdims=False),
        segment,
        axis=0,
        keepdims=False,
    )
    no_mask = jnp.zeros((1,), jnp.int32)
    ad_odd, terms_odd = fused_terms(
        1, q_odd, g_odd, k_all, v_all, k_all, v_all, my_partners[1::2], no_mask
    )
    sent_odd = scatter_group(ad_odd, within, nseg, group)

    first_masked = (segment == 0).astype(jnp.int32).reshape(1)
    ad_even, terms_even = fused_terms(
        0, q_even, g_even, k_all, v_all, window_kv[:, 0], window_kv[:, 1], my_partners[0::2], first_masked
    )

    ret = terms_even[:, 1]
    ret = jnp.where(segment == 0, jnp.roll(ret, -1, axis=0), ret)
    back_pairs = [(b, a) for a, b in next_segment_pairs(nseg, group)]
    window_back = lax.ppermute(ret, "seq", back_pairs)

    place_ids = jnp.arange(places, dtype=jnp.int32)
    hits = my_partners[None, :] == place_ids[:, None]
    inverse = jnp.sum(jnp.where(hits, place_ids[None, :], 0), axis=1)
    slot = (inverse % 2) * (places // 2) + inverse // 2
    partner_terms = jnp.concatenate([terms_even[:, 2], terms_odd[:, 2]], axis=0)
    partner_even = jnp.take(partner_terms, slot[0::2], axis=0)
    partner_odd = jnp.take(partner_terms, slot[1::2], axis=0)
    grads_even = (terms_even[:, 0] + terms_odd[:, 1] + partner_even).astype(jnp.bfloat16)
    sent_even = scatter_group((ad_even, grads_even), within, nseg, group)
    grads_odd = (terms_odd[:, 0] + window_back + partner_odd).astype(jnp.bfloat16)
    sent_last = scatter_group(grads_odd, within, nseg, group)

    shape = (heads, row_count, width)

    def joined(even, odd):
        return jnp.stack([even, odd], axis=1).reshape(shape)

    ad_e, grads_e = sent_even
    return (
        joined(ad_e[:, 0], sent_odd[:, 0]),
        joined(ad_e[:, 1], sent_odd[:, 1]),
        joined(grads_e[:, 0], sent_last[:, 0]),
        joined(grads_e[:, 1], sent_last[:, 1]),
    )


def solution(mesh):
    return jax.shard_map(
        body,
        mesh=mesh,
        in_specs=(
            P("head", "seq", None),
            P("head", "seq", None),
            P("head", "seq", None),
            P("head", "seq", None),
            P("head", None, None),
        ),
        out_specs=(
            P("head", "seq", None),
            P("head", "seq", None),
            P("head", "seq", None),
            P("head", "seq", None),
        ),
        check_vma=False,
    )
```

time: 337 us -> 271 us (0.80)
  waiting for transfers between devices: 128 us -> 79.7 us
  other arithmetic: 55.9 us -> 32.3 us
  local copies, waits for them, and re-layouts: 51.7 us -> 41.6 us
  starting transfers between devices: 65.3 us -> 73.6 us
  Pallas kernels: 33.3 us -> 39.3 us
    ppermute x18 -> x30, waiting for transfers between devices: 114 us -> 75.6 us  [the longest x18 39.7 us: gather_group(): lax.ppermute(pick(x, (within + shift) % group), 'seq', group_pairs(nseg,...]
    another operation x13 -> x10, other arithmetic: 28.6 us -> 10.4 us  [the longest x4 5.79 us: scatter_group(): jnp.stack(r)]
    slice x8 -> x6, local copies, waits for them, and re-layouts: 13 us -> 1.51 us  [the longest x1 0.6 us: body(): my_partners[1::2]]
    ppermute x1, waiting for transfers between devices: 14.7 us -> 4.11 us  [body(): window_back = lax.ppermute(ret, 'seq', back_pairs)]
    another operation x1 -> x0, local copies, waits for them, and re-layouts: 10.4 us -> none  [interleave(): return jnp.stack([even, odd], axis=1).reshape((-1,) + even.shape[1:])]
    ppermute x18 -> x30, starting transfers between devices: 62.4 us -> 70.6 us  [the longest x18 37.5 us: gather_group(): lax.ppermute(pick(x, (within + shift) % group), 'seq', group_pairs(nseg,...]
    dynamic_slice x4 -> x10, local copies, waits for them, and re-layouts: 2.86 us -> 9.39 us  [pick(): lax.dynamic_index_in_dim(x, index, axis=0, keepdims=False)]
    pallas_call x2, Pallas kernels: 33.3 us -> 39.3 us  [fused_terms(): pl.pallas_call(attention_kernel, grid_spec=pltpu.PrefetchScalarGridSpec(n...]
  transfers between devices with their start and end apart: 20 -> 32, of which waited for: 12 -> 10; matrix products, arithmetic and copies ran while one was open for 8% -> 14% of each run, Pallas kernels for 0% -> 7%
where the time goes in v4:
time: 271 us; the launch traced here: 268 us
  waiting for transfers between devices  79.7 us (29%)
  starting transfers between devices  73.6 us (27%)
  local copies, waits for them, and re-layouts  41.6 us (15%)
  Pallas kernels  39.3 us (15%)
  other arithmetic  32.3 us (12%)
    ppermute x18, waiting for transfers between devices, gather_group(): lax.ppermute(pick(x, (within + shift) % group), 'seq', group_pairs(nseg,...  39.7 us
    pallas_call x2, Pallas kernels, fused_terms(): pl.pallas_call(attention_kernel, grid_spec=pltpu.PrefetchScalarGridSpec(n...  39.3 us
    ppermute x18, starting transfers between devices, gather_group(): lax.ppermute(pick(x, (within + shift) % group), 'seq', group_pairs(nseg,...  37.5 us
    ppermute x12, waiting for transfers between devices, scatter_group(): lax.ppermute(pick(y, (within - shift) % group), 'seq', group_pairs(nseg,...  35.9 us
    ppermute x12, starting transfers between devices, scatter_group(): lax.ppermute(pick(y, (within - shift) % group), 'seq', group_pairs(nseg,...  33.1 us
    dynamic_slice x10, local copies, waits for them, and re-layouts, pick(): lax.dynamic_index_in_dim(x, index, axis=0, keepdims=False)  9.39 us
    gather x4, local copies, waits for them, and re-layouts, scatter_group(): jnp.take(jnp.stack(r), order, axis=0)  6.39 us
    another operation x4, other arithmetic, scatter_group(): jnp.stack(r)  5.79 us
  transfers between devices with their start and end apart: 32, of which 10 were waited for; matrix products, arithmetic and copies ran while one was open for 14% of the time, Pallas kernels for 7%

profile of v4, /device:TPU:0, one launch (start us, length us, event | category | flops | bytes accessed | tf_op | source)
XLA Modules:
  0.0 267.7 jit_solution(3696709554537045973)
XLA Ops:
  0.8 2.3 constant_dynamic-slice_fusion.8
  3.1 5.0 %collective-permute-start.5 = (bf16[2,512,128]{2,1,0:T(8,128)(2,1)}, bf16[2,512,128]{2,1,0:T(8,128)(2,1)}, u32[]{:S(2)}, u32[]{:S(2)}) collective-permute-start(bf16[2,512,128]{2,1,0:T(8,128)(2,1)} %get-tuple-element.64), channel_id=1, source_target_pairs={{0,24},{8,0},{16,8},{24,16},{4,28},{12,4},{20,12},{28,20},{1,25},{... | collective-permute-start | bytes 786440 | tf_op jit(solution)/shard_map/ppermute | solution.py:151
  10.1 2.8 %collective-permute-start.2 = (bf16[2,512,128]{2,1,0:T(8,128)(2,1)}, bf16[2,512,128]{2,1,0:T(8,128)(2,1)}, u32[]{:S(2)}, u32[]{:S(2)}) collective-permute-start(bf16[2,512,128]{2,1,0:T(8,128)(2,1)} %get-tuple-element.68), channel_id=1, source_target_pairs={{0,24},{8,0},{16,8},{24,16},{4,28},{12,4},{20,12},{28,20},{1,25},{... | collective-permute-start | bytes 786440 | tf_op jit(solution)/shard_map/ppermute | solution.py:151
  17.0 8.8 %collective-permute-start = (bf16[2,512,128]{2,1,0:T(8,128)(2,1)}, bf16[2,512,128]{2,1,0:T(8,128)(2,1)S(1)}, u32[]{:S(2)}, u32[]{:S(2)}) collective-permute-start(bf16[2,512,128]{2,1,0:T(8,128)(2,1)} %get-tuple-element.70), channel_id=1, source_target_pairs={{0,8},{8,16},{16,24},{24,0},{4,12},{12,20},{20,28},{28,4},{1,9},{9... | collective-permute-start | bytes 786440 | tf_op jit(solution)/shard_map/ppermute | solution.py:151
  27.0 6.1 %collective-permute-done.4 = bf16[2,512,128]{2,1,0:T(8,128)(2,1)} collective-permute-done((bf16[2,512,128]{2,1,0:T(8,128)(2,1)}, bf16[2,512,128]{2,1,0:T(8,128)(2,1)}, u32[]{:S(2)}, u32[]{:S(2)}) %collective-permute-start.4) | collective-permute-done | bytes 262176 | tf_op jit(solution)/shard_map/ppermute | solution.py:151
  35.1 18.1 %collective-permute-done.1 = bf16[2,512,128]{2,1,0:T(8,128)(2,1)} collective-permute-done((bf16[2,512,128]{2,1,0:T(8,128)(2,1)}, bf16[2,512,128]{2,1,0:T(8,128)(2,1)}, u32[]{:S(2)}, u32[]{:S(2)}) %collective-permute-start.1) | collective-permute-done | bytes 262176 | tf_op jit(solution)/shard_map/ppermute | solution.py:151
  57.1 2.8 %collective-permute-start.10 = (bf16[512,128]{1,0:T(8,128)(2,1)S(1)}, bf16[512,128]{1,0:T(8,128)(2,1)S(1)}, u32[]{:S(2)}, u32[]{:S(2)}) collective-permute-start(bf16[512,128]{1,0:T(8,128)(2,1)S(1)} %get-tuple-element.81), channel_id=1, source_target_pairs={{0,16},{8,24},{16,0},{24,8},{4,20},{12,28},{20,4},{28,12},{1,17},{... | collective-permute-start | bytes 393224 | tf_op jit(solution)/shard_map/ppermute | solution.py:151
  64.0 4.9 %collective-permute-start.6 = (bf16[512,128]{1,0:T(8,128)(2,1)S(1)}, bf16[512,128]{1,0:T(8,128)(2,1)S(1)}, u32[]{:S(2)}, u32[]{:S(2)}) collective-permute-start(bf16[512,128]{1,0:T(8,128)(2,1)S(1)} %get-tuple-element.86), channel_id=1, source_target_pairs={{0,8},{8,16},{16,24},{24,0},{4,12},{12,20},{20,28},{28,4},{1,9},{9... | collective-permute-start | bytes 393224 | tf_op jit(solution)/shard_map/ppermute | solution.py:151
  70.1 8.2 %collective-permute-done.10 = bf16[512,128]{1,0:T(8,128)(2,1)S(1)} collective-permute-done((bf16[512,128]{1,0:T(8,128)(2,1)S(1)}, bf16[512,128]{1,0:T(8,128)(2,1)S(1)}, u32[]{:S(2)}, u32[]{:S(2)}) %collective-permute-start.10) | collective-permute-done | bytes 131104 | tf_op jit(solution)/shard_map/ppermute | solution.py:151
  89.6 19.6 %shard_map.85 = (bf16[4,2,512,128]{3,2,1,0:T(8,128)(2,1)}, f32[4,3,2,512,128]{4,3,2,1,0:T(8,128)}) custom-call(s32[4]{0:T(128)} %slice.114.index_ref, s32[1]{0:T(128)} %constant.274.clone.1.flag_ref, bf16[4,512,128]{2,1,0:T(8,128)(2,1)} %get-tuple-element.26.q_ref, bf16[4,512,128]{2,1,0:T(8,128)(2,1)} %get-tuple-element.27.g_ref, ...), custom_call_target="tpu_custom_call" | custom-call | flops 4831838208 | bytes 15728640 | tf_op jit(solution)/shard_map/pallas_call | solution.py:117
  114.4 5.3 %collective-permute-done.13 = bf16[512,128]{1,0:T(8,128)(2,1)} collective-permute-done((bf16[512,128]{1,0:T(8,128)(2,1)}, bf16[512,128]{1,0:T(8,128)(2,1)}, u32[]{:S(2)}, u32[]{:S(2)}) %collective-permute-start.13) | collective-permute-done | bytes 131104 | tf_op jit(solution)/shard_map/ppermute | solution.py:151
  124.5 2.3 slice_bitcast_fusion.4
  126.8 19.6 %shard_map.84 = (bf16[4,2,512,128]{3,2,1,0:T(8,128)(2,1)}, f32[4,3,2,512,128]{4,3,2,1,0:T(8,128)}) custom-call(s32[4]{0:T(128)} %slice.102.index_ref, s32[1]{0:T(128)} %bitcast.1.flag_ref, bf16[4,512,128]{2,1,0:T(8,128)(2,1)} %get-tuple-element.92.q_ref, bf16[4,512,128]{2,1,0:T(8,128)(2,1)} %get-tuple-element.91.g_ref, bf16[8,512,128]{2,1,0:T(8,128)(2,1)} %bitcast.153, ...), custom_call_target="tpu_custom_call" | custom-call | flops 4831838208 | bytes 15728640 | tf_op jit(solution)/shard_map/pallas_call | solution.py:117
  150.0 2.7 slice_bitcast_fusion.3
  152.7 2.2 pad_maximum_fusion
  154.9 2.9 %gather_fusion.8 = f32[4,2,512,128]{3,2,1,0:T(8,128)S(1)} fusion(f32[8,2,512,128]{3,2,1,0:T(8,128)} %pad_maximum_fusion, s32[1024]{0:T(1024)S(1)} %pad_clamp_fusion.1), kind=kCustom, calls=%fused_computation.2.clone | custom fusion | bytes 4194320 | tf_op jit(solution)/shard_map/jit(_take)/gather | solution.py:221
  157.8 5.6 %fusion.3 = (bf16[4,2,512,128]{3,2,1,0:T(8,128)(2,1)S(1)}, f32[4,2,512,128]{3,2,1,0:T(8,128)}) fusion(f32[4,2,512,128]{3,2,1,0:T(8,128)S(1)} %gather_fusion.8, pred[4]{0:T(512)(128)(4,1)S(1)} %copy-done.16, f32[1,2,512,128]{3,2,1,0:T(8,128)} %slice_bitcast_fusion.10, f32[3,2,512,128]{3,2,1,0:T(8,128)} %slice_bitcast_fusion.3, pred[]{:T(512)S(6)} %eq.49, ...), kind=kLoop, calls=%fused_computation.19 | loop fusion | flops 3145728 | bytes 13631493 | tf_op jit(solution)/shard_map/convert_element_type | solution.py:223
  166.6 3.5 %collective-permute-start.22 = (bf16[2,512,128]{2,1,0:T(8,128)(2,1)S(1)}, bf16[2,512,128]{2,1,0:T(8,128)(2,1)S(1)}, u32[]{:S(2)}, u32[]{:S(2)}) collective-permute-start(bf16[2,512,128]{2,1,0:T(8,128)(2,1)S(1)} %get-tuple-element.58), channel_id=1, source_target_pairs={{0,24},{8,0},{16,8},{24,16},{4,28},{12,4},{20,12},{28,20},{1,25},{... | collective-permute-start | bytes 786440 | tf_op jit(solution)/shard_map/ppermute | solution.py:160
  171.6 5.8 %collective-permute-done.24 = bf16[2,512,128]{2,1,0:T(8,128)(2,1)S(1)} collective-permute-done((bf16[2,512,128]{2,1,0:T(8,128)(2,1)S(1)}, bf16[2,512,128]{2,1,0:T(8,128)(2,1)S(1)}, u32[]{:S(2)}, u32[]{:S(2)}) %collective-permute-start.24) | collective-permute-done | bytes 262176 | tf_op jit(solution)/shard_map/ppermute | solution.py:160
  177.4 11.3 %collective-permute-done.23 = bf16[2,512,128]{2,1,0:T(8,128)(2,1)S(1)} collective-permute-done((bf16[2,512,128]{2,1,0:T(8,128)(2,1)S(1)}, bf16[2,512,128]{2,1,0:T(8,128)(2,1)S(1)}, u32[]{:S(2)}, u32[]{:S(2)}) %collective-permute-start.23) | collective-permute-done | bytes 262176 | tf_op jit(solution)/shard_map/ppermute | solution.py:160
  189.6 8.5 %collective-permute-start.26 = (bf16[2,512,128]{2,1,0:T(8,128)(2,1)}, bf16[2,512,128]{2,1,0:T(8,128)(2,1)}, u32[]{:S(2)}, u32[]{:S(2)}) collective-permute-start(bf16[2,512,128]{2,1,0:T(8,128)(2,1)} %get-tuple-element.39), channel_id=1, source_target_pairs={{0,16},{8,24},{16,0},{24,8},{4,20},{12,28},{20,4},{28,12},{1,17},{... | collective-permute-start | bytes 786440 | tf_op jit(solution)/shard_map/ppermute | solution.py:160
  198.1 3.4 %collective-permute-start.25 = (bf16[2,512,128]{2,1,0:T(8,128)(2,1)}, bf16[2,512,128]{2,1,0:T(8,128)(2,1)}, u32[]{:S(2)}, u32[]{:S(2)}) collective-permute-start(bf16[2,512,128]{2,1,0:T(8,128)(2,1)} %get-tuple-element.40), channel_id=1, source_target_pairs={{0,24},{8,0},{16,8},{24,16},{4,28},{12,4},{20,12},{28,20},{1,25},{... | collective-permute-start | bytes 786440 | tf_op jit(solution)/shard_map/ppermute | solution.py:160
  201.5 2.9 %gather_fusion.10 = f32[4,2,512,128]{3,2,1,0:T(8,128)S(1)} fusion(f32[8,2,512,128]{3,2,1,0:T(8,128)} %pad_maximum_fusion, s32[1024]{0:T(1024)S(1)} %pad_clamp_fusion), kind=kCustom, calls=%fused_computation.11.clone | custom fusion | bytes 4194320 | tf_op jit(solution)/shard_map/jit(_take)/gather | solution.py:222
  207.1 4.1 %collective-permute-done.28 = f32[4,2,512,128]{3,2,1,0:T(8,128)} collective-permute-done((f32[4,2,512,128]{3,2,1,0:T(8,128)}, f32[4,2,512,128]{3,2,1,0:T(8,128)}, u32[]{:S(2)}, u32[]{:S(2)}) %collective-permute-start.28) | collective-permute-done | bytes 2097184 | tf_op jit(solution)/shard_map/ppermute | solution.py:214
  211.2 2.8 %fusion.5 = bf16[4,2,512,128]{3,2,1,0:T(8,128)(2,1)S(1)} fusion(f32[4,2,512,128]{3,2,1,0:T(8,128)} %collective-permute-done.28, f32[4,2,512,128]{3,2,1,0:T(8,128)S(1)} %gather_fusion.10, f32[4,3,2,512,128]{4,3,2,1,0:T(8,128)} %get-tuple-element.30, pred[4]{0:T(512)(128)(4,1)S(1)} %compare_and_fusion), kind=kLoop, calls=%fused_computation.22 | loop fusion | flops 2097152 | bytes 7340036 | tf_op jit(solution)/shard_map/convert_element_type | solution.py:225
  214.9 2.7 collective-permute-start.31
  217.6 10.2 %collective-permute-start.30 = (bf16[2,512,128]{2,1,0:T(8,128)(2,1)}, bf16[2,512,128]{2,1,0:T(8,128)(2,1)}, u32[]{:S(2)}, u32[]{:S(2)}) collective-permute-start(bf16[2,512,128]{2,1,0:T(8,128)(2,1)} %get-tuple-element.43), channel_id=1, source_target_pairs={{0,16},{8,24},{16,0},{24,8},{4,20},{12,28},{20,4},{28,12},{1,17},{... | collective-permute-start | bytes 786440 | tf_op jit(solution)/shard_map/ppermute | solution.py:160
  227.8 3.3 %collective-permute-start.29 = (bf16[2,512,128]{2,1,0:T(8,128)(2,1)}, bf16[2,512,128]{2,1,0:T(8,128)(2,1)}, u32[]{:S(2)}, u32[]{:S(2)}) collective-permute-start(bf16[2,512,128]{2,1,0:T(8,128)(2,1)} %get-tuple-element.44), channel_id=1, source_target_pairs={{0,24},{8,0},{16,8},{24,16},{4,28},{12,4},{20,12},{28,20},{1,25},{... | collective-permute-start | bytes 786440 | tf_op jit(solution)/shard_map/ppermute | solution.py:160
  233.2 11.8 %collective-permute-done.20 = bf16[2,512,128]{2,1,0:T(8,128)(2,1)} collective-permute-done((bf16[2,512,128]{2,1,0:T(8,128)(2,1)}, bf16[2,512,128]{2,1,0:T(8,128)(2,1)}, u32[]{:S(2)}, u32[]{:S(2)}) %collective-permute-start.20) | collective-permute-done | bytes 262176 | tf_op jit(solution)/shard_map/ppermute | solution.py:160
  245.0 2.2 pad_maximum_fusion.4
  249.3 7.0 %collective-permute-done.30 = bf16[2,512,128]{2,1,0:T(8,128)(2,1)} collective-permute-done((bf16[2,512,128]{2,1,0:T(8,128)(2,1)}, bf16[2,512,128]{2,1,0:T(8,128)(2,1)}, u32[]{:S(2)}, u32[]{:S(2)}) %collective-permute-start.30) | collective-permute-done | bytes 262176 | tf_op jit(solution)/shard_map/ppermute | solution.py:160
  258.5 2.9 %gather_fusion.11 = bf16[4,2,512,128]{3,2,1,0:T(8,128)(2,1)} fusion(bf16[4,2,512,128]{3,2,1,0:T(8,128)(2,1)} %pad_maximum_fusion.9, s32[1024]{0:T(1024)S(1)} %pad_clamp_fusion.2), kind=kCustom, calls=%fused_computation.7.clone | custom fusion | bytes 2097168 | tf_op jit(solution)/shard_map/jit(_take)/gather | solution.py:163
  (149 shorter events, 64.7 us)
Async XLA Ops:
  3.1 13.9 %collective-permute-start.5 = (bf16[2,512,128]{2,1,0:T(8,128)(2,1)}, bf16[2,512,128]{2,1,0:T(8,128)(2,1)}, u32[]{:S(2)}, u32[]{:S(2)}) collective-permute-start(bf16[2,512,128]{2,1,0:T(8,128)(2,1)} %get-tuple-element.64), channel_id=1, source_target_pairs={{0,24},{8,0},{16,8},{24,16},{4,28},{12,4},{20,12},{28,20},{1,25},{... | collective-permute-start | bytes 786440 | tf_op jit(solution)/shard_map/ppermute | solution.py:151
  8.1 24.9 %collective-permute-start.4 = (bf16[2,512,128]{2,1,0:T(8,128)(2,1)}, bf16[2,512,128]{2,1,0:T(8,128)(2,1)}, u32[]{:S(2)}, u32[]{:S(2)}) collective-permute-start(bf16[2,512,128]{2,1,0:T(8,128)(2,1)} %get-tuple-element.65), channel_id=1, source_target_pairs={{0,16},{8,24},{16,0},{24,8},{4,20},{12,28},{20,4},{28,12},{1,17},{... | collective-permute-start | bytes 786440 | tf_op jit(solution)/shard_map/ppermute | solution.py:151
  8.1 24.9 %collective-permute-start.3 = (bf16[2,512,128]{2,1,0:T(8,128)(2,1)}, bf16[2,512,128]{2,1,0:T(8,128)(2,1)}, u32[]{:S(2)}, u32[]{:S(2)}) collective-permute-start(bf16[2,512,128]{2,1,0:T(8,128)(2,1)} %get-tuple-element.66), channel_id=1, source_target_pairs={{0,8},{8,16},{16,24},{24,0},{4,12},{12,20},{20,28},{28,4},{1,9},{9... | collective-permute-start | bytes 786440 | tf_op jit(solution)/shard_map/ppermute | solution.py:151
  10.1 25.0 %collective-permute-start.2 = (bf16[2,512,128]{2,1,0:T(8,128)(2,1)}, bf16[2,512,128]{2,1,0:T(8,128)(2,1)}, u32[]{:S(2)}, u32[]{:S(2)}) collective-permute-start(bf16[2,512,128]{2,1,0:T(8,128)(2,1)} %get-tuple-element.68), channel_id=1, source_target_pairs={{0,24},{8,0},{16,8},{24,16},{4,28},{12,4},{20,12},{28,20},{1,25},{... | collective-permute-start | bytes 786440 | tf_op jit(solution)/shard_map/ppermute | solution.py:151
  12.9 40.3 %collective-permute-start.1 = (bf16[2,512,128]{2,1,0:T(8,128)(2,1)}, bf16[2,512,128]{2,1,0:T(8,128)(2,1)}, u32[]{:S(2)}, u32[]{:S(2)}) collective-permute-start(bf16[2,512,128]{2,1,0:T(8,128)(2,1)} %get-tuple-element.69), channel_id=1, source_target_pairs={{0,16},{8,24},{16,0},{24,8},{4,20},{12,28},{20,4},{28,12},{1,17},{... | collective-permute-start | bytes 786440 | tf_op jit(solution)/shard_map/ppermute | solution.py:151
  17.0 36.3 %collective-permute-start = (bf16[2,512,128]{2,1,0:T(8,128)(2,1)}, bf16[2,512,128]{2,1,0:T(8,128)(2,1)S(1)}, u32[]{:S(2)}, u32[]{:S(2)}) collective-permute-start(bf16[2,512,128]{2,1,0:T(8,128)(2,1)} %get-tuple-element.70), channel_id=1, source_target_pairs={{0,8},{8,16},{16,24},{24,0},{4,12},{12,20},{20,28},{28,4},{1,9},{9... | collective-permute-start | bytes 786440 | tf_op jit(solution)/shard_map/ppermute | solution.py:151
  57.0 7.0 %collective-permute-start.11 = (bf16[512,128]{1,0:T(8,128)(2,1)S(1)}, bf16[512,128]{1,0:T(8,128)(2,1)S(1)}, u32[]{:S(2)}, u32[]{:S(2)}) collective-permute-start(bf16[512,128]{1,0:T(8,128)(2,1)S(1)} %get-tuple-element.80), channel_id=1, source_target_pairs={{0,24},{8,0},{16,8},{24,16},{4,28},{12,4},{20,12},{28,20},{1,25},{... | collective-permute-start | bytes 393224 | tf_op jit(solution)/shard_map/ppermute | solution.py:151
  57.1 21.2 %collective-permute-start.10 = (bf16[512,128]{1,0:T(8,128)(2,1)S(1)}, bf16[512,128]{1,0:T(8,128)(2,1)S(1)}, u32[]{:S(2)}, u32[]{:S(2)}) collective-permute-start(bf16[512,128]{1,0:T(8,128)(2,1)S(1)} %get-tuple-element.81), channel_id=1, source_target_pairs={{0,16},{8,24},{16,0},{24,8},{4,20},{12,28},{20,4},{28,12},{1,17},{... | collective-permute-start | bytes 393224 | tf_op jit(solution)/shard_map/ppermute | solution.py:151
  59.9 19.9 %collective-permute-start.9 = (bf16[512,128]{1,0:T(8,128)(2,1)S(1)}, bf16[512,128]{1,0:T(8,128)(2,1)S(1)}, u32[]{:S(2)}, u32[]{:S(2)}) collective-permute-start(bf16[512,128]{1,0:T(8,128)(2,1)S(1)} %get-tuple-element.82), channel_id=1, source_target_pairs={{0,8},{8,16},{16,24},{24,0},{4,12},{12,20},{20,28},{28,4},{1,9},{9... | collective-permute-start | bytes 393224 | tf_op jit(solution)/shard_map/ppermute | solution.py:151
  61.9 18.6 %collective-permute-start.8 = (bf16[512,128]{1,0:T(8,128)(2,1)S(1)}, bf16[512,128]{1,0:T(8,128)(2,1)S(1)}, u32[]{:S(2)}, u32[]{:S(2)}) collective-permute-start(bf16[512,128]{1,0:T(8,128)(2,1)S(1)} %get-tuple-element.84), channel_id=1, source_target_pairs={{0,24},{8,0},{16,8},{24,16},{4,28},{12,4},{20,12},{28,20},{1,25},{... | collective-permute-start | bytes 393224 | tf_op jit(solution)/shard_map/ppermute | solution.py:151
  63.8 18.6 %collective-permute-start.7 = (bf16[512,128]{1,0:T(8,128)(2,1)S(1)}, bf16[512,128]{1,0:T(8,128)(2,1)S(1)}, u32[]{:S(2)}, u32[]{:S(2)}) collective-permute-start(bf16[512,128]{1,0:T(8,128)(2,1)S(1)} %get-tuple-element.85), channel_id=1, source_target_pairs={{0,16},{8,24},{16,0},{24,8},{4,20},{12,28},{20,4},{28,12},{1,17},{... | collective-permute-start | bytes 393224 | tf_op jit(solution)/shard_map/ppermute | solution.py:151
  64.0 18.3 %collective-permute-start.6 = (bf16[512,128]{1,0:T(8,128)(2,1)S(1)}, bf16[512,128]{1,0:T(8,128)(2,1)S(1)}, u32[]{:S(2)}, u32[]{:S(2)}) collective-permute-start(bf16[512,128]{1,0:T(8,128)(2,1)S(1)} %get-tuple-element.86), channel_id=1, source_target_pairs={{0,8},{8,16},{16,24},{24,0},{4,12},{12,20},{20,28},{28,4},{1,9},{9... | collective-permute-start | bytes 393224 | tf_op jit(solution)/shard_map/ppermute | solution.py:151
  78.3 46.2 %collective-permute-start.18 = (bf16[4,2,512,128]{3,2,0,1:T(8,128)(2,1)}, bf16[4,2,512,128]{3,2,0,1:T(8,128)(2,1)}, u32[]{:S(2)}, u32[]{:S(2)}) collective-permute-start(bf16[4,2,512,128]{3,2,0,1:T(8,128)(2,1)} %fusion.6), channel_id=1, source_target_pairs={{0,4},{8,12},{16,20},{24,28},{4,0},{12,8},{20,16},{28,24},{1,5},{9... | collective-permute-start | bytes 3145736 | tf_op jit(solution)/shard_map/ppermute | solution.py:192
  84.4 24.9 %collective-permute-start.17 = (bf16[512,128]{1,0:T(8,128)(2,1)S(1)}, bf16[512,128]{1,0:T(8,128)(2,1)S(1)}, u32[]{:S(2)}, u32[]{:S(2)}) collective-permute-start(bf16[512,128]{1,0:T(8,128)(2,1)S(1)} %get-tuple-element.72), channel_id=1, source_target_pairs={{0,24},{8,0},{16,8},{24,16},{4,28},{12,4},{20,12},{28,20},{1,25},{... | collective-permute-start | bytes 393224 | tf_op jit(solution)/shard_map/ppermute | solution.py:151
  84.5 25.5 %collective-permute-start.16 = (bf16[512,128]{1,0:T(8,128)(2,1)S(1)}, bf16[512,128]{1,0:T(8,128)(2,1)S(1)}, u32[]{:S(2)}, u32[]{:S(2)}) collective-permute-start(bf16[512,128]{1,0:T(8,128)(2,1)S(1)} %get-tuple-element.73), channel_id=1, source_target_pairs={{0,16},{8,24},{16,0},{24,8},{4,20},{12,28},{20,4},{28,12},{1,17},{... | collective-permute-start | bytes 393224 | tf_op jit(solution)/shard_map/ppermute | solution.py:151
  85.1 28.6 %collective-permute-start.15 = (bf16[512,128]{1,0:T(8,128)(2,1)S(1)}, bf16[512,128]{1,0:T(8,128)(2,1)S(1)}, u32[]{:S(2)}, u32[]{:S(2)}) collective-permute-start(bf16[512,128]{1,0:T(8,128)(2,1)S(1)} %get-tuple-element.74), channel_id=1, source_target_pairs={{0,8},{8,16},{16,24},{24,0},{4,12},{12,20},{20,28},{28,4},{1,9},{9... | collective-permute-start | bytes 393224 | tf_op jit(solution)/shard_map/ppermute | solution.py:151
  87.5 26.9 %collective-permute-start.14 = (bf16[512,128]{1,0:T(8,128)(2,1)}, bf16[512,128]{1,0:T(8,128)(2,1)}, u32[]{:S(2)}, u32[]{:S(2)}) collective-permute-start(bf16[512,128]{1,0:T(8,128)(2,1)} %get-tuple-element.76), channel_id=1, source_target_pairs={{0,24},{8,0},{16,8},{24,16},{4,28},{12,4},{20,12},{28,20},{1,25},{... | collective-permute-start | bytes 393224 | tf_op jit(solution)/shard_map/ppermute | solution.py:151
  109.3 10.4 %collective-permute-start.13 = (bf16[512,128]{1,0:T(8,128)(2,1)}, bf16[512,128]{1,0:T(8,128)(2,1)}, u32[]{:S(2)}, u32[]{:S(2)}) collective-permute-start(bf16[512,128]{1,0:T(8,128)(2,1)} %get-tuple-element.77), channel_id=1, source_target_pairs={{0,16},{8,24},{16,0},{24,8},{4,20},{12,28},{20,4},{28,12},{1,17},{... | collective-permute-start | bytes 393224 | tf_op jit(solution)/shard_map/ppermute | solution.py:151
  109.9 9.8 %collective-permute-start.12 = (bf16[512,128]{1,0:T(8,128)(2,1)S(1)}, bf16[512,128]{1,0:T(8,128)(2,1)}, u32[]{:S(2)}, u32[]{:S(2)}) collective-permute-start(bf16[512,128]{1,0:T(8,128)(2,1)S(1)} %get-tuple-element.78), channel_id=1, source_target_pairs={{0,8},{8,16},{16,24},{24,0},{4,12},{12,20},{20,28},{28,4},{1,9},{9... | collective-permute-start | bytes 393224 | tf_op jit(solution)/shard_map/ppermute | solution.py:151
  163.4 47.7 %collective-permute-start.28 = (f32[4,2,512,128]{3,2,1,0:T(8,128)}, f32[4,2,512,128]{3,2,1,0:T(8,128)}, u32[]{:S(2)}, u32[]{:S(2)}) collective-permute-start(f32[4,2,512,128]{3,2,1,0:T(8,128)} %get-tuple-element.32), channel_id=1, source_target_pairs={{4,0},{12,8},{20,16},{28,24},{0,4},{8,12},{16,20},{24,28},{5,1},{1... | collective-permute-start | bytes 6291464 | tf_op jit(solution)/shard_map/ppermute | solution.py:214
  166.3 11.2 %collective-permute-start.24 = (bf16[2,512,128]{2,1,0:T(8,128)(2,1)S(1)}, bf16[2,512,128]{2,1,0:T(8,128)(2,1)S(1)}, u32[]{:S(2)}, u32[]{:S(2)}) collective-permute-start(bf16[2,512,128]{2,1,0:T(8,128)(2,1)S(1)} %get-tuple-element.56), channel_id=1, source_target_pairs={{0,8},{8,16},{16,24},{24,0},{4,12},{12,20},{20,28},{28,4},{1,9},{9... | collective-permute-start | bytes 786440 | tf_op jit(solution)/shard_map/ppermute | solution.py:160
  166.3 22.4 %collective-permute-start.23 = (bf16[2,512,128]{2,1,0:T(8,128)(2,1)S(1)}, bf16[2,512,128]{2,1,0:T(8,128)(2,1)S(1)}, u32[]{:S(2)}, u32[]{:S(2)}) collective-permute-start(bf16[2,512,128]{2,1,0:T(8,128)(2,1)S(1)} %get-tuple-element.57), channel_id=1, source_target_pairs={{0,16},{8,24},{16,0},{24,8},{4,20},{12,28},{20,4},{28,12},{1,17},{... | collective-permute-start | bytes 786440 | tf_op jit(solution)/shard_map/ppermute | solution.py:160
  166.6 22.1 %collective-permute-start.22 = (bf16[2,512,128]{2,1,0:T(8,128)(2,1)S(1)}, bf16[2,512,128]{2,1,0:T(8,128)(2,1)S(1)}, u32[]{:S(2)}, u32[]{:S(2)}) collective-permute-start(bf16[2,512,128]{2,1,0:T(8,128)(2,1)S(1)} %get-tuple-element.58), channel_id=1, source_target_pairs={{0,24},{8,0},{16,8},{24,16},{4,28},{12,4},{20,12},{28,20},{1,25},{... | collective-permute-start | bytes 786440 | tf_op jit(solution)/shard_map/ppermute | solution.py:160
  171.0 35.5 %collective-permute-start.27 = (bf16[2,512,128]{2,1,0:T(8,128)(2,1)}, bf16[2,512,128]{2,1,0:T(8,128)(2,1)}, u32[]{:S(2)}, u32[]{:S(2)}) collective-permute-start(bf16[2,512,128]{2,1,0:T(8,128)(2,1)} %get-tuple-element.38), channel_id=1, source_target_pairs={{0,8},{8,16},{16,24},{24,0},{4,12},{12,20},{20,28},{28,4},{1,9},{9... | collective-permute-start | bytes 786440 | tf_op jit(solution)/shard_map/ppermute | solution.py:160
  189.6 25.3 %collective-permute-start.26 = (bf16[2,512,128]{2,1,0:T(8,128)(2,1)}, bf16[2,512,128]{2,1,0:T(8,128)(2,1)}, u32[]{:S(2)}, u32[]{:S(2)}) collective-permute-start(bf16[2,512,128]{2,1,0:T(8,128)(2,1)} %get-tuple-element.39), channel_id=1, source_target_pairs={{0,16},{8,24},{16,0},{24,8},{4,20},{12,28},{20,4},{28,12},{1,17},{... | collective-permute-start | bytes 786440 | tf_op jit(solution)/shard_map/ppermute | solution.py:160
  198.1 19.5 %collective-permute-start.25 = (bf16[2,512,128]{2,1,0:T(8,128)(2,1)}, bf16[2,512,128]{2,1,0:T(8,128)(2,1)}, u32[]{:S(2)}, u32[]{:S(2)}) collective-permute-start(bf16[2,512,128]{2,1,0:T(8,128)(2,1)} %get-tuple-element.40), channel_id=1, source_target_pairs={{0,24},{8,0},{16,8},{24,16},{4,28},{12,4},{20,12},{28,20},{1,25},{... | collective-permute-start | bytes 786440 | tf_op jit(solution)/shard_map/ppermute | solution.py:160
  206.5 21.3 %collective-permute-start.21 = (bf16[2,512,128]{2,1,0:T(8,128)(2,1)S(1)}, bf16[2,512,128]{2,1,0:T(8,128)(2,1)S(1)}, u32[]{:S(2)}, u32[]{:S(2)}) collective-permute-start(bf16[2,512,128]{2,1,0:T(8,128)(2,1)S(1)} %get-tuple-element.50), channel_id=1, source_target_pairs={{0,8},{8,16},{16,24},{24,0},{4,12},{12,20},{20,28},{28,4},{1,9},{9... | collective-permute-start | bytes 786440 | tf_op jit(solution)/shard_map/ppermute | solution.py:160
  206.5 38.5 %collective-permute-start.20 = (bf16[2,512,128]{2,1,0:T(8,128)(2,1)}, bf16[2,512,128]{2,1,0:T(8,128)(2,1)}, u32[]{:S(2)}, u32[]{:S(2)}) collective-permute-start(bf16[2,512,128]{2,1,0:T(8,128)(2,1)} %get-tuple-element.51), channel_id=1, source_target_pairs={{0,16},{8,24},{16,0},{24,8},{4,20},{12,28},{20,4},{28,12},{1,17},{... | collective-permute-start | bytes 786440 | tf_op jit(solution)/shard_map/ppermute | solution.py:160
  211.2 33.8 %collective-permute-start.19 = (bf16[2,512,128]{2,1,0:T(8,128)(2,1)}, bf16[2,512,128]{2,1,0:T(8,128)(2,1)}, u32[]{:S(2)}, u32[]{:S(2)}) collective-permute-start(bf16[2,512,128]{2,1,0:T(8,128)(2,1)} %get-tuple-element.52), channel_id=1, source_target_pairs={{0,24},{8,0},{16,8},{24,16},{4,28},{12,4},{20,12},{28,20},{1,25},{... | collective-permute-start | bytes 786440 | tf_op jit(solution)/shard_map/ppermute | solution.py:160
  214.9 34.3 %collective-permute-start.31 = (bf16[2,512,128]{2,1,0:T(8,128)(2,1)}, bf16[2,512,128]{2,1,0:T(8,128)(2,1)}, u32[]{:S(2)}, u32[]{:S(2)}) collective-permute-start(bf16[2,512,128]{2,1,0:T(8,128)(2,1)} %get-tuple-element.42), channel_id=1, source_target_pairs={{0,8},{8,16},{16,24},{24,0},{4,12},{12,20},{20,28},{28,4},{1,9},{9... | collective-permute-start | bytes 786440 | tf_op jit(solution)/shard_map/ppermute | solution.py:160
  217.6 38.6 %collective-permute-start.30 = (bf16[2,512,128]{2,1,0:T(8,128)(2,1)}, bf16[2,512,128]{2,1,0:T(8,128)(2,1)}, u32[]{:S(2)}, u32[]{:S(2)}) collective-permute-start(bf16[2,512,128]{2,1,0:T(8,128)(2,1)} %get-tuple-element.43), channel_id=1, source_target_pairs={{0,16},{8,24},{16,0},{24,8},{4,20},{12,28},{20,4},{28,12},{1,17},{... | collective-permute-start | bytes 786440 | tf_op jit(solution)/shard_map/ppermute | solution.py:160
  227.8 28.4 %collective-permute-start.29 = (bf16[2,512,128]{2,1,0:T(8,128)(2,1)}, bf16[2,512,128]{2,1,0:T(8,128)(2,1)}, u32[]{:S(2)}, u32[]{:S(2)}) collective-permute-start(bf16[2,512,128]{2,1,0:T(8,128)(2,1)} %get-tuple-element.44), channel_id=1, source_target_pairs={{0,24},{8,0},{16,8},{24,16},{4,28},{12,4},{20,12},{28,20},{1,25},{... | collective-permute-start | bytes 786440 | tf_op jit(solution)/shard_map/ppermute | solution.py:160
  (20 other events, 142.4 us)

commit v5 on v4

--- a/solution.py
+++ b/solution.py
@@ -5,9 +5,10 @@
 from jax import lax
 from jax.experimental import pallas as pl
 from jax.experimental.pallas import tpu as pltpu
-from jax.sharding import PartitionSpec as P
+from jax.sharding import Mesh, PartitionSpec as P
 
 BLK = 512
+GROUP = 4
 
 
 def group_pairs(nseg, group, shift):
@@ -141,26 +142,12 @@
     return jnp.stack([even, odd], axis=1).reshape((-1,) + even.shape[1:])
 
 
-def pick(tree, index):
-    return jax.tree.map(lambda x: lax.dynamic_index_in_dim(x, index, axis=0, keepdims=False), tree)
-
-
-def gather_group(x, within, nseg, group):
-    received = [pick(x, within)]
-    for shift in range(1, group):
-        received.append(lax.ppermute(pick(x, (within + shift) % group), "seq", group_pairs(nseg, group, shift)))
-    order = (within - jnp.arange(group, dtype=jnp.int32)) % group
-    return jax.tree.map(lambda *r: jnp.take(jnp.stack(r), order, axis=0), *received)
-
-
-def scatter_group(y, within, nseg, group):
-    returned = [pick(y, within)]
-    for shift in range(1, group):
-        returned.append(
-            lax.ppermute(pick(y, (within - shift) % group), "seq", group_pairs(nseg, group, group - shift))
-        )
-    order = (jnp.arange(group, dtype=jnp.int32) - within) % group
-    return jax.tree.map(lambda *r: jnp.take(jnp.stack(r), order, axis=0), *returned)
+def exchange(tree):
+    return jax.tree.map(lambda x: lax.all_to_all(x, "within", 0, 0), tree)
+
+
+def segment_pairs(nseg, step):
+    return [(seg, (seg + step) % nseg) for seg in range(nseg)]
 
 
 def body(queries, key_rows, value_rows, grad_out, partner_pos):
@@ -170,27 +157,28 @@
     group = places // blocks
     if heads != group or blocks != 2:
         raise ValueError("layout mismatch")
-    nseg = lax.axis_size("seq") // group
-    device = lax.axis_index("seq")
-    segment = device % nseg
-    within = device // nseg
+    if lax.axis_size("within") != group:
+        raise ValueError("group mismatch")
+    nseg = lax.axis_size("segment")
+    segment = lax.axis_index("segment")
 
     def split(x):
         return x.reshape(heads, blocks, BLK, width)
 
     q4, g4, k4, v4 = split(queries), split(grad_out), split(key_rows), split(value_rows)
-    k_local, v_local = gather_group((k4, v4), within, nseg, group)
+    k_local, v_local = exchange((k4, v4))
     k_all = k_local.reshape(places, BLK, width)
     v_all = v_local.reshape(places, BLK, width)
     k_all, v_all, q_odd_send, g_odd_send = lax.optimization_barrier((k_all, v_all, q4[:, 1], g4[:, 1]))
-    q_odd, g_odd = gather_group((q_odd_send, g_odd_send), within, nseg, group)
+    q_odd, g_odd = exchange((q_odd_send, g_odd_send))
     q_odd, g_odd, q_even_send, g_even_send = lax.optimization_barrier((q_odd, g_odd, q4[:, 0], g4[:, 0]))
-    q_even, g_even = gather_group((q_even_send, g_even_send), within, nseg, group)
+    q_even, g_even = exchange((q_even_send, g_even_send))
 
     odd_kv = jnp.stack([k_all[1::2], v_all[1::2]], axis=1)
     odd_send = jnp.where(segment == nseg - 1, jnp.roll(odd_kv, 1, axis=0), odd_kv)
-    window_kv = lax.ppermute(odd_send, "seq", next_segment_pairs(nseg, group))
-
+    window_kv = lax.ppermute(odd_send, "segment", segment_pairs(nseg, 1))
+
+    within = lax.axis_index("within")
     my_partners = lax.dynamic_index_in_dim(
         lax.dynamic_index_in_dim(partner_pos, within, axis=0, keepdims=False),
         segment,
@@ -201,7 +189,7 @@
     ad_odd, terms_odd = fused_terms(
         1, q_odd, g_odd, k_all, v_all, k_all, v_all, my_partners[1::2], no_mask
     )
-    sent_odd = scatter_group(ad_odd, within, nseg, group)
+    sent_odd = exchange(ad_odd)
 
     first_masked = (segment == 0).astype(jnp.int32).reshape(1)
     ad_even, terms_even = fused_terms(
@@ -210,8 +198,7 @@
 
     ret = terms_even[:, 1]
     ret = jnp.where(segment == 0, jnp.roll(ret, -1, axis=0), ret)
-    back_pairs = [(b, a) for a, b in next_segment_pairs(nseg, group)]
-    window_back = lax.ppermute(ret, "seq", back_pairs)
+    window_back = lax.ppermute(ret, "segment", segment_pairs(nseg, nseg - 1))
 
     place_ids = jnp.arange(places, dtype=jnp.int32)
     hits = my_partners[None, :] == place_ids[:, None]
@@ -221,9 +208,9 @@
     partner_even = jnp.take(partner_terms, slot[0::2], axis=0)
     partner_odd = jnp.take(partner_terms, slot[1::2], axis=0)
     grads_even = (terms_even[:, 0] + terms_odd[:, 1] + partner_even).astype(jnp.bfloat16)
-    sent_even = scatter_group((ad_even, grads_even), within, nseg, group)
+    sent_even = exchange((ad_even, grads_even))
     grads_odd = (terms_odd[:, 0] + window_back + partner_odd).astype(jnp.bfloat16)
-    sent_last = scatter_group(grads_odd, within, nseg, group)
+    sent_last = exchange(grads_odd)
 
     shape = (heads, row_count, width)
 
@@ -240,21 +227,16 @@
 
 
 def solution(mesh):
+    devices = mesh.devices
+    grouped = Mesh(
+        devices.reshape((GROUP, devices.shape[0] // GROUP) + devices.shape[1:]),
+        ("within", "segment", "head"),
+    )
+    rows = P("head", ("within", "segment"), None)
     return jax.shard_map(
         body,
-        mesh=mesh,
-        in_specs=(
-            P("head", "seq", None),
-            P("head", "seq", None),
-            P("head", "seq", None),
-            P("head", "seq", None),
-            P("head", None, None),
-        ),
-        out_specs=(
-            P("head", "seq", None),
-            P("head", "seq", None),
-            P("head", "seq", None),
-            P("head", "seq", None),
-        ),
+        mesh=grouped,
+        in_specs=(rows, rows, rows, rows, P("head", None, None)),
+        out_specs=(rows, rows, rows, rows),
         check_vma=False,
     )

time: 271 us -> 275 us (1.015)
  waiting for transfers between devices: 79.7 us -> 116 us
  starting transfers between devices: 73.6 us -> 40.9 us
  blocking collectives: 0 us -> 32.1 us
  local copies, waits for them, and re-layouts: 41.6 us -> 25.2 us
  other arithmetic: 32.3 us -> 19.4 us
    all_to_all x0 -> x9, waiting for transfers between devices: none -> 88.6 us  [exchange(): return jax.tree.map(lambda x: lax.all_to_all(x, 'within', 0, 0), tree)]
    ppermute x32 -> x2, starting transfers between devices: 73.6 us -> 2.95 us  [the longest x1 1.49 us: body(): window_kv = lax.ppermute(odd_send, 'segment', segment_pairs(nseg, 1))]
    ppermute x32 -> x2, waiting for transfers between devices: 79.7 us -> 27.2 us  [the longest x1 27.2 us: body(): window_back = lax.ppermute(ret, 'segment', segment_pairs(nseg, nseg - 1))]
    all_to_all x0 -> x9, starting transfers between devices: none -> 38 us  [exchange(): return jax.tree.map(lambda x: lax.all_to_all(x, 'within', 0, 0), tree)]
    all_to_all x0 -> x1, blocking collectives: none -> 32.1 us  [exchange(): return jax.tree.map(lambda x: lax.all_to_all(x, 'within', 0, 0), tree)]
    gather x10 -> x0, local copies, waits for them, and re-layouts: 11.5 us -> none  [the longest x4 6.39 us: scatter_group(): jnp.take(jnp.stack(r), order, axis=0)]
    another operation x10 -> x0, other arithmetic: 10.4 us -> none  [the longest x4 5.79 us: scatter_group(): jnp.stack(r)]
    dynamic_slice x10 -> x0, local copies, waits for them, and re-layouts: 9.39 us -> none  [pick(): lax.dynamic_index_in_dim(x, index, axis=0, keepdims=False)]
  transfers between devices with their start and end apart: 32 -> 11, of which waited for: 10 -> 7; matrix products, arithmetic and copies ran while one was open for 14% -> 15% of each run, Pallas kernels for 7% -> 14%
where the time goes in v5:
time: 275 us; the launch traced here: 274 us
  waiting for transfers between devices  116 us (42%)
  starting transfers between devices  40.9 us (15%)
  Pallas kernels  39.3 us (14%)
  blocking collectives  32.1 us (12%)
  local copies, waits for them, and re-layouts  25.2 us (9%)
  other arithmetic  19.4 us (7%)
    all_to_all x9, waiting for transfers between devices, exchange(): return jax.tree.map(lambda x: lax.all_to_all(x, 'within', 0, 0), tree)  88.6 us
    pallas_call x2, Pallas kernels, fused_terms(): pl.pallas_call(attention_kernel, grid_spec=pltpu.PrefetchScalarGridSpec(n...  39.3 us
    all_to_all x9, starting transfers between devices, exchange(): return jax.tree.map(lambda x: lax.all_to_all(x, 'within', 0, 0), tree)  38 us
    all_to_all x1, blocking collectives, exchange(): return jax.tree.map(lambda x: lax.all_to_all(x, 'within', 0, 0), tree)  32.1 us
    ppermute x1, waiting for transfers between devices, body(): window_back = lax.ppermute(ret, 'segment', segment_pairs(nseg, nseg - 1))  27.2 us
    convert_element_type x1, other arithmetic, body(): (terms_even[:, 0] + terms_odd[:, 1] + partner_even).astype(jnp.bfloat16)  5.95 us
  transfers between devices with their start and end apart: 11, of which 7 were waited for; matrix products, arithmetic and copies ran while one was open for 15% of the time, Pallas kernels for 14%

profile of v5, /device:TPU:0, one launch (start us, length us, event | category | flops | bytes accessed | tf_op | source)
XLA Modules:
  0.0 273.5 jit_solution(3288250059787968270)
XLA Ops:
  0.6 32.1 %all_to_all.50 = bf16[4,2,512,128]{3,2,1,0:T(8,128)(2,1)S(1)} all-to-all(bf16[4,2,512,128]{3,2,1,0:T(8,128)(2,1)} %bitcast.73), channel_id=1, replica_groups=mesh['within'=4,'segment'=2,'head'=4] {'within'}, dimensions={0} | all-to-all | bytes 2097152 | tf_op jit(solution)/shard_map/all_to_all | solution.py:146
  32.7 3.5 %all-to-all-start.1 = ((bf16[4,2,512,128]{3,2,1,0:T(8,128)(2,1)}), bf16[4,2,512,128]{3,2,1,0:T(8,128)(2,1)S(1)}, u32[]{:S(2)}, u32[]{:S(2)}) async-start(bf16[4,2,512,128]{3,2,1,0:T(8,128)(2,1)} %bitcast.74), calls=%async_computation.1 | async-start | bytes 2097152 | tf_op jit(solution)/shard_map/all_to_all | solution.py:146
  36.2 2.9 %slice_bitcast_fusion.6 = (bf16[4,512,128]{2,1,0:T(8,128)(2,1)}, bf16[4,512,128]{2,1,0:T(8,128)(2,1)}, bf16[4,512,128]{2,1,0:T(8,128)(2,1)}, bf16[4,512,128]{2,1,0:T(8,128)(2,1)}) fusion(bf16[4,2,512,128]{3,2,1,0:T(8,128)(2,1)} %bitcast.79, bf16[4,2,512,128]{3,2,1,0:T(8,128)(2,1)} %bitcast.80), kind=kLoop, calls=%fused_computation.28 | loop fusion | bytes 4194304 | tf_op jit(solution)/shard_map/squeeze | solution.py:174
  39.1 22.0 %all-to-all-done.1 = bf16[4,2,512,128]{3,2,1,0:T(8,128)(2,1)S(1)} async-done(((bf16[4,2,512,128]{3,2,1,0:T(8,128)(2,1)}), bf16[4,2,512,128]{3,2,1,0:T(8,128)(2,1)S(1)}, u32[]{:S(2)}, u32[]{:S(2)}) %all-to-all-start.1) | async-done | bytes 1048608 | tf_op jit(solution)/shard_map/all_to_all | solution.py:146
  61.1 3.5 %all-to-all-start.2 = ((bf16[4,512,128]{2,1,0:T(8,128)(2,1)}), bf16[4,512,128]{2,1,0:T(8,128)(2,1)S(1)}, u32[]{:S(2)}, u32[]{:S(2)}) async-start(bf16[4,512,128]{2,1,0:T(8,128)(2,1)} %get-tuple-element.17), calls=%async_computation.2 | async-start | bytes 1048576 | tf_op jit(solution)/shard_map/all_to_all | solution.py:146
  64.6 13.9 %all-to-all-done.2.q_ref = bf16[4,512,128]{2,1,0:T(8,128)(2,1)S(1)} async-done(((bf16[4,512,128]{2,1,0:T(8,128)(2,1)}), bf16[4,512,128]{2,1,0:T(8,128)(2,1)S(1)}, u32[]{:S(2)}, u32[]{:S(2)}) %all-to-all-start.2) | async-done | bytes 524320 | tf_op jit(solution)/shard_map/all_to_all | solution.py:146
  78.5 4.1 %all-to-all-start.3 = ((bf16[4,512,128]{2,1,0:T(8,128)(2,1)}), bf16[4,512,128]{2,1,0:T(8,128)(2,1)}, u32[]{:S(2)}, u32[]{:S(2)}) async-start(bf16[4,512,128]{2,1,0:T(8,128)(2,1)} %get-tuple-element.18), calls=%async_computation.3 | async-start | bytes 1048576 | tf_op jit(solution)/shard_map/all_to_all | solution.py:146
  82.9 13.8 %all-to-all-done.3.g_ref = bf16[4,512,128]{2,1,0:T(8,128)(2,1)} async-done(((bf16[4,512,128]{2,1,0:T(8,128)(2,1)}), bf16[4,512,128]{2,1,0:T(8,128)(2,1)}, u32[]{:S(2)}, u32[]{:S(2)}) %all-to-all-start.3) | async-done | bytes 524320 | tf_op jit(solution)/shard_map/all_to_all | solution.py:146
  96.7 4.1 %all-to-all-start.4 = ((bf16[4,512,128]{2,1,0:T(8,128)(2,1)}), bf16[4,512,128]{2,1,0:T(8,128)(2,1)}, u32[]{:S(2)}, u32[]{:S(2)}) async-start(bf16[4,512,128]{2,1,0:T(8,128)(2,1)} %get-tuple-element.19), calls=%async_computation.4 | async-start | bytes 1048576 | tf_op jit(solution)/shard_map/all_to_all | solution.py:146
  102.2 1.5 collective-permute-start
  103.7 11.2 %all-to-all-done.4.q_ref = bf16[4,512,128]{2,1,0:T(8,128)(2,1)} async-done(((bf16[4,512,128]{2,1,0:T(8,128)(2,1)}), bf16[4,512,128]{2,1,0:T(8,128)(2,1)}, u32[]{:S(2)}, u32[]{:S(2)}) %all-to-all-start.4) | async-done | bytes 524320 | tf_op jit(solution)/shard_map/all_to_all | solution.py:146
  114.9 3.5 %all-to-all-start.5 = ((bf16[4,512,128]{2,1,0:T(8,128)(2,1)}), bf16[4,512,128]{2,1,0:T(8,128)(2,1)S(1)}, u32[]{:S(2)}, u32[]{:S(2)}) async-start(bf16[4,512,128]{2,1,0:T(8,128)(2,1)} %get-tuple-element.20), calls=%async_computation.5 | async-start | bytes 1048576 | tf_op jit(solution)/shard_map/all_to_all | solution.py:146
  119.6 19.7 %shard_map.85 = (bf16[4,2,512,128]{3,2,1,0:T(8,128)(2,1)}, f32[4,3,2,512,128]{4,3,2,1,0:T(8,128)}) custom-call(s32[4]{0:T(128)} %slice.114.index_ref, s32[1]{0:T(128)} %constant.75.clone.1.flag_ref, bf16[4,512,128]{2,1,0:T(8,128)(2,1)} %copy-done.3, bf16[4,512,128]{2,1,0:T(8,128)(2,1)} %all-to-all-done.3.g_ref, bf16[8,512,128]{2,1,0:T(8,128)(2,1)} %bitcast.62, ...), custom_call_target="tpu_custom_call" | custom-call | flops 4831838208 | bytes 15728640 | tf_op jit(solution)/shard_map/pallas_call | solution.py:118
  139.3 1.7 slice_bitcast_fusion.2
  141.9 5.1 %all-to-all-start.7 = ((bf16[4,2,512,128]{3,2,1,0:T(8,128)(2,1)}), bf16[4,2,512,128]{3,2,1,0:T(8,128)(2,1)S(1)}, u32[]{:S(2)}, u32[]{:S(2)}) async-start(bf16[4,2,512,128]{3,2,1,0:T(8,128)(2,1)} %get-tuple-element.26), calls=%async_computation.7 | async-start | bytes 2097152 | tf_op jit(solution)/shard_map/all_to_all | solution.py:146
  146.9 2.3 slice_bitcast_fusion.4
  149.2 19.6 %shard_map.84 = (bf16[4,2,512,128]{3,2,1,0:T(8,128)(2,1)}, f32[4,3,2,512,128]{4,3,2,1,0:T(8,128)}) custom-call(s32[4]{0:T(128)} %slice.102.index_ref, s32[1]{0:T(128)} %bitcast.1.flag_ref, bf16[4,512,128]{2,1,0:T(8,128)(2,1)} %all-to-all-done.4.q_ref, bf16[4,512,128]{2,1,0:T(8,128)(2,1)} %copy-done.4, bf16[8,512,128]{2,1,0:T(8,128)(2,1)} %bitcast.65, ...), custom_call_target="tpu_custom_call" | custom-call | flops 4831838208 | bytes 15728640 | tf_op jit(solution)/shard_map/pallas_call | solution.py:118
  168.8 1.9 slice_bitcast_fusion.10
  170.7 2.6 slice_bitcast_fusion.3
  173.3 3.1 %slice_bitcast_fusion.1 = f32[4,2,512,128]{3,2,1,0:T(8,128)} fusion(f32[4,3,2,512,128]{4,3,2,1,0:T(8,128)} %get-tuple-element.27), kind=kLoop, calls=%fused_computation.5 | loop fusion | bytes 4194304 | tf_op jit(solution)/shard_map/squeeze | solution.py:207
  176.4 5.1 %all-to-all-start.6 = ((bf16[4,2,512,128]{3,2,1,0:T(8,128)(2,1)}), bf16[4,2,512,128]{3,2,1,0:T(8,128)(2,1)}, u32[]{:S(2)}, u32[]{:S(2)}) async-start(bf16[4,2,512,128]{3,2,1,0:T(8,128)(2,1)} %get-tuple-element.23), calls=%async_computation.6 | async-start | bytes 2097152 | tf_op jit(solution)/shard_map/all_to_all | solution.py:146
  181.5 4.1 %pad_maximum_fusion = f32[8,2,512,128]{3,2,1,0:T(8,128)} fusion(f32[4,2,512,128]{3,2,1,0:T(8,128)S(1)} %slice_bitcast_fusion.2, f32[4,2,512,128]{3,2,1,0:T(8,128)} %slice_bitcast_fusion.1), kind=kLoop, calls=%fused_computation.2 | loop fusion | flops 1048576 | bytes 8388608 | tf_op jit(solution)/shard_map/concatenate | solution.py:207
  185.6 2.9 %gather_fusion = f32[4,2,512,128]{3,2,1,0:T(8,128)S(1)} fusion(f32[8,2,512,128]{3,2,1,0:T(8,128)} %pad_maximum_fusion, s32[1024]{0:T(1024)S(1)} %pad_clamp_fusion.1), kind=kCustom, calls=%fused_computation.clone | custom fusion | bytes 4194320 | tf_op jit(solution)/shard_map/jit(_take)/gather | solution.py:208
  188.4 6.0 %fusion.3 = (bf16[4,2,512,128]{3,2,1,0:T(8,128)(2,1)}, f32[4,2,512,128]{3,2,1,0:T(8,128)}) fusion(f32[4,2,512,128]{3,2,1,0:T(8,128)S(1)} %gather_fusion, pred[4]{0:T(512)(128)(4,1)S(1)} %compare_and_fusion.1, f32[1,2,512,128]{3,2,1,0:T(8,128)} %slice_bitcast_fusion.10, f32[3,2,512,128]{3,2,1,0:T(8,128)} %slice_bitcast_fusion.3, pred[]{:T(512)S(6)} %eq.22, ...), kind=kLoop, calls=%fused_computation.9 | loop fusion | flops 3145728 | bytes 13631493 | tf_op jit(solution)/shard_map/convert_element_type | solution.py:210
  194.4 1.5 collective-permute-start.1
  195.9 9.8 %all-to-all-done.6 = bf16[4,2,512,128]{3,2,1,0:T(8,128)(2,1)} async-done(((bf16[4,2,512,128]{3,2,1,0:T(8,128)(2,1)}), bf16[4,2,512,128]{3,2,1,0:T(8,128)(2,1)}, u32[]{:S(2)}, u32[]{:S(2)}) %all-to-all-start.6) | async-done | bytes 1048608 | tf_op jit(solution)/shard_map/all_to_all | solution.py:146
  205.7 4.3 %all-to-all-start.8 = ((bf16[4,2,512,128]{3,2,1,0:T(8,128)(2,1)}), bf16[4,2,512,128]{3,2,1,0:T(8,128)(2,1)}, u32[]{:S(2)}, u32[]{:S(2)}) async-start(bf16[4,2,512,128]{3,2,1,0:T(8,128)(2,1)} %get-tuple-element.29), calls=%async_computation.8 | async-start | bytes 2097152 | tf_op jit(solution)/shard_map/all_to_all | solution.py:146
  210.1 2.9 %gather_fusion.1 = f32[4,2,512,128]{3,2,1,0:T(8,128)S(1)} fusion(f32[8,2,512,128]{3,2,1,0:T(8,128)} %pad_maximum_fusion, s32[1024]{0:T(1024)S(1)} %pad_clamp_fusion), kind=kCustom, calls=%fused_computation.1.clone | custom fusion | bytes 4194320 | tf_op jit(solution)/shard_map/jit(_take)/gather | solution.py:209
  213.0 27.2 %collective-permute-done.1 = f32[4,2,512,128]{3,2,1,0:T(8,128)} collective-permute-done((f32[4,2,512,128]{3,2,1,0:T(8,128)}, f32[4,2,512,128]{3,2,1,0:T(8,128)}, u32[]{:S(2)}, u32[]{:S(2)}) %collective-permute-start.1) | collective-permute-done | bytes 2097184 | tf_op jit(solution)/shard_map/ppermute | solution.py:201
  240.2 3.7 %fusion.5 = bf16[4,2,512,128]{3,2,1,0:T(8,128)(2,1)} fusion(f32[4,2,512,128]{3,2,1,0:T(8,128)} %collective-permute-done.1, f32[4,2,512,128]{3,2,1,0:T(8,128)S(1)} %gather_fusion.1, f32[4,3,2,512,128]{4,3,2,1,0:T(8,128)} %get-tuple-element.28, pred[4]{0:T(512)(128)(4,1)S(1)} %compare_and_fusion), kind=kLoop, calls=%fused_computation.12 | loop fusion | flops 2097152 | bytes 7340036 | tf_op jit(solution)/shard_map/convert_element_type | solution.py:212
  243.9 4.8 %all-to-all-start.9 = ((bf16[4,2,512,128]{3,2,1,0:T(8,128)(2,1)}), bf16[4,2,512,128]{3,2,1,0:T(8,128)(2,1)S(1)}, u32[]{:S(2)}, u32[]{:S(2)}) async-start(bf16[4,2,512,128]{3,2,1,0:T(8,128)(2,1)} %fusion.5), calls=%async_computation.9 | async-start | bytes 2097152 | tf_op jit(solution)/shard_map/all_to_all | solution.py:146
  253.5 17.9 %all-to-all-done.9 = bf16[4,2,512,128]{3,2,1,0:T(8,128)(2,1)S(1)} async-done(((bf16[4,2,512,128]{3,2,1,0:T(8,128)(2,1)}), bf16[4,2,512,128]{3,2,1,0:T(8,128)(2,1)S(1)}, u32[]{:S(2)}, u32[]{:S(2)}) %all-to-all-start.9) | async-done | bytes 1048608 | tf_op jit(solution)/shard_map/all_to_all | solution.py:146
  (40 shorter events, 10.7 us)
Async XLA Ops:
  0.6 63.9 %copy-start = (s32[4,2,8]{2,1,0:T(2,128)S(1)}, s32[4,2,8]{2,1,0:T(2,128)}, u32[]{:S(2)}) copy-start(s32[4,2,8]{2,1,0:T(2,128)} %param.11) | copy-start | bytes 772
  32.7 68.1 %copy-start.1 = (bf16[4,2,512,128]{3,2,1,0:T(8,128)(2,1)}, bf16[4,2,512,128]{3,2,1,0:T(8,128)(2,1)S(1)}, u32[]{:S(2)}) copy-start(bf16[4,2,512,128]{3,2,1,0:T(8,128)(2,1)S(1)} %all_to_all.50) | copy-start | bytes 3145732
  32.7 28.4 %all-to-all-start.1 = ((bf16[4,2,512,128]{3,2,1,0:T(8,128)(2,1)}), bf16[4,2,512,128]{3,2,1,0:T(8,128)(2,1)S(1)}, u32[]{:S(2)}, u32[]{:S(2)}) async-start(bf16[4,2,512,128]{3,2,1,0:T(8,128)(2,1)} %bitcast.74), calls=%async_computation.1 | async-start | bytes 2097152 | tf_op jit(solution)/shard_map/all_to_all | solution.py:146
  61.1 35.6 %copy-start.2 = (bf16[4,2,512,128]{3,2,1,0:T(8,128)(2,1)}, bf16[4,2,512,128]{3,2,1,0:T(8,128)(2,1)S(1)}, u32[]{:S(2)}) copy-start(bf16[4,2,512,128]{3,2,1,0:T(8,128)(2,1)S(1)} %all-to-all-done.1) | copy-start | bytes 3145732
  61.1 17.4 %all-to-all-start.2 = ((bf16[4,512,128]{2,1,0:T(8,128)(2,1)}), bf16[4,512,128]{2,1,0:T(8,128)(2,1)S(1)}, u32[]{:S(2)}, u32[]{:S(2)}) async-start(bf16[4,512,128]{2,1,0:T(8,128)(2,1)} %get-tuple-element.17), calls=%async_computation.2 | async-start | bytes 1048576 | tf_op jit(solution)/shard_map/all_to_all | solution.py:146
  78.5 22.4 %copy-start.3 = (bf16[4,512,128]{2,1,0:T(8,128)(2,1)}, bf16[4,512,128]{2,1,0:T(8,128)(2,1)S(1)}, u32[]{:S(2)}) copy-start(bf16[4,512,128]{2,1,0:T(8,128)(2,1)S(1)} %all-to-all-done.2.q_ref) | copy-start | bytes 1572868
  78.5 18.2 %all-to-all-start.3 = ((bf16[4,512,128]{2,1,0:T(8,128)(2,1)}), bf16[4,512,128]{2,1,0:T(8,128)(2,1)}, u32[]{:S(2)}, u32[]{:S(2)}) async-start(bf16[4,512,128]{2,1,0:T(8,128)(2,1)} %get-tuple-element.18), calls=%async_computation.3 | async-start | bytes 1048576 | tf_op jit(solution)/shard_map/all_to_all | solution.py:146
  96.7 18.2 %all-to-all-start.4 = ((bf16[4,512,128]{2,1,0:T(8,128)(2,1)}), bf16[4,512,128]{2,1,0:T(8,128)(2,1)}, u32[]{:S(2)}, u32[]{:S(2)}) async-start(bf16[4,512,128]{2,1,0:T(8,128)(2,1)} %get-tuple-element.19), calls=%async_computation.4 | async-start | bytes 1048576 | tf_op jit(solution)/shard_map/all_to_all | solution.py:146
  102.2 44.8 %collective-permute-start = (bf16[4,2,512,128]{3,2,0,1:T(8,128)(2,1)}, bf16[4,2,512,128]{3,2,0,1:T(8,128)(2,1)}, u32[]{:S(2)}, u32[]{:S(2)}) collective-permute-start(bf16[4,2,512,128]{3,2,0,1:T(8,128)(2,1)} %fusion.6), channel_id=1, source_target_pairs={{0,4},{4,0},{1,5},{5,1},{2,6},{6,2},{3,7},{7,3},{8,12},{12,8},{9,1... | collective-permute-start | bytes 3145736 | tf_op jit(solution)/shard_map/ppermute | solution.py:179
  114.9 26.2 %all-to-all-start.5 = ((bf16[4,512,128]{2,1,0:T(8,128)(2,1)}), bf16[4,512,128]{2,1,0:T(8,128)(2,1)S(1)}, u32[]{:S(2)}, u32[]{:S(2)}) async-start(bf16[4,512,128]{2,1,0:T(8,128)(2,1)} %get-tuple-element.20), calls=%async_computation.5 | async-start | bytes 1048576 | tf_op jit(solution)/shard_map/all_to_all | solution.py:146
  141.1 0.8 copy-start.4
  141.9 34.5 %all-to-all-start.7 = ((bf16[4,2,512,128]{3,2,1,0:T(8,128)(2,1)}), bf16[4,2,512,128]{3,2,1,0:T(8,128)(2,1)S(1)}, u32[]{:S(2)}, u32[]{:S(2)}) async-start(bf16[4,2,512,128]{3,2,1,0:T(8,128)(2,1)} %get-tuple-element.26), calls=%async_computation.7 | async-start | bytes 2097152 | tf_op jit(solution)/shard_map/all_to_all | solution.py:146
  176.4 29.3 %all-to-all-start.6 = ((bf16[4,2,512,128]{3,2,1,0:T(8,128)(2,1)}), bf16[4,2,512,128]{3,2,1,0:T(8,128)(2,1)}, u32[]{:S(2)}, u32[]{:S(2)}) async-start(bf16[4,2,512,128]{3,2,1,0:T(8,128)(2,1)} %get-tuple-element.23), calls=%async_computation.6 | async-start | bytes 2097152 | tf_op jit(solution)/shard_map/all_to_all | solution.py:146
  194.4 45.8 %collective-permute-start.1 = (f32[4,2,512,128]{3,2,1,0:T(8,128)}, f32[4,2,512,128]{3,2,1,0:T(8,128)}, u32[]{:S(2)}, u32[]{:S(2)}) collective-permute-start(f32[4,2,512,128]{3,2,1,0:T(8,128)} %get-tuple-element.30), channel_id=1, source_target_pairs={{0,4},{4,0},{1,5},{5,1},{2,6},{6,2},{3,7},{7,3},{8,12},{12,8},{9,1... | collective-permute-start | bytes 6291464 | tf_op jit(solution)/shard_map/ppermute | solution.py:201
  205.7 38.2 %all-to-all-start.8 = ((bf16[4,2,512,128]{3,2,1,0:T(8,128)(2,1)}), bf16[4,2,512,128]{3,2,1,0:T(8,128)(2,1)}, u32[]{:S(2)}, u32[]{:S(2)}) async-start(bf16[4,2,512,128]{3,2,1,0:T(8,128)(2,1)} %get-tuple-element.29), calls=%async_computation.8 | async-start | bytes 2097152 | tf_op jit(solution)/shard_map/all_to_all | solution.py:146
  243.9 27.4 %all-to-all-start.9 = ((bf16[4,2,512,128]{3,2,1,0:T(8,128)(2,1)}), bf16[4,2,512,128]{3,2,1,0:T(8,128)(2,1)S(1)}, u32[]{:S(2)}, u32[]{:S(2)}) async-start(bf16[4,2,512,128]{3,2,1,0:T(8,128)(2,1)} %fusion.5), calls=%async_computation.9 | async-start | bytes 2097152 | tf_op jit(solution)/shard_map/all_to_all | solution.py:146

commit v6 on v4

--- a/solution.py
+++ b/solution.py
@@ -56,7 +56,7 @@
     return attended, grad_query, key_terms, value_terms
 
 
-def attention_kernel(index_ref, flag_ref, q_ref, g_ref, ko_ref, kw_ref, kp_ref, vo_ref, vw_ref, vp_ref, ad_ref, terms_ref):
+def attention_kernel(index_ref, flag_ref, q_ref, g_ref, ko_ref, kw_ref, kp_ref, vo_ref, vw_ref, vp_ref, ad_ref, own_ref, win_ref, par_ref):
     place = pl.program_id(0)
     q = q_ref[0]
     g = g_ref[0]
@@ -95,10 +95,11 @@
         dscore = (shares[part] * (grad_probs - row_dot)).astype(jnp.bfloat16)
         term = jnp.dot(dscore, keys[part], preferred_element_type=jnp.float32)
         dq = term if dq is None else dq + term
-        terms_ref[0, part, 0] = (
+        out_ref = (own_ref, win_ref, par_ref)[part]
+        out_ref[0, 0] = (
             lax.dot_general(dscore, q, cols_by_cols, preferred_element_type=jnp.float32) * scaling
         )
-        terms_ref[0, part, 1] = lax.dot_general(
+        out_ref[0, 1] = lax.dot_general(
             shares_low[part], g, cols_by_cols, preferred_element_type=jnp.float32
         )
     ad_ref[0, 1] = (dq * scaling).astype(jnp.bfloat16)
@@ -120,15 +121,10 @@
             num_scalar_prefetch=2,
             grid=(places,),
             in_specs=[row_spec, row_spec, own_spec, window_spec, partner_spec, own_spec, window_spec, partner_spec],
-            out_specs=[
-                pl.BlockSpec((1, 2, rows, width), lambda p, idx, flag: (p, 0, 0, 0)),
-                pl.BlockSpec((1, 3, 2, rows, width), lambda p, idx, flag: (p, 0, 0, 0, 0)),
-            ],
-        ),
-        out_shape=[
-            jax.ShapeDtypeStruct((places, 2, rows, width), jnp.bfloat16),
-            jax.ShapeDtypeStruct((places, 3, 2, rows, width), jnp.float32),
-        ],
+            out_specs=[pl.BlockSpec((1, 2, rows, width), lambda p, idx, flag: (p, 0, 0, 0))] * 4,
+        ),
+        out_shape=[jax.ShapeDtypeStruct((places, 2, rows, width), jnp.bfloat16)]
+        + [jax.ShapeDtypeStruct((places, 2, rows, width), jnp.float32)] * 3,
         cost_estimate=pl.CostEstimate(
             flops=flops,
             transcendentals=3 * places * rows * rows,
@@ -198,17 +194,17 @@
         keepdims=False,
     )
     no_mask = jnp.zeros((1,), jnp.int32)
-    ad_odd, terms_odd = fused_terms(
+    ad_odd, own_odd, win_odd, par_odd = fused_terms(
         1, q_odd, g_odd, k_all, v_all, k_all, v_all, my_partners[1::2], no_mask
     )
     sent_odd = scatter_group(ad_odd, within, nseg, group)
 
     first_masked = (segment == 0).astype(jnp.int32).reshape(1)
-    ad_even, terms_even = fused_terms(
+    ad_even, own_even, win_even, par_even = fused_terms(
         0, q_even, g_even, k_all, v_all, window_kv[:, 0], window_kv[:, 1], my_partners[0::2], first_masked
     )
 
-    ret = terms_even[:, 1]
+    ret = win_even
     ret = jnp.where(segment == 0, jnp.roll(ret, -1, axis=0), ret)
     back_pairs = [(b, a) for a, b in next_segment_pairs(nseg, group)]
     window_back = lax.ppermute(ret, "seq", back_pairs)
@@ -217,12 +213,12 @@
     hits = my_partners[None, :] == place_ids[:, None]
     inverse = jnp.sum(jnp.where(hits, place_ids[None, :], 0), axis=1)
     slot = (inverse % 2) * (places // 2) + inverse // 2
-    partner_terms = jnp.concatenate([terms_even[:, 2], terms_odd[:, 2]], axis=0)
+    partner_terms = jnp.concatenate([par_even, par_odd], axis=0)
     partner_even = jnp.take(partner_terms, slot[0::2], axis=0)
     partner_odd = jnp.take(partner_terms, slot[1::2], axis=0)
-    grads_even = (terms_even[:, 0] + terms_odd[:, 1] + partner_even).astype(jnp.bfloat16)
+    grads_even = (own_even + win_odd + partner_even).astype(jnp.bfloat16)
     sent_even = scatter_group((ad_even, grads_even), within, nseg, group)
-    grads_odd = (terms_odd[:, 0] + window_back + partner_odd).astype(jnp.bfloat16)
+    grads_odd = (own_odd + window_back + partner_odd).astype(jnp.bfloat16)
     sent_last = scatter_group(grads_odd, within, nseg, group)
 
     shape = (heads, row_count, width)

time: 271 us -> 263 us (0.970)
  other arithmetic: 32.3 us -> 26.2 us
  local copies, waits for them, and re-layouts: 41.6 us -> 38.8 us
    ppermute x18, waiting for transfers between devices: 39.7 us -> 52.4 us  [gather_group(): lax.ppermute(pick(x, (within + shift) % group), 'seq', group_pairs(nseg,...]
    ppermute x12, waiting for transfers between devices: 35.9 us -> 29.8 us  [scatter_group(): lax.ppermute(pick(y, (within - shift) % group), 'seq', group_pairs(nseg,...]
    ppermute x1, waiting for transfers between devices: 4.11 us -> 0.01 us  [body(): window_back = lax.ppermute(ret, 'seq', back_pairs)]
    squeeze x2 -> x0, local copies, waits for them, and re-layouts: 3.47 us -> none  [body(): partner_terms = jnp.concatenate([terms_even[:, 2], terms_odd[:, 2]], axis=0)]
    convert_element_type x2, other arithmetic: 8.36 us -> 4.91 us  [the longest x1 2.76 us: body(): grads_even = (own_even + win_odd + partner_even).astype(jnp.bfloat16)]
  transfers between devices with their start and end apart: 32 -> 32, of which waited for: 10 -> 10; matrix products, arithmetic and copies ran while one was open for 14% -> 15% of each run, Pallas kernels for 7% -> 7%
where the time goes in v6:
time: 263 us; the launch traced here: 260 us
  waiting for transfers between devices  82.2 us (31%)
  starting transfers between devices  72.5 us (28%)
  local copies, waits for them, and re-layouts  38.8 us (15%)
  Pallas kernels  38.7 us (15%)
  other arithmetic  26.2 us (10%)
    ppermute x18, waiting for transfers between devices, gather_group(): lax.ppermute(pick(x, (within + shift) % group), 'seq', group_pairs(nseg,...  52.4 us
    pallas_call x2, Pallas kernels, fused_terms(): pl.pallas_call(attention_kernel, grid_spec=pltpu.PrefetchScalarGridSpec(n...  38.7 us
    ppermute x18, starting transfers between devices, gather_group(): lax.ppermute(pick(x, (within + shift) % group), 'seq', group_pairs(nseg,...  36.2 us
    ppermute x12, starting transfers between devices, scatter_group(): lax.ppermute(pick(y, (within - shift) % group), 'seq', group_pairs(nseg,...  33.3 us
    ppermute x12, waiting for transfers between devices, scatter_group(): lax.ppermute(pick(y, (within - shift) % group), 'seq', group_pairs(nseg,...  29.8 us
    dynamic_slice x10, local copies, waits for them, and re-layouts, pick(): lax.dynamic_index_in_dim(x, index, axis=0, keepdims=False)  9.02 us
    another operation x4, other arithmetic, scatter_group(): jnp.stack(r)  6.9 us
    gather x4, local copies, waits for them, and re-layouts, scatter_group(): jnp.take(jnp.stack(r), order, axis=0)  6.39 us
  transfers between devices with their start and end apart: 32, of which 10 were waited for; matrix products, arithmetic and copies ran while one was open for 15% of the time, Pallas kernels for 7%

profile of v6, /device:TPU:0, one launch (start us, length us, event | category | flops | bytes accessed | tf_op | source)
XLA Modules:
  0.0 259.6 jit_solution(8777613100024855649)
XLA Ops:
  0.8 2.3 constant_dynamic-slice_fusion.8
  3.1 5.0 %collective-permute-start.5 = (bf16[2,512,128]{2,1,0:T(8,128)(2,1)}, bf16[2,512,128]{2,1,0:T(8,128)(2,1)}, u32[]{:S(2)}, u32[]{:S(2)}) collective-permute-start(bf16[2,512,128]{2,1,0:T(8,128)(2,1)} %get-tuple-element.70), channel_id=1, source_target_pairs={{0,24},{8,0},{16,8},{24,16},{4,28},{12,4},{20,12},{28,20},{1,25},{... | collective-permute-start | bytes 786440 | tf_op jit(solution)/shard_map/ppermute | solution.py:147
  10.1 2.8 %collective-permute-start.2 = (bf16[2,512,128]{2,1,0:T(8,128)(2,1)}, bf16[2,512,128]{2,1,0:T(8,128)(2,1)}, u32[]{:S(2)}, u32[]{:S(2)}) collective-permute-start(bf16[2,512,128]{2,1,0:T(8,128)(2,1)} %get-tuple-element.74), channel_id=1, source_target_pairs={{0,24},{8,0},{16,8},{24,16},{4,28},{12,4},{20,12},{28,20},{1,25},{... | collective-permute-start | bytes 786440 | tf_op jit(solution)/shard_map/ppermute | solution.py:147
  15.8 10.0 %collective-permute-start = (bf16[2,512,128]{2,1,0:T(8,128)(2,1)}, bf16[2,512,128]{2,1,0:T(8,128)(2,1)S(1)}, u32[]{:S(2)}, u32[]{:S(2)}) collective-permute-start(bf16[2,512,128]{2,1,0:T(8,128)(2,1)} %get-tuple-element.76), channel_id=1, source_target_pairs={{0,8},{8,16},{16,24},{24,0},{4,12},{12,20},{20,28},{28,4},{1,9},{9... | collective-permute-start | bytes 786440 | tf_op jit(solution)/shard_map/ppermute | solution.py:147
  25.8 7.2 %collective-permute-done.4 = bf16[2,512,128]{2,1,0:T(8,128)(2,1)} collective-permute-done((bf16[2,512,128]{2,1,0:T(8,128)(2,1)}, bf16[2,512,128]{2,1,0:T(8,128)(2,1)}, u32[]{:S(2)}, u32[]{:S(2)}) %collective-permute-start.4) | collective-permute-done | bytes 262176 | tf_op jit(solution)/shard_map/ppermute | solution.py:147
  35.1 18.1 %collective-permute-done.1 = bf16[2,512,128]{2,1,0:T(8,128)(2,1)} collective-permute-done((bf16[2,512,128]{2,1,0:T(8,128)(2,1)}, bf16[2,512,128]{2,1,0:T(8,128)(2,1)}, u32[]{:S(2)}, u32[]{:S(2)}) %collective-permute-start.1) | collective-permute-done | bytes 262176 | tf_op jit(solution)/shard_map/ppermute | solution.py:147
  57.1 2.8 %collective-permute-start.10 = (bf16[512,128]{1,0:T(8,128)(2,1)S(1)}, bf16[512,128]{1,0:T(8,128)(2,1)S(1)}, u32[]{:S(2)}, u32[]{:S(2)}) collective-permute-start(bf16[512,128]{1,0:T(8,128)(2,1)S(1)} %get-tuple-element.87), channel_id=1, source_target_pairs={{0,16},{8,24},{16,0},{24,8},{4,20},{12,28},{20,4},{28,12},{1,17},{... | collective-permute-start | bytes 393224 | tf_op jit(solution)/shard_map/ppermute | solution.py:147
  64.0 4.9 %collective-permute-start.6 = (bf16[512,128]{1,0:T(8,128)(2,1)S(1)}, bf16[512,128]{1,0:T(8,128)(2,1)S(1)}, u32[]{:S(2)}, u32[]{:S(2)}) collective-permute-start(bf16[512,128]{1,0:T(8,128)(2,1)S(1)} %get-tuple-element.92), channel_id=1, source_target_pairs={{0,8},{8,16},{16,24},{24,0},{4,12},{12,20},{20,28},{28,4},{1,9},{9... | collective-permute-start | bytes 393224 | tf_op jit(solution)/shard_map/ppermute | solution.py:147
  70.1 8.2 %collective-permute-done.10 = bf16[512,128]{1,0:T(8,128)(2,1)S(1)} collective-permute-done((bf16[512,128]{1,0:T(8,128)(2,1)S(1)}, bf16[512,128]{1,0:T(8,128)(2,1)S(1)}, u32[]{:S(2)}, u32[]{:S(2)}) %collective-permute-start.10) | collective-permute-done | bytes 131104 | tf_op jit(solution)/shard_map/ppermute | solution.py:147
  89.0 2.4 collective-permute-done.17
  91.4 7.4 %collective-permute-done.16 = bf16[512,128]{1,0:T(8,128)(2,1)S(1)} collective-permute-done((bf16[512,128]{1,0:T(8,128)(2,1)S(1)}, bf16[512,128]{1,0:T(8,128)(2,1)S(1)}, u32[]{:S(2)}, u32[]{:S(2)}) %collective-permute-start.16) | collective-permute-done | bytes 131104 | tf_op jit(solution)/shard_map/ppermute | solution.py:147
  100.9 7.1 %collective-permute-done.13 = bf16[512,128]{1,0:T(8,128)(2,1)S(1)} collective-permute-done((bf16[512,128]{1,0:T(8,128)(2,1)S(1)}, bf16[512,128]{1,0:T(8,128)(2,1)S(1)}, u32[]{:S(2)}, u32[]{:S(2)}) %collective-permute-start.13) | collective-permute-done | bytes 131104 | tf_op jit(solution)/shard_map/ppermute | solution.py:147
  109.9 2.3 slice_bitcast_fusion
  112.1 19.2 %shard_map.84 = (bf16[4,2,512,128]{3,2,1,0:T(8,128)(2,1)}, f32[4,2,512,128]{3,2,1,0:T(8,128)}, f32[4,2,512,128]{3,2,1,0:T(8,128)}, f32[4,2,512,128]{3,2,1,0:T(8,128)}) custom-call(s32[4]{0:T(128)} %slice.76.index_ref, s32[1]{0:T(128)} %bitcast.1.flag_ref, bf16[4,512,128]{2,1,0:T(8,128)(2,1)} %get-tuple-element.98.q_ref, ...), custom_call_target="tpu_custom_call" | custom-call | flops 4831838208 | bytes 15728640 | tf_op jit(solution)/shard_map/pallas_call | solution.py:118
  137.2 19.4 %shard_map.85 = (bf16[4,2,512,128]{3,2,1,0:T(8,128)(2,1)}, f32[4,2,512,128]{3,2,1,0:T(8,128)}, f32[4,2,512,128]{3,2,1,0:T(8,128)}, f32[4,2,512,128]{3,2,1,0:T(8,128)}) custom-call(s32[4]{0:T(128)} %slice.88.index_ref, s32[1]{0:T(128)} %constant.274.clone.1.flag_ref, bf16[4,512,128]{2,1,0:T(8,128)(2,1)} %get-tuple-element.30.q_ref, ...), custom_call_target="tpu_custom_call" | custom-call | flops 4831838208 | bytes 15728640 | tf_op jit(solution)/shard_map/pallas_call | solution.py:118
  159.4 2.8 %collective-permute-start.22 = (bf16[2,512,128]{2,1,0:T(8,128)(2,1)S(1)}, bf16[2,512,128]{2,1,0:T(8,128)(2,1)}, u32[]{:S(2)}, u32[]{:S(2)}) collective-permute-start(bf16[2,512,128]{2,1,0:T(8,128)(2,1)S(1)} %get-tuple-element.64), channel_id=1, source_target_pairs={{0,24},{8,0},{16,8},{24,16},{4,28},{12,4},{20,12},{28,20},{1,25},{... | collective-permute-start | bytes 786440 | tf_op jit(solution)/shard_map/ppermute | solution.py:156
  166.1 2.9 %gather_fusion.8 = f32[4,2,512,128]{3,2,1,0:T(8,128)S(1)} fusion(f32[8,2,512,128]{3,2,1,0:T(8,128)} %constant_dynamic-update-slice_fusion, s32[1024]{0:T(1024)S(1)} %pad_clamp_fusion.1), kind=kCustom, calls=%fused_computation.2.clone | custom fusion | bytes 4194320 | tf_op jit(solution)/shard_map/jit(_take)/gather | solution.py:217
  168.9 2.8 %fusion.1 = bf16[4,2,512,128]{3,2,1,0:T(8,128)(2,1)S(1)} fusion(f32[4,2,512,128]{3,2,1,0:T(8,128)S(1)} %gather_fusion.8, f32[4,2,512,128]{3,2,1,0:T(8,128)} %get-tuple-element.33, f32[4,2,512,128]{3,2,1,0:T(8,128)} %get-tuple-element.34, pred[4]{0:T(512)(128)(4,1)S(1)} %get-tuple-element.105), kind=kLoop, calls=%fused_computation.16 | loop fusion | flops 2097152 | bytes 7340036 | tf_op jit(solution)/shard_map/convert_element_type | solution.py:219
  172.9 11.0 %collective-permute-done.23 = bf16[2,512,128]{2,1,0:T(8,128)(2,1)} collective-permute-done((bf16[2,512,128]{2,1,0:T(8,128)(2,1)S(1)}, bf16[2,512,128]{2,1,0:T(8,128)(2,1)}, u32[]{:S(2)}, u32[]{:S(2)}) %collective-permute-start.23) | collective-permute-done | bytes 262176 | tf_op jit(solution)/shard_map/ppermute | solution.py:156
  185.9 4.2 %collective-permute-start.26 = (bf16[2,512,128]{2,1,0:T(8,128)(2,1)}, bf16[2,512,128]{2,1,0:T(8,128)(2,1)}, u32[]{:S(2)}, u32[]{:S(2)}) collective-permute-start(bf16[2,512,128]{2,1,0:T(8,128)(2,1)} %get-tuple-element.45), channel_id=1, source_target_pairs={{0,16},{8,24},{16,0},{24,8},{4,20},{12,28},{20,4},{28,12},{1,17},{... | collective-permute-start | bytes 786440 | tf_op jit(solution)/shard_map/ppermute | solution.py:156
  190.1 3.5 %collective-permute-start.25 = (bf16[2,512,128]{2,1,0:T(8,128)(2,1)}, bf16[2,512,128]{2,1,0:T(8,128)(2,1)}, u32[]{:S(2)}, u32[]{:S(2)}) collective-permute-start(bf16[2,512,128]{2,1,0:T(8,128)(2,1)} %get-tuple-element.46), channel_id=1, source_target_pairs={{0,24},{8,0},{16,8},{24,16},{4,28},{12,4},{20,12},{28,20},{1,25},{... | collective-permute-start | bytes 786440 | tf_op jit(solution)/shard_map/ppermute | solution.py:156
  193.6 2.9 %gather_fusion.10 = f32[4,2,512,128]{3,2,1,0:T(8,128)S(1)} fusion(f32[8,2,512,128]{3,2,1,0:T(8,128)} %constant_dynamic-update-slice_fusion, s32[1024]{0:T(1024)S(1)} %pad_clamp_fusion), kind=kCustom, calls=%fused_computation.11.clone | custom fusion | bytes 4194320 | tf_op jit(solution)/shard_map/jit(_take)/gather | solution.py:218
  196.5 2.3 constant_dynamic-slice_fusion.3
  199.3 3.3 %collective-permute-start.19 = (bf16[2,512,128]{2,1,0:T(8,128)(2,1)}, bf16[2,512,128]{2,1,0:T(8,128)(2,1)}, u32[]{:S(2)}, u32[]{:S(2)}) collective-permute-start(bf16[2,512,128]{2,1,0:T(8,128)(2,1)} %get-tuple-element.58), channel_id=1, source_target_pairs={{0,24},{8,0},{16,8},{24,16},{4,28},{12,4},{20,12},{28,20},{1,25},{... | collective-permute-start | bytes 786440 | tf_op jit(solution)/shard_map/ppermute | solution.py:156
  205.8 3.8 %collective-permute-start.31 = (bf16[2,512,128]{2,1,0:T(8,128)(2,1)}, bf16[2,512,128]{2,1,0:T(8,128)(2,1)}, u32[]{:S(2)}, u32[]{:S(2)}) collective-permute-start(bf16[2,512,128]{2,1,0:T(8,128)(2,1)} %get-tuple-element.48), channel_id=1, source_target_pairs={{0,8},{8,16},{16,24},{24,0},{4,12},{12,20},{20,28},{28,4},{1,9},{9... | collective-permute-start | bytes 786440 | tf_op jit(solution)/shard_map/ppermute | solution.py:156
  209.6 10.2 %collective-permute-start.30 = (bf16[2,512,128]{2,1,0:T(8,128)(2,1)}, bf16[2,512,128]{2,1,0:T(8,128)(2,1)}, u32[]{:S(2)}, u32[]{:S(2)}) collective-permute-start(bf16[2,512,128]{2,1,0:T(8,128)(2,1)} %get-tuple-element.49), channel_id=1, source_target_pairs={{0,16},{8,24},{16,0},{24,8},{4,20},{12,28},{20,4},{28,12},{1,17},{... | collective-permute-start | bytes 786440 | tf_op jit(solution)/shard_map/ppermute | solution.py:156
  219.8 3.4 %collective-permute-start.29 = (bf16[2,512,128]{2,1,0:T(8,128)(2,1)}, bf16[2,512,128]{2,1,0:T(8,128)(2,1)}, u32[]{:S(2)}, u32[]{:S(2)}) collective-permute-start(bf16[2,512,128]{2,1,0:T(8,128)(2,1)} %get-tuple-element.50), channel_id=1, source_target_pairs={{0,24},{8,0},{16,8},{24,16},{4,28},{12,4},{20,12},{28,20},{1,25},{... | collective-permute-start | bytes 786440 | tf_op jit(solution)/shard_map/ppermute | solution.py:156
  225.2 11.8 %collective-permute-done.20 = bf16[2,512,128]{2,1,0:T(8,128)(2,1)} collective-permute-done((bf16[2,512,128]{2,1,0:T(8,128)(2,1)}, bf16[2,512,128]{2,1,0:T(8,128)(2,1)}, u32[]{:S(2)}, u32[]{:S(2)}) %collective-permute-start.20) | collective-permute-done | bytes 262176 | tf_op jit(solution)/shard_map/ppermute | solution.py:156
  237.0 2.2 pad_maximum_fusion.3
  241.2 7.0 %collective-permute-done.30 = bf16[2,512,128]{2,1,0:T(8,128)(2,1)} collective-permute-done((bf16[2,512,128]{2,1,0:T(8,128)(2,1)}, bf16[2,512,128]{2,1,0:T(8,128)(2,1)}, u32[]{:S(2)}, u32[]{:S(2)}) %collective-permute-start.30) | collective-permute-done | bytes 262176 | tf_op jit(solution)/shard_map/ppermute | solution.py:156
  248.2 2.2 pad_maximum_fusion.8
  250.4 2.9 %gather_fusion.11 = bf16[4,2,512,128]{3,2,1,0:T(8,128)(2,1)} fusion(bf16[4,2,512,128]{3,2,1,0:T(8,128)(2,1)} %pad_maximum_fusion.8, s32[1024]{0:T(1024)S(1)} %pad_clamp_fusion.2), kind=kCustom, calls=%fused_computation.7.clone | custom fusion | bytes 2097168 | tf_op jit(solution)/shard_map/jit(_take)/gather | solution.py:159
  (149 shorter events, 60.0 us)
Async XLA Ops:
  3.1 12.7 %collective-permute-start.5 = (bf16[2,512,128]{2,1,0:T(8,128)(2,1)}, bf16[2,512,128]{2,1,0:T(8,128)(2,1)}, u32[]{:S(2)}, u32[]{:S(2)}) collective-permute-start(bf16[2,512,128]{2,1,0:T(8,128)(2,1)} %get-tuple-element.70), channel_id=1, source_target_pairs={{0,24},{8,0},{16,8},{24,16},{4,28},{12,4},{20,12},{28,20},{1,25},{... | collective-permute-start | bytes 786440 | tf_op jit(solution)/shard_map/ppermute | solution.py:147
  8.1 24.9 %collective-permute-start.4 = (bf16[2,512,128]{2,1,0:T(8,128)(2,1)}, bf16[2,512,128]{2,1,0:T(8,128)(2,1)}, u32[]{:S(2)}, u32[]{:S(2)}) collective-permute-start(bf16[2,512,128]{2,1,0:T(8,128)(2,1)} %get-tuple-element.71), channel_id=1, source_target_pairs={{0,16},{8,24},{16,0},{24,8},{4,20},{12,28},{20,4},{28,12},{1,17},{... | collective-permute-start | bytes 786440 | tf_op jit(solution)/shard_map/ppermute | solution.py:147
  8.1 24.9 %collective-permute-start.3 = (bf16[2,512,128]{2,1,0:T(8,128)(2,1)}, bf16[2,512,128]{2,1,0:T(8,128)(2,1)}, u32[]{:S(2)}, u32[]{:S(2)}) collective-permute-start(bf16[2,512,128]{2,1,0:T(8,128)(2,1)} %get-tuple-element.72), channel_id=1, source_target_pairs={{0,8},{8,16},{16,24},{24,0},{4,12},{12,20},{20,28},{28,4},{1,9},{9... | collective-permute-start | bytes 786440 | tf_op jit(solution)/shard_map/ppermute | solution.py:147
  10.1 25.0 %collective-permute-start.2 = (bf16[2,512,128]{2,1,0:T(8,128)(2,1)}, bf16[2,512,128]{2,1,0:T(8,128)(2,1)}, u32[]{:S(2)}, u32[]{:S(2)}) collective-permute-start(bf16[2,512,128]{2,1,0:T(8,128)(2,1)} %get-tuple-element.74), channel_id=1, source_target_pairs={{0,24},{8,0},{16,8},{24,16},{4,28},{12,4},{20,12},{28,20},{1,25},{... | collective-permute-start | bytes 786440 | tf_op jit(solution)/shard_map/ppermute | solution.py:147
  12.9 40.3 %collective-permute-start.1 = (bf16[2,512,128]{2,1,0:T(8,128)(2,1)}, bf16[2,512,128]{2,1,0:T(8,128)(2,1)}, u32[]{:S(2)}, u32[]{:S(2)}) collective-permute-start(bf16[2,512,128]{2,1,0:T(8,128)(2,1)} %get-tuple-element.75), channel_id=1, source_target_pairs={{0,16},{8,24},{16,0},{24,8},{4,20},{12,28},{20,4},{28,12},{1,17},{... | collective-permute-start | bytes 786440 | tf_op jit(solution)/shard_map/ppermute | solution.py:147
  15.8 37.5 %collective-permute-start = (bf16[2,512,128]{2,1,0:T(8,128)(2,1)}, bf16[2,512,128]{2,1,0:T(8,128)(2,1)S(1)}, u32[]{:S(2)}, u32[]{:S(2)}) collective-permute-start(bf16[2,512,128]{2,1,0:T(8,128)(2,1)} %get-tuple-element.76), channel_id=1, source_target_pairs={{0,8},{8,16},{16,24},{24,0},{4,12},{12,20},{20,28},{28,4},{1,9},{9... | collective-permute-start | bytes 786440 | tf_op jit(solution)/shard_map/ppermute | solution.py:147
  57.0 7.0 %collective-permute-start.11 = (bf16[512,128]{1,0:T(8,128)(2,1)S(1)}, bf16[512,128]{1,0:T(8,128)(2,1)S(1)}, u32[]{:S(2)}, u32[]{:S(2)}) collective-permute-start(bf16[512,128]{1,0:T(8,128)(2,1)S(1)} %get-tuple-element.86), channel_id=1, source_target_pairs={{0,24},{8,0},{16,8},{24,16},{4,28},{12,4},{20,12},{28,20},{1,25},{... | collective-permute-start | bytes 393224 | tf_op jit(solution)/shard_map/ppermute | solution.py:147
  57.1 21.2 %collective-permute-start.10 = (bf16[512,128]{1,0:T(8,128)(2,1)S(1)}, bf16[512,128]{1,0:T(8,128)(2,1)S(1)}, u32[]{:S(2)}, u32[]{:S(2)}) collective-permute-start(bf16[512,128]{1,0:T(8,128)(2,1)S(1)} %get-tuple-element.87), channel_id=1, source_target_pairs={{0,16},{8,24},{16,0},{24,8},{4,20},{12,28},{20,4},{28,12},{1,17},{... | collective-permute-start | bytes 393224 | tf_op jit(solution)/shard_map/ppermute | solution.py:147
  59.9 19.9 %collective-permute-start.9 = (bf16[512,128]{1,0:T(8,128)(2,1)S(1)}, bf16[512,128]{1,0:T(8,128)(2,1)S(1)}, u32[]{:S(2)}, u32[]{:S(2)}) collective-permute-start(bf16[512,128]{1,0:T(8,128)(2,1)S(1)} %get-tuple-element.88), channel_id=1, source_target_pairs={{0,8},{8,16},{16,24},{24,0},{4,12},{12,20},{20,28},{28,4},{1,9},{9... | collective-permute-start | bytes 393224 | tf_op jit(solution)/shard_map/ppermute | solution.py:147
  61.9 18.6 %collective-permute-start.8 = (bf16[512,128]{1,0:T(8,128)(2,1)S(1)}, bf16[512,128]{1,0:T(8,128)(2,1)S(1)}, u32[]{:S(2)}, u32[]{:S(2)}) collective-permute-start(bf16[512,128]{1,0:T(8,128)(2,1)S(1)} %get-tuple-element.90), channel_id=1, source_target_pairs={{0,24},{8,0},{16,8},{24,16},{4,28},{12,4},{20,12},{28,20},{1,25},{... | collective-permute-start | bytes 393224 | tf_op jit(solution)/shard_map/ppermute | solution.py:147
  63.8 18.6 %collective-permute-start.7 = (bf16[512,128]{1,0:T(8,128)(2,1)S(1)}, bf16[512,128]{1,0:T(8,128)(2,1)S(1)}, u32[]{:S(2)}, u32[]{:S(2)}) collective-permute-start(bf16[512,128]{1,0:T(8,128)(2,1)S(1)} %get-tuple-element.91), channel_id=1, source_target_pairs={{0,16},{8,24},{16,0},{24,8},{4,20},{12,28},{20,4},{28,12},{1,17},{... | collective-permute-start | bytes 393224 | tf_op jit(solution)/shard_map/ppermute | solution.py:147
  64.0 18.3 %collective-permute-start.6 = (bf16[512,128]{1,0:T(8,128)(2,1)S(1)}, bf16[512,128]{1,0:T(8,128)(2,1)S(1)}, u32[]{:S(2)}, u32[]{:S(2)}) collective-permute-start(bf16[512,128]{1,0:T(8,128)(2,1)S(1)} %get-tuple-element.92), channel_id=1, source_target_pairs={{0,8},{8,16},{16,24},{24,0},{4,12},{12,20},{20,28},{28,4},{1,9},{9... | collective-permute-start | bytes 393224 | tf_op jit(solution)/shard_map/ppermute | solution.py:147
  78.3 31.6 %collective-permute-start.18 = (bf16[4,2,512,128]{3,2,0,1:T(8,128)(2,1)}, bf16[4,2,512,128]{3,2,0,1:T(8,128)(2,1)}, u32[]{:S(2)}, u32[]{:S(2)}) collective-permute-start(bf16[4,2,512,128]{3,2,0,1:T(8,128)(2,1)} %fusion.2), channel_id=1, source_target_pairs={{0,4},{8,12},{16,20},{24,28},{4,0},{12,8},{20,16},{28,24},{1,5},{9... | collective-permute-start | bytes 3145736 | tf_op jit(solution)/shard_map/ppermute | solution.py:188
  84.3 7.1 %collective-permute-start.17 = (bf16[512,128]{1,0:T(8,128)(2,1)S(1)}, bf16[512,128]{1,0:T(8,128)(2,1)S(1)}, u32[]{:S(2)}, u32[]{:S(2)}) collective-permute-start(bf16[512,128]{1,0:T(8,128)(2,1)S(1)} %get-tuple-element.78), channel_id=1, source_target_pairs={{0,24},{8,0},{16,8},{24,16},{4,28},{12,4},{20,12},{28,20},{1,25},{... | collective-permute-start | bytes 393224 | tf_op jit(solution)/shard_map/ppermute | solution.py:147
  84.4 14.4 %collective-permute-start.16 = (bf16[512,128]{1,0:T(8,128)(2,1)S(1)}, bf16[512,128]{1,0:T(8,128)(2,1)S(1)}, u32[]{:S(2)}, u32[]{:S(2)}) collective-permute-start(bf16[512,128]{1,0:T(8,128)(2,1)S(1)} %get-tuple-element.79), channel_id=1, source_target_pairs={{0,16},{8,24},{16,0},{24,8},{4,20},{12,28},{20,4},{28,12},{1,17},{... | collective-permute-start | bytes 393224 | tf_op jit(solution)/shard_map/ppermute | solution.py:147
  85.0 15.1 %collective-permute-start.15 = (bf16[512,128]{1,0:T(8,128)(2,1)S(1)}, bf16[512,128]{1,0:T(8,128)(2,1)S(1)}, u32[]{:S(2)}, u32[]{:S(2)}) collective-permute-start(bf16[512,128]{1,0:T(8,128)(2,1)S(1)} %get-tuple-element.80), channel_id=1, source_target_pairs={{0,8},{8,16},{16,24},{24,0},{4,12},{12,20},{20,28},{28,4},{1,9},{9... | collective-permute-start | bytes 393224 | tf_op jit(solution)/shard_map/ppermute | solution.py:147
  86.7 14.1 %collective-permute-start.14 = (bf16[512,128]{1,0:T(8,128)(2,1)S(1)}, bf16[512,128]{1,0:T(8,128)(2,1)S(1)}, u32[]{:S(2)}, u32[]{:S(2)}) collective-permute-start(bf16[512,128]{1,0:T(8,128)(2,1)S(1)} %get-tuple-element.82), channel_id=1, source_target_pairs={{0,24},{8,0},{16,8},{24,16},{4,28},{12,4},{20,12},{28,20},{1,25},{... | collective-permute-start | bytes 393224 | tf_op jit(solution)/shard_map/ppermute | solution.py:147
  91.4 16.6 %collective-permute-start.13 = (bf16[512,128]{1,0:T(8,128)(2,1)S(1)}, bf16[512,128]{1,0:T(8,128)(2,1)S(1)}, u32[]{:S(2)}, u32[]{:S(2)}) collective-permute-start(bf16[512,128]{1,0:T(8,128)(2,1)S(1)} %get-tuple-element.83), channel_id=1, source_target_pairs={{0,16},{8,24},{16,0},{24,8},{4,20},{12,28},{20,4},{28,12},{1,17},{... | collective-permute-start | bytes 393224 | tf_op jit(solution)/shard_map/ppermute | solution.py:147
  98.8 9.2 %collective-permute-start.12 = (bf16[512,128]{1,0:T(8,128)(2,1)S(1)}, bf16[512,128]{1,0:T(8,128)(2,1)S(1)}, u32[]{:S(2)}, u32[]{:S(2)}) collective-permute-start(bf16[512,128]{1,0:T(8,128)(2,1)S(1)} %get-tuple-element.84), channel_id=1, source_target_pairs={{0,8},{8,16},{16,24},{24,0},{4,12},{12,20},{20,28},{28,4},{1,9},{9... | collective-permute-start | bytes 393224 | tf_op jit(solution)/shard_map/ppermute | solution.py:147
  135.7 63.6 %collective-permute-start.28 = (f32[4,2,512,128]{3,2,1,0:T(8,128)}, f32[4,2,512,128]{3,2,1,0:T(8,128)}, u32[]{:S(2)}, u32[]{:S(2)}) collective-permute-start(f32[4,2,512,128]{3,2,1,0:T(8,128)} %maximum_select_fusion), channel_id=1, source_target_pairs={{4,0},{12,8},{20,16},{28,24},{0,4},{8,12},{16,20},{24,28},{5,1},{1... | collective-permute-start | bytes 6291464 | tf_op jit(solution)/shard_map/ppermute | solution.py:210
  158.1 14.8 %collective-permute-start.24 = (bf16[2,512,128]{2,1,0:T(8,128)(2,1)S(1)}, bf16[2,512,128]{2,1,0:T(8,128)(2,1)}, u32[]{:S(2)}, u32[]{:S(2)}) collective-permute-start(bf16[2,512,128]{2,1,0:T(8,128)(2,1)S(1)} %get-tuple-element.62), channel_id=1, source_target_pairs={{0,8},{8,16},{16,24},{24,0},{4,12},{12,20},{20,28},{28,4},{1,9},{9... | collective-permute-start | bytes 786440 | tf_op jit(solution)/shard_map/ppermute | solution.py:156
  158.1 25.8 %collective-permute-start.23 = (bf16[2,512,128]{2,1,0:T(8,128)(2,1)S(1)}, bf16[2,512,128]{2,1,0:T(8,128)(2,1)}, u32[]{:S(2)}, u32[]{:S(2)}) collective-permute-start(bf16[2,512,128]{2,1,0:T(8,128)(2,1)S(1)} %get-tuple-element.63), channel_id=1, source_target_pairs={{0,16},{8,24},{16,0},{24,8},{4,20},{12,28},{20,4},{28,12},{1,17},{... | collective-permute-start | bytes 786440 | tf_op jit(solution)/shard_map/ppermute | solution.py:156
  159.4 24.5 %collective-permute-start.22 = (bf16[2,512,128]{2,1,0:T(8,128)(2,1)S(1)}, bf16[2,512,128]{2,1,0:T(8,128)(2,1)}, u32[]{:S(2)}, u32[]{:S(2)}) collective-permute-start(bf16[2,512,128]{2,1,0:T(8,128)(2,1)S(1)} %get-tuple-element.64), channel_id=1, source_target_pairs={{0,24},{8,0},{16,8},{24,16},{4,28},{12,4},{20,12},{28,20},{1,25},{... | collective-permute-start | bytes 786440 | tf_op jit(solution)/shard_map/ppermute | solution.py:156
  172.6 26.1 %collective-permute-start.27 = (bf16[2,512,128]{2,1,0:T(8,128)(2,1)}, bf16[2,512,128]{2,1,0:T(8,128)(2,1)}, u32[]{:S(2)}, u32[]{:S(2)}) collective-permute-start(bf16[2,512,128]{2,1,0:T(8,128)(2,1)} %get-tuple-element.44), channel_id=1, source_target_pairs={{0,8},{8,16},{16,24},{24,0},{4,12},{12,20},{20,28},{28,4},{1,9},{9... | collective-permute-start | bytes 786440 | tf_op jit(solution)/shard_map/ppermute | solution.py:156
  185.9 19.9 %collective-permute-start.26 = (bf16[2,512,128]{2,1,0:T(8,128)(2,1)}, bf16[2,512,128]{2,1,0:T(8,128)(2,1)}, u32[]{:S(2)}, u32[]{:S(2)}) collective-permute-start(bf16[2,512,128]{2,1,0:T(8,128)(2,1)} %get-tuple-element.45), channel_id=1, source_target_pairs={{0,16},{8,24},{16,0},{24,8},{4,20},{12,28},{20,4},{28,12},{1,17},{... | collective-permute-start | bytes 786440 | tf_op jit(solution)/shard_map/ppermute | solution.py:156
  190.1 19.5 %collective-permute-start.25 = (bf16[2,512,128]{2,1,0:T(8,128)(2,1)}, bf16[2,512,128]{2,1,0:T(8,128)(2,1)}, u32[]{:S(2)}, u32[]{:S(2)}) collective-permute-start(bf16[2,512,128]{2,1,0:T(8,128)(2,1)} %get-tuple-element.46), channel_id=1, source_target_pairs={{0,24},{8,0},{16,8},{24,16},{4,28},{12,4},{20,12},{28,20},{1,25},{... | collective-permute-start | bytes 786440 | tf_op jit(solution)/shard_map/ppermute | solution.py:156
  198.7 21.0 %collective-permute-start.21 = (bf16[2,512,128]{2,1,0:T(8,128)(2,1)S(1)}, bf16[2,512,128]{2,1,0:T(8,128)(2,1)S(1)}, u32[]{:S(2)}, u32[]{:S(2)}) collective-permute-start(bf16[2,512,128]{2,1,0:T(8,128)(2,1)S(1)} %get-tuple-element.56), channel_id=1, source_target_pairs={{0,8},{8,16},{16,24},{24,0},{4,12},{12,20},{20,28},{28,4},{1,9},{9... | collective-permute-start | bytes 786440 | tf_op jit(solution)/shard_map/ppermute | solution.py:156
  198.7 38.2 %collective-permute-start.20 = (bf16[2,512,128]{2,1,0:T(8,128)(2,1)}, bf16[2,512,128]{2,1,0:T(8,128)(2,1)}, u32[]{:S(2)}, u32[]{:S(2)}) collective-permute-start(bf16[2,512,128]{2,1,0:T(8,128)(2,1)} %get-tuple-element.57), channel_id=1, source_target_pairs={{0,16},{8,24},{16,0},{24,8},{4,20},{12,28},{20,4},{28,12},{1,17},{... | collective-permute-start | bytes 786440 | tf_op jit(solution)/shard_map/ppermute | solution.py:156
  199.3 37.7 %collective-permute-start.19 = (bf16[2,512,128]{2,1,0:T(8,128)(2,1)}, bf16[2,512,128]{2,1,0:T(8,128)(2,1)}, u32[]{:S(2)}, u32[]{:S(2)}) collective-permute-start(bf16[2,512,128]{2,1,0:T(8,128)(2,1)} %get-tuple-element.58), channel_id=1, source_target_pairs={{0,24},{8,0},{16,8},{24,16},{4,28},{12,4},{20,12},{28,20},{1,25},{... | collective-permute-start | bytes 786440 | tf_op jit(solution)/shard_map/ppermute | solution.py:156
  205.8 35.4 %collective-permute-start.31 = (bf16[2,512,128]{2,1,0:T(8,128)(2,1)}, bf16[2,512,128]{2,1,0:T(8,128)(2,1)}, u32[]{:S(2)}, u32[]{:S(2)}) collective-permute-start(bf16[2,512,128]{2,1,0:T(8,128)(2,1)} %get-tuple-element.48), channel_id=1, source_target_pairs={{0,8},{8,16},{16,24},{24,0},{4,12},{12,20},{20,28},{28,4},{1,9},{9... | collective-permute-start | bytes 786440 | tf_op jit(solution)/shard_map/ppermute | solution.py:156
  209.6 38.6 %collective-permute-start.30 = (bf16[2,512,128]{2,1,0:T(8,128)(2,1)}, bf16[2,512,128]{2,1,0:T(8,128)(2,1)}, u32[]{:S(2)}, u32[]{:S(2)}) collective-permute-start(bf16[2,512,128]{2,1,0:T(8,128)(2,1)} %get-tuple-element.49), channel_id=1, source_target_pairs={{0,16},{8,24},{16,0},{24,8},{4,20},{12,28},{20,4},{28,12},{1,17},{... | collective-permute-start | bytes 786440 | tf_op jit(solution)/shard_map/ppermute | solution.py:156
  219.8 28.5 %collective-permute-start.29 = (bf16[2,512,128]{2,1,0:T(8,128)(2,1)}, bf16[2,512,128]{2,1,0:T(8,128)(2,1)}, u32[]{:S(2)}, u32[]{:S(2)}) collective-permute-start(bf16[2,512,128]{2,1,0:T(8,128)(2,1)} %get-tuple-element.50), channel_id=1, source_target_pairs={{0,24},{8,0},{16,8},{24,16},{4,28},{12,4},{20,12},{28,20},{1,25},{... | collective-permute-start | bytes 786440 | tf_op jit(solution)/shard_map/ppermute | solution.py:156
  (20 other events, 141.0 us)

commit v7 on v6

--- a/solution.py
+++ b/solution.py
@@ -145,8 +145,14 @@
     received = [pick(x, within)]
     for shift in range(1, group):
         received.append(lax.ppermute(pick(x, (within + shift) % group), "seq", group_pairs(nseg, group, shift)))
-    order = (within - jnp.arange(group, dtype=jnp.int32)) % group
-    return jax.tree.map(lambda *r: jnp.take(jnp.stack(r), order, axis=0), *received)
+
+    def place(*pieces):
+        out = jnp.zeros((group,) + pieces[0].shape, pieces[0].dtype)
+        for shift, piece in enumerate(pieces):
+            out = lax.dynamic_update_index_in_dim(out, piece, (within - shift) % group, 0)
+        return out
+
+    return jax.tree.map(place, *received)
 
 
 def scatter_group(y, within, nseg, group):
@@ -155,8 +161,19 @@
         returned.append(
             lax.ppermute(pick(y, (within - shift) % group), "seq", group_pairs(nseg, group, group - shift))
         )
-    order = (jnp.arange(group, dtype=jnp.int32) - within) % group
-    return jax.tree.map(lambda *r: jnp.take(jnp.stack(r), order, axis=0), *returned)
+    return [((within + shift) % group, piece) for shift, piece in enumerate(returned)]
+
+
+def assemble(even_parts, odd_parts, heads, shape):
+    first = even_parts[0][1]
+    out = jnp.zeros((heads, 2) + first.shape, first.dtype)
+    zero = jnp.zeros((), jnp.int32)
+    for column, parts in ((0, even_parts), (1, odd_parts)):
+        for head, piece in parts:
+            out = lax.dynamic_update_slice(
+                out, piece[None, None], (head, jnp.int32(column), zero, zero)
+            )
+    return out.reshape(shape)
 
 
 def body(queries, key_rows, value_rows, grad_out, partner_pos):
@@ -223,15 +240,16 @@
 
     shape = (heads, row_count, width)
 
-    def joined(even, odd):
-        return jnp.stack([even, odd], axis=1).reshape(shape)
-
-    ad_e, grads_e = sent_even
+    def column(parts, index, entry=None):
+        if entry is None:
+            return [(h, piece[index]) for h, piece in parts]
+        return [(h, piece[entry][index]) for h, piece in parts]
+
     return (
-        joined(ad_e[:, 0], sent_odd[:, 0]),
-        joined(ad_e[:, 1], sent_odd[:, 1]),
-        joined(grads_e[:, 0], sent_last[:, 0]),
-        joined(grads_e[:, 1], sent_last[:, 1]),
+        assemble(column(sent_even, 0, 0), column(sent_odd, 0), heads, shape),
+        assemble(column(sent_even, 1, 0), column(sent_odd, 1), heads, shape),
+        assemble(column(sent_even, 0, 1), column(sent_last, 0), heads, shape),
+        assemble(column(sent_even, 1, 1), column(sent_last, 1), heads, shape),
     )
 
 

time: 263 us -> 250 us (0.951); the launches traced: 260 us -> 249 us
  other arithmetic: 26.2 us -> 7.37 us
  local copies, waits for them, and re-layouts: 38.8 us -> 50.3 us
  waiting for transfers between devices: 82.2 us -> 74.4 us
  starting transfers between devices: 72.5 us -> 77.2 us
    dynamic_update_slice x0 -> x36, local copies, waits for them, and re-layouts: none -> 21.8 us  [the longest x18 14.8 us: assemble(): lax.dynamic_update_slice(out, piece[None, None], (head, jnp.int32(column)...]
    ppermute x18, waiting for transfers between devices: 52.4 us -> 34.9 us  [gather_group(): lax.ppermute(pick(x, (within + shift) % group), 'seq', group_pairs(nseg,...]
    another operation x14 -> x0, other arithmetic: 13.9 us -> none  [the longest x4 6.9 us: scatter_group(): jnp.stack(r)]
    gather x10 -> x0, local copies, waits for them, and re-layouts: 10.5 us -> none  [the longest x4 6.39 us: scatter_group(): jnp.take(jnp.stack(r), order, axis=0)]
    ppermute x12, waiting for transfers between devices: 29.8 us -> 39.5 us  [scatter_group(): lax.ppermute(pick(y, (within - shift) % group), 'seq', group_pairs(nseg,...]
    squeeze x0 -> x10, local copies, waits for them, and re-layouts: none -> 9.15 us  [pick(): lax.dynamic_index_in_dim(x, index, axis=0, keepdims=False)]
    dynamic_slice x10 -> x0, local copies, waits for them, and re-layouts: 9.02 us -> none  [pick(): lax.dynamic_index_in_dim(x, index, axis=0, keepdims=False)]
    select_n x6 -> x0, other arithmetic: 4.36 us -> none  [the longest x4 2.58 us: gather_group(): jnp.take(jnp.stack(r), order, axis=0)]
  transfers between devices with their start and end apart: 32 -> 32, of which waited for: 10 -> 13; matrix products, arithmetic and copies ran while one was open for 15% -> 21% of each run, Pallas kernels for 7% -> 16%
where the time goes in v7:
time: 250 us; the launch traced here: 249 us
  starting transfers between devices  77.2 us (31%)
  waiting for transfers between devices  74.4 us (30%)
  local copies, waits for them, and re-layouts  50.3 us (20%)
  Pallas kernels  38.7 us (15%)
  other arithmetic  7.37 us (3%)
    ppermute x12, waiting for transfers between devices, scatter_group(): lax.ppermute(pick(y, (within - shift) % group), 'seq', group_pairs(nseg,...  39.5 us
    pallas_call x2, Pallas kernels, fused_terms(): pl.pallas_call(attention_kernel, grid_spec=pltpu.PrefetchScalarGridSpec(n...  38.7 us
    ppermute x18, starting transfers between devices, gather_group(): lax.ppermute(pick(x, (within + shift) % group), 'seq', group_pairs(nseg,...  38.6 us
    ppermute x12, starting transfers between devices, scatter_group(): lax.ppermute(pick(y, (within - shift) % group), 'seq', group_pairs(nseg,...  35.9 us
    ppermute x18, waiting for transfers between devices, gather_group(): lax.ppermute(pick(x, (within + shift) % group), 'seq', group_pairs(nseg,...  34.9 us
    dynamic_update_slice x18, local copies, waits for them, and re-layouts, assemble(): lax.dynamic_update_slice(out, piece[None, None], (head, jnp.int32(column)...  14.8 us
    squeeze x10, local copies, waits for them, and re-layouts, pick(): lax.dynamic_index_in_dim(x, index, axis=0, keepdims=False)  9.15 us
    dynamic_update_slice x18, local copies, waits for them, and re-layouts, place(): lax.dynamic_update_index_in_dim(out, piece, (within - shift) % group, 0)  6.97 us
  transfers between devices with their start and end apart: 32, of which 13 were waited for; matrix products, arithmetic and copies ran while one was open for 21% of the time, Pallas kernels for 16%

profile of v7, /device:TPU:0, one launch (start us, length us, event | category | flops | bytes accessed | tf_op | source)
XLA Modules:
  0.0 249.4 jit_solution(11950775949942794678)
XLA Ops:
  0.9 2.3 dynamic-slice_bitcast_fusion.12
  3.2 3.0 %collective-permute-start.3 = (bf16[2,512,128]{2,1,0:T(8,128)(2,1)}, bf16[2,512,128]{2,1,0:T(8,128)(2,1)}, u32[]{:S(2)}, u32[]{:S(2)}) collective-permute-start(bf16[2,512,128]{2,1,0:T(8,128)(2,1)} %get-tuple-element.61), channel_id=1, source_target_pairs={{0,8},{8,16},{16,24},{24,0},{4,12},{12,20},{20,28},{28,4},{1,9},{9... | collective-permute-start | bytes 786440 | tf_op jit(solution)/shard_map/ppermute | solution.py:147
  6.2 2.6 %collective-permute-start.4 = (bf16[2,512,128]{2,1,0:T(8,128)(2,1)}, bf16[2,512,128]{2,1,0:T(8,128)(2,1)}, u32[]{:S(2)}, u32[]{:S(2)}) collective-permute-start(bf16[2,512,128]{2,1,0:T(8,128)(2,1)} %get-tuple-element.60), channel_id=1, source_target_pairs={{0,16},{8,24},{16,0},{24,8},{4,20},{12,28},{20,4},{28,12},{1,17},{... | collective-permute-start | bytes 786440 | tf_op jit(solution)/shard_map/ppermute | solution.py:147
  12.6 2.7 %slice_bitcast_fusion.2 = (bf16[4,512,128]{2,1,0:T(8,128)(2,1)S(1)}, bf16[4,512,128]{2,1,0:T(8,128)(2,1)}, bf16[4,512,128]{2,1,0:T(8,128)(2,1)}, bf16[4,512,128]{2,1,0:T(8,128)(2,1)S(1)}) fusion(bf16[4,2,512,128]{3,2,1,0:T(8,128)(2,1)} %bitcast.247, bf16[4,2,512,128]{3,2,1,0:T(8,128)(2,1)} %bitcast.248), kind=kLoop, calls=%fused_computation.16 | loop fusion | bytes 4194304 | tf_op jit(solution)/shard_map/squeeze | solution.py:200
  17.0 2.8 %collective-permute-start.2 = (bf16[2,512,128]{2,1,0:T(8,128)(2,1)}, bf16[2,512,128]{2,1,0:T(8,128)(2,1)S(1)}, u32[]{:S(2)}, u32[]{:S(2)}) collective-permute-start(bf16[2,512,128]{2,1,0:T(8,128)(2,1)} %get-tuple-element.63), channel_id=1, source_target_pairs={{0,24},{8,0},{16,8},{24,16},{4,28},{12,4},{20,12},{28,20},{1,25},{... | collective-permute-start | bytes 786440 | tf_op jit(solution)/shard_map/ppermute | solution.py:147
  20.8 11.9 %collective-permute-done = bf16[2,512,128]{2,1,0:T(8,128)(2,1)} collective-permute-done((bf16[2,512,128]{2,1,0:T(8,128)(2,1)}, bf16[2,512,128]{2,1,0:T(8,128)(2,1)}, u32[]{:S(2)}, u32[]{:S(2)}) %collective-permute-start) | collective-permute-done | bytes 262176 | tf_op jit(solution)/shard_map/ppermute | solution.py:147
  34.7 14.0 %collective-permute-done.1 = bf16[2,512,128]{2,1,0:T(8,128)(2,1)} collective-permute-done((bf16[2,512,128]{2,1,0:T(8,128)(2,1)}, bf16[2,512,128]{2,1,0:T(8,128)(2,1)}, u32[]{:S(2)}, u32[]{:S(2)}) %collective-permute-start.1) | collective-permute-done | bytes 262176 | tf_op jit(solution)/shard_map/ppermute | solution.py:147
  51.4 4.9 %collective-permute-start.9 = (bf16[512,128]{1,0:T(8,128)(2,1)S(1)}, bf16[512,128]{1,0:T(8,128)(2,1)S(1)}, u32[]{:S(2)}, u32[]{:S(2)}) collective-permute-start(bf16[512,128]{1,0:T(8,128)(2,1)S(1)} %get-tuple-element.77), channel_id=1, source_target_pairs={{0,8},{8,16},{16,24},{24,0},{4,12},{12,20},{20,28},{28,4},{1,9},{9... | collective-permute-start | bytes 393224 | tf_op jit(solution)/shard_map/ppermute | solution.py:147
  58.0 2.9 %collective-permute-start.10 = (bf16[512,128]{1,0:T(8,128)(2,1)S(1)}, bf16[512,128]{1,0:T(8,128)(2,1)S(1)}, u32[]{:S(2)}, u32[]{:S(2)}) collective-permute-start(bf16[512,128]{1,0:T(8,128)(2,1)S(1)} %get-tuple-element.76), channel_id=1, source_target_pairs={{0,16},{8,24},{16,0},{24,8},{4,20},{12,28},{20,4},{28,12},{1,17},{... | collective-permute-start | bytes 393224 | tf_op jit(solution)/shard_map/ppermute | solution.py:147
  61.0 2.1 collective-permute-start.6
  63.5 4.7 %collective-permute-done.10 = bf16[512,128]{1,0:T(8,128)(2,1)S(1)} collective-permute-done((bf16[512,128]{1,0:T(8,128)(2,1)S(1)}, bf16[512,128]{1,0:T(8,128)(2,1)S(1)}, u32[]{:S(2)}, u32[]{:S(2)}) %collective-permute-start.10) | collective-permute-done | bytes 131104 | tf_op jit(solution)/shard_map/ppermute | solution.py:147
  68.2 8.3 %collective-permute-start.8 = (bf16[512,128]{1,0:T(8,128)(2,1)S(1)}, bf16[512,128]{1,0:T(8,128)(2,1)S(1)}, u32[]{:S(2)}, u32[]{:S(2)}) collective-permute-start(bf16[512,128]{1,0:T(8,128)(2,1)S(1)} %get-tuple-element.79), channel_id=1, source_target_pairs={{0,24},{8,0},{16,8},{24,16},{4,28},{12,4},{20,12},{28,20},{1,25},{... | collective-permute-start | bytes 393224 | tf_op jit(solution)/shard_map/ppermute | solution.py:147
  80.0 2.8 %collective-permute-start.15 = (bf16[512,128]{1,0:T(8,128)(2,1)}, bf16[512,128]{1,0:T(8,128)(2,1)}, u32[]{:S(2)}, u32[]{:S(2)}) collective-permute-start(bf16[512,128]{1,0:T(8,128)(2,1)} %get-tuple-element.69), channel_id=1, source_target_pairs={{0,8},{8,16},{16,24},{24,0},{4,12},{12,20},{20,28},{28,4},{1,9},{9... | collective-permute-start | bytes 393224 | tf_op jit(solution)/shard_map/ppermute | solution.py:147
  82.8 2.0 collective-permute-start.16
  87.7 19.5 %shard_map.85 = (bf16[4,2,512,128]{3,2,1,0:T(8,128)(2,1)}, f32[4,2,512,128]{3,2,1,0:T(8,128)}, f32[4,2,512,128]{3,2,1,0:T(8,128)}, f32[4,2,512,128]{3,2,1,0:T(8,128)}) custom-call(s32[4]{0:T(128)} %slice.171.index_ref, s32[1]{0:T(128)} %constant.358.clone.1.flag_ref, bf16[4,512,128]{2,1,0:T(8,128)(2,1)} %copy-done.16, bf16[4,512,128]{2,1,0:T(8,128)(2,1)} %copy-done.15, ...), custom_call_target="tpu_custom_call" | custom-call | flops 4831838208 | bytes 15728640 | tf_op jit(solution)/shard_map/pallas_call | solution.py:118
  107.2 2.0 dynamic-slice_bitcast_fusion.6
  113.5 2.2 collective-permute-start.22
  119.9 19.2 %shard_map.84 = (bf16[4,2,512,128]{3,2,1,0:T(8,128)(2,1)}, f32[4,2,512,128]{3,2,1,0:T(8,128)}, f32[4,2,512,128]{3,2,1,0:T(8,128)}, f32[4,2,512,128]{3,2,1,0:T(8,128)}) custom-call(s32[4]{0:T(128)} %slice.156.index_ref, s32[1]{0:T(128)} %bitcast.1.flag_ref, bf16[4,512,128]{2,1,0:T(8,128)(2,1)} %copy-done.20, bf16[4,512,128]{2,1,0:T(8,128)(2,1)} %copy-done.19, ...), custom_call_target="tpu_custom_call" | custom-call | flops 4831838208 | bytes 15728640 | tf_op jit(solution)/shard_map/pallas_call | solution.py:118
  147.7 2.9 %gather_fusion = f32[4,2,512,128]{3,2,1,0:T(8,128)S(1)} fusion(f32[8,2,512,128]{3,2,1,0:T(8,128)} %constant_dynamic-update-slice_fusion, s32[1024]{0:T(1024)S(1)} %pad_clamp_fusion.1), kind=kCustom, calls=%fused_computation.clone | custom fusion | bytes 4194320 | tf_op jit(solution)/shard_map/jit(_take)/gather | solution.py:234
  150.6 2.8 %fusion.1 = bf16[4,2,512,128]{3,2,1,0:T(8,128)(2,1)S(1)} fusion(f32[4,2,512,128]{3,2,1,0:T(8,128)S(1)} %gather_fusion, f32[4,2,512,128]{3,2,1,0:T(8,128)} %get-tuple-element.31, f32[4,2,512,128]{3,2,1,0:T(8,128)} %get-tuple-element.32, pred[4]{0:T(512)(128)(4,1)S(1)} %copy-done.21), kind=kLoop, calls=%fused_computation.6 | loop fusion | flops 2097152 | bytes 7340036 | tf_op jit(solution)/shard_map/convert_element_type | solution.py:236
  154.5 15.5 %collective-permute-start.25 = (bf16[2,512,128]{2,1,0:T(8,128)(2,1)}, bf16[2,512,128]{2,1,0:T(8,128)(2,1)}, u32[]{:S(2)}, u32[]{:S(2)}) collective-permute-start(bf16[2,512,128]{2,1,0:T(8,128)(2,1)} %get-tuple-element.44), channel_id=1, source_target_pairs={{0,24},{8,0},{16,8},{24,16},{4,28},{12,4},{20,12},{28,20},{1,25},{... | collective-permute-start | bytes 786440 | tf_op jit(solution)/shard_map/ppermute | solution.py:162
  171.9 2.9 %gather_fusion.1 = f32[4,2,512,128]{3,2,1,0:T(8,128)S(1)} fusion(f32[8,2,512,128]{3,2,1,0:T(8,128)} %constant_dynamic-update-slice_fusion, s32[1024]{0:T(1024)S(1)} %pad_clamp_fusion), kind=kCustom, calls=%fused_computation.1.clone | custom fusion | bytes 4194320 | tf_op jit(solution)/shard_map/jit(_take)/gather | solution.py:235
  174.7 2.4 collective-permute-done.25
  177.1 9.9 %collective-permute-start.27 = (bf16[2,512,128]{2,1,0:T(8,128)(2,1)}, bf16[2,512,128]{2,1,0:T(8,128)(2,1)S(1)}, u32[]{:S(2)}, u32[]{:S(2)}) collective-permute-start(bf16[2,512,128]{2,1,0:T(8,128)(2,1)} %get-tuple-element.42), channel_id=1, source_target_pairs={{0,8},{8,16},{16,24},{24,0},{4,12},{12,20},{20,28},{28,4},{1,9},{9... | collective-permute-start | bytes 786440 | tf_op jit(solution)/shard_map/ppermute | solution.py:162
  188.7 2.5 collective-permute-done.26
  193.0 2.4 collective-permute-start.20
  196.1 2.6 %collective-permute-done.19 = bf16[2,512,128]{2,1,0:T(8,128)(2,1)S(1)} collective-permute-done((bf16[2,512,128]{2,1,0:T(8,128)(2,1)}, bf16[2,512,128]{2,1,0:T(8,128)(2,1)S(1)}, u32[]{:S(2)}, u32[]{:S(2)}) %collective-permute-start.19) | collective-permute-done | bytes 262176 | tf_op jit(solution)/shard_map/ppermute | solution.py:162
  199.4 13.2 %collective-permute-done.20 = bf16[2,512,128]{2,1,0:T(8,128)(2,1)S(1)} collective-permute-done((bf16[2,512,128]{2,1,0:T(8,128)(2,1)}, bf16[2,512,128]{2,1,0:T(8,128)(2,1)S(1)}, u32[]{:S(2)}, u32[]{:S(2)}) %collective-permute-start.20) | collective-permute-done | bytes 262176 | tf_op jit(solution)/shard_map/ppermute | solution.py:162
  218.9 2.2 fusion
  221.2 3.9 %collective-permute-start.29 = (bf16[2,512,128]{2,1,0:T(8,128)(2,1)S(1)}, bf16[2,512,128]{2,1,0:T(8,128)(2,1)S(1)}, u32[]{:S(2)}, u32[]{:S(2)}) collective-permute-start(bf16[2,512,128]{2,1,0:T(8,128)(2,1)S(1)} %get-tuple-element.41), channel_id=1, source_target_pairs={{0,24},{8,0},{16,8},{24,16},{4,28},{12,4},{20,12},{28,20},{1,25},{... | collective-permute-start | bytes 786440 | tf_op jit(solution)/shard_map/ppermute | solution.py:162
  228.4 3.5 %collective-permute-done.29 = bf16[2,512,128]{2,1,0:T(8,128)(2,1)S(1)} collective-permute-done((bf16[2,512,128]{2,1,0:T(8,128)(2,1)S(1)}, bf16[2,512,128]{2,1,0:T(8,128)(2,1)S(1)}, u32[]{:S(2)}, u32[]{:S(2)}) %collective-permute-start.29) | collective-permute-done | bytes 262176 | tf_op jit(solution)/shard_map/ppermute | solution.py:162
  232.6 15.3 %collective-permute-done.30 = bf16[2,512,128]{2,1,0:T(8,128)(2,1)S(1)} collective-permute-done((bf16[2,512,128]{2,1,0:T(8,128)(2,1)S(1)}, bf16[2,512,128]{2,1,0:T(8,128)(2,1)S(1)}, u32[]{:S(2)}, u32[]{:S(2)}) %collective-permute-start.30) | collective-permute-done | bytes 262176 | tf_op jit(solution)/shard_map/ppermute | solution.py:162
  (162 shorter events, 56.4 us)
Async XLA Ops:
  3.2 13.8 %collective-permute-start.3 = (bf16[2,512,128]{2,1,0:T(8,128)(2,1)}, bf16[2,512,128]{2,1,0:T(8,128)(2,1)}, u32[]{:S(2)}, u32[]{:S(2)}) collective-permute-start(bf16[2,512,128]{2,1,0:T(8,128)(2,1)} %get-tuple-element.61), channel_id=1, source_target_pairs={{0,8},{8,16},{16,24},{24,0},{4,12},{12,20},{20,28},{28,4},{1,9},{9... | collective-permute-start | bytes 786440 | tf_op jit(solution)/shard_map/ppermute | solution.py:147
  6.2 27.5 %collective-permute-start.4 = (bf16[2,512,128]{2,1,0:T(8,128)(2,1)}, bf16[2,512,128]{2,1,0:T(8,128)(2,1)}, u32[]{:S(2)}, u32[]{:S(2)}) collective-permute-start(bf16[2,512,128]{2,1,0:T(8,128)(2,1)} %get-tuple-element.60), channel_id=1, source_target_pairs={{0,16},{8,24},{16,0},{24,8},{4,20},{12,28},{20,4},{28,12},{1,17},{... | collective-permute-start | bytes 786440 | tf_op jit(solution)/shard_map/ppermute | solution.py:147
  8.8 40.9 %collective-permute-start.5 = (bf16[2,512,128]{2,1,0:T(8,128)(2,1)}, bf16[2,512,128]{2,1,0:T(8,128)(2,1)S(1)}, u32[]{:S(2)}, u32[]{:S(2)}) collective-permute-start(bf16[2,512,128]{2,1,0:T(8,128)(2,1)} %get-tuple-element.59), channel_id=1, source_target_pairs={{0,24},{8,0},{16,8},{24,16},{4,28},{12,4},{20,12},{28,20},{1,25},{... | collective-permute-start | bytes 786440 | tf_op jit(solution)/shard_map/ppermute | solution.py:147
  11.2 21.5 %collective-permute-start = (bf16[2,512,128]{2,1,0:T(8,128)(2,1)}, bf16[2,512,128]{2,1,0:T(8,128)(2,1)}, u32[]{:S(2)}, u32[]{:S(2)}) collective-permute-start(bf16[2,512,128]{2,1,0:T(8,128)(2,1)} %get-tuple-element.65), channel_id=1, source_target_pairs={{0,8},{8,16},{16,24},{24,0},{4,12},{12,20},{20,28},{28,4},{1,9},{9... | collective-permute-start | bytes 786440 | tf_op jit(solution)/shard_map/ppermute | solution.py:147
  11.9 36.8 %collective-permute-start.1 = (bf16[2,512,128]{2,1,0:T(8,128)(2,1)}, bf16[2,512,128]{2,1,0:T(8,128)(2,1)}, u32[]{:S(2)}, u32[]{:S(2)}) collective-permute-start(bf16[2,512,128]{2,1,0:T(8,128)(2,1)} %get-tuple-element.64), channel_id=1, source_target_pairs={{0,16},{8,24},{16,0},{24,8},{4,20},{12,28},{20,4},{28,12},{1,17},{... | collective-permute-start | bytes 786440 | tf_op jit(solution)/shard_map/ppermute | solution.py:147
  17.0 32.8 %collective-permute-start.2 = (bf16[2,512,128]{2,1,0:T(8,128)(2,1)}, bf16[2,512,128]{2,1,0:T(8,128)(2,1)S(1)}, u32[]{:S(2)}, u32[]{:S(2)}) collective-permute-start(bf16[2,512,128]{2,1,0:T(8,128)(2,1)} %get-tuple-element.63), channel_id=1, source_target_pairs={{0,24},{8,0},{16,8},{24,16},{4,28},{12,4},{20,12},{28,20},{1,25},{... | collective-permute-start | bytes 786440 | tf_op jit(solution)/shard_map/ppermute | solution.py:147
  51.4 11.7 %collective-permute-start.9 = (bf16[512,128]{1,0:T(8,128)(2,1)S(1)}, bf16[512,128]{1,0:T(8,128)(2,1)S(1)}, u32[]{:S(2)}, u32[]{:S(2)}) collective-permute-start(bf16[512,128]{1,0:T(8,128)(2,1)S(1)} %get-tuple-element.77), channel_id=1, source_target_pairs={{0,8},{8,16},{16,24},{24,0},{4,12},{12,20},{20,28},{28,4},{1,9},{9... | collective-permute-start | bytes 393224 | tf_op jit(solution)/shard_map/ppermute | solution.py:147
  56.5 62.2 %collective-permute-start.18 = (bf16[4,2,512,128]{3,2,0,1:T(8,128)(2,1)S(1)}, bf16[4,2,512,128]{3,2,0,1:T(8,128)(2,1)S(1)}, u32[]{:S(2)}, u32[]{:S(2)}) collective-permute-start(bf16[4,2,512,128]{3,2,0,1:T(8,128)(2,1)S(1)} %fusion.2), channel_id=1, source_target_pairs={{0,4},{8,12},{16,20},{24,28},{4,0},{12,8},{20,16},{28,24},{1,5},{9... | collective-permute-start | bytes 3145736 | tf_op jit(solution)/shard_map/ppermute | solution.py:205
  58.0 10.2 %collective-permute-start.10 = (bf16[512,128]{1,0:T(8,128)(2,1)S(1)}, bf16[512,128]{1,0:T(8,128)(2,1)S(1)}, u32[]{:S(2)}, u32[]{:S(2)}) collective-permute-start(bf16[512,128]{1,0:T(8,128)(2,1)S(1)} %get-tuple-element.76), channel_id=1, source_target_pairs={{0,16},{8,24},{16,0},{24,8},{4,20},{12,28},{20,4},{28,12},{1,17},{... | collective-permute-start | bytes 393224 | tf_op jit(solution)/shard_map/ppermute | solution.py:147
  60.9 15.7 %collective-permute-start.11 = (bf16[512,128]{1,0:T(8,128)(2,1)S(1)}, bf16[512,128]{1,0:T(8,128)(2,1)S(1)}, u32[]{:S(2)}, u32[]{:S(2)}) collective-permute-start(bf16[512,128]{1,0:T(8,128)(2,1)S(1)} %get-tuple-element.75), channel_id=1, source_target_pairs={{0,24},{8,0},{16,8},{24,16},{4,28},{12,4},{20,12},{28,20},{1,25},{... | collective-permute-start | bytes 393224 | tf_op jit(solution)/shard_map/ppermute | solution.py:147
  61.0 15.6 %collective-permute-start.6 = (bf16[512,128]{1,0:T(8,128)(2,1)S(1)}, bf16[512,128]{1,0:T(8,128)(2,1)S(1)}, u32[]{:S(2)}, u32[]{:S(2)}) collective-permute-start(bf16[512,128]{1,0:T(8,128)(2,1)S(1)} %get-tuple-element.81), channel_id=1, source_target_pairs={{0,8},{8,16},{16,24},{24,0},{4,12},{12,20},{20,28},{28,4},{1,9},{9... | collective-permute-start | bytes 393224 | tf_op jit(solution)/shard_map/ppermute | solution.py:147
  63.1 15.4 %collective-permute-start.7 = (bf16[512,128]{1,0:T(8,128)(2,1)S(1)}, bf16[512,128]{1,0:T(8,128)(2,1)S(1)}, u32[]{:S(2)}, u32[]{:S(2)}) collective-permute-start(bf16[512,128]{1,0:T(8,128)(2,1)S(1)} %get-tuple-element.80), channel_id=1, source_target_pairs={{0,16},{8,24},{16,0},{24,8},{4,20},{12,28},{20,4},{28,12},{1,17},{... | collective-permute-start | bytes 393224 | tf_op jit(solution)/shard_map/ppermute | solution.py:147
  68.2 10.8 %collective-permute-start.8 = (bf16[512,128]{1,0:T(8,128)(2,1)S(1)}, bf16[512,128]{1,0:T(8,128)(2,1)S(1)}, u32[]{:S(2)}, u32[]{:S(2)}) collective-permute-start(bf16[512,128]{1,0:T(8,128)(2,1)S(1)} %get-tuple-element.79), channel_id=1, source_target_pairs={{0,24},{8,0},{16,8},{24,16},{4,28},{12,4},{20,12},{28,20},{1,25},{... | collective-permute-start | bytes 393224 | tf_op jit(solution)/shard_map/ppermute | solution.py:147
  80.0 29.2 %collective-permute-start.15 = (bf16[512,128]{1,0:T(8,128)(2,1)}, bf16[512,128]{1,0:T(8,128)(2,1)}, u32[]{:S(2)}, u32[]{:S(2)}) collective-permute-start(bf16[512,128]{1,0:T(8,128)(2,1)} %get-tuple-element.69), channel_id=1, source_target_pairs={{0,8},{8,16},{16,24},{24,0},{4,12},{12,20},{20,28},{28,4},{1,9},{9... | collective-permute-start | bytes 393224 | tf_op jit(solution)/shard_map/ppermute | solution.py:147
  82.8 28.2 %collective-permute-start.16 = (bf16[512,128]{1,0:T(8,128)(2,1)}, bf16[512,128]{1,0:T(8,128)(2,1)}, u32[]{:S(2)}, u32[]{:S(2)}) collective-permute-start(bf16[512,128]{1,0:T(8,128)(2,1)} %get-tuple-element.68), channel_id=1, source_target_pairs={{0,16},{8,24},{16,0},{24,8},{4,20},{12,28},{20,4},{28,12},{1,17},{... | collective-permute-start | bytes 393224 | tf_op jit(solution)/shard_map/ppermute | solution.py:147
  84.8 28.7 %collective-permute-start.17 = (bf16[512,128]{1,0:T(8,128)(2,1)}, bf16[512,128]{1,0:T(8,128)(2,1)}, u32[]{:S(2)}, u32[]{:S(2)}) collective-permute-start(bf16[512,128]{1,0:T(8,128)(2,1)} %get-tuple-element.67), channel_id=1, source_target_pairs={{0,24},{8,0},{16,8},{24,16},{4,28},{12,4},{20,12},{28,20},{1,25},{... | collective-permute-start | bytes 393224 | tf_op jit(solution)/shard_map/ppermute | solution.py:147
  86.0 30.7 %collective-permute-start.12 = (bf16[512,128]{1,0:T(8,128)(2,1)}, bf16[512,128]{1,0:T(8,128)(2,1)S(1)}, u32[]{:S(2)}, u32[]{:S(2)}) collective-permute-start(bf16[512,128]{1,0:T(8,128)(2,1)} %get-tuple-element.73), channel_id=1, source_target_pairs={{0,8},{8,16},{16,24},{24,0},{4,12},{12,20},{20,28},{28,4},{1,9},{9... | collective-permute-start | bytes 393224 | tf_op jit(solution)/shard_map/ppermute | solution.py:147
  109.2 8.6 %collective-permute-start.13 = (bf16[512,128]{1,0:T(8,128)(2,1)}, bf16[512,128]{1,0:T(8,128)(2,1)S(1)}, u32[]{:S(2)}, u32[]{:S(2)}) collective-permute-start(bf16[512,128]{1,0:T(8,128)(2,1)} %get-tuple-element.72), channel_id=1, source_target_pairs={{0,16},{8,24},{16,0},{24,8},{4,20},{12,28},{20,4},{28,12},{1,17},{... | collective-permute-start | bytes 393224 | tf_op jit(solution)/shard_map/ppermute | solution.py:147
  111.0 7.7 %collective-permute-start.14 = (bf16[512,128]{1,0:T(8,128)(2,1)}, bf16[512,128]{1,0:T(8,128)(2,1)S(1)}, u32[]{:S(2)}, u32[]{:S(2)}) collective-permute-start(bf16[512,128]{1,0:T(8,128)(2,1)} %get-tuple-element.71), channel_id=1, source_target_pairs={{0,24},{8,0},{16,8},{24,16},{4,28},{12,4},{20,12},{28,20},{1,25},{... | collective-permute-start | bytes 393224 | tf_op jit(solution)/shard_map/ppermute | solution.py:147
  113.5 102.2 %collective-permute-start.22 = (bf16[2,512,128]{2,1,0:T(8,128)(2,1)}, bf16[2,512,128]{2,1,0:T(8,128)(2,1)}, u32[]{:S(2)}, u32[]{:S(2)}) collective-permute-start(bf16[2,512,128]{2,1,0:T(8,128)(2,1)} %get-tuple-element.49), channel_id=1, source_target_pairs={{0,24},{8,0},{16,8},{24,16},{4,28},{12,4},{20,12},{28,20},{1,25},{... | collective-permute-start | bytes 786440 | tf_op jit(solution)/shard_map/ppermute | solution.py:162
  116.7 100.6 %collective-permute-start.23 = (bf16[2,512,128]{2,1,0:T(8,128)(2,1)}, bf16[2,512,128]{2,1,0:T(8,128)(2,1)}, u32[]{:S(2)}, u32[]{:S(2)}) collective-permute-start(bf16[2,512,128]{2,1,0:T(8,128)(2,1)} %get-tuple-element.48), channel_id=1, source_target_pairs={{0,16},{8,24},{16,0},{24,8},{4,20},{12,28},{20,4},{28,12},{1,17},{... | collective-permute-start | bytes 786440 | tf_op jit(solution)/shard_map/ppermute | solution.py:162
  142.7 76.2 %collective-permute-start.28 = (f32[4,2,512,128]{3,2,1,0:T(8,128)}, f32[4,2,512,128]{3,2,1,0:T(8,128)}, u32[]{:S(2)}, u32[]{:S(2)}) collective-permute-start(f32[4,2,512,128]{3,2,1,0:T(8,128)} %maximum_select_fusion), channel_id=1, source_target_pairs={{4,0},{12,8},{20,16},{28,24},{0,4},{8,12},{16,20},{24,28},{5,1},{1... | collective-permute-start | bytes 6291464 | tf_op jit(solution)/shard_map/ppermute | solution.py:227
  154.5 22.6 %collective-permute-start.25 = (bf16[2,512,128]{2,1,0:T(8,128)(2,1)}, bf16[2,512,128]{2,1,0:T(8,128)(2,1)}, u32[]{:S(2)}, u32[]{:S(2)}) collective-permute-start(bf16[2,512,128]{2,1,0:T(8,128)(2,1)} %get-tuple-element.44), channel_id=1, source_target_pairs={{0,24},{8,0},{16,8},{24,16},{4,28},{12,4},{20,12},{28,20},{1,25},{... | collective-permute-start | bytes 786440 | tf_op jit(solution)/shard_map/ppermute | solution.py:162
  170.0 21.1 %collective-permute-start.26 = (bf16[2,512,128]{2,1,0:T(8,128)(2,1)}, bf16[2,512,128]{2,1,0:T(8,128)(2,1)}, u32[]{:S(2)}, u32[]{:S(2)}) collective-permute-start(bf16[2,512,128]{2,1,0:T(8,128)(2,1)} %get-tuple-element.43), channel_id=1, source_target_pairs={{0,16},{8,24},{16,0},{24,8},{4,20},{12,28},{20,4},{28,12},{1,17},{... | collective-permute-start | bytes 786440 | tf_op jit(solution)/shard_map/ppermute | solution.py:162
  177.1 15.9 %collective-permute-start.27 = (bf16[2,512,128]{2,1,0:T(8,128)(2,1)}, bf16[2,512,128]{2,1,0:T(8,128)(2,1)S(1)}, u32[]{:S(2)}, u32[]{:S(2)}) collective-permute-start(bf16[2,512,128]{2,1,0:T(8,128)(2,1)} %get-tuple-element.42), channel_id=1, source_target_pairs={{0,8},{8,16},{16,24},{24,0},{4,12},{12,20},{20,28},{28,4},{1,9},{9... | collective-permute-start | bytes 786440 | tf_op jit(solution)/shard_map/ppermute | solution.py:162
  191.1 7.6 %collective-permute-start.19 = (bf16[2,512,128]{2,1,0:T(8,128)(2,1)}, bf16[2,512,128]{2,1,0:T(8,128)(2,1)S(1)}, u32[]{:S(2)}, u32[]{:S(2)}) collective-permute-start(bf16[2,512,128]{2,1,0:T(8,128)(2,1)} %get-tuple-element.52), channel_id=1, source_target_pairs={{0,24},{8,0},{16,8},{24,16},{4,28},{12,4},{20,12},{28,20},{1,25},{... | collective-permute-start | bytes 786440 | tf_op jit(solution)/shard_map/ppermute | solution.py:162
  193.0 19.7 %collective-permute-start.20 = (bf16[2,512,128]{2,1,0:T(8,128)(2,1)}, bf16[2,512,128]{2,1,0:T(8,128)(2,1)S(1)}, u32[]{:S(2)}, u32[]{:S(2)}) collective-permute-start(bf16[2,512,128]{2,1,0:T(8,128)(2,1)} %get-tuple-element.51), channel_id=1, source_target_pairs={{0,16},{8,24},{16,0},{24,8},{4,20},{12,28},{20,4},{28,12},{1,17},{... | collective-permute-start | bytes 786440 | tf_op jit(solution)/shard_map/ppermute | solution.py:162
  198.7 14.6 %collective-permute-start.21 = (bf16[2,512,128]{2,1,0:T(8,128)(2,1)}, bf16[2,512,128]{2,1,0:T(8,128)(2,1)S(1)}, u32[]{:S(2)}, u32[]{:S(2)}) collective-permute-start(bf16[2,512,128]{2,1,0:T(8,128)(2,1)} %get-tuple-element.50), channel_id=1, source_target_pairs={{0,8},{8,16},{16,24},{24,0},{4,12},{12,20},{20,28},{28,4},{1,9},{9... | collective-permute-start | bytes 786440 | tf_op jit(solution)/shard_map/ppermute | solution.py:162
  212.6 12.4 %collective-permute-start.24 = (bf16[2,512,128]{2,1,0:T(8,128)(2,1)S(1)}, bf16[2,512,128]{2,1,0:T(8,128)(2,1)S(1)}, u32[]{:S(2)}, u32[]{:S(2)}) collective-permute-start(bf16[2,512,128]{2,1,0:T(8,128)(2,1)S(1)} %get-tuple-element.47), channel_id=1, source_target_pairs={{0,8},{8,16},{16,24},{24,0},{4,12},{12,20},{20,28},{28,4},{1,9},{9... | collective-permute-start | bytes 786440 | tf_op jit(solution)/shard_map/ppermute | solution.py:162
  221.2 10.7 %collective-permute-start.29 = (bf16[2,512,128]{2,1,0:T(8,128)(2,1)S(1)}, bf16[2,512,128]{2,1,0:T(8,128)(2,1)S(1)}, u32[]{:S(2)}, u32[]{:S(2)}) collective-permute-start(bf16[2,512,128]{2,1,0:T(8,128)(2,1)S(1)} %get-tuple-element.41), channel_id=1, source_target_pairs={{0,24},{8,0},{16,8},{24,16},{4,28},{12,4},{20,12},{28,20},{1,25},{... | collective-permute-start | bytes 786440 | tf_op jit(solution)/shard_map/ppermute | solution.py:162
  225.7 22.2 %collective-permute-start.30 = (bf16[2,512,128]{2,1,0:T(8,128)(2,1)S(1)}, bf16[2,512,128]{2,1,0:T(8,128)(2,1)S(1)}, u32[]{:S(2)}, u32[]{:S(2)}) collective-permute-start(bf16[2,512,128]{2,1,0:T(8,128)(2,1)S(1)} %get-tuple-element.40), channel_id=1, source_target_pairs={{0,16},{8,24},{16,0},{24,8},{4,20},{12,28},{20,4},{28,12},{1,17},{... | collective-permute-start | bytes 786440 | tf_op jit(solution)/shard_map/ppermute | solution.py:162
  225.7 22.9 %collective-permute-start.31 = (bf16[2,512,128]{2,1,0:T(8,128)(2,1)S(1)}, bf16[2,512,128]{2,1,0:T(8,128)(2,1)S(1)}, u32[]{:S(2)}, u32[]{:S(2)}) collective-permute-start(bf16[2,512,128]{2,1,0:T(8,128)(2,1)S(1)} %get-tuple-element.39), channel_id=1, source_target_pairs={{0,8},{8,16},{16,24},{24,0},{4,12},{12,20},{20,28},{28,4},{1,9},{9... | collective-permute-start | bytes 786440 | tf_op jit(solution)/shard_map/ppermute | solution.py:162
  (22 other events, 179.3 us)

commit v8 on v7

--- a/solution.py
+++ b/solution.py
@@ -192,13 +192,19 @@
         return x.reshape(heads, blocks, BLK, width)
 
     q4, g4, k4, v4 = split(queries), split(grad_out), split(key_rows), split(value_rows)
-    k_local, v_local = gather_group((k4, v4), within, nseg, group)
-    k_all = k_local.reshape(places, BLK, width)
-    v_all = v_local.reshape(places, BLK, width)
-    k_all, v_all, q_odd_send, g_odd_send = lax.optimization_barrier((k_all, v_all, q4[:, 1], g4[:, 1]))
-    q_odd, g_odd = gather_group((q_odd_send, g_odd_send), within, nseg, group)
-    q_odd, g_odd, q_even_send, g_even_send = lax.optimization_barrier((q_odd, g_odd, q4[:, 0], g4[:, 0]))
-    q_even, g_even = gather_group((q_even_send, g_even_send), within, nseg, group)
+    kv_local = gather_group(jnp.stack([k4, v4], axis=1), within, nseg, group)
+    k_all = kv_local[:, 0].reshape(places, BLK, width)
+    v_all = kv_local[:, 1].reshape(places, BLK, width)
+    k_all, v_all, qd_odd_send = lax.optimization_barrier(
+        (k_all, v_all, jnp.stack([q4[:, 1], g4[:, 1]], axis=1))
+    )
+    qd_odd = gather_group(qd_odd_send, within, nseg, group)
+    q_odd, g_odd = qd_odd[:, 0], qd_odd[:, 1]
+    q_odd, g_odd, qd_even_send = lax.optimization_barrier(
+        (q_odd, g_odd, jnp.stack([q4[:, 0], g4[:, 0]], axis=1))
+    )
+    qd_even = gather_group(qd_even_send, within, nseg, group)
+    q_even, g_even = qd_even[:, 0], qd_even[:, 1]
 
     odd_kv = jnp.stack([k_all[1::2], v_all[1::2]], axis=1)
     odd_send = jnp.where(segment == nseg - 1, jnp.roll(odd_kv, 1, axis=0), odd_kv)
@@ -234,7 +240,7 @@
     partner_even = jnp.take(partner_terms, slot[0::2], axis=0)
     partner_odd = jnp.take(partner_terms, slot[1::2], axis=0)
     grads_even = (own_even + win_odd + partner_even).astype(jnp.bfloat16)
-    sent_even = scatter_group((ad_even, grads_even), within, nseg, group)
+    sent_even = scatter_group(jnp.concatenate([ad_even, grads_even], axis=1), within, nseg, group)
     grads_odd = (own_odd + window_back + partner_odd).astype(jnp.bfloat16)
     sent_last = scatter_group(grads_odd, within, nseg, group)
 
@@ -246,10 +252,10 @@
         return [(h, piece[entry][index]) for h, piece in parts]
 
     return (
-        assemble(column(sent_even, 0, 0), column(sent_odd, 0), heads, shape),
-        assemble(column(sent_even, 1, 0), column(sent_odd, 1), heads, shape),
-        assemble(column(sent_even, 0, 1), column(sent_last, 0), heads, shape),
-        assemble(column(sent_even, 1, 1), column(sent_last, 1), heads, shape),
+        assemble(column(sent_even, 0), column(sent_odd, 0), heads, shape),
+        assemble(column(sent_even, 1), column(sent_odd, 1), heads, shape),
+        assemble(column(sent_even, 2), column(sent_last, 0), heads, shape),
+        assemble(column(sent_even, 3), column(sent_last, 1), heads, shape),
     )
 
 

time: 250 us -> 241 us (0.964)
  starting transfers between devices: 77.2 us -> 65.1 us
  waiting for transfers between devices: 74.4 us -> 80 us
  local copies, waits for them, and re-layouts: 50.3 us -> 45 us
  other arithmetic: 7.37 us -> 10.7 us
    ppermute x18 -> x9, starting transfers between devices: 38.6 us -> 28.7 us  [gather_group(): lax.ppermute(pick(x, (within + shift) % group), 'seq', group_pairs(nseg,...]
    ppermute x18 -> x9, waiting for transfers between devices: 34.9 us -> 42.1 us  [gather_group(): lax.ppermute(pick(x, (within + shift) % group), 'seq', group_pairs(nseg,...]
    squeeze x10 -> x4, local copies, waits for them, and re-layouts: 9.15 us -> 3.05 us  [pick(): lax.dynamic_index_in_dim(x, index, axis=0, keepdims=False)]
    unnamed x45 -> x43, local copies, waits for them, and re-layouts: 4.07 us -> 7.96 us
    dynamic_update_slice x18 -> x9, local copies, waits for them, and re-layouts: 6.97 us -> 3.56 us  [place(): lax.dynamic_update_index_in_dim(out, piece, (within - shift) % group, 0)]
    ppermute x12 -> x9, starting transfers between devices: 35.9 us -> 33.3 us  [scatter_group(): lax.ppermute(pick(y, (within - shift) % group), 'seq', group_pairs(nseg,...]
    ppermute x12 -> x9, waiting for transfers between devices: 39.5 us -> 37.9 us  [scatter_group(): lax.ppermute(pick(y, (within - shift) % group), 'seq', group_pairs(nseg,...]
    dynamic_update_slice x18 -> x19, local copies, waits for them, and re-layouts: 14.8 us -> 14.1 us  [assemble(): lax.dynamic_update_slice(out, piece[None, None], (head, jnp.int32(column)...]
  transfers between devices with their start and end apart: 32 -> 20, of which waited for: 13 -> 9; matrix products, arithmetic and copies ran while one was open for 21% -> 18% of each run, Pallas kernels for 16% -> 16%
where the time goes in v8:
time: 241 us
  waiting for transfers between devices  80 us (33%)
  starting transfers between devices  65.1 us (27%)
  local copies, waits for them, and re-layouts  45 us (19%)
  Pallas kernels  38.5 us (16%)
  other arithmetic  10.7 us (4%)
    ppermute x9, waiting for transfers between devices, gather_group(): lax.ppermute(pick(x, (within + shift) % group), 'seq', group_pairs(nseg,...  42.1 us
    pallas_call x2, Pallas kernels, fused_terms(): pl.pallas_call(attention_kernel, grid_spec=pltpu.PrefetchScalarGridSpec(n...  38.5 us
    ppermute x9, waiting for transfers between devices, scatter_group(): lax.ppermute(pick(y, (within - shift) % group), 'seq', group_pairs(nseg,...  37.9 us
    ppermute x9, starting transfers between devices, scatter_group(): lax.ppermute(pick(y, (within - shift) % group), 'seq', group_pairs(nseg,...  33.3 us
    ppermute x9, starting transfers between devices, gather_group(): lax.ppermute(pick(x, (within + shift) % group), 'seq', group_pairs(nseg,...  28.7 us
    dynamic_update_slice x19, local copies, waits for them, and re-layouts, assemble(): lax.dynamic_update_slice(out, piece[None, None], (head, jnp.int32(column)...  14.1 us
    unnamed x43, local copies, waits for them, and re-layouts  7.96 us
  transfers between devices with their start and end apart: 20, of which 9 were waited for; matrix products, arithmetic and copies ran while one was open for 18% of the time, Pallas kernels for 16%

profile of v8, /device:TPU:0, one launch (start us, length us, event | category | flops | bytes accessed | tf_op | source)
XLA Modules:
  0.0 240.5 jit_solution(16695574906416283830)
XLA Ops:
  3.5 3.0 %collective-permute-start = (bf16[2,2,512,128]{3,2,1,0:T(8,128)(2,1)}, bf16[2,2,512,128]{3,2,1,0:T(8,128)(2,1)}, u32[]{:S(2)}, u32[]{:S(2)}) collective-permute-start(bf16[2,2,512,128]{3,2,1,0:T(8,128)(2,1)} %get-tuple-element.41), channel_id=1, source_target_pairs={{0,8},{8,16},{16,24},{24,0},{4,12},{12,20},{20,28},{28,4},{1,9},{9... | collective-permute-start | bytes 1572872 | tf_op jit(solution)/shard_map/ppermute | solution.py:147
  6.5 2.6 %collective-permute-start.1 = (bf16[2,2,512,128]{3,2,1,0:T(8,128)(2,1)}, bf16[2,2,512,128]{3,2,1,0:T(8,128)(2,1)}, u32[]{:S(2)}, u32[]{:S(2)}) collective-permute-start(bf16[2,2,512,128]{3,2,1,0:T(8,128)(2,1)} %get-tuple-element.42), channel_id=1, source_target_pairs={{0,16},{8,24},{16,0},{24,8},{4,20},{12,28},{20,4},{28,12},{1,17},{... | collective-permute-start | bytes 1572872 | tf_op jit(solution)/shard_map/ppermute | solution.py:147
  14.5 7.2 %collective-permute-done = bf16[2,2,512,128]{3,2,1,0:T(8,128)(2,1)} collective-permute-done((bf16[2,2,512,128]{3,2,1,0:T(8,128)(2,1)}, bf16[2,2,512,128]{3,2,1,0:T(8,128)(2,1)}, u32[]{:S(2)}, u32[]{:S(2)}) %collective-permute-start) | collective-permute-done | bytes 524320 | tf_op jit(solution)/shard_map/ppermute | solution.py:147
  22.8 20.5 %collective-permute-done.1 = bf16[2,2,512,128]{3,2,1,0:T(8,128)(2,1)} collective-permute-done((bf16[2,2,512,128]{3,2,1,0:T(8,128)(2,1)}, bf16[2,2,512,128]{3,2,1,0:T(8,128)(2,1)}, u32[]{:S(2)}, u32[]{:S(2)}) %collective-permute-start.1) | collective-permute-done | bytes 524320 | tf_op jit(solution)/shard_map/ppermute | solution.py:147
  47.9 10.6 %collective-permute-start.3 = (bf16[2,512,128]{2,1,0:T(8,128)(2,1)S(1)}, bf16[2,512,128]{2,1,0:T(8,128)(2,1)S(1)}, u32[]{:S(2)}, u32[]{:S(2)}) collective-permute-start(bf16[2,512,128]{2,1,0:T(8,128)(2,1)S(1)} %get-tuple-element.69), channel_id=1, source_target_pairs={{0,8},{8,16},{16,24},{24,0},{4,12},{12,20},{20,28},{28,4},{1,9},{9... | collective-permute-start | bytes 786440 | tf_op jit(solution)/shard_map/ppermute | solution.py:147
  58.5 2.7 %collective-permute-start.4 = (bf16[2,512,128]{2,1,0:T(8,128)(2,1)S(1)}, bf16[2,512,128]{2,1,0:T(8,128)(2,1)S(1)}, u32[]{:S(2)}, u32[]{:S(2)}) collective-permute-start(bf16[2,512,128]{2,1,0:T(8,128)(2,1)S(1)} %get-tuple-element.68), channel_id=1, source_target_pairs={{0,16},{8,24},{16,0},{24,8},{4,20},{12,28},{20,4},{28,12},{1,17},{... | collective-permute-start | bytes 786440 | tf_op jit(solution)/shard_map/ppermute | solution.py:147
  61.5 1.6 collective-permute-start.9
  63.0 4.9 %collective-permute-done.3 = bf16[2,512,128]{2,1,0:T(8,128)(2,1)S(1)} collective-permute-done((bf16[2,512,128]{2,1,0:T(8,128)(2,1)S(1)}, bf16[2,512,128]{2,1,0:T(8,128)(2,1)S(1)}, u32[]{:S(2)}, u32[]{:S(2)}) %collective-permute-start.3) | collective-permute-done | bytes 262176 | tf_op jit(solution)/shard_map/ppermute | solution.py:147
  68.0 9.4 %collective-permute-done.4 = bf16[2,512,128]{2,1,0:T(8,128)(2,1)S(1)} collective-permute-done((bf16[2,512,128]{2,1,0:T(8,128)(2,1)S(1)}, bf16[2,512,128]{2,1,0:T(8,128)(2,1)S(1)}, u32[]{:S(2)}, u32[]{:S(2)}) %collective-permute-start.4) | collective-permute-done | bytes 262176 | tf_op jit(solution)/shard_map/ppermute | solution.py:147
  79.6 6.0 %collective-permute-start.6 = (bf16[2,512,128]{2,1,0:T(8,128)(2,1)}, bf16[2,512,128]{2,1,0:T(8,128)(2,1)S(1)}, u32[]{:S(2)}, u32[]{:S(2)}) collective-permute-start(bf16[2,512,128]{2,1,0:T(8,128)(2,1)} %get-tuple-element.59), channel_id=1, source_target_pairs={{0,8},{8,16},{16,24},{24,0},{4,12},{12,20},{20,28},{28,4},{1,9},{9... | collective-permute-start | bytes 786440 | tf_op jit(solution)/shard_map/ppermute | solution.py:147
  88.0 19.3 %shard_map.85 = (bf16[4,2,512,128]{3,2,1,0:T(8,128)(2,1)}, f32[4,2,512,128]{3,2,1,0:T(8,128)}, f32[4,2,512,128]{3,2,1,0:T(8,128)}, f32[4,2,512,128]{3,2,1,0:T(8,128)}) custom-call(s32[4]{0:T(128)} %slice.191.index_ref, s32[1]{0:T(128)} %constant.280.clone.1.flag_ref, bf16[4,512,128]{2,1,0:T(8,128)(2,1)} %get-tuple-element.25.q_ref, ...), custom_call_target="tpu_custom_call" | custom-call | flops 4831838208 | bytes 15728640 | tf_op jit(solution)/shard_map/pallas_call | solution.py:118
  107.3 2.0 dynamic-slice_bitcast_fusion.3
  109.3 2.0 collective-permute-start.13
  112.5 2.3 slice_bitcast_fusion
  114.8 19.2 %shard_map.84 = (bf16[4,2,512,128]{3,2,1,0:T(8,128)(2,1)}, f32[4,2,512,128]{3,2,1,0:T(8,128)}, f32[4,2,512,128]{3,2,1,0:T(8,128)}, f32[4,2,512,128]{3,2,1,0:T(8,128)}) custom-call(s32[4]{0:T(128)} %slice.174.index_ref, s32[1]{0:T(128)} %bitcast.1.flag_ref, bf16[4,512,128]{2,1,0:T(8,128)(2,1)} %get-tuple-element.56.q_ref, ...), custom_call_target="tpu_custom_call" | custom-call | flops 4831838208 | bytes 15728640 | tf_op jit(solution)/shard_map/pallas_call | solution.py:118
  134.1 1.7 copy.88
  144.3 2.9 %gather_fusion = f32[4,2,512,128]{3,2,1,0:T(8,128)S(1)} fusion(f32[8,2,512,128]{3,2,1,0:T(8,128)} %constant_dynamic-update-slice_fusion, s32[1024]{0:T(1024)S(1)} %pad_clamp_fusion.1), kind=kCustom, calls=%fused_computation.clone | custom fusion | bytes 4194320 | tf_op jit(solution)/shard_map/jit(_take)/gather | solution.py:240
  147.2 2.8 %fusion.3 = bf16[4,2,512,128]{3,2,0,1:T(8,128)(2,1)S(1)} fusion(f32[4,2,512,128]{3,2,1,0:T(8,128)S(1)} %gather_fusion, f32[4,2,512,128]{3,2,1,0:T(8,128)} %get-tuple-element.27, f32[4,2,512,128]{3,2,1,0:T(8,128)} %get-tuple-element.24, pred[4]{0:T(512)(128)(4,1)S(1)} %compare_and_fusion.1), kind=kLoop, calls=%fused_computation.25 | loop fusion | flops 2097152 | bytes 7340036 | tf_op jit(solution)/shard_map/convert_element_type | solution.py:242
  154.6 2.9 %gather_fusion.1 = f32[4,2,512,128]{3,2,1,0:T(8,128)S(1)} fusion(f32[8,2,512,128]{3,2,1,0:T(8,128)} %constant_dynamic-update-slice_fusion, s32[1024]{0:T(1024)S(1)} %pad_clamp_fusion), kind=kCustom, calls=%fused_computation.1.clone | custom fusion | bytes 4194320 | tf_op jit(solution)/shard_map/jit(_take)/gather | solution.py:241
  157.5 7.0 %collective-permute-done.10 = bf16[4,512,128]{2,1,0:T(8,128)(2,1)} collective-permute-done((bf16[4,512,128]{2,1,0:T(8,128)(2,1)}, bf16[4,512,128]{2,1,0:T(8,128)(2,1)}, u32[]{:S(2)}, u32[]{:S(2)}) %collective-permute-start.10) | collective-permute-done | bytes 524320 | tf_op jit(solution)/shard_map/ppermute | solution.py:162
  164.4 26.3 %collective-permute-start.14 = (bf16[2,512,128]{2,1,0:T(8,128)(2,1)}, bf16[2,512,128]{2,1,0:T(8,128)(2,1)S(1)}, u32[]{:S(2)}, u32[]{:S(2)}) collective-permute-start(bf16[2,512,128]{2,1,0:T(8,128)(2,1)} %get-tuple-element.51), channel_id=1, source_target_pairs={{0,16},{8,24},{16,0},{24,8},{4,20},{12,28},{20,4},{28,12},{1,17},{... | collective-permute-start | bytes 786440 | tf_op jit(solution)/shard_map/ppermute | solution.py:162
  190.7 1.8 fusion.27
  192.6 12.7 %collective-permute-done.11 = bf16[4,512,128]{2,1,0:T(8,128)(2,1)} collective-permute-done((bf16[4,512,128]{2,1,0:T(8,128)(2,1)}, bf16[4,512,128]{2,1,0:T(8,128)(2,1)}, u32[]{:S(2)}, u32[]{:S(2)}) %collective-permute-start.11) | collective-permute-done | bytes 524320 | tf_op jit(solution)/shard_map/ppermute | solution.py:162
  205.2 1.8 fusion.26
  207.1 1.8 fusion.25
  208.9 1.7 dynamic-slice_dynamic-update-slice_fusion.4
  210.6 1.7 fusion.36
  212.3 2.0 collective-permute-done.14
  215.1 2.3 fusion.1
  217.4 1.8 collective-permute-start.17
  222.1 4.0 %collective-permute-done.17 = bf16[2,512,128]{2,1,0:T(8,128)(2,1)S(1)} collective-permute-done((bf16[2,512,128]{2,1,0:T(8,128)(2,1)S(1)}, bf16[2,512,128]{2,1,0:T(8,128)(2,1)S(1)}, u32[]{:S(2)}, u32[]{:S(2)}) %collective-permute-start.17) | collective-permute-done | bytes 262176 | tf_op jit(solution)/shard_map/ppermute | solution.py:162
  226.1 12.3 %collective-permute-done.18 = bf16[2,512,128]{2,1,0:T(8,128)(2,1)S(1)} collective-permute-done((bf16[2,512,128]{2,1,0:T(8,128)(2,1)S(1)}, bf16[2,512,128]{2,1,0:T(8,128)(2,1)S(1)}, u32[]{:S(2)}, u32[]{:S(2)}) %collective-permute-start.18) | collective-permute-done | bytes 262176 | tf_op jit(solution)/shard_map/ppermute | solution.py:162
  (125 shorter events, 38.3 us)
Async XLA Ops:
  0.6 9.8 %copy-start = (s32[4,2,8]{2,1,0:T(2,128)S(1)}, s32[4,2,8]{2,1,0:T(2,128)}, u32[]{:S(2)}) copy-start(s32[4,2,8]{2,1,0:T(2,128)} %param.11) | copy-start | bytes 772
  2.3 8.5 %copy-start.15 = (bf16[4,1024,128]{2,1,0:T(8,128)(2,1)S(1)}, bf16[4,1024,128]{2,1,0:T(8,128)(2,1)}, u32[]{:S(2)}) copy-start(bf16[4,1024,128]{2,1,0:T(8,128)(2,1)} %param.7) | copy-start | bytes 3145732
  3.5 18.3 %collective-permute-start = (bf16[2,2,512,128]{3,2,1,0:T(8,128)(2,1)}, bf16[2,2,512,128]{3,2,1,0:T(8,128)(2,1)}, u32[]{:S(2)}, u32[]{:S(2)}) collective-permute-start(bf16[2,2,512,128]{3,2,1,0:T(8,128)(2,1)} %get-tuple-element.41), channel_id=1, source_target_pairs={{0,8},{8,16},{16,24},{24,0},{4,12},{12,20},{20,28},{28,4},{1,9},{9... | collective-permute-start | bytes 1572872 | tf_op jit(solution)/shard_map/ppermute | solution.py:147
  6.5 36.9 %collective-permute-start.1 = (bf16[2,2,512,128]{3,2,1,0:T(8,128)(2,1)}, bf16[2,2,512,128]{3,2,1,0:T(8,128)(2,1)}, u32[]{:S(2)}, u32[]{:S(2)}) collective-permute-start(bf16[2,2,512,128]{3,2,1,0:T(8,128)(2,1)} %get-tuple-element.42), channel_id=1, source_target_pairs={{0,16},{8,24},{16,0},{24,8},{4,20},{12,28},{20,4},{28,12},{1,17},{... | collective-permute-start | bytes 1572872 | tf_op jit(solution)/shard_map/ppermute | solution.py:147
  9.1 35.4 %collective-permute-start.2 = (bf16[2,2,512,128]{3,2,1,0:T(8,128)(2,1)}, bf16[2,2,512,128]{3,2,1,0:T(8,128)(2,1)}, u32[]{:S(2)}, u32[]{:S(2)}) collective-permute-start(bf16[2,2,512,128]{3,2,1,0:T(8,128)(2,1)} %get-tuple-element.39), channel_id=1, source_target_pairs={{0,24},{8,0},{16,8},{24,16},{4,28},{12,4},{20,12},{28,20},{1,25},{... | collective-permute-start | bytes 1572872 | tf_op jit(solution)/shard_map/ppermute | solution.py:147
  47.9 20.1 %collective-permute-start.3 = (bf16[2,512,128]{2,1,0:T(8,128)(2,1)S(1)}, bf16[2,512,128]{2,1,0:T(8,128)(2,1)S(1)}, u32[]{:S(2)}, u32[]{:S(2)}) collective-permute-start(bf16[2,512,128]{2,1,0:T(8,128)(2,1)S(1)} %get-tuple-element.69), channel_id=1, source_target_pairs={{0,8},{8,16},{16,24},{24,0},{4,12},{12,20},{20,28},{28,4},{1,9},{9... | collective-permute-start | bytes 786440 | tf_op jit(solution)/shard_map/ppermute | solution.py:147
  58.5 18.9 %collective-permute-start.4 = (bf16[2,512,128]{2,1,0:T(8,128)(2,1)S(1)}, bf16[2,512,128]{2,1,0:T(8,128)(2,1)S(1)}, u32[]{:S(2)}, u32[]{:S(2)}) collective-permute-start(bf16[2,512,128]{2,1,0:T(8,128)(2,1)S(1)} %get-tuple-element.68), channel_id=1, source_target_pairs={{0,16},{8,24},{16,0},{24,8},{4,20},{12,28},{20,4},{28,12},{1,17},{... | collective-permute-start | bytes 786440 | tf_op jit(solution)/shard_map/ppermute | solution.py:147
  61.5 51.0 %collective-permute-start.9 = (bf16[4,2,512,128]{3,2,0,1:T(8,128)(2,1)S(1)}, bf16[4,2,512,128]{3,2,0,1:T(8,128)(2,1)}, u32[]{:S(2)}, u32[]{:S(2)}) collective-permute-start(bf16[4,2,512,128]{3,2,0,1:T(8,128)(2,1)S(1)} %fusion.4), channel_id=1, source_target_pairs={{0,4},{8,12},{16,20},{24,28},{4,0},{12,8},{20,16},{28,24},{1,5},{9... | collective-permute-start | bytes 3145736 | tf_op jit(solution)/shard_map/ppermute | solution.py:211
  63.0 14.4 %collective-permute-start.5 = (bf16[2,512,128]{2,1,0:T(8,128)(2,1)S(1)}, bf16[2,512,128]{2,1,0:T(8,128)(2,1)S(1)}, u32[]{:S(2)}, u32[]{:S(2)}) collective-permute-start(bf16[2,512,128]{2,1,0:T(8,128)(2,1)S(1)} %get-tuple-element.67), channel_id=1, source_target_pairs={{0,24},{8,0},{16,8},{24,16},{4,28},{12,4},{20,12},{28,20},{1,25},{... | collective-permute-start | bytes 786440 | tf_op jit(solution)/shard_map/ppermute | solution.py:147
  79.6 31.7 %collective-permute-start.6 = (bf16[2,512,128]{2,1,0:T(8,128)(2,1)}, bf16[2,512,128]{2,1,0:T(8,128)(2,1)S(1)}, u32[]{:S(2)}, u32[]{:S(2)}) collective-permute-start(bf16[2,512,128]{2,1,0:T(8,128)(2,1)} %get-tuple-element.59), channel_id=1, source_target_pairs={{0,8},{8,16},{16,24},{24,0},{4,12},{12,20},{20,28},{28,4},{1,9},{9... | collective-permute-start | bytes 786440 | tf_op jit(solution)/shard_map/ppermute | solution.py:147
  85.6 25.7 %collective-permute-start.7 = (bf16[2,512,128]{2,1,0:T(8,128)(2,1)}, bf16[2,512,128]{2,1,0:T(8,128)(2,1)S(1)}, u32[]{:S(2)}, u32[]{:S(2)}) collective-permute-start(bf16[2,512,128]{2,1,0:T(8,128)(2,1)} %get-tuple-element.58), channel_id=1, source_target_pairs={{0,16},{8,24},{16,0},{24,8},{4,20},{12,28},{20,4},{28,12},{1,17},{... | collective-permute-start | bytes 786440 | tf_op jit(solution)/shard_map/ppermute | solution.py:147
  87.0 24.5 %collective-permute-start.8 = (bf16[2,512,128]{2,1,0:T(8,128)(2,1)}, bf16[2,512,128]{2,1,0:T(8,128)(2,1)S(1)}, u32[]{:S(2)}, u32[]{:S(2)}) collective-permute-start(bf16[2,512,128]{2,1,0:T(8,128)(2,1)} %get-tuple-element.57), channel_id=1, source_target_pairs={{0,24},{8,0},{16,8},{24,16},{4,28},{12,4},{20,12},{28,20},{1,25},{... | collective-permute-start | bytes 786440 | tf_op jit(solution)/shard_map/ppermute | solution.py:147
  109.3 101.3 %collective-permute-start.13 = (bf16[2,512,128]{2,1,0:T(8,128)(2,1)}, bf16[2,512,128]{2,1,0:T(8,128)(2,1)}, u32[]{:S(2)}, u32[]{:S(2)}) collective-permute-start(bf16[2,512,128]{2,1,0:T(8,128)(2,1)} %get-tuple-element.52), channel_id=1, source_target_pairs={{0,24},{8,0},{16,8},{24,16},{4,28},{12,4},{20,12},{28,20},{1,25},{... | collective-permute-start | bytes 786440 | tf_op jit(solution)/shard_map/ppermute | solution.py:162
  137.4 3.0 %copy-start.13 = (f32[4,2,512,128]{3,2,1,0:T(8,128)S(1)}, f32[4,2,512,128]{3,2,1,0:T(8,128)}, u32[]{:S(2)}) copy-start(f32[4,2,512,128]{3,2,1,0:T(8,128)} %get-tuple-element.28) | copy-start | bytes 6291460
  138.9 76.1 %collective-permute-start.16 = (f32[4,2,512,128]{3,2,0,1:T(8,128)}, f32[4,2,512,128]{3,2,0,1:T(8,128)}, u32[]{:S(2)}, u32[]{:S(2)}) collective-permute-start(f32[4,2,512,128]{3,2,0,1:T(8,128)} %maximum_select_fusion), channel_id=1, source_target_pairs={{4,0},{12,8},{20,16},{28,24},{0,4},{8,12},{16,20},{24,28},{5,1},{1... | collective-permute-start | bytes 6291464 | tf_op jit(solution)/shard_map/ppermute | solution.py:233
  140.4 2.3 copy-start.12
  147.2 2.9 %copy-start.19 = (bf16[4,2,512,128]{3,2,1,0:T(8,128)(2,1)S(1)}, bf16[4,2,512,128]{3,2,1,0:T(8,128)(2,1)}, u32[]{:S(2)}) copy-start(bf16[4,2,512,128]{3,2,1,0:T(8,128)(2,1)} %get-tuple-element.23) | copy-start | bytes 3145732
  151.3 13.2 %collective-permute-start.10 = (bf16[4,512,128]{2,1,0:T(8,128)(2,1)}, bf16[4,512,128]{2,1,0:T(8,128)(2,1)}, u32[]{:S(2)}, u32[]{:S(2)}) collective-permute-start(bf16[4,512,128]{2,1,0:T(8,128)(2,1)} %get-tuple-element.35), channel_id=1, source_target_pairs={{0,24},{8,0},{16,8},{24,16},{4,28},{12,4},{20,12},{28,20},{1,25},{... | collective-permute-start | bytes 1572872 | tf_op jit(solution)/shard_map/ppermute | solution.py:162
  151.7 2.8 %copy-start.3 = (bf16[4,2,512,128]{3,2,0,1:T(8,128)(2,1)}, bf16[4,2,512,128]{3,2,0,1:T(8,128)(2,1)S(1)}, u32[]{:S(2)}) copy-start(bf16[4,2,512,128]{3,2,0,1:T(8,128)(2,1)S(1)} %slice_dynamic-update-slice_fusion.1) | copy-start | bytes 3145732
  151.9 2.6 %copy-start.5 = (bf16[4,2,512,128]{3,2,0,1:T(8,128)(2,1)}, bf16[4,2,512,128]{3,2,0,1:T(8,128)(2,1)S(1)}, u32[]{:S(2)}) copy-start(bf16[4,2,512,128]{3,2,0,1:T(8,128)(2,1)S(1)} %slice_dynamic-update-slice_fusion.2) | copy-start | bytes 3145732
  151.9 53.3 %collective-permute-start.11 = (bf16[4,512,128]{2,1,0:T(8,128)(2,1)}, bf16[4,512,128]{2,1,0:T(8,128)(2,1)}, u32[]{:S(2)}, u32[]{:S(2)}) collective-permute-start(bf16[4,512,128]{2,1,0:T(8,128)(2,1)} %get-tuple-element.36), channel_id=1, source_target_pairs={{0,16},{8,24},{16,0},{24,8},{4,20},{12,28},{20,4},{28,12},{1,17},{... | collective-permute-start | bytes 1572872 | tf_op jit(solution)/shard_map/ppermute | solution.py:162
  153.4 53.7 %collective-permute-start.12 = (bf16[4,512,128]{2,1,0:T(8,128)(2,1)}, bf16[4,512,128]{2,1,0:T(8,128)(2,1)}, u32[]{:S(2)}, u32[]{:S(2)}) collective-permute-start(bf16[4,512,128]{2,1,0:T(8,128)(2,1)} %get-tuple-element.33), channel_id=1, source_target_pairs={{0,8},{8,16},{16,24},{24,0},{4,12},{12,20},{20,28},{28,4},{1,9},{9... | collective-permute-start | bytes 1572872 | tf_op jit(solution)/shard_map/ppermute | solution.py:162
  164.4 49.9 %collective-permute-start.14 = (bf16[2,512,128]{2,1,0:T(8,128)(2,1)}, bf16[2,512,128]{2,1,0:T(8,128)(2,1)S(1)}, u32[]{:S(2)}, u32[]{:S(2)}) collective-permute-start(bf16[2,512,128]{2,1,0:T(8,128)(2,1)} %get-tuple-element.51), channel_id=1, source_target_pairs={{0,16},{8,24},{16,0},{24,8},{4,20},{12,28},{20,4},{28,12},{1,17},{... | collective-permute-start | bytes 786440 | tf_op jit(solution)/shard_map/ppermute | solution.py:162
  192.6 22.5 %copy-start.14 = (f32[4,2,512,128]{3,2,1,0:T(8,128)S(1)}, f32[4,2,512,128]{3,2,1,0:T(8,128)}, u32[]{:S(2)}) copy-start(f32[4,2,512,128]{3,2,1,0:T(8,128)} %get-tuple-element.31) | copy-start | bytes 6291460
  205.2 14.1 %collective-permute-start.15 = (bf16[2,512,128]{2,1,0:T(8,128)(2,1)S(1)}, bf16[2,512,128]{2,1,0:T(8,128)(2,1)S(1)}, u32[]{:S(2)}, u32[]{:S(2)}) collective-permute-start(bf16[2,512,128]{2,1,0:T(8,128)(2,1)S(1)} %get-tuple-element.50), channel_id=1, source_target_pairs={{0,8},{8,16},{16,24},{24,0},{4,12},{12,20},{20,28},{28,4},{1,9},{9... | collective-permute-start | bytes 786440 | tf_op jit(solution)/shard_map/ppermute | solution.py:162
  215.0 4.2 %copy-start.6 = (bf16[4,2,512,128]{3,2,0,1:T(8,128)(2,1)S(1)}, bf16[4,2,512,128]{3,2,0,1:T(8,128)(2,1)}, u32[]{:S(2)}) copy-start(bf16[4,2,512,128]{3,2,0,1:T(8,128)(2,1)} %get-tuple-element.91) | copy-start | bytes 3145732
  215.1 4.2 %copy-start.8 = (bf16[4,2,512,128]{3,2,0,1:T(8,128)(2,1)S(1)}, bf16[4,2,512,128]{3,2,0,1:T(8,128)(2,1)}, u32[]{:S(2)}) copy-start(bf16[4,2,512,128]{3,2,0,1:T(8,128)(2,1)} %get-tuple-element.92) | copy-start | bytes 3145732
  217.4 8.6 %collective-permute-start.17 = (bf16[2,512,128]{2,1,0:T(8,128)(2,1)S(1)}, bf16[2,512,128]{2,1,0:T(8,128)(2,1)S(1)}, u32[]{:S(2)}, u32[]{:S(2)}) collective-permute-start(bf16[2,512,128]{2,1,0:T(8,128)(2,1)S(1)} %get-tuple-element.47), channel_id=1, source_target_pairs={{0,24},{8,0},{16,8},{24,16},{4,28},{12,4},{20,12},{28,20},{1,25},{... | collective-permute-start | bytes 786440 | tf_op jit(solution)/shard_map/ppermute | solution.py:162
  219.3 2.7 %copy-start.4 = (bf16[4,2,512,128]{3,2,0,1:T(8,128)(2,1)S(1)}, bf16[4,2,512,128]{3,2,0,1:T(8,128)(2,1)}, u32[]{:S(2)}) copy-start(bf16[4,2,512,128]{3,2,0,1:T(8,128)(2,1)} %get-tuple-element.72) | copy-start | bytes 3145732
  221.4 16.9 %collective-permute-start.18 = (bf16[2,512,128]{2,1,0:T(8,128)(2,1)S(1)}, bf16[2,512,128]{2,1,0:T(8,128)(2,1)S(1)}, u32[]{:S(2)}, u32[]{:S(2)}) collective-permute-start(bf16[2,512,128]{2,1,0:T(8,128)(2,1)S(1)} %get-tuple-element.46), channel_id=1, source_target_pairs={{0,16},{8,24},{16,0},{24,8},{4,20},{12,28},{20,4},{28,12},{1,17},{... | collective-permute-start | bytes 786440 | tf_op jit(solution)/shard_map/ppermute | solution.py:162
  221.4 16.9 %collective-permute-start.19 = (bf16[2,512,128]{2,1,0:T(8,128)(2,1)S(1)}, bf16[2,512,128]{2,1,0:T(8,128)(2,1)S(1)}, u32[]{:S(2)}, u32[]{:S(2)}) collective-permute-start(bf16[2,512,128]{2,1,0:T(8,128)(2,1)S(1)} %get-tuple-element.45), channel_id=1, source_target_pairs={{0,8},{8,16},{16,24},{24,0},{4,12},{12,20},{20,28},{28,4},{1,9},{9... | collective-permute-start | bytes 786440 | tf_op jit(solution)/shard_map/ppermute | solution.py:162
  238.4 2.1 copy-start.1
  (8 other events, 11.8 us)

commit v9 on v8

--- a/solution.py
+++ b/solution.py
@@ -56,7 +56,8 @@
     return attended, grad_query, key_terms, value_terms
 
 
-def attention_kernel(index_ref, flag_ref, q_ref, g_ref, ko_ref, kw_ref, kp_ref, vo_ref, vw_ref, vp_ref, ad_ref, own_ref, win_ref, par_ref):
+def attention_kernel(index_ref, flag_ref, q_ref, g_ref, ko_ref, kw_ref, kp_ref, vo_ref, vw_ref, vp_ref, *rest):
+    ad_ref, own_ref, win_ref, par_ref = rest[-4:]
     place = pl.program_id(0)
     q = q_ref[0]
     g = g_ref[0]
@@ -95,17 +96,17 @@
         dscore = (shares[part] * (grad_probs - row_dot)).astype(jnp.bfloat16)
         term = jnp.dot(dscore, keys[part], preferred_element_type=jnp.float32)
         dq = term if dq is None else dq + term
-        out_ref = (own_ref, win_ref, par_ref)[part]
-        out_ref[0, 0] = (
+        out_ref = (own_ref.at[0], win_ref.at[0], par_ref.at[0, 0])[part]
+        out_ref[0] = (
             lax.dot_general(dscore, q, cols_by_cols, preferred_element_type=jnp.float32) * scaling
         )
-        out_ref[0, 1] = lax.dot_general(
+        out_ref[1] = lax.dot_general(
             shares_low[part], g, cols_by_cols, preferred_element_type=jnp.float32
         )
     ad_ref[0, 1] = (dq * scaling).astype(jnp.bfloat16)
 
 
-def fused_terms(parity, q_rows, g_rows, k_all, v_all, k_window, v_window, partner_index, first_masked):
+def fused_terms(parity, q_rows, g_rows, k_all, v_all, k_window, v_window, partner_index, first_masked, partner_buffer=None):
     places, rows, width = q_rows.shape
     row_spec = pl.BlockSpec((1, rows, width), lambda p, idx, flag: (p, 0, 0))
     own_spec = pl.BlockSpec((1, rows, width), lambda p, idx, flag: (2 * p + parity, 0, 0))
@@ -114,23 +115,36 @@
         window_spec = pl.BlockSpec((1, rows, width), lambda p, idx, flag: (2 * p, 0, 0))
     else:
         window_spec = row_spec
+    pair_spec = pl.BlockSpec((1, 2, rows, width), lambda p, idx, flag: (p, 0, 0, 0))
+    target_spec = pl.BlockSpec(
+        (1, 1, 2, rows, width), lambda p, idx, flag: (idx[p] % 2, idx[p] // 2, 0, 0, 0)
+    )
+    in_specs = [row_spec, row_spec, own_spec, window_spec, partner_spec, own_spec, window_spec, partner_spec]
+    operands = [partner_index, first_masked, q_rows, g_rows, k_all, k_window, k_all, v_all, v_window, v_all]
+    aliases = {}
+    if partner_buffer is not None:
+        in_specs.append(pl.BlockSpec(memory_space=pl.ANY))
+        aliases = {len(operands): 3}
+        operands.append(partner_buffer)
     flops = 36 * places * rows * rows * width
     return pl.pallas_call(
         attention_kernel,
         grid_spec=pltpu.PrefetchScalarGridSpec(
             num_scalar_prefetch=2,
             grid=(places,),
-            in_specs=[row_spec, row_spec, own_spec, window_spec, partner_spec, own_spec, window_spec, partner_spec],
-            out_specs=[pl.BlockSpec((1, 2, rows, width), lambda p, idx, flag: (p, 0, 0, 0))] * 4,
+            in_specs=in_specs,
+            out_specs=[pair_spec, pair_spec, pair_spec, target_spec],
         ),
         out_shape=[jax.ShapeDtypeStruct((places, 2, rows, width), jnp.bfloat16)]
-        + [jax.ShapeDtypeStruct((places, 2, rows, width), jnp.float32)] * 3,
+        + [jax.ShapeDtypeStruct((places, 2, rows, width), jnp.float32)] * 2
+        + [jax.ShapeDtypeStruct((2, places, 2, rows, width), jnp.float32)],
+        input_output_aliases=aliases,
         cost_estimate=pl.CostEstimate(
             flops=flops,
             transcendentals=3 * places * rows * rows,
             bytes_accessed=places * rows * width * 60,
         ),
-    )(partner_index, first_masked, q_rows, g_rows, k_all, k_window, k_all, v_all, v_window, v_all)
+    )(*operands)
 
 
 def interleave(even, odd):
@@ -223,8 +237,8 @@
     sent_odd = scatter_group(ad_odd, within, nseg, group)
 
     first_masked = (segment == 0).astype(jnp.int32).reshape(1)
-    ad_even, own_even, win_even, par_even = fused_terms(
-        0, q_even, g_even, k_all, v_all, window_kv[:, 0], window_kv[:, 1], my_partners[0::2], first_masked
+    ad_even, own_even, win_even, par_all = fused_terms(
+        0, q_even, g_even, k_all, v_all, window_kv[:, 0], window_kv[:, 1], my_partners[0::2], first_masked, par_odd
     )
 
     ret = win_even
@@ -232,13 +246,8 @@
     back_pairs = [(b, a) for a, b in next_segment_pairs(nseg, group)]
     window_back = lax.ppermute(ret, "seq", back_pairs)
 
-    place_ids = jnp.arange(places, dtype=jnp.int32)
-    hits = my_partners[None, :] == place_ids[:, None]
-    inverse = jnp.sum(jnp.where(hits, place_ids[None, :], 0), axis=1)
-    slot = (inverse % 2) * (places // 2) + inverse // 2
-    partner_terms = jnp.concatenate([par_even, par_odd], axis=0)
-    partner_even = jnp.take(partner_terms, slot[0::2], axis=0)
-    partner_odd = jnp.take(partner_terms, slot[1::2], axis=0)
+    partner_even = par_all[0]
+    partner_odd = par_all[1]
     grads_even = (own_even + win_odd + partner_even).astype(jnp.bfloat16)
     sent_even = scatter_group(jnp.concatenate([ad_even, grads_even], axis=1), within, nseg, group)
     grads_odd = (own_odd + window_back + partner_odd).astype(jnp.bfloat16)

time: 241 us -> 270 us (1.12)
  waiting for transfers between devices: 80 us -> 122 us
  local copies, waits for them, and re-layouts: 45 us -> 23.9 us
  starting transfers between devices: 65.1 us -> 72.7 us
    ppermute x1, waiting for transfers between devices: 0.01 us -> 41.4 us  [body(): window_back = lax.ppermute(ret, 'seq', back_pairs)]
    dynamic_update_slice x19 -> x18, local copies, waits for them, and re-layouts: 14.1 us -> 4.78 us  [assemble(): lax.dynamic_update_slice(out, piece[None, None], (head, jnp.int32(column)...]
    ppermute x9, starting transfers between devices: 33.3 us -> 41 us  [scatter_group(): lax.ppermute(pick(y, (within - shift) % group), 'seq', group_pairs(nseg,...]
    gather x2 -> x0, local copies, waits for them, and re-layouts: 5.74 us -> none  [the longest x1 2.87 us: body(): partner_odd = jnp.take(partner_terms, slot[1::2], axis=0)]
    convert_element_type x1 -> x0, other arithmetic: 2.85 us -> none  [body(): grads_even = (own_even + win_odd + partner_even).astype(jnp.bfloat16)]
    convert_element_type x1, other arithmetic: 2.3 us -> 5.12 us  [body(): grads_odd = (own_odd + window_back + partner_odd).astype(jnp.bfloat16)]
    unnamed x43 -> x28, local copies, waits for them, and re-layouts: 7.96 us -> 5.48 us
  transfers between devices with their start and end apart: 20 -> 20, of which waited for: 9 -> 9; matrix products, arithmetic and copies ran while one was open for 18% -> 7% of each run, Pallas kernels for 16% -> 7%
where the time goes in v9:
time: 270 us; the launch traced here: 269 us
  waiting for transfers between devices  122 us (45%)
  starting transfers between devices  72.7 us (27%)
  Pallas kernels  38.7 us (14%)
  local copies, waits for them, and re-layouts  23.9 us (9%)
  other arithmetic  10.6 us (4%)
    ppermute x1, waiting for transfers between devices, body(): window_back = lax.ppermute(ret, 'seq', back_pairs)  41.4 us
    ppermute x9, starting transfers between devices, scatter_group(): lax.ppermute(pick(y, (within - shift) % group), 'seq', group_pairs(nseg,...  41 us
    ppermute x9, waiting for transfers between devices, gather_group(): lax.ppermute(pick(x, (within + shift) % group), 'seq', group_pairs(nseg,...  40.6 us
    ppermute x9, waiting for transfers between devices, scatter_group(): lax.ppermute(pick(y, (within - shift) % group), 'seq', group_pairs(nseg,...  40.2 us
    pallas_call x2, Pallas kernels, fused_terms(): pl.pallas_call(attention_kernel, grid_spec=pltpu.PrefetchScalarGridSpec(n...  38.7 us
    ppermute x9, starting transfers between devices, gather_group(): lax.ppermute(pick(x, (within + shift) % group), 'seq', group_pairs(nseg,...  28.7 us
    unnamed x28, local copies, waits for them, and re-layouts  5.48 us
  transfers between devices with their start and end apart: 20, of which 9 were waited for; matrix products, arithmetic and copies ran while one was open for 7% of the time, Pallas kernels for 7%

profile of v9, /device:TPU:0, one launch (start us, length us, event | category | flops | bytes accessed | tf_op | source)
XLA Modules:
  0.0 269.4 jit_solution(11338785732034881789)
XLA Ops:
  2.2 1.2 fusion.14
  3.4 3.0 %collective-permute-start = (bf16[2,2,512,128]{3,2,1,0:T(8,128)(2,1)}, bf16[2,2,512,128]{3,2,1,0:T(8,128)(2,1)}, u32[]{:S(2)}, u32[]{:S(2)}) collective-permute-start(bf16[2,2,512,128]{3,2,1,0:T(8,128)(2,1)} %get-tuple-element.42), channel_id=1, source_target_pairs={{0,8},{8,16},{16,24},{24,0},{4,12},{12,20},{20,28},{28,4},{1,9},{9... | collective-permute-start | bytes 1572872 | tf_op jit(solution)/shard_map/ppermute | solution.py:161
  6.4 2.6 collective-permute-start.1
  9.0 1.3 collective-permute-start.2
  13.2 1.3 pad_maximum_fusion.2
  15.8 5.8 %collective-permute-done = bf16[2,2,512,128]{3,2,1,0:T(8,128)(2,1)} collective-permute-done((bf16[2,2,512,128]{3,2,1,0:T(8,128)(2,1)}, bf16[2,2,512,128]{3,2,1,0:T(8,128)(2,1)}, u32[]{:S(2)}, u32[]{:S(2)}) %collective-permute-start) | collective-permute-done | bytes 524320 | tf_op jit(solution)/shard_map/ppermute | solution.py:161
  22.8 20.5 %collective-permute-done.1 = bf16[2,2,512,128]{3,2,1,0:T(8,128)(2,1)} collective-permute-done((bf16[2,2,512,128]{3,2,1,0:T(8,128)(2,1)}, bf16[2,2,512,128]{3,2,1,0:T(8,128)(2,1)}, u32[]{:S(2)}, u32[]{:S(2)}) %collective-permute-start.1) | collective-permute-done | bytes 524320 | tf_op jit(solution)/shard_map/ppermute | solution.py:161
  45.9 1.2 copy-done.3
  47.2 10.6 %collective-permute-start.3 = (bf16[2,512,128]{2,1,0:T(8,128)(2,1)S(1)}, bf16[2,512,128]{2,1,0:T(8,128)(2,1)S(1)}, u32[]{:S(2)}, u32[]{:S(2)}) collective-permute-start(bf16[2,512,128]{2,1,0:T(8,128)(2,1)S(1)} %get-tuple-element.70), channel_id=1, source_target_pairs={{0,8},{8,16},{16,24},{24,0},{4,12},{12,20},{20,28},{28,4},{1,9},{9... | collective-permute-start | bytes 786440 | tf_op jit(solution)/shard_map/ppermute | solution.py:161
  57.8 2.7 %collective-permute-start.4 = (bf16[2,512,128]{2,1,0:T(8,128)(2,1)S(1)}, bf16[2,512,128]{2,1,0:T(8,128)(2,1)S(1)}, u32[]{:S(2)}, u32[]{:S(2)}) collective-permute-start(bf16[2,512,128]{2,1,0:T(8,128)(2,1)S(1)} %get-tuple-element.69), channel_id=1, source_target_pairs={{0,16},{8,24},{16,0},{24,8},{4,20},{12,28},{20,4},{28,12},{1,17},{... | collective-permute-start | bytes 786440 | tf_op jit(solution)/shard_map/ppermute | solution.py:161
  60.9 1.6 collective-permute-start.9
  62.5 4.9 %collective-permute-done.3 = bf16[2,512,128]{2,1,0:T(8,128)(2,1)S(1)} collective-permute-done((bf16[2,512,128]{2,1,0:T(8,128)(2,1)S(1)}, bf16[2,512,128]{2,1,0:T(8,128)(2,1)S(1)}, u32[]{:S(2)}, u32[]{:S(2)}) %collective-permute-start.3) | collective-permute-done | bytes 262176 | tf_op jit(solution)/shard_map/ppermute | solution.py:161
  67.4 9.4 %collective-permute-done.4 = bf16[2,512,128]{2,1,0:T(8,128)(2,1)S(1)} collective-permute-done((bf16[2,512,128]{2,1,0:T(8,128)(2,1)S(1)}, bf16[2,512,128]{2,1,0:T(8,128)(2,1)S(1)}, u32[]{:S(2)}, u32[]{:S(2)}) %collective-permute-start.4) | collective-permute-done | bytes 262176 | tf_op jit(solution)/shard_map/ppermute | solution.py:161
  79.0 6.0 %collective-permute-start.6 = (bf16[2,512,128]{2,1,0:T(8,128)(2,1)}, bf16[2,512,128]{2,1,0:T(8,128)(2,1)S(1)}, u32[]{:S(2)}, u32[]{:S(2)}) collective-permute-start(bf16[2,512,128]{2,1,0:T(8,128)(2,1)} %get-tuple-element.60), channel_id=1, source_target_pairs={{0,8},{8,16},{16,24},{24,0},{4,12},{12,20},{20,28},{28,4},{1,9},{9... | collective-permute-start | bytes 786440 | tf_op jit(solution)/shard_map/ppermute | solution.py:161
  85.0 1.3 collective-permute-start.7
  87.4 19.4 %shard_map.84 = (bf16[4,2,512,128]{3,2,1,0:T(8,128)(2,1)}, f32[4,2,512,128]{3,2,1,0:T(8,128)}, f32[4,2,512,128]{3,2,1,0:T(8,128)}, f32[2,4,2,512,128]{4,3,2,1,0:T(8,128)}) custom-call(s32[4]{0:T(128)} %slice.191.index_ref, s32[1]{0:T(128)} %constant.252.clone.1.flag_ref, bf16[4,512,128]{2,1,0:T(8,128)(2,1)} %get-tuple-element.22.q_ref, ...), custom_call_target="tpu_custom_call" | custom-call | flops 4831838208 | bytes 15728640 | tf_op jit(solution)/shard_map/pallas_call | solution.py:130
  108.0 2.2 slice_bitcast_fusion.2
  110.2 19.3 %shard_map.85 = (bf16[4,2,512,128]{3,2,1,0:T(8,128)(2,1)}, f32[4,2,512,128]{3,2,1,0:T(8,128)}, f32[4,2,512,128]{3,2,1,0:T(8,128)}, f32[2,4,2,512,128]{4,3,2,1,0:T(8,128)}) custom-call(s32[4]{0:T(128)} %slice.174.index_ref, s32[1]{0:T(128)} %bitcast.1.flag_ref, bf16[4,512,128]{2,1,0:T(8,128)(2,1)} %get-tuple-element.57.q_ref, ...), custom_call_target="tpu_custom_call", output_to_operand_aliasing={{3}: (10, {})} | custom-call | flops 4831838208 | bytes 15728640 | tf_op jit(solution)/shard_map/pallas_call | solution.py:130
  129.5 1.7 copy.58
  131.4 1.4 copy-done.2
  132.9 1.5 maximum_select_fusion
  134.4 1.5 collective-permute-start.16
  135.9 4.5 %collective-permute-start.13 = (bf16[2,512,128]{2,1,0:T(8,128)(2,1)S(1)}, bf16[2,512,128]{2,1,0:T(8,128)(2,1)S(1)}, u32[]{:S(2)}, u32[]{:S(2)}) collective-permute-start(bf16[2,512,128]{2,1,0:T(8,128)(2,1)S(1)} %get-tuple-element.53), channel_id=1, source_target_pairs={{0,24},{8,0},{16,8},{24,16},{4,28},{12,4},{20,12},{28,20},{1,25},{... | collective-permute-start | bytes 786440 | tf_op jit(solution)/shard_map/ppermute | solution.py:176
  140.4 41.4 %collective-permute-done.16 = f32[4,2,512,128]{3,2,0,1:T(8,128)} collective-permute-done((f32[4,2,512,128]{3,2,0,1:T(8,128)}, f32[4,2,512,128]{3,2,0,1:T(8,128)}, u32[]{:S(2)}, u32[]{:S(2)}) %collective-permute-start.16) | collective-permute-done | bytes 2097184 | tf_op jit(solution)/shard_map/ppermute | solution.py:247
  181.8 5.1 %fusion.1 = (bf16[4,2,512,128]{3,2,0,1:T(8,128)(2,1)S(1)}, bf16[4,2,512,128]{3,2,0,1:T(8,128)(2,1)S(1)}) fusion(f32[4,2,512,128]{3,2,0,1:T(8,128)} %collective-permute-done.16, f32[4,2,512,128]{3,2,1,0:T(8,128)S(1)} %copy-done.6, f32[4,2,512,128]{3,2,1,0:T(8,128)} %get-tuple-element.27, f32[4,2,512,128]{3,2,1,0:T(8,128)} %get-tuple-element.26, ...), kind=kLoop, calls=%fused_computation.18 | loop fusion | flops 3145728 | bytes 14680064 | tf_op jit(solution)/shard_map/convert_element_type | solution.py:253
  187.5 4.3 %collective-permute-start.10 = (bf16[4,512,128]{2,1,0:T(8,128)(2,1)S(1)}, bf16[4,512,128]{2,1,0:T(8,128)(2,1)S(1)}, u32[]{:S(2)}, u32[]{:S(2)}) collective-permute-start(bf16[4,512,128]{2,1,0:T(8,128)(2,1)S(1)} %get-tuple-element.36), channel_id=1, source_target_pairs={{0,24},{8,0},{16,8},{24,16},{4,28},{12,4},{20,12},{28,20},{1,25},{... | collective-permute-start | bytes 1572872 | tf_op jit(solution)/shard_map/ppermute | solution.py:176
  192.9 11.4 %collective-permute-done.10 = bf16[4,512,128]{2,1,0:T(8,128)(2,1)S(1)} collective-permute-done((bf16[4,512,128]{2,1,0:T(8,128)(2,1)S(1)}, bf16[4,512,128]{2,1,0:T(8,128)(2,1)S(1)}, u32[]{:S(2)}, u32[]{:S(2)}) %collective-permute-start.10) | collective-permute-done | bytes 524320 | tf_op jit(solution)/shard_map/ppermute | solution.py:176
  204.2 29.4 %collective-permute-start.15 = (bf16[2,512,128]{2,1,0:T(8,128)(2,1)S(1)}, bf16[2,512,128]{2,1,0:T(8,128)(2,1)S(1)}, u32[]{:S(2)}, u32[]{:S(2)}) collective-permute-start(bf16[2,512,128]{2,1,0:T(8,128)(2,1)S(1)} %get-tuple-element.51), channel_id=1, source_target_pairs={{0,8},{8,16},{16,24},{24,0},{4,12},{12,20},{20,28},{28,4},{1,9},{9... | collective-permute-start | bytes 786440 | tf_op jit(solution)/shard_map/ppermute | solution.py:176
  233.7 10.0 %collective-permute-done.11 = bf16[4,512,128]{2,1,0:T(8,128)(2,1)S(1)} collective-permute-done((bf16[4,512,128]{2,1,0:T(8,128)(2,1)S(1)}, bf16[4,512,128]{2,1,0:T(8,128)(2,1)S(1)}, u32[]{:S(2)}, u32[]{:S(2)}) %collective-permute-start.11) | collective-permute-done | bytes 524320 | tf_op jit(solution)/shard_map/ppermute | solution.py:176
  244.0 2.1 collective-permute-start.19
  246.3 4.8 %collective-permute-done.17 = bf16[2,512,128]{2,1,0:T(8,128)(2,1)S(1)} collective-permute-done((bf16[2,512,128]{2,1,0:T(8,128)(2,1)S(1)}, bf16[2,512,128]{2,1,0:T(8,128)(2,1)S(1)}, u32[]{:S(2)}, u32[]{:S(2)}) %collective-permute-start.17) | collective-permute-done | bytes 262176 | tf_op jit(solution)/shard_map/ppermute | solution.py:176
  251.1 14.0 %collective-permute-done.18 = bf16[2,512,128]{2,1,0:T(8,128)(2,1)S(1)} collective-permute-done((bf16[2,512,128]{2,1,0:T(8,128)(2,1)S(1)}, bf16[2,512,128]{2,1,0:T(8,128)(2,1)S(1)}, u32[]{:S(2)}, u32[]{:S(2)}) %collective-permute-start.18) | collective-permute-done | bytes 262176 | tf_op jit(solution)/shard_map/ppermute | solution.py:176
  (97 shorter events, 20.6 us)
Async XLA Ops:
  0.6 13.8 %copy-start = (s32[4,2,8]{2,1,0:T(2,128)S(1)}, s32[4,2,8]{2,1,0:T(2,128)}, u32[]{:S(2)}) copy-start(s32[4,2,8]{2,1,0:T(2,128)} %param.9) | copy-start | bytes 772
  0.8 1.5 copy-start.11
  2.2 8.2 %copy-start.8 = (bf16[4,1024,128]{2,1,0:T(8,128)(2,1)S(1)}, bf16[4,1024,128]{2,1,0:T(8,128)(2,1)}, u32[]{:S(2)}) copy-start(bf16[4,1024,128]{2,1,0:T(8,128)(2,1)} %param.5) | copy-start | bytes 3145732
  3.4 7.8 %copy-start.9 = (bf16[4,1024,128]{2,1,0:T(8,128)(2,1)S(1)}, bf16[4,1024,128]{2,1,0:T(8,128)(2,1)}, u32[]{:S(2)}) copy-start(bf16[4,1024,128]{2,1,0:T(8,128)(2,1)} %param.8) | copy-start | bytes 3145732
  3.4 18.3 %collective-permute-start = (bf16[2,2,512,128]{3,2,1,0:T(8,128)(2,1)}, bf16[2,2,512,128]{3,2,1,0:T(8,128)(2,1)}, u32[]{:S(2)}, u32[]{:S(2)}) collective-permute-start(bf16[2,2,512,128]{3,2,1,0:T(8,128)(2,1)} %get-tuple-element.42), channel_id=1, source_target_pairs={{0,8},{8,16},{16,24},{24,0},{4,12},{12,20},{20,28},{28,4},{1,9},{9... | collective-permute-start | bytes 1572872 | tf_op jit(solution)/shard_map/ppermute | solution.py:161
  6.4 36.9 %collective-permute-start.1 = (bf16[2,2,512,128]{3,2,1,0:T(8,128)(2,1)}, bf16[2,2,512,128]{3,2,1,0:T(8,128)(2,1)}, u32[]{:S(2)}, u32[]{:S(2)}) collective-permute-start(bf16[2,2,512,128]{3,2,1,0:T(8,128)(2,1)} %get-tuple-element.43), channel_id=1, source_target_pairs={{0,16},{8,24},{16,0},{24,8},{4,20},{12,28},{20,4},{28,12},{1,17},{... | collective-permute-start | bytes 1572872 | tf_op jit(solution)/shard_map/ppermute | solution.py:161
  9.0 35.4 %collective-permute-start.2 = (bf16[2,2,512,128]{3,2,1,0:T(8,128)(2,1)}, bf16[2,2,512,128]{3,2,1,0:T(8,128)(2,1)}, u32[]{:S(2)}, u32[]{:S(2)}) collective-permute-start(bf16[2,2,512,128]{3,2,1,0:T(8,128)(2,1)} %get-tuple-element.40), channel_id=1, source_target_pairs={{0,24},{8,0},{16,8},{24,16},{4,28},{12,4},{20,12},{28,20},{1,25},{... | collective-permute-start | bytes 1572872 | tf_op jit(solution)/shard_map/ppermute | solution.py:161
  45.5 1.6 copy-start.3
  45.7 14.9 %copy-start.4 = (bf16[4,1,2,512,128]{4,3,2,0,1:T(8,128)(2,1)}, bf16[4,1,2,512,128]{4,3,2,0,1:T(8,128)(2,1)S(1)}, u32[]{:S(2)}) copy-start(bf16[4,1,2,512,128]{4,3,2,0,1:T(8,128)(2,1)S(1)} %get-tuple-element.38) | copy-start | bytes 3145732
  45.7 14.9 %copy-start.5 = (bf16[4,1,2,512,128]{4,3,2,0,1:T(8,128)(2,1)}, bf16[4,1,2,512,128]{4,3,2,0,1:T(8,128)(2,1)S(1)}, u32[]{:S(2)}) copy-start(bf16[4,1,2,512,128]{4,3,2,0,1:T(8,128)(2,1)S(1)} %get-tuple-element.39) | copy-start | bytes 3145732
  47.2 20.1 %collective-permute-start.3 = (bf16[2,512,128]{2,1,0:T(8,128)(2,1)S(1)}, bf16[2,512,128]{2,1,0:T(8,128)(2,1)S(1)}, u32[]{:S(2)}, u32[]{:S(2)}) collective-permute-start(bf16[2,512,128]{2,1,0:T(8,128)(2,1)S(1)} %get-tuple-element.70), channel_id=1, source_target_pairs={{0,8},{8,16},{16,24},{24,0},{4,12},{12,20},{20,28},{28,4},{1,9},{9... | collective-permute-start | bytes 786440 | tf_op jit(solution)/shard_map/ppermute | solution.py:161
  57.8 19.0 %collective-permute-start.4 = (bf16[2,512,128]{2,1,0:T(8,128)(2,1)S(1)}, bf16[2,512,128]{2,1,0:T(8,128)(2,1)S(1)}, u32[]{:S(2)}, u32[]{:S(2)}) collective-permute-start(bf16[2,512,128]{2,1,0:T(8,128)(2,1)S(1)} %get-tuple-element.69), channel_id=1, source_target_pairs={{0,16},{8,24},{16,0},{24,8},{4,20},{12,28},{20,4},{28,12},{1,17},{... | collective-permute-start | bytes 786440 | tf_op jit(solution)/shard_map/ppermute | solution.py:161
  60.5 16.3 %collective-permute-start.5 = (bf16[2,512,128]{2,1,0:T(8,128)(2,1)S(1)}, bf16[2,512,128]{2,1,0:T(8,128)(2,1)S(1)}, u32[]{:S(2)}, u32[]{:S(2)}) collective-permute-start(bf16[2,512,128]{2,1,0:T(8,128)(2,1)S(1)} %get-tuple-element.68), channel_id=1, source_target_pairs={{0,24},{8,0},{16,8},{24,16},{4,28},{12,4},{20,12},{28,20},{1,25},{... | collective-permute-start | bytes 786440 | tf_op jit(solution)/shard_map/ppermute | solution.py:161
  60.9 47.0 %collective-permute-start.9 = (bf16[4,2,512,128]{3,2,0,1:T(8,128)(2,1)S(1)}, bf16[4,2,512,128]{3,2,0,1:T(8,128)(2,1)}, u32[]{:S(2)}, u32[]{:S(2)}) collective-permute-start(bf16[4,2,512,128]{3,2,0,1:T(8,128)(2,1)S(1)} %fusion.4), channel_id=1, source_target_pairs={{0,4},{8,12},{16,20},{24,28},{4,0},{12,8},{20,16},{28,24},{1,5},{9... | collective-permute-start | bytes 3145736 | tf_op jit(solution)/shard_map/ppermute | solution.py:225
  79.0 27.8 %collective-permute-start.6 = (bf16[2,512,128]{2,1,0:T(8,128)(2,1)}, bf16[2,512,128]{2,1,0:T(8,128)(2,1)S(1)}, u32[]{:S(2)}, u32[]{:S(2)}) collective-permute-start(bf16[2,512,128]{2,1,0:T(8,128)(2,1)} %get-tuple-element.60), channel_id=1, source_target_pairs={{0,8},{8,16},{16,24},{24,0},{4,12},{12,20},{20,28},{28,4},{1,9},{9... | collective-permute-start | bytes 786440 | tf_op jit(solution)/shard_map/ppermute | solution.py:161
  85.0 21.8 %collective-permute-start.7 = (bf16[2,512,128]{2,1,0:T(8,128)(2,1)}, bf16[2,512,128]{2,1,0:T(8,128)(2,1)S(1)}, u32[]{:S(2)}, u32[]{:S(2)}) collective-permute-start(bf16[2,512,128]{2,1,0:T(8,128)(2,1)} %get-tuple-element.59), channel_id=1, source_target_pairs={{0,16},{8,24},{16,0},{24,8},{4,20},{12,28},{20,4},{28,12},{1,17},{... | collective-permute-start | bytes 786440 | tf_op jit(solution)/shard_map/ppermute | solution.py:161
  86.3 20.6 %collective-permute-start.8 = (bf16[2,512,128]{2,1,0:T(8,128)(2,1)S(1)}, bf16[2,512,128]{2,1,0:T(8,128)(2,1)S(1)}, u32[]{:S(2)}, u32[]{:S(2)}) collective-permute-start(bf16[2,512,128]{2,1,0:T(8,128)(2,1)S(1)} %get-tuple-element.58), channel_id=1, source_target_pairs={{0,24},{8,0},{16,8},{24,16},{4,28},{12,4},{20,12},{28,20},{1,25},{... | collective-permute-start | bytes 786440 | tf_op jit(solution)/shard_map/ppermute | solution.py:161
  131.3 1.6 copy-start.2
  132.9 3.0 %copy-start.7 = (bf16[4,2,512,128]{3,2,1,0:T(8,128)(2,1)S(1)}, bf16[4,2,512,128]{3,2,1,0:T(8,128)(2,1)}, u32[]{:S(2)}) copy-start(bf16[4,2,512,128]{3,2,1,0:T(8,128)(2,1)} %get-tuple-element.29) | copy-start | bytes 3145732
  132.9 48.9 %copy-start.6 = (f32[4,2,512,128]{3,2,1,0:T(8,128)S(1)}, f32[4,2,512,128]{3,2,1,0:T(8,128)}, u32[]{:S(2)}) copy-start(f32[4,2,512,128]{3,2,1,0:T(8,128)} %get-tuple-element.30) | copy-start | bytes 6291460
  134.4 47.4 %collective-permute-start.16 = (f32[4,2,512,128]{3,2,0,1:T(8,128)}, f32[4,2,512,128]{3,2,0,1:T(8,128)}, u32[]{:S(2)}, u32[]{:S(2)}) collective-permute-start(f32[4,2,512,128]{3,2,0,1:T(8,128)} %maximum_select_fusion), channel_id=1, source_target_pairs={{4,0},{12,8},{20,16},{28,24},{0,4},{8,12},{16,20},{24,28},{5,1},{1... | collective-permute-start | bytes 6291464 | tf_op jit(solution)/shard_map/ppermute | solution.py:247
  135.9 108.1 %collective-permute-start.13 = (bf16[2,512,128]{2,1,0:T(8,128)(2,1)S(1)}, bf16[2,512,128]{2,1,0:T(8,128)(2,1)S(1)}, u32[]{:S(2)}, u32[]{:S(2)}) collective-permute-start(bf16[2,512,128]{2,1,0:T(8,128)(2,1)S(1)} %get-tuple-element.53), channel_id=1, source_target_pairs={{0,24},{8,0},{16,8},{24,16},{4,28},{12,4},{20,12},{28,20},{1,25},{... | collective-permute-start | bytes 786440 | tf_op jit(solution)/shard_map/ppermute | solution.py:176
  140.4 105.8 %collective-permute-start.14 = (bf16[2,512,128]{2,1,0:T(8,128)(2,1)S(1)}, bf16[2,512,128]{2,1,0:T(8,128)(2,1)S(1)}, u32[]{:S(2)}, u32[]{:S(2)}) collective-permute-start(bf16[2,512,128]{2,1,0:T(8,128)(2,1)S(1)} %get-tuple-element.52), channel_id=1, source_target_pairs={{0,16},{8,24},{16,0},{24,8},{4,20},{12,28},{20,4},{28,12},{1,17},{... | collective-permute-start | bytes 786440 | tf_op jit(solution)/shard_map/ppermute | solution.py:176
  181.8 5.1 %copy-start.12 = (bf16[4,2,512,128]{3,2,1,0:T(8,128)(2,1)S(1)}, bf16[4,2,512,128]{3,2,1,0:T(8,128)(2,1)}, u32[]{:S(2)}) copy-start(bf16[4,2,512,128]{3,2,1,0:T(8,128)(2,1)} %get-tuple-element.25) | copy-start | bytes 3145732
  187.5 16.7 %collective-permute-start.10 = (bf16[4,512,128]{2,1,0:T(8,128)(2,1)S(1)}, bf16[4,512,128]{2,1,0:T(8,128)(2,1)S(1)}, u32[]{:S(2)}, u32[]{:S(2)}) collective-permute-start(bf16[4,512,128]{2,1,0:T(8,128)(2,1)S(1)} %get-tuple-element.36), channel_id=1, source_target_pairs={{0,24},{8,0},{16,8},{24,16},{4,28},{12,4},{20,12},{28,20},{1,25},{... | collective-permute-start | bytes 1572872 | tf_op jit(solution)/shard_map/ppermute | solution.py:176
  191.8 51.9 %collective-permute-start.11 = (bf16[4,512,128]{2,1,0:T(8,128)(2,1)S(1)}, bf16[4,512,128]{2,1,0:T(8,128)(2,1)S(1)}, u32[]{:S(2)}, u32[]{:S(2)}) collective-permute-start(bf16[4,512,128]{2,1,0:T(8,128)(2,1)S(1)} %get-tuple-element.37), channel_id=1, source_target_pairs={{0,16},{8,24},{16,0},{24,8},{4,20},{12,28},{20,4},{28,12},{1,17},{... | collective-permute-start | bytes 1572872 | tf_op jit(solution)/shard_map/ppermute | solution.py:176
  192.1 51.7 %collective-permute-start.12 = (bf16[4,512,128]{2,1,0:T(8,128)(2,1)S(1)}, bf16[4,512,128]{2,1,0:T(8,128)(2,1)S(1)}, u32[]{:S(2)}, u32[]{:S(2)}) collective-permute-start(bf16[4,512,128]{2,1,0:T(8,128)(2,1)S(1)} %get-tuple-element.34), channel_id=1, source_target_pairs={{0,8},{8,16},{16,24},{24,0},{4,12},{12,20},{20,28},{28,4},{1,9},{9... | collective-permute-start | bytes 1572872 | tf_op jit(solution)/shard_map/ppermute | solution.py:176
  204.2 60.9 %collective-permute-start.15 = (bf16[2,512,128]{2,1,0:T(8,128)(2,1)S(1)}, bf16[2,512,128]{2,1,0:T(8,128)(2,1)S(1)}, u32[]{:S(2)}, u32[]{:S(2)}) collective-permute-start(bf16[2,512,128]{2,1,0:T(8,128)(2,1)S(1)} %get-tuple-element.51), channel_id=1, source_target_pairs={{0,8},{8,16},{16,24},{24,0},{4,12},{12,20},{20,28},{28,4},{1,9},{9... | collective-permute-start | bytes 786440 | tf_op jit(solution)/shard_map/ppermute | solution.py:176
  243.7 7.3 %collective-permute-start.17 = (bf16[2,512,128]{2,1,0:T(8,128)(2,1)S(1)}, bf16[2,512,128]{2,1,0:T(8,128)(2,1)S(1)}, u32[]{:S(2)}, u32[]{:S(2)}) collective-permute-start(bf16[2,512,128]{2,1,0:T(8,128)(2,1)S(1)} %get-tuple-element.48), channel_id=1, source_target_pairs={{0,24},{8,0},{16,8},{24,16},{4,28},{12,4},{20,12},{28,20},{1,25},{... | collective-permute-start | bytes 786440 | tf_op jit(solution)/shard_map/ppermute | solution.py:176
  243.8 21.3 %collective-permute-start.18 = (bf16[2,512,128]{2,1,0:T(8,128)(2,1)S(1)}, bf16[2,512,128]{2,1,0:T(8,128)(2,1)S(1)}, u32[]{:S(2)}, u32[]{:S(2)}) collective-permute-start(bf16[2,512,128]{2,1,0:T(8,128)(2,1)S(1)} %get-tuple-element.47), channel_id=1, source_target_pairs={{0,16},{8,24},{16,0},{24,8},{4,20},{12,28},{20,4},{28,12},{1,17},{... | collective-permute-start | bytes 786440 | tf_op jit(solution)/shard_map/ppermute | solution.py:176
  244.0 21.1 %collective-permute-start.19 = (bf16[2,512,128]{2,1,0:T(8,128)(2,1)S(1)}, bf16[2,512,128]{2,1,0:T(8,128)(2,1)S(1)}, u32[]{:S(2)}, u32[]{:S(2)}) collective-permute-start(bf16[2,512,128]{2,1,0:T(8,128)(2,1)S(1)} %get-tuple-element.46), channel_id=1, source_target_pairs={{0,8},{8,16},{16,24},{24,0},{4,12},{12,20},{20,28},{28,4},{1,9},{9... | collective-permute-start | bytes 786440 | tf_op jit(solution)/shard_map/ppermute | solution.py:176
  267.3 2.1 copy-start.1
  (1 other events, 1.2 us)

commit v10 on v9

--- a/solution.py
+++ b/solution.py
@@ -250,6 +250,7 @@
     partner_odd = par_all[1]
     grads_even = (own_even + win_odd + partner_even).astype(jnp.bfloat16)
     sent_even = scatter_group(jnp.concatenate([ad_even, grads_even], axis=1), within, nseg, group)
+    grads_even, own_odd, partner_odd = lax.optimization_barrier((grads_even, own_odd, partner_odd))
     grads_odd = (own_odd + window_back + partner_odd).astype(jnp.bfloat16)
     sent_last = scatter_group(grads_odd, within, nseg, group)
 

time: 270 us -> 235 us (0.87)
  waiting for transfers between devices: 122 us -> 89 us
  local copies, waits for them, and re-layouts: 23.9 us -> 34.9 us
  starting transfers between devices: 72.7 us -> 65.3 us
  other arithmetic: 10.6 us -> 4.78 us
    ppermute x1, waiting for transfers between devices: 41.4 us -> 0.01 us  [body(): window_back = lax.ppermute(ret, 'seq', back_pairs)]
    ppermute x9, waiting for transfers between devices: 40.2 us -> 48.3 us  [scatter_group(): lax.ppermute(pick(y, (within - shift) % group), 'seq', group_pairs(nseg,...]
    ppermute x9, starting transfers between devices: 41 us -> 33.6 us  [scatter_group(): lax.ppermute(pick(y, (within - shift) % group), 'seq', group_pairs(nseg,...]
    unnamed x28 -> x34, local copies, waits for them, and re-layouts: 5.48 us -> 11.9 us
    convert_element_type x1, other arithmetic: 5.12 us -> 0.3 us  [body(): grads_odd = (own_odd + window_back + partner_odd).astype(jnp.bfloat16)]
  transfers between devices with their start and end apart: 20 -> 20, of which waited for: 9 -> 9; matrix products, arithmetic and copies ran while one was open for 7% -> 9% of each run, Pallas kernels for 7% -> 17%
where the time goes in v10:
time: 235 us; the launch traced here: 234 us
  waiting for transfers between devices  89 us (38%)
  starting transfers between devices  65.3 us (28%)
  Pallas kernels  38.7 us (16%)
  local copies, waits for them, and re-layouts  34.9 us (15%)
  other arithmetic  4.78 us (2%)
    ppermute x9, waiting for transfers between devices, scatter_group(): lax.ppermute(pick(y, (within - shift) % group), 'seq', group_pairs(nseg,...  48.3 us
    ppermute x9, waiting for transfers between devices, gather_group(): lax.ppermute(pick(x, (within + shift) % group), 'seq', group_pairs(nseg,...  40.7 us
    pallas_call x2, Pallas kernels, fused_terms(): pl.pallas_call(attention_kernel, grid_spec=pltpu.PrefetchScalarGridSpec(n...  38.7 us
    ppermute x9, starting transfers between devices, scatter_group(): lax.ppermute(pick(y, (within - shift) % group), 'seq', group_pairs(nseg,...  33.6 us
    ppermute x9, starting transfers between devices, gather_group(): lax.ppermute(pick(x, (within + shift) % group), 'seq', group_pairs(nseg,...  28.7 us
    unnamed x34, local copies, waits for them, and re-layouts  11.9 us
    dynamic_update_slice x18, local copies, waits for them, and re-layouts, assemble(): lax.dynamic_update_slice(out, piece[None, None], (head, jnp.int32(column)...  5.75 us
    dynamic_update_slice x9, local copies, waits for them, and re-layouts, place(): lax.dynamic_update_index_in_dim(out, piece, (within - shift) % group, 0)  5.46 us
  transfers between devices with their start and end apart: 20, of which 9 were waited for; matrix products, arithmetic and copies ran while one was open for 9% of the time, Pallas kernels for 17%

profile of v10, /device:TPU:0, one launch (start us, length us, event | category | flops | bytes accessed | tf_op | source)
XLA Modules:
  0.0 233.9 jit_solution(400960842697976042)
XLA Ops:
  2.2 1.2 fusion.14
  3.4 3.0 %collective-permute-start = (bf16[2,2,512,128]{3,2,1,0:T(8,128)(2,1)}, bf16[2,2,512,128]{3,2,1,0:T(8,128)(2,1)}, u32[]{:S(2)}, u32[]{:S(2)}) collective-permute-start(bf16[2,2,512,128]{3,2,1,0:T(8,128)(2,1)} %get-tuple-element.44), channel_id=1, source_target_pairs={{0,8},{8,16},{16,24},{24,0},{4,12},{12,20},{20,28},{28,4},{1,9},{9... | collective-permute-start | bytes 1572872 | tf_op jit(solution)/shard_map/ppermute | solution.py:161
  6.4 2.6 %collective-permute-start.1 = (bf16[2,2,512,128]{3,2,1,0:T(8,128)(2,1)}, bf16[2,2,512,128]{3,2,1,0:T(8,128)(2,1)}, u32[]{:S(2)}, u32[]{:S(2)}) collective-permute-start(bf16[2,2,512,128]{3,2,1,0:T(8,128)(2,1)} %get-tuple-element.45), channel_id=1, source_target_pairs={{0,16},{8,24},{16,0},{24,8},{4,20},{12,28},{20,4},{28,12},{1,17},{... | collective-permute-start | bytes 1572872 | tf_op jit(solution)/shard_map/ppermute | solution.py:161
  9.0 1.3 collective-permute-start.2
  13.2 1.3 pad_maximum_fusion.2
  15.9 5.8 %collective-permute-done = bf16[2,2,512,128]{3,2,1,0:T(8,128)(2,1)} collective-permute-done((bf16[2,2,512,128]{3,2,1,0:T(8,128)(2,1)}, bf16[2,2,512,128]{3,2,1,0:T(8,128)(2,1)}, u32[]{:S(2)}, u32[]{:S(2)}) %collective-permute-start) | collective-permute-done | bytes 524320 | tf_op jit(solution)/shard_map/ppermute | solution.py:161
  22.8 20.5 %collective-permute-done.1 = bf16[2,2,512,128]{3,2,1,0:T(8,128)(2,1)} collective-permute-done((bf16[2,2,512,128]{3,2,1,0:T(8,128)(2,1)}, bf16[2,2,512,128]{3,2,1,0:T(8,128)(2,1)}, u32[]{:S(2)}, u32[]{:S(2)}) %collective-permute-start.1) | collective-permute-done | bytes 524320 | tf_op jit(solution)/shard_map/ppermute | solution.py:161
  47.9 10.6 %collective-permute-start.3 = (bf16[2,512,128]{2,1,0:T(8,128)(2,1)S(1)}, bf16[2,512,128]{2,1,0:T(8,128)(2,1)S(1)}, u32[]{:S(2)}, u32[]{:S(2)}) collective-permute-start(bf16[2,512,128]{2,1,0:T(8,128)(2,1)S(1)} %get-tuple-element.72), channel_id=1, source_target_pairs={{0,8},{8,16},{16,24},{24,0},{4,12},{12,20},{20,28},{28,4},{1,9},{9... | collective-permute-start | bytes 786440 | tf_op jit(solution)/shard_map/ppermute | solution.py:161
  58.5 2.7 %collective-permute-start.4 = (bf16[2,512,128]{2,1,0:T(8,128)(2,1)S(1)}, bf16[2,512,128]{2,1,0:T(8,128)(2,1)S(1)}, u32[]{:S(2)}, u32[]{:S(2)}) collective-permute-start(bf16[2,512,128]{2,1,0:T(8,128)(2,1)S(1)} %get-tuple-element.71), channel_id=1, source_target_pairs={{0,16},{8,24},{16,0},{24,8},{4,20},{12,28},{20,4},{28,12},{1,17},{... | collective-permute-start | bytes 786440 | tf_op jit(solution)/shard_map/ppermute | solution.py:161
  61.5 1.6 collective-permute-start.9
  63.0 4.9 %collective-permute-done.3 = bf16[2,512,128]{2,1,0:T(8,128)(2,1)S(1)} collective-permute-done((bf16[2,512,128]{2,1,0:T(8,128)(2,1)S(1)}, bf16[2,512,128]{2,1,0:T(8,128)(2,1)S(1)}, u32[]{:S(2)}, u32[]{:S(2)}) %collective-permute-start.3) | collective-permute-done | bytes 262176 | tf_op jit(solution)/shard_map/ppermute | solution.py:161
  68.0 9.4 %collective-permute-done.4 = bf16[2,512,128]{2,1,0:T(8,128)(2,1)S(1)} collective-permute-done((bf16[2,512,128]{2,1,0:T(8,128)(2,1)S(1)}, bf16[2,512,128]{2,1,0:T(8,128)(2,1)S(1)}, u32[]{:S(2)}, u32[]{:S(2)}) %collective-permute-start.4) | collective-permute-done | bytes 262176 | tf_op jit(solution)/shard_map/ppermute | solution.py:161
  79.6 6.0 %collective-permute-start.6 = (bf16[2,512,128]{2,1,0:T(8,128)(2,1)}, bf16[2,512,128]{2,1,0:T(8,128)(2,1)}, u32[]{:S(2)}, u32[]{:S(2)}) collective-permute-start(bf16[2,512,128]{2,1,0:T(8,128)(2,1)} %get-tuple-element.62), channel_id=1, source_target_pairs={{0,8},{8,16},{16,24},{24,0},{4,12},{12,20},{20,28},{28,4},{1,9},{9... | collective-permute-start | bytes 786440 | tf_op jit(solution)/shard_map/ppermute | solution.py:161
  85.7 1.3 collective-permute-start.7
  88.0 19.4 %shard_map.84 = (bf16[4,2,512,128]{3,2,1,0:T(8,128)(2,1)}, f32[4,2,512,128]{3,2,1,0:T(8,128)}, f32[4,2,512,128]{3,2,1,0:T(8,128)}, f32[2,4,2,512,128]{4,3,2,1,0:T(8,128)}) custom-call(s32[4]{0:T(128)} %slice.191.index_ref, s32[1]{0:T(128)} %constant.252.clone.1.flag_ref, bf16[4,512,128]{2,1,0:T(8,128)(2,1)} %get-tuple-element.24.q_ref, ...), custom_call_target="tpu_custom_call" | custom-call | flops 4831838208 | bytes 15728640 | tf_op jit(solution)/shard_map/pallas_call | solution.py:130
  107.4 1.2 dynamic-slice_bitcast_fusion.3
  108.6 2.4 %collective-permute-start.13 = (bf16[2,512,128]{2,1,0:T(8,128)(2,1)S(1)}, bf16[2,512,128]{2,1,0:T(8,128)(2,1)S(1)}, u32[]{:S(2)}, u32[]{:S(2)}) collective-permute-start(bf16[2,512,128]{2,1,0:T(8,128)(2,1)S(1)} %get-tuple-element.55), channel_id=1, source_target_pairs={{0,24},{8,0},{16,8},{24,16},{4,28},{12,4},{20,12},{28,20},{1,25},{... | collective-permute-start | bytes 786440 | tf_op jit(solution)/shard_map/ppermute | solution.py:176
  114.0 2.3 slice_bitcast_fusion.2
  116.3 19.3 %shard_map.85 = (bf16[4,2,512,128]{3,2,1,0:T(8,128)(2,1)}, f32[4,2,512,128]{3,2,1,0:T(8,128)}, f32[4,2,512,128]{3,2,1,0:T(8,128)}, f32[2,4,2,512,128]{4,3,2,1,0:T(8,128)}) custom-call(s32[4]{0:T(128)} %slice.174.index_ref, s32[1]{0:T(128)} %bitcast.1.flag_ref, bf16[4,512,128]{2,1,0:T(8,128)(2,1)} %get-tuple-element.59.q_ref, ...), custom_call_target="tpu_custom_call", output_to_operand_aliasing={{3}: (10, {})} | custom-call | flops 4831838208 | bytes 15728640 | tf_op jit(solution)/shard_map/pallas_call | solution.py:130
  135.6 1.7 copy.59
  137.4 1.3 copy-done.3
  138.7 1.7 copy-done.4
  140.5 1.4 copy-done.9
  144.0 1.4 copy-done.2
  146.1 1.4 collective-permute-start.16
  149.2 7.6 %collective-permute-done.10 = bf16[4,512,128]{2,1,0:T(8,128)(2,1)S(1)} collective-permute-done((bf16[4,512,128]{2,1,0:T(8,128)(2,1)S(1)}, bf16[4,512,128]{2,1,0:T(8,128)(2,1)S(1)}, u32[]{:S(2)}, u32[]{:S(2)}) %collective-permute-start.10) | collective-permute-done | bytes 524320 | tf_op jit(solution)/shard_map/ppermute | solution.py:176
  156.8 26.2 %collective-permute-start.14 = (bf16[2,512,128]{2,1,0:T(8,128)(2,1)S(1)}, bf16[2,512,128]{2,1,0:T(8,128)(2,1)S(1)}, u32[]{:S(2)}, u32[]{:S(2)}) collective-permute-start(bf16[2,512,128]{2,1,0:T(8,128)(2,1)S(1)} %get-tuple-element.54), channel_id=1, source_target_pairs={{0,16},{8,24},{16,0},{24,8},{4,20},{12,28},{20,4},{28,12},{1,17},{... | collective-permute-start | bytes 786440 | tf_op jit(solution)/shard_map/ppermute | solution.py:176
  183.1 14.4 %collective-permute-done.11 = bf16[4,512,128]{2,1,0:T(8,128)(2,1)S(1)} collective-permute-done((bf16[4,512,128]{2,1,0:T(8,128)(2,1)S(1)}, bf16[4,512,128]{2,1,0:T(8,128)(2,1)S(1)}, u32[]{:S(2)}, u32[]{:S(2)}) %collective-permute-start.11) | collective-permute-done | bytes 524320 | tf_op jit(solution)/shard_map/ppermute | solution.py:176
  199.1 3.9 %collective-permute-start.17 = (bf16[2,512,128]{2,1,0:T(8,128)(2,1)S(1)}, bf16[2,512,128]{2,1,0:T(8,128)(2,1)S(1)}, u32[]{:S(2)}, u32[]{:S(2)}) collective-permute-start(bf16[2,512,128]{2,1,0:T(8,128)(2,1)S(1)} %get-tuple-element.50), channel_id=1, source_target_pairs={{0,24},{8,0},{16,8},{24,16},{4,28},{12,4},{20,12},{28,20},{1,25},{... | collective-permute-start | bytes 786440 | tf_op jit(solution)/shard_map/ppermute | solution.py:176
  203.0 8.6 %collective-permute-done.14 = bf16[2,512,128]{2,1,0:T(8,128)(2,1)S(1)} collective-permute-done((bf16[2,512,128]{2,1,0:T(8,128)(2,1)S(1)}, bf16[2,512,128]{2,1,0:T(8,128)(2,1)S(1)}, u32[]{:S(2)}, u32[]{:S(2)}) %collective-permute-start.14) | collective-permute-done | bytes 262176 | tf_op jit(solution)/shard_map/ppermute | solution.py:176
  211.9 2.0 collective-permute-done.17
  213.9 15.7 %collective-permute-done.18 = bf16[2,512,128]{2,1,0:T(8,128)(2,1)S(1)} collective-permute-done((bf16[2,512,128]{2,1,0:T(8,128)(2,1)S(1)}, bf16[2,512,128]{2,1,0:T(8,128)(2,1)S(1)}, u32[]{:S(2)}, u32[]{:S(2)}) %collective-permute-start.18) | collective-permute-done | bytes 262176 | tf_op jit(solution)/shard_map/ppermute | solution.py:176
  (107 shorter events, 28.5 us)
Async XLA Ops:
  0.6 13.8 %copy-start = (s32[4,2,8]{2,1,0:T(2,128)S(1)}, s32[4,2,8]{2,1,0:T(2,128)}, u32[]{:S(2)}) copy-start(s32[4,2,8]{2,1,0:T(2,128)} %param.9) | copy-start | bytes 772
  2.2 8.2 %copy-start.11 = (bf16[4,1024,128]{2,1,0:T(8,128)(2,1)S(1)}, bf16[4,1024,128]{2,1,0:T(8,128)(2,1)}, u32[]{:S(2)}) copy-start(bf16[4,1024,128]{2,1,0:T(8,128)(2,1)} %param.5) | copy-start | bytes 3145732
  3.4 7.8 %copy-start.12 = (bf16[4,1024,128]{2,1,0:T(8,128)(2,1)S(1)}, bf16[4,1024,128]{2,1,0:T(8,128)(2,1)}, u32[]{:S(2)}) copy-start(bf16[4,1024,128]{2,1,0:T(8,128)(2,1)} %param.8) | copy-start | bytes 3145732
  3.4 18.3 %collective-permute-start = (bf16[2,2,512,128]{3,2,1,0:T(8,128)(2,1)}, bf16[2,2,512,128]{3,2,1,0:T(8,128)(2,1)}, u32[]{:S(2)}, u32[]{:S(2)}) collective-permute-start(bf16[2,2,512,128]{3,2,1,0:T(8,128)(2,1)} %get-tuple-element.44), channel_id=1, source_target_pairs={{0,8},{8,16},{16,24},{24,0},{4,12},{12,20},{20,28},{28,4},{1,9},{9... | collective-permute-start | bytes 1572872 | tf_op jit(solution)/shard_map/ppermute | solution.py:161
  6.4 36.9 %collective-permute-start.1 = (bf16[2,2,512,128]{3,2,1,0:T(8,128)(2,1)}, bf16[2,2,512,128]{3,2,1,0:T(8,128)(2,1)}, u32[]{:S(2)}, u32[]{:S(2)}) collective-permute-start(bf16[2,2,512,128]{3,2,1,0:T(8,128)(2,1)} %get-tuple-element.45), channel_id=1, source_target_pairs={{0,16},{8,24},{16,0},{24,8},{4,20},{12,28},{20,4},{28,12},{1,17},{... | collective-permute-start | bytes 1572872 | tf_op jit(solution)/shard_map/ppermute | solution.py:161
  9.0 35.4 %collective-permute-start.2 = (bf16[2,2,512,128]{3,2,1,0:T(8,128)(2,1)}, bf16[2,2,512,128]{3,2,1,0:T(8,128)(2,1)}, u32[]{:S(2)}, u32[]{:S(2)}) collective-permute-start(bf16[2,2,512,128]{3,2,1,0:T(8,128)(2,1)} %get-tuple-element.42), channel_id=1, source_target_pairs={{0,24},{8,0},{16,8},{24,16},{4,28},{12,4},{20,12},{28,20},{1,25},{... | collective-permute-start | bytes 1572872 | tf_op jit(solution)/shard_map/ppermute | solution.py:161
  45.8 2.1 copy-start.7
  45.8 2.0 copy-start.5
  47.9 20.1 %collective-permute-start.3 = (bf16[2,512,128]{2,1,0:T(8,128)(2,1)S(1)}, bf16[2,512,128]{2,1,0:T(8,128)(2,1)S(1)}, u32[]{:S(2)}, u32[]{:S(2)}) collective-permute-start(bf16[2,512,128]{2,1,0:T(8,128)(2,1)S(1)} %get-tuple-element.72), channel_id=1, source_target_pairs={{0,8},{8,16},{16,24},{24,0},{4,12},{12,20},{20,28},{28,4},{1,9},{9... | collective-permute-start | bytes 786440 | tf_op jit(solution)/shard_map/ppermute | solution.py:161
  58.5 18.9 %collective-permute-start.4 = (bf16[2,512,128]{2,1,0:T(8,128)(2,1)S(1)}, bf16[2,512,128]{2,1,0:T(8,128)(2,1)S(1)}, u32[]{:S(2)}, u32[]{:S(2)}) collective-permute-start(bf16[2,512,128]{2,1,0:T(8,128)(2,1)S(1)} %get-tuple-element.71), channel_id=1, source_target_pairs={{0,16},{8,24},{16,0},{24,8},{4,20},{12,28},{20,4},{28,12},{1,17},{... | collective-permute-start | bytes 786440 | tf_op jit(solution)/shard_map/ppermute | solution.py:161
  61.5 52.6 %collective-permute-start.9 = (bf16[4,2,512,128]{3,2,0,1:T(8,128)(2,1)S(1)}, bf16[4,2,512,128]{3,2,0,1:T(8,128)(2,1)}, u32[]{:S(2)}, u32[]{:S(2)}) collective-permute-start(bf16[4,2,512,128]{3,2,0,1:T(8,128)(2,1)S(1)} %fusion.4), channel_id=1, source_target_pairs={{0,4},{8,12},{16,20},{24,28},{4,0},{12,8},{20,16},{28,24},{1,5},{9... | collective-permute-start | bytes 3145736 | tf_op jit(solution)/shard_map/ppermute | solution.py:225
  63.0 14.4 %collective-permute-start.5 = (bf16[2,512,128]{2,1,0:T(8,128)(2,1)S(1)}, bf16[2,512,128]{2,1,0:T(8,128)(2,1)S(1)}, u32[]{:S(2)}, u32[]{:S(2)}) collective-permute-start(bf16[2,512,128]{2,1,0:T(8,128)(2,1)S(1)} %get-tuple-element.70), channel_id=1, source_target_pairs={{0,24},{8,0},{16,8},{24,16},{4,28},{12,4},{20,12},{28,20},{1,25},{... | collective-permute-start | bytes 786440 | tf_op jit(solution)/shard_map/ppermute | solution.py:161
  79.6 31.3 %collective-permute-start.6 = (bf16[2,512,128]{2,1,0:T(8,128)(2,1)}, bf16[2,512,128]{2,1,0:T(8,128)(2,1)}, u32[]{:S(2)}, u32[]{:S(2)}) collective-permute-start(bf16[2,512,128]{2,1,0:T(8,128)(2,1)} %get-tuple-element.62), channel_id=1, source_target_pairs={{0,8},{8,16},{16,24},{24,0},{4,12},{12,20},{20,28},{28,4},{1,9},{9... | collective-permute-start | bytes 786440 | tf_op jit(solution)/shard_map/ppermute | solution.py:161
  85.7 26.3 %collective-permute-start.7 = (bf16[2,512,128]{2,1,0:T(8,128)(2,1)}, bf16[2,512,128]{2,1,0:T(8,128)(2,1)}, u32[]{:S(2)}, u32[]{:S(2)}) collective-permute-start(bf16[2,512,128]{2,1,0:T(8,128)(2,1)} %get-tuple-element.61), channel_id=1, source_target_pairs={{0,16},{8,24},{16,0},{24,8},{4,20},{12,28},{20,4},{28,12},{1,17},{... | collective-permute-start | bytes 786440 | tf_op jit(solution)/shard_map/ppermute | solution.py:161
  87.0 25.9 %collective-permute-start.8 = (bf16[2,512,128]{2,1,0:T(8,128)(2,1)}, bf16[2,512,128]{2,1,0:T(8,128)(2,1)S(1)}, u32[]{:S(2)}, u32[]{:S(2)}) collective-permute-start(bf16[2,512,128]{2,1,0:T(8,128)(2,1)} %get-tuple-element.60), channel_id=1, source_target_pairs={{0,24},{8,0},{16,8},{24,16},{4,28},{12,4},{20,12},{28,20},{1,25},{... | collective-permute-start | bytes 786440 | tf_op jit(solution)/shard_map/ppermute | solution.py:161
  108.6 90.1 %collective-permute-start.13 = (bf16[2,512,128]{2,1,0:T(8,128)(2,1)S(1)}, bf16[2,512,128]{2,1,0:T(8,128)(2,1)S(1)}, u32[]{:S(2)}, u32[]{:S(2)}) collective-permute-start(bf16[2,512,128]{2,1,0:T(8,128)(2,1)S(1)} %get-tuple-element.55), channel_id=1, source_target_pairs={{0,24},{8,0},{16,8},{24,16},{4,28},{12,4},{20,12},{28,20},{1,25},{... | collective-permute-start | bytes 786440 | tf_op jit(solution)/shard_map/ppermute | solution.py:176
  137.4 2.9 %copy-start.4 = (f32[2,4,2,512,128]{4,3,2,1,0:T(8,128)S(1)}, f32[2,4,2,512,128]{4,3,2,1,0:T(8,128)}, u32[]{:S(2)}) copy-start(f32[2,4,2,512,128]{4,3,2,1,0:T(8,128)} %get-tuple-element.30) | copy-start | bytes 12582916
  140.3 1.6 copy-start.9
  140.3 2.2 copy-start.10
  143.8 2.0 slice-start
  143.8 2.1 slice-start.1
  143.9 12.8 %collective-permute-start.10 = (bf16[4,512,128]{2,1,0:T(8,128)(2,1)S(1)}, bf16[4,512,128]{2,1,0:T(8,128)(2,1)S(1)}, u32[]{:S(2)}, u32[]{:S(2)}) collective-permute-start(bf16[4,512,128]{2,1,0:T(8,128)(2,1)S(1)} %get-tuple-element.38), channel_id=1, source_target_pairs={{0,24},{8,0},{16,8},{24,16},{4,28},{12,4},{20,12},{28,20},{1,25},{... | collective-permute-start | bytes 1572872 | tf_op jit(solution)/shard_map/ppermute | solution.py:176
  146.1 52.6 %collective-permute-start.16 = (f32[4,2,512,128]{3,2,0,1:T(8,128)S(1)}, f32[4,2,512,128]{3,2,0,1:T(8,128)S(1)}, u32[]{:S(2)}, u32[]{:S(2)}) collective-permute-start(f32[4,2,512,128]{3,2,0,1:T(8,128)S(1)} %maximum_select_fusion), channel_id=1, source_target_pairs={{4,0},{12,8},{20,16},{28,24},{0,4},{8,12},{16,20},{24,28},{5,1},{1... | collective-permute-start | bytes 6291464 | tf_op jit(solution)/shard_map/ppermute | solution.py:247
  147.9 49.6 %collective-permute-start.11 = (bf16[4,512,128]{2,1,0:T(8,128)(2,1)S(1)}, bf16[4,512,128]{2,1,0:T(8,128)(2,1)S(1)}, u32[]{:S(2)}, u32[]{:S(2)}) collective-permute-start(bf16[4,512,128]{2,1,0:T(8,128)(2,1)S(1)} %get-tuple-element.39), channel_id=1, source_target_pairs={{0,16},{8,24},{16,0},{24,8},{4,20},{12,28},{20,4},{28,12},{1,17},{... | collective-permute-start | bytes 1572872 | tf_op jit(solution)/shard_map/ppermute | solution.py:176
  148.7 48.9 %collective-permute-start.12 = (bf16[4,512,128]{2,1,0:T(8,128)(2,1)S(1)}, bf16[4,512,128]{2,1,0:T(8,128)(2,1)S(1)}, u32[]{:S(2)}, u32[]{:S(2)}) collective-permute-start(bf16[4,512,128]{2,1,0:T(8,128)(2,1)S(1)} %get-tuple-element.36), channel_id=1, source_target_pairs={{0,8},{8,16},{16,24},{24,0},{4,12},{12,20},{20,28},{28,4},{1,9},{9... | collective-permute-start | bytes 1572872 | tf_op jit(solution)/shard_map/ppermute | solution.py:176
  156.8 42.0 %copy-start.8 = (f32[4,2,512,128]{3,2,1,0:T(8,128)S(1)}, f32[4,2,512,128]{3,2,1,0:T(8,128)}, u32[]{:S(2)}) copy-start(f32[4,2,512,128]{3,2,1,0:T(8,128)} %get-tuple-element.33) | copy-start | bytes 6291460
  156.8 54.9 %collective-permute-start.14 = (bf16[2,512,128]{2,1,0:T(8,128)(2,1)S(1)}, bf16[2,512,128]{2,1,0:T(8,128)(2,1)S(1)}, u32[]{:S(2)}, u32[]{:S(2)}) collective-permute-start(bf16[2,512,128]{2,1,0:T(8,128)(2,1)S(1)} %get-tuple-element.54), channel_id=1, source_target_pairs={{0,16},{8,24},{16,0},{24,8},{4,20},{12,28},{20,4},{28,12},{1,17},{... | collective-permute-start | bytes 786440 | tf_op jit(solution)/shard_map/ppermute | solution.py:176
  197.5 32.1 %collective-permute-start.15 = (bf16[2,512,128]{2,1,0:T(8,128)(2,1)S(1)}, bf16[2,512,128]{2,1,0:T(8,128)(2,1)S(1)}, u32[]{:S(2)}, u32[]{:S(2)}) collective-permute-start(bf16[2,512,128]{2,1,0:T(8,128)(2,1)S(1)} %get-tuple-element.53), channel_id=1, source_target_pairs={{0,8},{8,16},{16,24},{24,0},{4,12},{12,20},{20,28},{28,4},{1,9},{9... | collective-permute-start | bytes 786440 | tf_op jit(solution)/shard_map/ppermute | solution.py:176
  199.1 14.7 %collective-permute-start.17 = (bf16[2,512,128]{2,1,0:T(8,128)(2,1)S(1)}, bf16[2,512,128]{2,1,0:T(8,128)(2,1)S(1)}, u32[]{:S(2)}, u32[]{:S(2)}) collective-permute-start(bf16[2,512,128]{2,1,0:T(8,128)(2,1)S(1)} %get-tuple-element.50), channel_id=1, source_target_pairs={{0,24},{8,0},{16,8},{24,16},{4,28},{12,4},{20,12},{28,20},{1,25},{... | collective-permute-start | bytes 786440 | tf_op jit(solution)/shard_map/ppermute | solution.py:176
  211.7 17.9 %collective-permute-start.18 = (bf16[2,512,128]{2,1,0:T(8,128)(2,1)S(1)}, bf16[2,512,128]{2,1,0:T(8,128)(2,1)S(1)}, u32[]{:S(2)}, u32[]{:S(2)}) collective-permute-start(bf16[2,512,128]{2,1,0:T(8,128)(2,1)S(1)} %get-tuple-element.49), channel_id=1, source_target_pairs={{0,16},{8,24},{16,0},{24,8},{4,20},{12,28},{20,4},{28,12},{1,17},{... | collective-permute-start | bytes 786440 | tf_op jit(solution)/shard_map/ppermute | solution.py:176
  211.8 17.9 %collective-permute-start.19 = (bf16[2,512,128]{2,1,0:T(8,128)(2,1)S(1)}, bf16[2,512,128]{2,1,0:T(8,128)(2,1)S(1)}, u32[]{:S(2)}, u32[]{:S(2)}) collective-permute-start(bf16[2,512,128]{2,1,0:T(8,128)(2,1)S(1)} %get-tuple-element.48), channel_id=1, source_target_pairs={{0,8},{8,16},{16,24},{24,0},{4,12},{12,20},{20,28},{28,4},{1,9},{9... | collective-permute-start | bytes 786440 | tf_op jit(solution)/shard_map/ppermute | solution.py:176
  231.8 2.1 copy-start.1
  (6 other events, 7.8 us)

commit v11 on v9

--- a/solution.py
+++ b/solution.py
@@ -209,16 +209,16 @@
     kv_local = gather_group(jnp.stack([k4, v4], axis=1), within, nseg, group)
     k_all = kv_local[:, 0].reshape(places, BLK, width)
     v_all = kv_local[:, 1].reshape(places, BLK, width)
-    k_all, v_all, qd_odd_send = lax.optimization_barrier(
-        (k_all, v_all, jnp.stack([q4[:, 1], g4[:, 1]], axis=1))
+    k_all, v_all, qd_even_send = lax.optimization_barrier(
+        (k_all, v_all, jnp.stack([q4[:, 0], g4[:, 0]], axis=1))
+    )
+    qd_even = gather_group(qd_even_send, within, nseg, group)
+    q_even, g_even = qd_even[:, 0], qd_even[:, 1]
+    q_even, g_even, qd_odd_send = lax.optimization_barrier(
+        (q_even, g_even, jnp.stack([q4[:, 1], g4[:, 1]], axis=1))
     )
     qd_odd = gather_group(qd_odd_send, within, nseg, group)
     q_odd, g_odd = qd_odd[:, 0], qd_odd[:, 1]
-    q_odd, g_odd, qd_even_send = lax.optimization_barrier(
-        (q_odd, g_odd, jnp.stack([q4[:, 0], g4[:, 0]], axis=1))
-    )
-    qd_even = gather_group(qd_even_send, within, nseg, group)
-    q_even, g_even = qd_even[:, 0], qd_even[:, 1]
 
     odd_kv = jnp.stack([k_all[1::2], v_all[1::2]], axis=1)
     odd_send = jnp.where(segment == nseg - 1, jnp.roll(odd_kv, 1, axis=0), odd_kv)
@@ -230,28 +230,24 @@
         axis=0,
         keepdims=False,
     )
-    no_mask = jnp.zeros((1,), jnp.int32)
-    ad_odd, own_odd, win_odd, par_odd = fused_terms(
-        1, q_odd, g_odd, k_all, v_all, k_all, v_all, my_partners[1::2], no_mask
-    )
-    sent_odd = scatter_group(ad_odd, within, nseg, group)
-
     first_masked = (segment == 0).astype(jnp.int32).reshape(1)
-    ad_even, own_even, win_even, par_all = fused_terms(
-        0, q_even, g_even, k_all, v_all, window_kv[:, 0], window_kv[:, 1], my_partners[0::2], first_masked, par_odd
-    )
+    ad_even, own_even, win_even, par_even = fused_terms(
+        0, q_even, g_even, k_all, v_all, window_kv[:, 0], window_kv[:, 1], my_partners[0::2], first_masked
+    )
+    sent_even = scatter_group(ad_even, within, nseg, group)
 
     ret = win_even
     ret = jnp.where(segment == 0, jnp.roll(ret, -1, axis=0), ret)
     back_pairs = [(b, a) for a, b in next_segment_pairs(nseg, group)]
     window_back = lax.ppermute(ret, "seq", back_pairs)
 
-    partner_even = par_all[0]
-    partner_odd = par_all[1]
-    grads_even = (own_even + win_odd + partner_even).astype(jnp.bfloat16)
-    sent_even = scatter_group(jnp.concatenate([ad_even, grads_even], axis=1), within, nseg, group)
-    grads_odd = (own_odd + window_back + partner_odd).astype(jnp.bfloat16)
-    sent_last = scatter_group(grads_odd, within, nseg, group)
+    no_mask = jnp.zeros((1,), jnp.int32)
+    ad_odd, own_odd, win_odd, par_all = fused_terms(
+        1, q_odd, g_odd, k_all, v_all, k_all, v_all, my_partners[1::2], no_mask, par_even
+    )
+    grads_even = (own_even + win_odd + par_all[0]).astype(jnp.bfloat16)
+    grads_odd = (own_odd + window_back + par_all[1]).astype(jnp.bfloat16)
+    sent_rest = scatter_group(jnp.concatenate([ad_odd, grads_even, grads_odd], axis=1), within, nseg, group)
 
     shape = (heads, row_count, width)
 
@@ -261,10 +257,10 @@
         return [(h, piece[entry][index]) for h, piece in parts]
 
     return (
-        assemble(column(sent_even, 0), column(sent_odd, 0), heads, shape),
-        assemble(column(sent_even, 1), column(sent_odd, 1), heads, shape),
-        assemble(column(sent_even, 2), column(sent_last, 0), heads, shape),
-        assemble(column(sent_even, 3), column(sent_last, 1), heads, shape),
+        assemble(column(sent_even, 0), column(sent_rest, 0), heads, shape),
+        assemble(column(sent_even, 1), column(sent_rest, 1), heads, shape),
+        assemble(column(sent_rest, 2), column(sent_rest, 4), heads, shape),
+        assemble(column(sent_rest, 3), column(sent_rest, 5), heads, shape),
     )
 
 

time: 270 us -> 239 us (0.89)
  starting transfers between devices: 72.7 us -> 42 us
  local copies, waits for them, and re-layouts: 23.9 us -> 27.9 us
  waiting for transfers between devices: 122 us -> 119 us
    ppermute x1, waiting for transfers between devices: 41.4 us -> 2.74 us  [body(): window_back = lax.ppermute(ret, 'seq', back_pairs)]
    ppermute x9 -> x6, starting transfers between devices: 41 us -> 10.2 us  [scatter_group(): lax.ppermute(pick(y, (within - shift) % group), 'seq', group_pairs(nseg,...]
    ppermute x9 -> x6, waiting for transfers between devices: 40.2 us -> 62.7 us  [scatter_group(): lax.ppermute(pick(y, (within - shift) % group), 'seq', group_pairs(nseg,...]
    ppermute x9, waiting for transfers between devices: 40.6 us -> 53.1 us  [gather_group(): lax.ppermute(pick(x, (within + shift) % group), 'seq', group_pairs(nseg,...]
    dynamic_update_slice x18, local copies, waits for them, and re-layouts: 4.78 us -> 7.71 us  [assemble(): lax.dynamic_update_slice(out, piece[None, None], (head, jnp.int32(column)...]
    unnamed x28 -> x30, local copies, waits for them, and re-layouts: 5.48 us -> 6.88 us
  transfers between devices with their start and end apart: 20 -> 17, of which waited for: 9 -> 9; matrix products, arithmetic and copies ran while one was open for 7% -> 11% of each run, Pallas kernels for 7% -> 16%
where the time goes in v11:
time: 239 us; the launch traced here: 238 us
  waiting for transfers between devices  119 us (50%)
  starting transfers between devices  42 us (18%)
  Pallas kernels  38.7 us (16%)
  local copies, waits for them, and re-layouts  27.9 us (12%)
  other arithmetic  9.85 us (4%)
    ppermute x6, waiting for transfers between devices, scatter_group(): lax.ppermute(pick(y, (within - shift) % group), 'seq', group_pairs(nseg,...  62.7 us
    ppermute x9, waiting for transfers between devices, gather_group(): lax.ppermute(pick(x, (within + shift) % group), 'seq', group_pairs(nseg,...  53.1 us
    pallas_call x2, Pallas kernels, fused_terms(): pl.pallas_call(attention_kernel, grid_spec=pltpu.PrefetchScalarGridSpec(n...  38.7 us
    ppermute x9, starting transfers between devices, gather_group(): lax.ppermute(pick(x, (within + shift) % group), 'seq', group_pairs(nseg,...  28.7 us
    ppermute x6, starting transfers between devices, scatter_group(): lax.ppermute(pick(y, (within - shift) % group), 'seq', group_pairs(nseg,...  10.2 us
    dynamic_update_slice x18, local copies, waits for them, and re-layouts, assemble(): lax.dynamic_update_slice(out, piece[None, None], (head, jnp.int32(column)...  7.71 us
    unnamed x30, local copies, waits for them, and re-layouts  6.88 us
    convert_element_type x1, other arithmetic, body(): grads_even = (own_even + win_odd + par_all[0]).astype(jnp.bfloat16)  5.46 us
  transfers between devices with their start and end apart: 17, of which 9 were waited for; matrix products, arithmetic and copies ran while one was open for 11% of the time, Pallas kernels for 16%

profile of v11, /device:TPU:0, one launch (start us, length us, event | category | flops | bytes accessed | tf_op | source)
XLA Modules:
  0.0 238.1 jit_solution(8293994275927716718)
XLA Ops:
  2.3 1.2 fusion.7
  3.5 3.0 %collective-permute-start = (bf16[2,2,512,128]{3,2,1,0:T(8,128)(2,1)}, bf16[2,2,512,128]{3,2,1,0:T(8,128)(2,1)}, u32[]{:S(2)}, u32[]{:S(2)}) collective-permute-start(bf16[2,2,512,128]{3,2,1,0:T(8,128)(2,1)} %get-tuple-element.45), channel_id=1, source_target_pairs={{0,8},{8,16},{16,24},{24,0},{4,12},{12,20},{20,28},{28,4},{1,9},{9... | collective-permute-start | bytes 1572872 | tf_op jit(solution)/shard_map/ppermute | solution.py:161
  6.5 2.6 %collective-permute-start.1 = (bf16[2,2,512,128]{3,2,1,0:T(8,128)(2,1)}, bf16[2,2,512,128]{3,2,1,0:T(8,128)(2,1)}, u32[]{:S(2)}, u32[]{:S(2)}) collective-permute-start(bf16[2,2,512,128]{3,2,1,0:T(8,128)(2,1)} %get-tuple-element.46), channel_id=1, source_target_pairs={{0,16},{8,24},{16,0},{24,8},{4,20},{12,28},{20,4},{28,12},{1,17},{... | collective-permute-start | bytes 1572872 | tf_op jit(solution)/shard_map/ppermute | solution.py:161
  9.1 1.3 collective-permute-start.2
  11.5 1.4 slice_bitcast_fusion.6
  13.0 1.2 pad_maximum_fusion.2
  14.8 7.0 %collective-permute-done = bf16[2,2,512,128]{3,2,1,0:T(8,128)(2,1)} collective-permute-done((bf16[2,2,512,128]{3,2,1,0:T(8,128)(2,1)}, bf16[2,2,512,128]{3,2,1,0:T(8,128)(2,1)}, u32[]{:S(2)}, u32[]{:S(2)}) %collective-permute-start) | collective-permute-done | bytes 524320 | tf_op jit(solution)/shard_map/ppermute | solution.py:161
  21.7 1.1 bitcast_dynamic-update-slice_fusion.2
  22.8 20.5 %collective-permute-done.1 = bf16[2,2,512,128]{3,2,1,0:T(8,128)(2,1)} collective-permute-done((bf16[2,2,512,128]{3,2,1,0:T(8,128)(2,1)}, bf16[2,2,512,128]{3,2,1,0:T(8,128)(2,1)}, u32[]{:S(2)}, u32[]{:S(2)}) %collective-permute-start.1) | collective-permute-done | bytes 524320 | tf_op jit(solution)/shard_map/ppermute | solution.py:161
  43.4 1.1 bitcast_dynamic-update-slice_fusion.1
  44.5 1.1 bitcast_dynamic-update-slice_fusion
  47.9 10.6 %collective-permute-start.3 = (bf16[2,512,128]{2,1,0:T(8,128)(2,1)S(1)}, bf16[2,512,128]{2,1,0:T(8,128)(2,1)S(1)}, u32[]{:S(2)}, u32[]{:S(2)}) collective-permute-start(bf16[2,512,128]{2,1,0:T(8,128)(2,1)S(1)} %get-tuple-element.66), channel_id=1, source_target_pairs={{0,8},{8,16},{16,24},{24,0},{4,12},{12,20},{20,28},{28,4},{1,9},{9... | collective-permute-start | bytes 786440 | tf_op jit(solution)/shard_map/ppermute | solution.py:161
  58.5 2.7 %collective-permute-start.4 = (bf16[2,512,128]{2,1,0:T(8,128)(2,1)S(1)}, bf16[2,512,128]{2,1,0:T(8,128)(2,1)S(1)}, u32[]{:S(2)}, u32[]{:S(2)}) collective-permute-start(bf16[2,512,128]{2,1,0:T(8,128)(2,1)S(1)} %get-tuple-element.65), channel_id=1, source_target_pairs={{0,16},{8,24},{16,0},{24,8},{4,20},{12,28},{20,4},{28,12},{1,17},{... | collective-permute-start | bytes 786440 | tf_op jit(solution)/shard_map/ppermute | solution.py:161
  61.5 1.6 collective-permute-start.6
  63.0 4.9 %collective-permute-done.3 = bf16[2,512,128]{2,1,0:T(8,128)(2,1)S(1)} collective-permute-done((bf16[2,512,128]{2,1,0:T(8,128)(2,1)S(1)}, bf16[2,512,128]{2,1,0:T(8,128)(2,1)S(1)}, u32[]{:S(2)}, u32[]{:S(2)}) %collective-permute-start.3) | collective-permute-done | bytes 262176 | tf_op jit(solution)/shard_map/ppermute | solution.py:161
  68.0 9.4 %collective-permute-done.4 = bf16[2,512,128]{2,1,0:T(8,128)(2,1)S(1)} collective-permute-done((bf16[2,512,128]{2,1,0:T(8,128)(2,1)S(1)}, bf16[2,512,128]{2,1,0:T(8,128)(2,1)S(1)}, u32[]{:S(2)}, u32[]{:S(2)}) %collective-permute-start.4) | collective-permute-done | bytes 262176 | tf_op jit(solution)/shard_map/ppermute | solution.py:161
  79.6 6.0 %collective-permute-start.10 = (bf16[2,512,128]{2,1,0:T(8,128)(2,1)}, bf16[2,512,128]{2,1,0:T(8,128)(2,1)S(1)}, u32[]{:S(2)}, u32[]{:S(2)}) collective-permute-start(bf16[2,512,128]{2,1,0:T(8,128)(2,1)} %get-tuple-element.51), channel_id=1, source_target_pairs={{0,8},{8,16},{16,24},{24,0},{4,12},{12,20},{20,28},{28,4},{1,9},{9... | collective-permute-start | bytes 786440 | tf_op jit(solution)/shard_map/ppermute | solution.py:161
  86.7 19.3 %shard_map.84 = (bf16[4,2,512,128]{3,2,1,0:T(8,128)(2,1)}, f32[4,2,512,128]{3,2,1,0:T(8,128)}, f32[4,2,512,128]{3,2,1,0:T(8,128)}, f32[2,4,2,512,128]{4,3,2,1,0:T(8,128)}) custom-call(s32[4]{0:T(128)} %slice.174.index_ref, s32[1]{0:T(128)} %bitcast.1.flag_ref, bf16[4,512,128]{2,1,0:T(8,128)(2,1)} %get-tuple-element.19.q_ref, ...), custom_call_target="tpu_custom_call" | custom-call | flops 4831838208 | bytes 15728640 | tf_op jit(solution)/shard_map/pallas_call | solution.py:130
  106.0 1.7 copy.49
  107.9 1.4 copy-done.2
  109.3 1.5 maximum_select_fusion
  110.9 1.6 collective-permute-start.13
  112.4 1.2 collective-permute-start.11
  115.4 11.0 %collective-permute-done.11 = bf16[2,512,128]{2,1,0:T(8,128)(2,1)S(1)} collective-permute-done((bf16[2,512,128]{2,1,0:T(8,128)(2,1)S(1)}, bf16[2,512,128]{2,1,0:T(8,128)(2,1)S(1)}, u32[]{:S(2)}, u32[]{:S(2)}) %collective-permute-start.11) | collective-permute-done | bytes 262176 | tf_op jit(solution)/shard_map/ppermute | solution.py:161
  128.7 6.0 %collective-permute-start.7 = (bf16[2,512,128]{2,1,0:T(8,128)(2,1)}, bf16[2,512,128]{2,1,0:T(8,128)(2,1)}, u32[]{:S(2)}, u32[]{:S(2)}) collective-permute-start(bf16[2,512,128]{2,1,0:T(8,128)(2,1)} %get-tuple-element.55), channel_id=1, source_target_pairs={{0,24},{8,0},{16,8},{24,16},{4,28},{12,4},{20,12},{28,20},{1,25},{... | collective-permute-start | bytes 786440 | tf_op jit(solution)/shard_map/ppermute | solution.py:176
  134.8 1.2 collective-permute-start.8
  136.3 19.4 %shard_map.85 = (bf16[4,2,512,128]{3,2,1,0:T(8,128)(2,1)}, f32[4,2,512,128]{3,2,1,0:T(8,128)}, f32[4,2,512,128]{3,2,1,0:T(8,128)}, f32[2,4,2,512,128]{4,3,2,1,0:T(8,128)}) custom-call(s32[4]{0:T(128)} %slice.193.index_ref, s32[1]{0:T(128)} %constant.230.clone.1.flag_ref, ...), custom_call_target="tpu_custom_call", output_to_operand_aliasing={{3}: (10, {})} | custom-call | flops 4831838208 | bytes 15728640 | tf_op jit(solution)/shard_map/pallas_call | solution.py:130
  155.7 2.7 %collective-permute-done.13 = f32[4,2,512,128]{3,2,0,1:T(8,128)} collective-permute-done((f32[4,2,512,128]{3,2,0,1:T(8,128)}, f32[4,2,512,128]{3,2,0,1:T(8,128)}, u32[]{:S(2)}, u32[]{:S(2)}) %collective-permute-start.13) | collective-permute-done | bytes 2097184 | tf_op jit(solution)/shard_map/ppermute | solution.py:242
  158.5 5.5 %fusion.3 = (bf16[4,2,512,128]{3,2,0,1:T(8,128)(2,1)S(1)}, bf16[4,2,512,128]{3,2,0,1:T(8,128)(2,1)S(1)}) fusion(f32[4,2,512,128]{3,2,1,0:T(8,128)} %get-tuple-element.28, f32[4,2,512,128]{3,2,1,0:T(8,128)} %get-tuple-element.27, f32[4,2,512,128]{3,2,0,1:T(8,128)} %collective-permute-done.13, f32[4,2,512,128]{3,2,1,0:T(8,128)} %get-tuple-element.30, ...), kind=kLoop, calls=%fused_computation.14 | loop fusion | flops 3145728 | bytes 14680064 | tf_op jit(solution)/shard_map/convert_element_type | solution.py:248
  164.4 1.1 collective-permute-start.14
  170.8 12.8 %collective-permute-done.14 = bf16[6,512,128]{2,1,0:T(8,128)(2,1)S(1)} collective-permute-done((bf16[6,512,128]{2,1,0:T(8,128)(2,1)S(1)}, bf16[6,512,128]{2,1,0:T(8,128)(2,1)S(1)}, u32[]{:S(2)}, u32[]{:S(2)}) %collective-permute-start.14) | collective-permute-done | bytes 786464 | tf_op jit(solution)/shard_map/ppermute | solution.py:176
  183.7 49.8 %collective-permute-done.15 = bf16[6,512,128]{2,1,0:T(8,128)(2,1)S(1)} collective-permute-done((bf16[6,512,128]{2,1,0:T(8,128)(2,1)S(1)}, bf16[6,512,128]{2,1,0:T(8,128)(2,1)S(1)}, u32[]{:S(2)}, u32[]{:S(2)}) %collective-permute-start.15) | collective-permute-done | bytes 786464 | tf_op jit(solution)/shard_map/ppermute | solution.py:176
  (92 shorter events, 23.8 us)
Async XLA Ops:
  0.6 13.5 %copy-start = (s32[4,2,8]{2,1,0:T(2,128)S(1)}, s32[4,2,8]{2,1,0:T(2,128)}, u32[]{:S(2)}) copy-start(s32[4,2,8]{2,1,0:T(2,128)} %param.9) | copy-start | bytes 772
  0.7 1.2 copy-start.10
  0.8 1.5 copy-start.11
  2.3 8.1 %copy-start.9 = (bf16[4,1024,128]{2,1,0:T(8,128)(2,1)S(1)}, bf16[4,1024,128]{2,1,0:T(8,128)(2,1)}, u32[]{:S(2)}) copy-start(bf16[4,1024,128]{2,1,0:T(8,128)(2,1)} %param.5) | copy-start | bytes 3145732
  3.5 18.3 %collective-permute-start = (bf16[2,2,512,128]{3,2,1,0:T(8,128)(2,1)}, bf16[2,2,512,128]{3,2,1,0:T(8,128)(2,1)}, u32[]{:S(2)}, u32[]{:S(2)}) collective-permute-start(bf16[2,2,512,128]{3,2,1,0:T(8,128)(2,1)} %get-tuple-element.45), channel_id=1, source_target_pairs={{0,8},{8,16},{16,24},{24,0},{4,12},{12,20},{20,28},{28,4},{1,9},{9... | collective-permute-start | bytes 1572872 | tf_op jit(solution)/shard_map/ppermute | solution.py:161
  6.5 36.9 %collective-permute-start.1 = (bf16[2,2,512,128]{3,2,1,0:T(8,128)(2,1)}, bf16[2,2,512,128]{3,2,1,0:T(8,128)(2,1)}, u32[]{:S(2)}, u32[]{:S(2)}) collective-permute-start(bf16[2,2,512,128]{3,2,1,0:T(8,128)(2,1)} %get-tuple-element.46), channel_id=1, source_target_pairs={{0,16},{8,24},{16,0},{24,8},{4,20},{12,28},{20,4},{28,12},{1,17},{... | collective-permute-start | bytes 1572872 | tf_op jit(solution)/shard_map/ppermute | solution.py:161
  9.1 35.4 %collective-permute-start.2 = (bf16[2,2,512,128]{3,2,1,0:T(8,128)(2,1)}, bf16[2,2,512,128]{3,2,1,0:T(8,128)(2,1)}, u32[]{:S(2)}, u32[]{:S(2)}) collective-permute-start(bf16[2,2,512,128]{3,2,1,0:T(8,128)(2,1)} %get-tuple-element.43), channel_id=1, source_target_pairs={{0,24},{8,0},{16,8},{24,16},{4,28},{12,4},{20,12},{28,20},{1,25},{... | collective-permute-start | bytes 1572872 | tf_op jit(solution)/shard_map/ppermute | solution.py:161
  11.5 1.4 copy-start.6
  11.5 1.5 copy-start.7
  45.8 1.0 copy-start.4
  45.8 2.1 copy-start.5
  45.8 2.0 copy-start.3
  47.9 20.1 %collective-permute-start.3 = (bf16[2,512,128]{2,1,0:T(8,128)(2,1)S(1)}, bf16[2,512,128]{2,1,0:T(8,128)(2,1)S(1)}, u32[]{:S(2)}, u32[]{:S(2)}) collective-permute-start(bf16[2,512,128]{2,1,0:T(8,128)(2,1)S(1)} %get-tuple-element.66), channel_id=1, source_target_pairs={{0,8},{8,16},{16,24},{24,0},{4,12},{12,20},{20,28},{28,4},{1,9},{9... | collective-permute-start | bytes 786440 | tf_op jit(solution)/shard_map/ppermute | solution.py:161
  58.5 18.9 %collective-permute-start.4 = (bf16[2,512,128]{2,1,0:T(8,128)(2,1)S(1)}, bf16[2,512,128]{2,1,0:T(8,128)(2,1)S(1)}, u32[]{:S(2)}, u32[]{:S(2)}) collective-permute-start(bf16[2,512,128]{2,1,0:T(8,128)(2,1)S(1)} %get-tuple-element.65), channel_id=1, source_target_pairs={{0,16},{8,24},{16,0},{24,8},{4,20},{12,28},{20,4},{28,12},{1,17},{... | collective-permute-start | bytes 786440 | tf_op jit(solution)/shard_map/ppermute | solution.py:161
  61.5 24.1 %collective-permute-start.6 = (bf16[4,2,512,128]{3,2,0,1:T(8,128)(2,1)S(1)}, bf16[4,2,512,128]{3,2,0,1:T(8,128)(2,1)S(1)}, u32[]{:S(2)}, u32[]{:S(2)}) collective-permute-start(bf16[4,2,512,128]{3,2,0,1:T(8,128)(2,1)S(1)} %fusion.4), channel_id=1, source_target_pairs={{0,4},{8,12},{16,20},{24,28},{4,0},{12,8},{20,16},{28,24},{1,5},{9... | collective-permute-start | bytes 3145736 | tf_op jit(solution)/shard_map/ppermute | solution.py:225
  63.0 14.4 %collective-permute-start.5 = (bf16[2,512,128]{2,1,0:T(8,128)(2,1)S(1)}, bf16[2,512,128]{2,1,0:T(8,128)(2,1)S(1)}, u32[]{:S(2)}, u32[]{:S(2)}) collective-permute-start(bf16[2,512,128]{2,1,0:T(8,128)(2,1)S(1)} %get-tuple-element.64), channel_id=1, source_target_pairs={{0,24},{8,0},{16,8},{24,16},{4,28},{12,4},{20,12},{28,20},{1,25},{... | collective-permute-start | bytes 786440 | tf_op jit(solution)/shard_map/ppermute | solution.py:161
  79.6 35.8 %collective-permute-start.10 = (bf16[2,512,128]{2,1,0:T(8,128)(2,1)}, bf16[2,512,128]{2,1,0:T(8,128)(2,1)S(1)}, u32[]{:S(2)}, u32[]{:S(2)}) collective-permute-start(bf16[2,512,128]{2,1,0:T(8,128)(2,1)} %get-tuple-element.51), channel_id=1, source_target_pairs={{0,8},{8,16},{16,24},{24,0},{4,12},{12,20},{20,28},{28,4},{1,9},{9... | collective-permute-start | bytes 786440 | tf_op jit(solution)/shard_map/ppermute | solution.py:161
  107.7 1.6 copy-start.2
  109.3 3.1 %copy-start.13 = (bf16[2,512,128]{2,1,0:T(8,128)(2,1)S(1)}, bf16[2,512,128]{2,1,0:T(8,128)(2,1)}, u32[]{:S(2)}) copy-start(bf16[2,512,128]{2,1,0:T(8,128)(2,1)} %get-tuple-element.50) | copy-start | bytes 786436
  110.9 17.0 %copy-start.8 = (bf16[4,2,512,128]{3,2,1,0:T(8,128)(2,1)S(1)}, bf16[4,2,512,128]{3,2,1,0:T(8,128)(2,1)}, u32[]{:S(2)}) copy-start(bf16[4,2,512,128]{3,2,1,0:T(8,128)(2,1)} %get-tuple-element.23) | copy-start | bytes 3145732
  110.9 47.6 %collective-permute-start.13 = (f32[4,2,512,128]{3,2,0,1:T(8,128)}, f32[4,2,512,128]{3,2,0,1:T(8,128)}, u32[]{:S(2)}, u32[]{:S(2)}) collective-permute-start(f32[4,2,512,128]{3,2,0,1:T(8,128)} %maximum_select_fusion), channel_id=1, source_target_pairs={{4,0},{12,8},{20,16},{28,24},{0,4},{8,12},{16,20},{24,28},{5,1},{1... | collective-permute-start | bytes 6291464 | tf_op jit(solution)/shard_map/ppermute | solution.py:242
  112.4 14.0 %collective-permute-start.11 = (bf16[2,512,128]{2,1,0:T(8,128)(2,1)S(1)}, bf16[2,512,128]{2,1,0:T(8,128)(2,1)S(1)}, u32[]{:S(2)}, u32[]{:S(2)}) collective-permute-start(bf16[2,512,128]{2,1,0:T(8,128)(2,1)S(1)} %copy-done.13), channel_id=1, source_target_pairs={{0,16},{8,24},{16,0},{24,8},{4,20},{12,28},{20,4},{28,12},{1,17},{... | collective-permute-start | bytes 786440 | tf_op jit(solution)/shard_map/ppermute | solution.py:161
  114.3 12.5 %collective-permute-start.12 = (bf16[2,512,128]{2,1,0:T(8,128)(2,1)S(1)}, bf16[2,512,128]{2,1,0:T(8,128)(2,1)S(1)}, u32[]{:S(2)}, u32[]{:S(2)}) collective-permute-start(bf16[2,512,128]{2,1,0:T(8,128)(2,1)S(1)} %get-tuple-element.49), channel_id=1, source_target_pairs={{0,24},{8,0},{16,8},{24,16},{4,28},{12,4},{20,12},{28,20},{1,25},{... | collective-permute-start | bytes 786440 | tf_op jit(solution)/shard_map/ppermute | solution.py:161
  128.7 36.8 %collective-permute-start.7 = (bf16[2,512,128]{2,1,0:T(8,128)(2,1)}, bf16[2,512,128]{2,1,0:T(8,128)(2,1)}, u32[]{:S(2)}, u32[]{:S(2)}) collective-permute-start(bf16[2,512,128]{2,1,0:T(8,128)(2,1)} %get-tuple-element.55), channel_id=1, source_target_pairs={{0,24},{8,0},{16,8},{24,16},{4,28},{12,4},{20,12},{28,20},{1,25},{... | collective-permute-start | bytes 786440 | tf_op jit(solution)/shard_map/ppermute | solution.py:176
  134.8 32.6 %collective-permute-start.8 = (bf16[2,512,128]{2,1,0:T(8,128)(2,1)}, bf16[2,512,128]{2,1,0:T(8,128)(2,1)}, u32[]{:S(2)}, u32[]{:S(2)}) collective-permute-start(bf16[2,512,128]{2,1,0:T(8,128)(2,1)} %get-tuple-element.54), channel_id=1, source_target_pairs={{0,16},{8,24},{16,0},{24,8},{4,20},{12,28},{20,4},{28,12},{1,17},{... | collective-permute-start | bytes 786440 | tf_op jit(solution)/shard_map/ppermute | solution.py:176
  136.0 33.4 %collective-permute-start.9 = (bf16[2,512,128]{2,1,0:T(8,128)(2,1)S(1)}, bf16[2,512,128]{2,1,0:T(8,128)(2,1)}, u32[]{:S(2)}, u32[]{:S(2)}) collective-permute-start(bf16[2,512,128]{2,1,0:T(8,128)(2,1)S(1)} %get-tuple-element.53), channel_id=1, source_target_pairs={{0,8},{8,16},{16,24},{24,0},{4,12},{12,20},{20,28},{28,4},{1,9},{9... | collective-permute-start | bytes 786440 | tf_op jit(solution)/shard_map/ppermute | solution.py:176
  158.5 5.5 %copy-start.12 = (bf16[4,2,512,128]{3,2,1,0:T(8,128)(2,1)S(1)}, bf16[4,2,512,128]{3,2,1,0:T(8,128)(2,1)}, u32[]{:S(2)}) copy-start(bf16[4,2,512,128]{3,2,1,0:T(8,128)(2,1)} %get-tuple-element.26) | copy-start | bytes 3145732
  164.4 19.2 %collective-permute-start.14 = (bf16[6,512,128]{2,1,0:T(8,128)(2,1)S(1)}, bf16[6,512,128]{2,1,0:T(8,128)(2,1)S(1)}, u32[]{:S(2)}, u32[]{:S(2)}) collective-permute-start(bf16[6,512,128]{2,1,0:T(8,128)(2,1)S(1)} %get-tuple-element.40), channel_id=1, source_target_pairs={{0,24},{8,0},{16,8},{24,16},{4,28},{12,4},{20,12},{28,20},{1,25},{... | collective-permute-start | bytes 2359304 | tf_op jit(solution)/shard_map/ppermute | solution.py:176
  166.6 66.9 %collective-permute-start.15 = (bf16[6,512,128]{2,1,0:T(8,128)(2,1)S(1)}, bf16[6,512,128]{2,1,0:T(8,128)(2,1)S(1)}, u32[]{:S(2)}, u32[]{:S(2)}) collective-permute-start(bf16[6,512,128]{2,1,0:T(8,128)(2,1)S(1)} %get-tuple-element.39), channel_id=1, source_target_pairs={{0,16},{8,24},{16,0},{24,8},{4,20},{12,28},{20,4},{28,12},{1,17},{... | collective-permute-start | bytes 2359304 | tf_op jit(solution)/shard_map/ppermute | solution.py:176
  168.4 65.2 %collective-permute-start.16 = (bf16[6,512,128]{2,1,0:T(8,128)(2,1)S(1)}, bf16[6,512,128]{2,1,0:T(8,128)(2,1)S(1)}, u32[]{:S(2)}, u32[]{:S(2)}) collective-permute-start(bf16[6,512,128]{2,1,0:T(8,128)(2,1)S(1)} %get-tuple-element.38), channel_id=1, source_target_pairs={{0,8},{8,16},{16,24},{24,0},{4,12},{12,20},{20,28},{28,4},{1,9},{9... | collective-permute-start | bytes 2359304 | tf_op jit(solution)/shard_map/ppermute | solution.py:176
  236.0 2.1 copy-start.1

commit v12 on v10

--- a/solution.py
+++ b/solution.py
@@ -234,7 +234,6 @@
     ad_odd, own_odd, win_odd, par_odd = fused_terms(
         1, q_odd, g_odd, k_all, v_all, k_all, v_all, my_partners[1::2], no_mask
     )
-    sent_odd = scatter_group(ad_odd, within, nseg, group)
 
     first_masked = (segment == 0).astype(jnp.int32).reshape(1)
     ad_even, own_even, win_even, par_all = fused_terms(
@@ -249,7 +248,7 @@
     partner_even = par_all[0]
     partner_odd = par_all[1]
     grads_even = (own_even + win_odd + partner_even).astype(jnp.bfloat16)
-    sent_even = scatter_group(jnp.concatenate([ad_even, grads_even], axis=1), within, nseg, group)
+    sent_even = scatter_group(jnp.concatenate([ad_odd, ad_even, grads_even], axis=1), within, nseg, group)
     grads_even, own_odd, partner_odd = lax.optimization_barrier((grads_even, own_odd, partner_odd))
     grads_odd = (own_odd + window_back + partner_odd).astype(jnp.bfloat16)
     sent_last = scatter_group(grads_odd, within, nseg, group)
@@ -262,10 +261,10 @@
         return [(h, piece[entry][index]) for h, piece in parts]
 
     return (
-        assemble(column(sent_even, 0), column(sent_odd, 0), heads, shape),
-        assemble(column(sent_even, 1), column(sent_odd, 1), heads, shape),
-        assemble(column(sent_even, 2), column(sent_last, 0), heads, shape),
-        assemble(column(sent_even, 3), column(sent_last, 1), heads, shape),
+        assemble(column(sent_even, 2), column(sent_even, 0), heads, shape),
+        assemble(column(sent_even, 3), column(sent_even, 1), heads, shape),
+        assemble(column(sent_even, 4), column(sent_last, 0), heads, shape),
+        assemble(column(sent_even, 5), column(sent_last, 1), heads, shape),
     )
 
 

time: 235 us -> 244 us (1.038)
  waiting for transfers between devices: 89 us -> 123 us
  starting transfers between devices: 65.3 us -> 40.4 us
    ppermute x9 -> x6, waiting for transfers between devices: 48.3 us -> 82.2 us  [scatter_group(): lax.ppermute(pick(y, (within - shift) % group), 'seq', group_pairs(nseg,...]
    ppermute x9 -> x6, starting transfers between devices: 33.6 us -> 8.65 us  [scatter_group(): lax.ppermute(pick(y, (within - shift) % group), 'seq', group_pairs(nseg,...]
    unnamed x34 -> x38, local copies, waits for them, and re-layouts: 11.9 us -> 8.99 us
  transfers between devices with their start and end apart: 20 -> 17, of which waited for: 9 -> 8; matrix products, arithmetic and copies ran while one was open for 9% -> 8% of each run, Pallas kernels for 17% -> 8%
where the time goes in v12:
time: 244 us; the launch traced here: 243 us
  waiting for transfers between devices  123 us (50%)
  starting transfers between devices  40.4 us (17%)
  Pallas kernels  38.7 us (16%)
  local copies, waits for them, and re-layouts  32.8 us (13%)
  other arithmetic  6.86 us (3%)
    ppermute x6, waiting for transfers between devices, scatter_group(): lax.ppermute(pick(y, (within - shift) % group), 'seq', group_pairs(nseg,...  82.2 us
    ppermute x9, waiting for transfers between devices, gather_group(): lax.ppermute(pick(x, (within + shift) % group), 'seq', group_pairs(nseg,...  41.2 us
    pallas_call x2, Pallas kernels, fused_terms(): pl.pallas_call(attention_kernel, grid_spec=pltpu.PrefetchScalarGridSpec(n...  38.7 us
    ppermute x9, starting transfers between devices, gather_group(): lax.ppermute(pick(x, (within + shift) % group), 'seq', group_pairs(nseg,...  28.7 us
    unnamed x38, local copies, waits for them, and re-layouts  8.99 us
    ppermute x6, starting transfers between devices, scatter_group(): lax.ppermute(pick(y, (within - shift) % group), 'seq', group_pairs(nseg,...  8.65 us
    dynamic_update_slice x18, local copies, waits for them, and re-layouts, assemble(): lax.dynamic_update_slice(out, piece[None, None], (head, jnp.int32(column)...  6.98 us
  transfers between devices with their start and end apart: 17, of which 8 were waited for; matrix products, arithmetic and copies ran while one was open for 8% of the time, Pallas kernels for 8%

profile of v12, /device:TPU:0, one launch (start us, length us, event | category | flops | bytes accessed | tf_op | source)
XLA Modules:
  0.0 243.3 jit_solution(8880561355601532484)
XLA Ops:
  2.3 1.2 fusion.7
  3.5 3.0 %collective-permute-start = (bf16[2,2,512,128]{3,2,1,0:T(8,128)(2,1)}, bf16[2,2,512,128]{3,2,1,0:T(8,128)(2,1)}, u32[]{:S(2)}, u32[]{:S(2)}) collective-permute-start(bf16[2,2,512,128]{3,2,1,0:T(8,128)(2,1)} %get-tuple-element.46), channel_id=1, source_target_pairs={{0,8},{8,16},{16,24},{24,0},{4,12},{12,20},{20,28},{28,4},{1,9},{9... | collective-permute-start | bytes 1572872 | tf_op jit(solution)/shard_map/ppermute | solution.py:161
  6.5 2.6 %collective-permute-start.1 = (bf16[2,2,512,128]{3,2,1,0:T(8,128)(2,1)}, bf16[2,2,512,128]{3,2,1,0:T(8,128)(2,1)}, u32[]{:S(2)}, u32[]{:S(2)}) collective-permute-start(bf16[2,2,512,128]{3,2,1,0:T(8,128)(2,1)} %get-tuple-element.47), channel_id=1, source_target_pairs={{0,16},{8,24},{16,0},{24,8},{4,20},{12,28},{20,4},{28,12},{1,17},{... | collective-permute-start | bytes 1572872 | tf_op jit(solution)/shard_map/ppermute | solution.py:161
  9.1 1.3 collective-permute-start.2
  11.5 1.4 slice_bitcast_fusion.6
  15.4 6.3 %collective-permute-done = bf16[2,2,512,128]{3,2,1,0:T(8,128)(2,1)} collective-permute-done((bf16[2,2,512,128]{3,2,1,0:T(8,128)(2,1)}, bf16[2,2,512,128]{3,2,1,0:T(8,128)(2,1)}, u32[]{:S(2)}, u32[]{:S(2)}) %collective-permute-start) | collective-permute-done | bytes 524320 | tf_op jit(solution)/shard_map/ppermute | solution.py:161
  22.9 20.5 %collective-permute-done.1 = bf16[2,2,512,128]{3,2,1,0:T(8,128)(2,1)} collective-permute-done((bf16[2,2,512,128]{3,2,1,0:T(8,128)(2,1)}, bf16[2,2,512,128]{3,2,1,0:T(8,128)(2,1)}, u32[]{:S(2)}, u32[]{:S(2)}) %collective-permute-start.1) | collective-permute-done | bytes 524320 | tf_op jit(solution)/shard_map/ppermute | solution.py:161
  47.9 10.6 %collective-permute-start.3 = (bf16[2,512,128]{2,1,0:T(8,128)(2,1)S(1)}, bf16[2,512,128]{2,1,0:T(8,128)(2,1)S(1)}, u32[]{:S(2)}, u32[]{:S(2)}) collective-permute-start(bf16[2,512,128]{2,1,0:T(8,128)(2,1)S(1)} %get-tuple-element.69), channel_id=1, source_target_pairs={{0,8},{8,16},{16,24},{24,0},{4,12},{12,20},{20,28},{28,4},{1,9},{9... | collective-permute-start | bytes 786440 | tf_op jit(solution)/shard_map/ppermute | solution.py:161
  58.5 2.7 %collective-permute-start.4 = (bf16[2,512,128]{2,1,0:T(8,128)(2,1)S(1)}, bf16[2,512,128]{2,1,0:T(8,128)(2,1)S(1)}, u32[]{:S(2)}, u32[]{:S(2)}) collective-permute-start(bf16[2,512,128]{2,1,0:T(8,128)(2,1)S(1)} %get-tuple-element.68), channel_id=1, source_target_pairs={{0,16},{8,24},{16,0},{24,8},{4,20},{12,28},{20,4},{28,12},{1,17},{... | collective-permute-start | bytes 786440 | tf_op jit(solution)/shard_map/ppermute | solution.py:161
  61.5 1.6 collective-permute-start.9
  63.1 4.9 %collective-permute-done.3 = bf16[2,512,128]{2,1,0:T(8,128)(2,1)S(1)} collective-permute-done((bf16[2,512,128]{2,1,0:T(8,128)(2,1)S(1)}, bf16[2,512,128]{2,1,0:T(8,128)(2,1)S(1)}, u32[]{:S(2)}, u32[]{:S(2)}) %collective-permute-start.3) | collective-permute-done | bytes 262176 | tf_op jit(solution)/shard_map/ppermute | solution.py:161
  68.0 9.4 %collective-permute-done.4 = bf16[2,512,128]{2,1,0:T(8,128)(2,1)S(1)} collective-permute-done((bf16[2,512,128]{2,1,0:T(8,128)(2,1)S(1)}, bf16[2,512,128]{2,1,0:T(8,128)(2,1)S(1)}, u32[]{:S(2)}, u32[]{:S(2)}) %collective-permute-start.4) | collective-permute-done | bytes 262176 | tf_op jit(solution)/shard_map/ppermute | solution.py:161
  79.6 6.0 %collective-permute-start.6 = (bf16[2,512,128]{2,1,0:T(8,128)(2,1)}, bf16[2,512,128]{2,1,0:T(8,128)(2,1)S(1)}, u32[]{:S(2)}, u32[]{:S(2)}) collective-permute-start(bf16[2,512,128]{2,1,0:T(8,128)(2,1)} %get-tuple-element.59), channel_id=1, source_target_pairs={{0,8},{8,16},{16,24},{24,0},{4,12},{12,20},{20,28},{28,4},{1,9},{9... | collective-permute-start | bytes 786440 | tf_op jit(solution)/shard_map/ppermute | solution.py:161
  85.7 1.3 collective-permute-start.7
  88.0 19.4 %shard_map.84 = (bf16[4,2,512,128]{3,2,1,0:T(8,128)(2,1)}, f32[4,2,512,128]{3,2,1,0:T(8,128)}, f32[4,2,512,128]{3,2,1,0:T(8,128)}, f32[2,4,2,512,128]{4,3,2,1,0:T(8,128)}) custom-call(s32[4]{0:T(128)} %slice.174.index_ref, s32[1]{0:T(128)} %constant.228.clone.1.flag_ref, bf16[4,512,128]{2,1,0:T(8,128)(2,1)} %get-tuple-element.21.q_ref, ...), custom_call_target="tpu_custom_call" | custom-call | flops 4831838208 | bytes 15728640 | tf_op jit(solution)/shard_map/pallas_call | solution.py:130
  108.6 2.2 slice_bitcast_fusion.2
  110.9 19.3 %shard_map.85 = (bf16[4,2,512,128]{3,2,1,0:T(8,128)(2,1)}, f32[4,2,512,128]{3,2,1,0:T(8,128)}, f32[4,2,512,128]{3,2,1,0:T(8,128)}, f32[2,4,2,512,128]{4,3,2,1,0:T(8,128)}) custom-call(s32[4]{0:T(128)} %slice.183.index_ref, s32[1]{0:T(128)} %bitcast.21.flag_ref, bf16[4,512,128]{2,1,0:T(8,128)(2,1)} %get-tuple-element.56.q_ref, ...), custom_call_target="tpu_custom_call", output_to_operand_aliasing={{3}: (10, {})} | custom-call | flops 4831838208 | bytes 15728640 | tf_op jit(solution)/shard_map/pallas_call | solution.py:130
  130.2 1.7 copy.65
  132.1 1.4 copy-done.2
  133.5 1.6 maximum_select_fusion
  135.1 1.5 collective-permute-start.13
  139.1 1.5 dynamic-slice_bitcast_fusion
  140.5 4.2 %collective-permute-start.10 = (bf16[6,512,128]{2,1,0:T(8,128)(2,1)}, bf16[6,512,128]{2,1,0:T(8,128)(2,1)}, u32[]{:S(2)}, u32[]{:S(2)}) collective-permute-start(bf16[6,512,128]{2,1,0:T(8,128)(2,1)} %get-tuple-element.41), channel_id=1, source_target_pairs={{0,24},{8,0},{16,8},{24,16},{4,28},{12,4},{20,12},{28,20},{1,25},{... | collective-permute-start | bytes 2359304 | tf_op jit(solution)/shard_map/ppermute | solution.py:176
  144.8 1.8 slice_bitcast_fusion
  147.7 15.4 %collective-permute-done.10 = bf16[6,512,128]{2,1,0:T(8,128)(2,1)} collective-permute-done((bf16[6,512,128]{2,1,0:T(8,128)(2,1)}, bf16[6,512,128]{2,1,0:T(8,128)(2,1)}, u32[]{:S(2)}, u32[]{:S(2)}) %collective-permute-start.10) | collective-permute-done | bytes 786464 | tf_op jit(solution)/shard_map/ppermute | solution.py:176
  164.1 48.6 %collective-permute-done.11 = bf16[6,512,128]{2,1,0:T(8,128)(2,1)S(1)} collective-permute-done((bf16[6,512,128]{2,1,0:T(8,128)(2,1)}, bf16[6,512,128]{2,1,0:T(8,128)(2,1)S(1)}, u32[]{:S(2)}, u32[]{:S(2)}) %collective-permute-start.11) | collective-permute-done | bytes 786464 | tf_op jit(solution)/shard_map/ppermute | solution.py:176
  213.1 1.3 fusion.20
  214.7 2.1 fusion.3
  219.1 1.8 collective-permute-start.15
  220.9 2.0 collective-permute-start.16
  222.9 2.2 collective-permute-done.14
  225.2 15.9 %collective-permute-done.15 = bf16[2,512,128]{2,1,0:T(8,128)(2,1)S(1)} collective-permute-done((bf16[2,512,128]{2,1,0:T(8,128)(2,1)S(1)}, bf16[2,512,128]{2,1,0:T(8,128)(2,1)S(1)}, u32[]{:S(2)}, u32[]{:S(2)}) %collective-permute-start.15) | collective-permute-done | bytes 262176 | tf_op jit(solution)/shard_map/ppermute | solution.py:176
  (102 shorter events, 25.2 us)
Async XLA Ops:
  0.6 13.5 %copy-start = (s32[4,2,8]{2,1,0:T(2,128)S(1)}, s32[4,2,8]{2,1,0:T(2,128)}, u32[]{:S(2)}) copy-start(s32[4,2,8]{2,1,0:T(2,128)} %param.9) | copy-start | bytes 772
  0.8 1.5 copy-start.14
  2.3 8.2 %copy-start.12 = (bf16[4,1024,128]{2,1,0:T(8,128)(2,1)S(1)}, bf16[4,1024,128]{2,1,0:T(8,128)(2,1)}, u32[]{:S(2)}) copy-start(bf16[4,1024,128]{2,1,0:T(8,128)(2,1)} %param.5) | copy-start | bytes 3145732
  3.5 18.3 %collective-permute-start = (bf16[2,2,512,128]{3,2,1,0:T(8,128)(2,1)}, bf16[2,2,512,128]{3,2,1,0:T(8,128)(2,1)}, u32[]{:S(2)}, u32[]{:S(2)}) collective-permute-start(bf16[2,2,512,128]{3,2,1,0:T(8,128)(2,1)} %get-tuple-element.46), channel_id=1, source_target_pairs={{0,8},{8,16},{16,24},{24,0},{4,12},{12,20},{20,28},{28,4},{1,9},{9... | collective-permute-start | bytes 1572872 | tf_op jit(solution)/shard_map/ppermute | solution.py:161
  6.5 36.9 %collective-permute-start.1 = (bf16[2,2,512,128]{3,2,1,0:T(8,128)(2,1)}, bf16[2,2,512,128]{3,2,1,0:T(8,128)(2,1)}, u32[]{:S(2)}, u32[]{:S(2)}) collective-permute-start(bf16[2,2,512,128]{3,2,1,0:T(8,128)(2,1)} %get-tuple-element.47), channel_id=1, source_target_pairs={{0,16},{8,24},{16,0},{24,8},{4,20},{12,28},{20,4},{28,12},{1,17},{... | collective-permute-start | bytes 1572872 | tf_op jit(solution)/shard_map/ppermute | solution.py:161
  9.1 35.4 %collective-permute-start.2 = (bf16[2,2,512,128]{3,2,1,0:T(8,128)(2,1)}, bf16[2,2,512,128]{3,2,1,0:T(8,128)(2,1)}, u32[]{:S(2)}, u32[]{:S(2)}) collective-permute-start(bf16[2,2,512,128]{3,2,1,0:T(8,128)(2,1)} %get-tuple-element.44), channel_id=1, source_target_pairs={{0,24},{8,0},{16,8},{24,16},{4,28},{12,4},{20,12},{28,20},{1,25},{... | collective-permute-start | bytes 1572872 | tf_op jit(solution)/shard_map/ppermute | solution.py:161
  11.5 1.4 copy-start.10
  11.5 1.5 copy-start.11
  45.8 2.1 copy-start.6
  45.8 2.0 copy-start.4
  47.9 20.1 %collective-permute-start.3 = (bf16[2,512,128]{2,1,0:T(8,128)(2,1)S(1)}, bf16[2,512,128]{2,1,0:T(8,128)(2,1)S(1)}, u32[]{:S(2)}, u32[]{:S(2)}) collective-permute-start(bf16[2,512,128]{2,1,0:T(8,128)(2,1)S(1)} %get-tuple-element.69), channel_id=1, source_target_pairs={{0,8},{8,16},{16,24},{24,0},{4,12},{12,20},{20,28},{28,4},{1,9},{9... | collective-permute-start | bytes 786440 | tf_op jit(solution)/shard_map/ppermute | solution.py:161
  58.5 18.9 %collective-permute-start.4 = (bf16[2,512,128]{2,1,0:T(8,128)(2,1)S(1)}, bf16[2,512,128]{2,1,0:T(8,128)(2,1)S(1)}, u32[]{:S(2)}, u32[]{:S(2)}) collective-permute-start(bf16[2,512,128]{2,1,0:T(8,128)(2,1)S(1)} %get-tuple-element.68), channel_id=1, source_target_pairs={{0,16},{8,24},{16,0},{24,8},{4,20},{12,28},{20,4},{28,12},{1,17},{... | collective-permute-start | bytes 786440 | tf_op jit(solution)/shard_map/ppermute | solution.py:161
  61.5 47.1 %collective-permute-start.9 = (bf16[4,2,512,128]{3,2,0,1:T(8,128)(2,1)S(1)}, bf16[4,2,512,128]{3,2,0,1:T(8,128)(2,1)}, u32[]{:S(2)}, u32[]{:S(2)}) collective-permute-start(bf16[4,2,512,128]{3,2,0,1:T(8,128)(2,1)S(1)} %fusion.4), channel_id=1, source_target_pairs={{0,4},{8,12},{16,20},{24,28},{4,0},{12,8},{20,16},{28,24},{1,5},{9... | collective-permute-start | bytes 3145736 | tf_op jit(solution)/shard_map/ppermute | solution.py:225
  63.1 14.4 %collective-permute-start.5 = (bf16[2,512,128]{2,1,0:T(8,128)(2,1)S(1)}, bf16[2,512,128]{2,1,0:T(8,128)(2,1)S(1)}, u32[]{:S(2)}, u32[]{:S(2)}) collective-permute-start(bf16[2,512,128]{2,1,0:T(8,128)(2,1)S(1)} %get-tuple-element.67), channel_id=1, source_target_pairs={{0,24},{8,0},{16,8},{24,16},{4,28},{12,4},{20,12},{28,20},{1,25},{... | collective-permute-start | bytes 786440 | tf_op jit(solution)/shard_map/ppermute | solution.py:161
  79.6 27.8 %collective-permute-start.6 = (bf16[2,512,128]{2,1,0:T(8,128)(2,1)}, bf16[2,512,128]{2,1,0:T(8,128)(2,1)S(1)}, u32[]{:S(2)}, u32[]{:S(2)}) collective-permute-start(bf16[2,512,128]{2,1,0:T(8,128)(2,1)} %get-tuple-element.59), channel_id=1, source_target_pairs={{0,8},{8,16},{16,24},{24,0},{4,12},{12,20},{20,28},{28,4},{1,9},{9... | collective-permute-start | bytes 786440 | tf_op jit(solution)/shard_map/ppermute | solution.py:161
  85.7 21.8 %collective-permute-start.7 = (bf16[2,512,128]{2,1,0:T(8,128)(2,1)}, bf16[2,512,128]{2,1,0:T(8,128)(2,1)S(1)}, u32[]{:S(2)}, u32[]{:S(2)}) collective-permute-start(bf16[2,512,128]{2,1,0:T(8,128)(2,1)} %get-tuple-element.58), channel_id=1, source_target_pairs={{0,16},{8,24},{16,0},{24,8},{4,20},{12,28},{20,4},{28,12},{1,17},{... | collective-permute-start | bytes 786440 | tf_op jit(solution)/shard_map/ppermute | solution.py:161
  87.0 20.5 %collective-permute-start.8 = (bf16[2,512,128]{2,1,0:T(8,128)(2,1)S(1)}, bf16[2,512,128]{2,1,0:T(8,128)(2,1)S(1)}, u32[]{:S(2)}, u32[]{:S(2)}) collective-permute-start(bf16[2,512,128]{2,1,0:T(8,128)(2,1)S(1)} %get-tuple-element.57), channel_id=1, source_target_pairs={{0,24},{8,0},{16,8},{24,16},{4,28},{12,4},{20,12},{28,20},{1,25},{... | collective-permute-start | bytes 786440 | tf_op jit(solution)/shard_map/ppermute | solution.py:161
  131.9 1.6 copy-start.2
  131.9 4.6 %copy-start.9 = (f32[4,2,512,128]{3,2,1,0:T(8,128)S(1)}, f32[4,2,512,128]{3,2,1,0:T(8,128)}, u32[]{:S(2)}) copy-start(f32[4,2,512,128]{3,2,1,0:T(8,128)} %get-tuple-element.29) | copy-start | bytes 6291460
  133.5 3.1 %copy-start.3 = (f32[2,4,2,512,128]{4,3,2,1,0:T(8,128)S(1)}, f32[2,4,2,512,128]{4,3,2,1,0:T(8,128)}, u32[]{:S(2)}) copy-start(f32[2,4,2,512,128]{4,3,2,1,0:T(8,128)} %get-tuple-element.31) | copy-start | bytes 12582916
  133.5 3.7 %copy-start.8 = (f32[4,2,512,128]{3,2,1,0:T(8,128)S(1)}, f32[4,2,512,128]{3,2,1,0:T(8,128)}, u32[]{:S(2)}) copy-start(f32[4,2,512,128]{3,2,1,0:T(8,128)} %get-tuple-element.30) | copy-start | bytes 6291460
  135.1 79.4 %collective-permute-start.13 = (f32[4,2,512,128]{3,2,0,1:T(8,128)}, f32[4,2,512,128]{3,2,0,1:T(8,128)}, u32[]{:S(2)}, u32[]{:S(2)}) collective-permute-start(f32[4,2,512,128]{3,2,0,1:T(8,128)} %maximum_select_fusion), channel_id=1, source_target_pairs={{4,0},{12,8},{20,16},{28,24},{0,4},{8,12},{16,20},{24,28},{5,1},{1... | collective-permute-start | bytes 6291464 | tf_op jit(solution)/shard_map/ppermute | solution.py:246
  137.2 1.5 copy-start.16
  140.5 22.6 %collective-permute-start.10 = (bf16[6,512,128]{2,1,0:T(8,128)(2,1)}, bf16[6,512,128]{2,1,0:T(8,128)(2,1)}, u32[]{:S(2)}, u32[]{:S(2)}) collective-permute-start(bf16[6,512,128]{2,1,0:T(8,128)(2,1)} %get-tuple-element.41), channel_id=1, source_target_pairs={{0,24},{8,0},{16,8},{24,16},{4,28},{12,4},{20,12},{28,20},{1,25},{... | collective-permute-start | bytes 2359304 | tf_op jit(solution)/shard_map/ppermute | solution.py:176
  144.8 1.8 copy-start.17
  144.8 68.0 %collective-permute-start.11 = (bf16[6,512,128]{2,1,0:T(8,128)(2,1)}, bf16[6,512,128]{2,1,0:T(8,128)(2,1)S(1)}, u32[]{:S(2)}, u32[]{:S(2)}) collective-permute-start(bf16[6,512,128]{2,1,0:T(8,128)(2,1)} %get-tuple-element.40), channel_id=1, source_target_pairs={{0,16},{8,24},{16,0},{24,8},{4,20},{12,28},{20,4},{28,12},{1,17},{... | collective-permute-start | bytes 2359304 | tf_op jit(solution)/shard_map/ppermute | solution.py:176
  146.6 66.2 %collective-permute-start.12 = (bf16[6,512,128]{2,1,0:T(8,128)(2,1)S(1)}, bf16[6,512,128]{2,1,0:T(8,128)(2,1)S(1)}, u32[]{:S(2)}, u32[]{:S(2)}) collective-permute-start(bf16[6,512,128]{2,1,0:T(8,128)(2,1)S(1)} %copy-done.17), channel_id=1, source_target_pairs={{0,8},{8,16},{16,24},{24,0},{4,12},{12,20},{20,28},{28,4},{1,9},{9... | collective-permute-start | bytes 2359304 | tf_op jit(solution)/shard_map/ppermute | solution.py:176
  212.8 1.8 copy-start.7
  216.9 8.3 %collective-permute-start.14 = (bf16[2,512,128]{2,1,0:T(8,128)(2,1)S(1)}, bf16[2,512,128]{2,1,0:T(8,128)(2,1)S(1)}, u32[]{:S(2)}, u32[]{:S(2)}) collective-permute-start(bf16[2,512,128]{2,1,0:T(8,128)(2,1)S(1)} %get-tuple-element.52), channel_id=1, source_target_pairs={{0,24},{8,0},{16,8},{24,16},{4,28},{12,4},{20,12},{28,20},{1,25},{... | collective-permute-start | bytes 786440 | tf_op jit(solution)/shard_map/ppermute | solution.py:176
  219.1 22.0 %collective-permute-start.15 = (bf16[2,512,128]{2,1,0:T(8,128)(2,1)S(1)}, bf16[2,512,128]{2,1,0:T(8,128)(2,1)S(1)}, u32[]{:S(2)}, u32[]{:S(2)}) collective-permute-start(bf16[2,512,128]{2,1,0:T(8,128)(2,1)S(1)} %get-tuple-element.51), channel_id=1, source_target_pairs={{0,16},{8,24},{16,0},{24,8},{4,20},{12,28},{20,4},{28,12},{1,17},{... | collective-permute-start | bytes 786440 | tf_op jit(solution)/shard_map/ppermute | solution.py:176
  220.9 20.3 %collective-permute-start.16 = (bf16[2,512,128]{2,1,0:T(8,128)(2,1)S(1)}, bf16[2,512,128]{2,1,0:T(8,128)(2,1)S(1)}, u32[]{:S(2)}, u32[]{:S(2)}) collective-permute-start(bf16[2,512,128]{2,1,0:T(8,128)(2,1)S(1)} %get-tuple-element.50), channel_id=1, source_target_pairs={{0,8},{8,16},{16,24},{24,0},{4,12},{12,20},{20,28},{28,4},{1,9},{9... | collective-permute-start | bytes 786440 | tf_op jit(solution)/shard_map/ppermute | solution.py:176
  241.2 2.1 copy-start.1
  (3 other events, 3.4 us)

commit v13 on v10

--- a/solution.py
+++ b/solution.py
@@ -206,14 +206,11 @@
         return x.reshape(heads, blocks, BLK, width)
 
     q4, g4, k4, v4 = split(queries), split(grad_out), split(key_rows), split(value_rows)
-    kv_local = gather_group(jnp.stack([k4, v4], axis=1), within, nseg, group)
-    k_all = kv_local[:, 0].reshape(places, BLK, width)
-    v_all = kv_local[:, 1].reshape(places, BLK, width)
-    k_all, v_all, qd_odd_send = lax.optimization_barrier(
-        (k_all, v_all, jnp.stack([q4[:, 1], g4[:, 1]], axis=1))
-    )
-    qd_odd = gather_group(qd_odd_send, within, nseg, group)
-    q_odd, g_odd = qd_odd[:, 0], qd_odd[:, 1]
+    first = jnp.concatenate([k4, v4, q4[:, 1:], g4[:, 1:]], axis=1)
+    first_local = gather_group(first, within, nseg, group)
+    k_all = first_local[:, 0:2].reshape(places, BLK, width)
+    v_all = first_local[:, 2:4].reshape(places, BLK, width)
+    q_odd, g_odd = first_local[:, 4], first_local[:, 5]
     q_odd, g_odd, qd_even_send = lax.optimization_barrier(
         (q_odd, g_odd, jnp.stack([q4[:, 0], g4[:, 0]], axis=1))
     )

time: 235 us -> 234 us (level)
  waiting for transfers between devices: 89 us -> 92.3 us
  starting transfers between devices: 65.3 us -> 62.9 us
    ppermute x9 -> x6, waiting for transfers between devices: 40.7 us -> 45.9 us  [gather_group(): lax.ppermute(pick(x, (within + shift) % group), 'seq', group_pairs(nseg,...]
    ppermute x9 -> x6, starting transfers between devices: 28.7 us -> 25.9 us  [gather_group(): lax.ppermute(pick(x, (within + shift) % group), 'seq', group_pairs(nseg,...]
    unnamed x34 -> x27, local copies, waits for them, and re-layouts: 11.9 us -> 9.46 us
    dynamic_update_slice x9 -> x6, local copies, waits for them, and re-layouts: 5.46 us -> 6.68 us  [place(): lax.dynamic_update_index_in_dim(out, piece, (within - shift) % group, 0)]
    dynamic_update_slice x18 -> x19, local copies, waits for them, and re-layouts: 5.75 us -> 6.71 us  [assemble(): lax.dynamic_update_slice(out, piece[None, None], (head, jnp.int32(column)...]
  transfers between devices with their start and end apart: 20 -> 17, of which waited for: 9 -> 7; matrix products, arithmetic and copies ran while one was open for 9% -> 9% of each run, Pallas kernels for 17% -> 17%
where the time goes in v13:
time: 234 us; the launch traced here: 233 us
  waiting for transfers between devices  92.3 us (39%)
  starting transfers between devices  62.9 us (27%)
  Pallas kernels  38.7 us (17%)
  local copies, waits for them, and re-layouts  35.5 us (15%)
  other arithmetic  2.77 us (1%)
    ppermute x9, waiting for transfers between devices, scatter_group(): lax.ppermute(pick(y, (within - shift) % group), 'seq', group_pairs(nseg,...  46.4 us
    ppermute x6, waiting for transfers between devices, gather_group(): lax.ppermute(pick(x, (within + shift) % group), 'seq', group_pairs(nseg,...  45.9 us
    pallas_call x2, Pallas kernels, fused_terms(): pl.pallas_call(attention_kernel, grid_spec=pltpu.PrefetchScalarGridSpec(n...  38.7 us
    ppermute x9, starting transfers between devices, scatter_group(): lax.ppermute(pick(y, (within - shift) % group), 'seq', group_pairs(nseg,...  34.8 us
    ppermute x6, starting transfers between devices, gather_group(): lax.ppermute(pick(x, (within + shift) % group), 'seq', group_pairs(nseg,...  25.9 us
    unnamed x27, local copies, waits for them, and re-layouts  9.46 us
    dynamic_update_slice x19, local copies, waits for them, and re-layouts, assemble(): lax.dynamic_update_slice(out, piece[None, None], (head, jnp.int32(column)...  6.71 us
    dynamic_update_slice x6, local copies, waits for them, and re-layouts, place(): lax.dynamic_update_index_in_dim(out, piece, (within - shift) % group, 0)  6.68 us
  transfers between devices with their start and end apart: 17, of which 7 were waited for; matrix products, arithmetic and copies ran while one was open for 9% of the time, Pallas kernels for 17%

profile of v13, /device:TPU:0, one launch (start us, length us, event | category | flops | bytes accessed | tf_op | source)
XLA Modules:
  0.0 233.2 jit_solution(3752135230176495552)
XLA Ops:
  0.8 2.7 %slice_bitcast_fusion.6 = (bf16[4,1,512,128]{3,2,0,1:T(8,128)(2,1)}, bf16[4,1,512,128]{3,2,0,1:T(8,128)(2,1)S(1)}, bf16[4,1,512,128]{3,2,0,1:T(8,128)(2,1)S(1)}, bf16[4,1,512,128]{3,2,0,1:T(8,128)(2,1)}) fusion(bf16[4,2,512,128]{3,2,1,0:T(8,128)(2,1)} %bitcast.229, bf16[4,2,512,128]{3,2,1,0:T(8,128)(2,1)} %bitcast.230), kind=kLoop, calls=%fused_computation.44 | loop fusion | bytes 4194304
  4.5 1.5 dynamic-slice_bitcast_fusion
  5.9 3.0 %collective-permute-start = (bf16[6,512,128]{2,1,0:T(8,128)(2,1)}, bf16[6,512,128]{2,1,0:T(8,128)(2,1)}, u32[]{:S(2)}, u32[]{:S(2)}) collective-permute-start(bf16[6,512,128]{2,1,0:T(8,128)(2,1)} %get-tuple-element.36), channel_id=1, source_target_pairs={{0,8},{8,16},{16,24},{24,0},{4,12},{12,20},{20,28},{28,4},{1,9},{9... | collective-permute-start | bytes 2359304 | tf_op jit(solution)/shard_map/ppermute | solution.py:161
  8.9 2.6 %collective-permute-start.1 = (bf16[6,512,128]{2,1,0:T(8,128)(2,1)}, bf16[6,512,128]{2,1,0:T(8,128)(2,1)}, u32[]{:S(2)}, u32[]{:S(2)}) collective-permute-start(bf16[6,512,128]{2,1,0:T(8,128)(2,1)} %get-tuple-element.35), channel_id=1, source_target_pairs={{0,16},{8,24},{16,0},{24,8},{4,20},{12,28},{20,4},{28,12},{1,17},{... | collective-permute-start | bytes 2359304 | tf_op jit(solution)/shard_map/ppermute | solution.py:161
  11.5 1.3 collective-permute-start.2
  14.2 1.3 pad_maximum_fusion.2
  15.5 14.2 %collective-permute-done = bf16[6,512,128]{2,1,0:T(8,128)(2,1)} collective-permute-done((bf16[6,512,128]{2,1,0:T(8,128)(2,1)}, bf16[6,512,128]{2,1,0:T(8,128)(2,1)}, u32[]{:S(2)}, u32[]{:S(2)}) %collective-permute-start) | collective-permute-done | bytes 786464 | tf_op jit(solution)/shard_map/ppermute | solution.py:161
  29.8 1.2 bitcast_dynamic-update-slice_fusion.2
  31.0 31.6 %collective-permute-done.1 = bf16[6,512,128]{2,1,0:T(8,128)(2,1)} collective-permute-done((bf16[6,512,128]{2,1,0:T(8,128)(2,1)}, bf16[6,512,128]{2,1,0:T(8,128)(2,1)}, u32[]{:S(2)}, u32[]{:S(2)}) %collective-permute-start.1) | collective-permute-done | bytes 786464 | tf_op jit(solution)/shard_map/ppermute | solution.py:161
  62.7 1.2 bitcast_dynamic-update-slice_fusion.1
  63.9 1.2 bitcast_dynamic-update-slice_fusion
  67.4 1.1 slice_bitcast_fusion.8
  68.7 1.6 collective-permute-start.6
  71.3 16.1 %collective-permute-start.3 = (bf16[2,512,128]{2,1,0:T(8,128)(2,1)}, bf16[2,512,128]{2,1,0:T(8,128)(2,1)}, u32[]{:S(2)}, u32[]{:S(2)}) collective-permute-start(bf16[2,512,128]{2,1,0:T(8,128)(2,1)} %get-tuple-element.58), channel_id=1, source_target_pairs={{0,8},{8,16},{16,24},{24,0},{4,12},{12,20},{20,28},{28,4},{1,9},{9... | collective-permute-start | bytes 786440 | tf_op jit(solution)/shard_map/ppermute | solution.py:161
  87.3 2.8 %collective-permute-start.4 = (bf16[2,512,128]{2,1,0:T(8,128)(2,1)}, bf16[2,512,128]{2,1,0:T(8,128)(2,1)}, u32[]{:S(2)}, u32[]{:S(2)}) collective-permute-start(bf16[2,512,128]{2,1,0:T(8,128)(2,1)} %get-tuple-element.57), channel_id=1, source_target_pairs={{0,16},{8,24},{16,0},{24,8},{4,20},{12,28},{20,4},{28,12},{1,17},{... | collective-permute-start | bytes 786440 | tf_op jit(solution)/shard_map/ppermute | solution.py:161
  90.2 19.4 %shard_map.84 = (bf16[4,2,512,128]{3,2,1,0:T(8,128)(2,1)}, f32[4,2,512,128]{3,2,1,0:T(8,128)}, f32[4,2,512,128]{3,2,1,0:T(8,128)}, f32[2,4,2,512,128]{4,3,2,1,0:T(8,128)}) custom-call(s32[4]{0:T(128)} %slice.191.index_ref, s32[1]{0:T(128)} %constant.222.clone.1.flag_ref, bf16[4,512,128]{2,1,0:T(8,128)(2,1)} %get-tuple-element.18.q_ref, ...), custom_call_target="tpu_custom_call" | custom-call | flops 4831838208 | bytes 15728640 | tf_op jit(solution)/shard_map/pallas_call | solution.py:130
  109.5 2.0 dynamic-slice_bitcast_fusion.6
  111.5 1.6 collective-permute-start.10
  117.1 1.1 slice_bitcast_fusion.2
  118.2 19.3 %shard_map.85 = (bf16[4,2,512,128]{3,2,1,0:T(8,128)(2,1)}, f32[4,2,512,128]{3,2,1,0:T(8,128)}, f32[4,2,512,128]{3,2,1,0:T(8,128)}, f32[2,4,2,512,128]{4,3,2,1,0:T(8,128)}) custom-call(s32[4]{0:T(128)} %slice.174.index_ref, s32[1]{0:T(128)} %bitcast.1.flag_ref, bf16[4,512,128]{2,1,0:T(8,128)(2,1)} %get-tuple-element.55.q_ref, ...), custom_call_target="tpu_custom_call", output_to_operand_aliasing={{3}: (10, {})} | custom-call | flops 4831838208 | bytes 15728640 | tf_op jit(solution)/shard_map/pallas_call | solution.py:130
  137.5 1.7 copy.65
  139.4 1.4 copy-done.2
  141.7 1.4 copy-done.3
  145.8 1.4 collective-permute-start.7
  148.4 2.1 collective-permute-start.9
  150.6 9.0 %collective-permute-done.7 = bf16[4,512,128]{2,1,0:T(8,128)(2,1)S(1)} collective-permute-done((bf16[4,512,128]{2,1,0:T(8,128)(2,1)S(1)}, bf16[4,512,128]{2,1,0:T(8,128)(2,1)S(1)}, u32[]{:S(2)}, u32[]{:S(2)}) %collective-permute-start.7) | collective-permute-done | bytes 524320 | tf_op jit(solution)/shard_map/ppermute | solution.py:176
  159.6 25.8 %collective-permute-start.11 = (bf16[2,512,128]{2,1,0:T(8,128)(2,1)S(1)}, bf16[2,512,128]{2,1,0:T(8,128)(2,1)S(1)}, u32[]{:S(2)}, u32[]{:S(2)}) collective-permute-start(bf16[2,512,128]{2,1,0:T(8,128)(2,1)S(1)} %copy-done.12), channel_id=1, source_target_pairs={{0,16},{8,24},{16,0},{24,8},{4,20},{12,28},{20,4},{28,12},{1,17},{... | collective-permute-start | bytes 786440 | tf_op jit(solution)/shard_map/ppermute | solution.py:176
  185.5 17.2 %collective-permute-done.8 = bf16[4,512,128]{2,1,0:T(8,128)(2,1)S(1)} collective-permute-done((bf16[4,512,128]{2,1,0:T(8,128)(2,1)S(1)}, bf16[4,512,128]{2,1,0:T(8,128)(2,1)S(1)}, u32[]{:S(2)}, u32[]{:S(2)}) %collective-permute-start.8) | collective-permute-done | bytes 524320 | tf_op jit(solution)/shard_map/ppermute | solution.py:176
  204.9 1.1 collective-permute-done.11
  206.5 2.7 %collective-permute-start.14 = (bf16[2,512,128]{2,1,0:T(8,128)(2,1)S(1)}, bf16[2,512,128]{2,1,0:T(8,128)(2,1)S(1)}, u32[]{:S(2)}, u32[]{:S(2)}) collective-permute-start(bf16[2,512,128]{2,1,0:T(8,128)(2,1)S(1)} %get-tuple-element.46), channel_id=1, source_target_pairs={{0,24},{8,0},{16,8},{24,16},{4,28},{12,4},{20,12},{28,20},{1,25},{... | collective-permute-start | bytes 786440 | tf_op jit(solution)/shard_map/ppermute | solution.py:176
  209.3 3.5 %collective-permute-done.12 = bf16[2,512,128]{2,1,0:T(8,128)(2,1)S(1)} collective-permute-done((bf16[2,512,128]{2,1,0:T(8,128)(2,1)S(1)}, bf16[2,512,128]{2,1,0:T(8,128)(2,1)S(1)}, u32[]{:S(2)}, u32[]{:S(2)}) %collective-permute-start.12) | collective-permute-done | bytes 262176 | tf_op jit(solution)/shard_map/ppermute | solution.py:176
  215.6 15.5 %collective-permute-done.15 = bf16[2,512,128]{2,1,0:T(8,128)(2,1)S(1)} collective-permute-done((bf16[2,512,128]{2,1,0:T(8,128)(2,1)S(1)}, bf16[2,512,128]{2,1,0:T(8,128)(2,1)S(1)}, u32[]{:S(2)}, u32[]{:S(2)}) %collective-permute-start.15) | collective-permute-done | bytes 262176 | tf_op jit(solution)/shard_map/ppermute | solution.py:176
  (90 shorter events, 22.3 us)
Async XLA Ops:
  0.6 12.2 %copy-start = (s32[4,2,8]{2,1,0:T(2,128)S(1)}, s32[4,2,8]{2,1,0:T(2,128)}, u32[]{:S(2)}) copy-start(s32[4,2,8]{2,1,0:T(2,128)} %param.9) | copy-start | bytes 772
  0.6 2.9 %copy-start.9 = (bf16[4,1024,128]{2,1,0:T(8,128)(2,1)S(1)}, bf16[4,1024,128]{2,1,0:T(8,128)(2,1)}, u32[]{:S(2)}) copy-start(bf16[4,1024,128]{2,1,0:T(8,128)(2,1)} %param.6) | copy-start | bytes 3145732
  0.7 2.9 %copy-start.10 = (bf16[4,1024,128]{2,1,0:T(8,128)(2,1)S(1)}, bf16[4,1024,128]{2,1,0:T(8,128)(2,1)}, u32[]{:S(2)}) copy-start(bf16[4,1024,128]{2,1,0:T(8,128)(2,1)} %param.7) | copy-start | bytes 3145732
  5.9 23.9 %collective-permute-start = (bf16[6,512,128]{2,1,0:T(8,128)(2,1)}, bf16[6,512,128]{2,1,0:T(8,128)(2,1)}, u32[]{:S(2)}, u32[]{:S(2)}) collective-permute-start(bf16[6,512,128]{2,1,0:T(8,128)(2,1)} %get-tuple-element.36), channel_id=1, source_target_pairs={{0,8},{8,16},{16,24},{24,0},{4,12},{12,20},{20,28},{28,4},{1,9},{9... | collective-permute-start | bytes 2359304 | tf_op jit(solution)/shard_map/ppermute | solution.py:161
  8.9 53.7 %collective-permute-start.1 = (bf16[6,512,128]{2,1,0:T(8,128)(2,1)}, bf16[6,512,128]{2,1,0:T(8,128)(2,1)}, u32[]{:S(2)}, u32[]{:S(2)}) collective-permute-start(bf16[6,512,128]{2,1,0:T(8,128)(2,1)} %get-tuple-element.35), channel_id=1, source_target_pairs={{0,16},{8,24},{16,0},{24,8},{4,20},{12,28},{20,4},{28,12},{1,17},{... | collective-permute-start | bytes 2359304 | tf_op jit(solution)/shard_map/ppermute | solution.py:161
  11.5 52.4 %collective-permute-start.2 = (bf16[6,512,128]{2,1,0:T(8,128)(2,1)}, bf16[6,512,128]{2,1,0:T(8,128)(2,1)}, u32[]{:S(2)}, u32[]{:S(2)}) collective-permute-start(bf16[6,512,128]{2,1,0:T(8,128)(2,1)} %get-tuple-element.34), channel_id=1, source_target_pairs={{0,24},{8,0},{16,8},{24,16},{4,28},{12,4},{20,12},{28,20},{1,25},{... | collective-permute-start | bytes 2359304 | tf_op jit(solution)/shard_map/ppermute | solution.py:161
  65.4 1.0 copy-start.4
  66.4 1.0 copy-start.5
  68.7 48.5 %collective-permute-start.6 = (bf16[4,2,512,128]{3,2,0,1:T(8,128)(2,1)S(1)}, bf16[4,2,512,128]{3,2,0,1:T(8,128)(2,1)S(1)}, u32[]{:S(2)}, u32[]{:S(2)}) collective-permute-start(bf16[4,2,512,128]{3,2,0,1:T(8,128)(2,1)S(1)} %fusion.4), channel_id=1, source_target_pairs={{0,4},{8,12},{16,20},{24,28},{4,0},{12,8},{20,16},{28,24},{1,5},{9... | collective-permute-start | bytes 3145736 | tf_op jit(solution)/shard_map/ppermute | solution.py:222
  71.3 41.8 %collective-permute-start.3 = (bf16[2,512,128]{2,1,0:T(8,128)(2,1)}, bf16[2,512,128]{2,1,0:T(8,128)(2,1)}, u32[]{:S(2)}, u32[]{:S(2)}) collective-permute-start(bf16[2,512,128]{2,1,0:T(8,128)(2,1)} %get-tuple-element.58), channel_id=1, source_target_pairs={{0,8},{8,16},{16,24},{24,0},{4,12},{12,20},{20,28},{28,4},{1,9},{9... | collective-permute-start | bytes 786440 | tf_op jit(solution)/shard_map/ppermute | solution.py:161
  87.3 26.7 %collective-permute-start.4 = (bf16[2,512,128]{2,1,0:T(8,128)(2,1)}, bf16[2,512,128]{2,1,0:T(8,128)(2,1)}, u32[]{:S(2)}, u32[]{:S(2)}) collective-permute-start(bf16[2,512,128]{2,1,0:T(8,128)(2,1)} %get-tuple-element.57), channel_id=1, source_target_pairs={{0,16},{8,24},{16,0},{24,8},{4,20},{12,28},{20,4},{28,12},{1,17},{... | collective-permute-start | bytes 786440 | tf_op jit(solution)/shard_map/ppermute | solution.py:161
  90.2 24.9 %collective-permute-start.5 = (bf16[2,512,128]{2,1,0:T(8,128)(2,1)}, bf16[2,512,128]{2,1,0:T(8,128)(2,1)}, u32[]{:S(2)}, u32[]{:S(2)}) collective-permute-start(bf16[2,512,128]{2,1,0:T(8,128)(2,1)} %get-tuple-element.56), channel_id=1, source_target_pairs={{0,24},{8,0},{16,8},{24,16},{4,28},{12,4},{20,12},{28,20},{1,25},{... | collective-permute-start | bytes 786440 | tf_op jit(solution)/shard_map/ppermute | solution.py:161
  111.5 92.4 %collective-permute-start.10 = (bf16[2,512,128]{2,1,0:T(8,128)(2,1)}, bf16[2,512,128]{2,1,0:T(8,128)(2,1)}, u32[]{:S(2)}, u32[]{:S(2)}) collective-permute-start(bf16[2,512,128]{2,1,0:T(8,128)(2,1)} %get-tuple-element.51), channel_id=1, source_target_pairs={{0,24},{8,0},{16,8},{24,16},{4,28},{12,4},{20,12},{28,20},{1,25},{... | collective-permute-start | bytes 786440 | tf_op jit(solution)/shard_map/ppermute | solution.py:176
  139.3 1.6 copy-start.2
  140.9 2.2 copy-start.3
  141.1 2.7 %copy-start.7 = (f32[4,2,512,128]{3,2,1,0:T(8,128)S(1)}, f32[4,2,512,128]{3,2,1,0:T(8,128)}, u32[]{:S(2)}) copy-start(f32[4,2,512,128]{3,2,1,0:T(8,128)} %get-tuple-element.23) | copy-start | bytes 6291460
  141.1 3.3 %copy-start.8 = (f32[4,2,512,128]{3,2,1,0:T(8,128)S(1)}, f32[4,2,512,128]{3,2,1,0:T(8,128)}, u32[]{:S(2)}) copy-start(f32[4,2,512,128]{3,2,1,0:T(8,128)} %get-tuple-element.22) | copy-start | bytes 6291460
  141.1 65.0 %collective-permute-start.13 = (f32[4,2,512,128]{3,2,0,1:T(8,128)S(1)}, f32[4,2,512,128]{3,2,0,1:T(8,128)S(1)}, u32[]{:S(2)}, u32[]{:S(2)}) collective-permute-start(f32[4,2,512,128]{3,2,0,1:T(8,128)S(1)} %maximum_select_fusion), channel_id=1, source_target_pairs={{4,0},{12,8},{20,16},{28,24},{0,4},{8,12},{16,20},{24,28},{5,1},{1... | collective-permute-start | bytes 6291464 | tf_op jit(solution)/shard_map/ppermute | solution.py:244
  144.4 1.2 copy-start.11
  145.8 13.9 %copy-start.12 = (bf16[2,512,128]{2,1,0:T(8,128)(2,1)S(1)}, bf16[2,512,128]{2,1,0:T(8,128)(2,1)}, u32[]{:S(2)}) copy-start(bf16[2,512,128]{2,1,0:T(8,128)(2,1)} %get-tuple-element.50) | copy-start | bytes 786436
  145.8 13.9 %collective-permute-start.7 = (bf16[4,512,128]{2,1,0:T(8,128)(2,1)S(1)}, bf16[4,512,128]{2,1,0:T(8,128)(2,1)S(1)}, u32[]{:S(2)}, u32[]{:S(2)}) collective-permute-start(bf16[4,512,128]{2,1,0:T(8,128)(2,1)S(1)} %get-tuple-element.40), channel_id=1, source_target_pairs={{0,24},{8,0},{16,8},{24,16},{4,28},{12,4},{20,12},{28,20},{1,25},{... | collective-permute-start | bytes 1572872 | tf_op jit(solution)/shard_map/ppermute | solution.py:176
  147.6 55.2 %collective-permute-start.8 = (bf16[4,512,128]{2,1,0:T(8,128)(2,1)S(1)}, bf16[4,512,128]{2,1,0:T(8,128)(2,1)S(1)}, u32[]{:S(2)}, u32[]{:S(2)}) collective-permute-start(bf16[4,512,128]{2,1,0:T(8,128)(2,1)S(1)} %get-tuple-element.41), channel_id=1, source_target_pairs={{0,16},{8,24},{16,0},{24,8},{4,20},{12,28},{20,4},{28,12},{1,17},{... | collective-permute-start | bytes 1572872 | tf_op jit(solution)/shard_map/ppermute | solution.py:176
  148.3 57.8 %copy-start.6 = (f32[4,2,512,128]{3,2,1,0:T(8,128)S(1)}, f32[4,2,512,128]{3,2,1,0:T(8,128)}, u32[]{:S(2)}) copy-start(f32[4,2,512,128]{3,2,1,0:T(8,128)} %get-tuple-element.27) | copy-start | bytes 6291460
  148.4 54.4 %collective-permute-start.9 = (bf16[4,512,128]{2,1,0:T(8,128)(2,1)S(1)}, bf16[4,512,128]{2,1,0:T(8,128)(2,1)S(1)}, u32[]{:S(2)}, u32[]{:S(2)}) collective-permute-start(bf16[4,512,128]{2,1,0:T(8,128)(2,1)S(1)} %get-tuple-element.38), channel_id=1, source_target_pairs={{0,8},{8,16},{16,24},{24,0},{4,12},{12,20},{20,28},{28,4},{1,9},{9... | collective-permute-start | bytes 1572872 | tf_op jit(solution)/shard_map/ppermute | solution.py:176
  159.6 46.5 %collective-permute-start.11 = (bf16[2,512,128]{2,1,0:T(8,128)(2,1)S(1)}, bf16[2,512,128]{2,1,0:T(8,128)(2,1)S(1)}, u32[]{:S(2)}, u32[]{:S(2)}) collective-permute-start(bf16[2,512,128]{2,1,0:T(8,128)(2,1)S(1)} %copy-done.12), channel_id=1, source_target_pairs={{0,16},{8,24},{16,0},{24,8},{4,20},{12,28},{20,4},{28,12},{1,17},{... | collective-permute-start | bytes 786440 | tf_op jit(solution)/shard_map/ppermute | solution.py:176
  202.7 10.0 %collective-permute-start.12 = (bf16[2,512,128]{2,1,0:T(8,128)(2,1)S(1)}, bf16[2,512,128]{2,1,0:T(8,128)(2,1)S(1)}, u32[]{:S(2)}, u32[]{:S(2)}) collective-permute-start(bf16[2,512,128]{2,1,0:T(8,128)(2,1)S(1)} %get-tuple-element.49), channel_id=1, source_target_pairs={{0,8},{8,16},{16,24},{24,0},{4,12},{12,20},{20,28},{28,4},{1,9},{9... | collective-permute-start | bytes 786440 | tf_op jit(solution)/shard_map/ppermute | solution.py:176
  206.5 9.0 %collective-permute-start.14 = (bf16[2,512,128]{2,1,0:T(8,128)(2,1)S(1)}, bf16[2,512,128]{2,1,0:T(8,128)(2,1)S(1)}, u32[]{:S(2)}, u32[]{:S(2)}) collective-permute-start(bf16[2,512,128]{2,1,0:T(8,128)(2,1)S(1)} %get-tuple-element.46), channel_id=1, source_target_pairs={{0,24},{8,0},{16,8},{24,16},{4,28},{12,4},{20,12},{28,20},{1,25},{... | collective-permute-start | bytes 786440 | tf_op jit(solution)/shard_map/ppermute | solution.py:176
  214.9 16.1 %collective-permute-start.15 = (bf16[2,512,128]{2,1,0:T(8,128)(2,1)S(1)}, bf16[2,512,128]{2,1,0:T(8,128)(2,1)S(1)}, u32[]{:S(2)}, u32[]{:S(2)}) collective-permute-start(bf16[2,512,128]{2,1,0:T(8,128)(2,1)S(1)} %get-tuple-element.45), channel_id=1, source_target_pairs={{0,16},{8,24},{16,0},{24,8},{4,20},{12,28},{20,4},{28,12},{1,17},{... | collective-permute-start | bytes 786440 | tf_op jit(solution)/shard_map/ppermute | solution.py:176
  215.5 15.6 %collective-permute-start.16 = (bf16[2,512,128]{2,1,0:T(8,128)(2,1)S(1)}, bf16[2,512,128]{2,1,0:T(8,128)(2,1)S(1)}, u32[]{:S(2)}, u32[]{:S(2)}) collective-permute-start(bf16[2,512,128]{2,1,0:T(8,128)(2,1)S(1)} %get-tuple-element.44), channel_id=1, source_target_pairs={{0,8},{8,16},{16,24},{24,0},{4,12},{12,20},{20,28},{28,4},{1,9},{9... | collective-permute-start | bytes 786440 | tf_op jit(solution)/shard_map/ppermute | solution.py:176
  215.5 17.7 %copy-start.1 = (s32[4,2,8]{2,1,0:T(2,128)S(1)}, s32[4,2,8]{2,1,0:T(2,128)}, u32[]{:S(2)}) copy-start(s32[4,2,8]{2,1,0:T(2,128)} %param.9) | copy-start | bytes 772

commit v14 on v13

--- a/solution.py
+++ b/solution.py
@@ -241,15 +241,14 @@
     ret = win_even
     ret = jnp.where(segment == 0, jnp.roll(ret, -1, axis=0), ret)
     back_pairs = [(b, a) for a, b in next_segment_pairs(nseg, group)]
-    window_back = lax.ppermute(ret, "seq", back_pairs)
+    window_back = lax.ppermute(ret.astype(jnp.bfloat16), "seq", back_pairs)
+    sent_even = scatter_group(ad_even, within, nseg, group)
 
     partner_even = par_all[0]
     partner_odd = par_all[1]
     grads_even = (own_even + win_odd + partner_even).astype(jnp.bfloat16)
-    sent_even = scatter_group(jnp.concatenate([ad_even, grads_even], axis=1), within, nseg, group)
-    grads_even, own_odd, partner_odd = lax.optimization_barrier((grads_even, own_odd, partner_odd))
-    grads_odd = (own_odd + window_back + partner_odd).astype(jnp.bfloat16)
-    sent_last = scatter_group(grads_odd, within, nseg, group)
+    grads_odd = (own_odd + window_back.astype(jnp.float32) + partner_odd).astype(jnp.bfloat16)
+    sent_last = scatter_group(jnp.concatenate([grads_even, grads_odd], axis=1), within, nseg, group)
 
     shape = (heads, row_count, width)
 
@@ -261,8 +260,8 @@
     return (
         assemble(column(sent_even, 0), column(sent_odd, 0), heads, shape),
         assemble(column(sent_even, 1), column(sent_odd, 1), heads, shape),
-        assemble(column(sent_even, 2), column(sent_last, 0), heads, shape),
-        assemble(column(sent_even, 3), column(sent_last, 1), heads, shape),
+        assemble(column(sent_last, 0), column(sent_last, 2), heads, shape),
+        assemble(column(sent_last, 1), column(sent_last, 3), heads, shape),
     )
 
 

time: 234 us -> 233 us (level)
  waiting for transfers between devices: 92.3 us -> 109 us
  starting transfers between devices: 62.9 us -> 48.8 us
  local copies, waits for them, and re-layouts: 35.5 us -> 31.6 us
    ppermute x1, waiting for transfers between devices: 0.01 us -> 17.1 us  [body(): window_back = lax.ppermute(ret.astype(jnp.bfloat16), 'seq', back_pairs)]
    ppermute x9, starting transfers between devices: 34.8 us -> 20.9 us  [scatter_group(): lax.ppermute(pick(y, (within - shift) % group), 'seq', group_pairs(nseg,...]
    unnamed x27 -> x25, local copies, waits for them, and re-layouts: 9.46 us -> 3.65 us
    dynamic_update_slice x19 -> x22, local copies, waits for them, and re-layouts: 6.71 us -> 8.68 us  [assemble(): lax.dynamic_update_slice(out, piece[None, None], (head, jnp.int32(column)...]
  transfers between devices with their start and end apart: 17 -> 17, of which waited for: 7 -> 8; matrix products, arithmetic and copies ran while one was open for 9% -> 10% of each run, Pallas kernels for 17% -> 17%
where the time goes in v14:
time: 233 us; the launch traced here: 232 us
  waiting for transfers between devices  109 us (47%)
  starting transfers between devices  48.8 us (21%)
  Pallas kernels  38.7 us (17%)
  local copies, waits for them, and re-layouts  31.6 us (14%)
  other arithmetic  2.9 us (1%)
    ppermute x6, waiting for transfers between devices, gather_group(): lax.ppermute(pick(x, (within + shift) % group), 'seq', group_pairs(nseg,...  46 us
    ppermute x9, waiting for transfers between devices, scatter_group(): lax.ppermute(pick(y, (within - shift) % group), 'seq', group_pairs(nseg,...  45.8 us
    pallas_call x2, Pallas kernels, fused_terms(): pl.pallas_call(attention_kernel, grid_spec=pltpu.PrefetchScalarGridSpec(n...  38.7 us
    ppermute x6, starting transfers between devices, gather_group(): lax.ppermute(pick(x, (within + shift) % group), 'seq', group_pairs(nseg,...  25.9 us
    ppermute x9, starting transfers between devices, scatter_group(): lax.ppermute(pick(y, (within - shift) % group), 'seq', group_pairs(nseg,...  20.9 us
    ppermute x1, waiting for transfers between devices, body(): window_back = lax.ppermute(ret.astype(jnp.bfloat16), 'seq', back_pairs)  17.1 us
    dynamic_update_slice x22, local copies, waits for them, and re-layouts, assemble(): lax.dynamic_update_slice(out, piece[None, None], (head, jnp.int32(column)...  8.68 us
    dynamic_update_slice x6, local copies, waits for them, and re-layouts, place(): lax.dynamic_update_index_in_dim(out, piece, (within - shift) % group, 0)  6.67 us
  transfers between devices with their start and end apart: 17, of which 8 were waited for; matrix products, arithmetic and copies ran while one was open for 10% of the time, Pallas kernels for 17%

profile of v14, /device:TPU:0, one launch (start us, length us, event | category | flops | bytes accessed | tf_op | source)
XLA Modules:
  0.0 232.1 jit_solution(16441163556609725354)
XLA Ops:
  0.8 2.7 %slice_bitcast_fusion.6 = (bf16[4,1,512,128]{3,2,0,1:T(8,128)(2,1)}, bf16[4,1,512,128]{3,2,0,1:T(8,128)(2,1)S(1)}, bf16[4,1,512,128]{3,2,0,1:T(8,128)(2,1)S(1)}, bf16[4,1,512,128]{3,2,0,1:T(8,128)(2,1)}) fusion(bf16[4,2,512,128]{3,2,1,0:T(8,128)(2,1)} %bitcast.233, bf16[4,2,512,128]{3,2,1,0:T(8,128)(2,1)} %bitcast.234), kind=kLoop, calls=%fused_computation.45 | loop fusion | bytes 4194304
  4.5 1.5 dynamic-slice_bitcast_fusion
  5.9 3.0 %collective-permute-start = (bf16[6,512,128]{2,1,0:T(8,128)(2,1)}, bf16[6,512,128]{2,1,0:T(8,128)(2,1)}, u32[]{:S(2)}, u32[]{:S(2)}) collective-permute-start(bf16[6,512,128]{2,1,0:T(8,128)(2,1)} %get-tuple-element.34), channel_id=1, source_target_pairs={{0,8},{8,16},{16,24},{24,0},{4,12},{12,20},{20,28},{28,4},{1,9},{9... | collective-permute-start | bytes 2359304 | tf_op jit(solution)/shard_map/ppermute | solution.py:161
  8.9 2.6 %collective-permute-start.1 = (bf16[6,512,128]{2,1,0:T(8,128)(2,1)}, bf16[6,512,128]{2,1,0:T(8,128)(2,1)}, u32[]{:S(2)}, u32[]{:S(2)}) collective-permute-start(bf16[6,512,128]{2,1,0:T(8,128)(2,1)} %get-tuple-element.33), channel_id=1, source_target_pairs={{0,16},{8,24},{16,0},{24,8},{4,20},{12,28},{20,4},{28,12},{1,17},{... | collective-permute-start | bytes 2359304 | tf_op jit(solution)/shard_map/ppermute | solution.py:161
  11.5 1.3 collective-permute-start.2
  14.2 1.3 pad_maximum_fusion.2
  15.5 14.3 %collective-permute-done = bf16[6,512,128]{2,1,0:T(8,128)(2,1)} collective-permute-done((bf16[6,512,128]{2,1,0:T(8,128)(2,1)}, bf16[6,512,128]{2,1,0:T(8,128)(2,1)}, u32[]{:S(2)}, u32[]{:S(2)}) %collective-permute-start) | collective-permute-done | bytes 786464 | tf_op jit(solution)/shard_map/ppermute | solution.py:161
  29.8 1.2 bitcast_dynamic-update-slice_fusion.2
  31.0 31.6 %collective-permute-done.1 = bf16[6,512,128]{2,1,0:T(8,128)(2,1)} collective-permute-done((bf16[6,512,128]{2,1,0:T(8,128)(2,1)}, bf16[6,512,128]{2,1,0:T(8,128)(2,1)}, u32[]{:S(2)}, u32[]{:S(2)}) %collective-permute-start.1) | collective-permute-done | bytes 786464 | tf_op jit(solution)/shard_map/ppermute | solution.py:161
  62.7 1.2 bitcast_dynamic-update-slice_fusion.1
  63.9 1.2 bitcast_dynamic-update-slice_fusion
  65.3 1.0 slice_bitcast_fusion.8
  67.7 1.5 collective-permute-start.6
  70.3 16.1 %collective-permute-start.3 = (bf16[2,512,128]{2,1,0:T(8,128)(2,1)}, bf16[2,512,128]{2,1,0:T(8,128)(2,1)}, u32[]{:S(2)}, u32[]{:S(2)}) collective-permute-start(bf16[2,512,128]{2,1,0:T(8,128)(2,1)} %get-tuple-element.54), channel_id=1, source_target_pairs={{0,8},{8,16},{16,24},{24,0},{4,12},{12,20},{20,28},{28,4},{1,9},{9... | collective-permute-start | bytes 786440 | tf_op jit(solution)/shard_map/ppermute | solution.py:161
  86.4 2.8 %collective-permute-start.4 = (bf16[2,512,128]{2,1,0:T(8,128)(2,1)}, bf16[2,512,128]{2,1,0:T(8,128)(2,1)}, u32[]{:S(2)}, u32[]{:S(2)}) collective-permute-start(bf16[2,512,128]{2,1,0:T(8,128)(2,1)} %get-tuple-element.53), channel_id=1, source_target_pairs={{0,16},{8,24},{16,0},{24,8},{4,20},{12,28},{20,4},{28,12},{1,17},{... | collective-permute-start | bytes 786440 | tf_op jit(solution)/shard_map/ppermute | solution.py:161
  89.3 19.4 %shard_map.84 = (bf16[4,2,512,128]{3,2,1,0:T(8,128)(2,1)}, f32[4,2,512,128]{3,2,1,0:T(8,128)}, f32[4,2,512,128]{3,2,1,0:T(8,128)}, f32[2,4,2,512,128]{4,3,2,1,0:T(8,128)}) custom-call(s32[4]{0:T(128)} %slice.191.index_ref, s32[1]{0:T(128)} %constant.222.clone.1.flag_ref, bf16[4,512,128]{2,1,0:T(8,128)(2,1)} %get-tuple-element.16.q_ref, ...), custom_call_target="tpu_custom_call" | custom-call | flops 4831838208 | bytes 15728640 | tf_op jit(solution)/shard_map/pallas_call | solution.py:130
  108.6 2.0 dynamic-slice_bitcast_fusion.3
  110.6 1.6 collective-permute-start.10
  112.2 1.9 collective-permute-start.11
  117.3 1.1 slice_bitcast_fusion.4
  119.4 19.3 %shard_map.85 = (bf16[4,2,512,128]{3,2,1,0:T(8,128)(2,1)}, f32[4,2,512,128]{3,2,1,0:T(8,128)}, f32[4,2,512,128]{3,2,1,0:T(8,128)}, f32[2,4,2,512,128]{4,3,2,1,0:T(8,128)}) custom-call(s32[4]{0:T(128)} %slice.174.index_ref, s32[1]{0:T(128)} %bitcast.1.flag_ref, bf16[4,512,128]{2,1,0:T(8,128)(2,1)} %get-tuple-element.51.q_ref, ...), custom_call_target="tpu_custom_call", output_to_operand_aliasing={{3}: (10, {})} | custom-call | flops 4831838208 | bytes 15728640 | tf_op jit(solution)/shard_map/pallas_call | solution.py:130
  138.7 1.9 copy.58
  140.8 3.8 %collective-permute-start.7 = (bf16[2,512,128]{2,1,0:T(8,128)(2,1)S(1)}, bf16[2,512,128]{2,1,0:T(8,128)(2,1)S(1)}, u32[]{:S(2)}, u32[]{:S(2)}) collective-permute-start(bf16[2,512,128]{2,1,0:T(8,128)(2,1)S(1)} %get-tuple-element.47), channel_id=1, source_target_pairs={{0,24},{8,0},{16,8},{24,16},{4,28},{12,4},{20,12},{28,20},{1,25},{... | collective-permute-start | bytes 786440 | tf_op jit(solution)/shard_map/ppermute | solution.py:176
  145.2 6.2 %collective-permute-done.7 = bf16[2,512,128]{2,1,0:T(8,128)(2,1)S(1)} collective-permute-done((bf16[2,512,128]{2,1,0:T(8,128)(2,1)S(1)}, bf16[2,512,128]{2,1,0:T(8,128)(2,1)S(1)}, u32[]{:S(2)}, u32[]{:S(2)}) %collective-permute-start.7) | collective-permute-done | bytes 262176 | tf_op jit(solution)/shard_map/ppermute | solution.py:176
  151.4 11.3 %collective-permute-start.9 = (bf16[2,512,128]{2,1,0:T(8,128)(2,1)S(1)}, bf16[2,512,128]{2,1,0:T(8,128)(2,1)S(1)}, u32[]{:S(2)}, u32[]{:S(2)}) collective-permute-start(bf16[2,512,128]{2,1,0:T(8,128)(2,1)S(1)} %get-tuple-element.45), channel_id=1, source_target_pairs={{0,8},{8,16},{16,24},{24,0},{4,12},{12,20},{20,28},{28,4},{1,9},{9... | collective-permute-start | bytes 786440 | tf_op jit(solution)/shard_map/ppermute | solution.py:176
  162.7 2.2 collective-permute-done.8
  165.5 1.1 collective-permute-done.9
  169.7 17.1 %collective-permute-done.13 = bf16[4,2,512,128]{3,2,0,1:T(8,128)(2,1)S(1)} collective-permute-done((bf16[4,2,512,128]{3,2,0,1:T(8,128)(2,1)S(1)}, bf16[4,2,512,128]{3,2,0,1:T(8,128)(2,1)S(1)}, u32[]{:S(2)}, u32[]{:S(2)}) %collective-permute-start.13) | collective-permute-done | bytes 1048608 | tf_op jit(solution)/shard_map/ppermute | solution.py:244
  191.0 2.0 collective-permute-start.16
  193.3 7.0 %collective-permute-done.14 = bf16[4,512,128]{2,1,0:T(8,128)(2,1)S(1)} collective-permute-done((bf16[4,512,128]{2,1,0:T(8,128)(2,1)S(1)}, bf16[4,512,128]{2,1,0:T(8,128)(2,1)S(1)}, u32[]{:S(2)}, u32[]{:S(2)}) %collective-permute-start.14) | collective-permute-done | bytes 524320 | tf_op jit(solution)/shard_map/ppermute | solution.py:176
  200.4 29.3 %collective-permute-done.15 = bf16[4,512,128]{2,1,0:T(8,128)(2,1)S(1)} collective-permute-done((bf16[4,512,128]{2,1,0:T(8,128)(2,1)S(1)}, bf16[4,512,128]{2,1,0:T(8,128)(2,1)S(1)}, u32[]{:S(2)}, u32[]{:S(2)}) %collective-permute-start.15) | collective-permute-done | bytes 524320 | tf_op jit(solution)/shard_map/ppermute | solution.py:176
  230.0 1.0 copy.69
  (89 shorter events, 19.1 us)
Async XLA Ops:
  0.6 12.3 %copy-start = (s32[4,2,8]{2,1,0:T(2,128)S(1)}, s32[4,2,8]{2,1,0:T(2,128)}, u32[]{:S(2)}) copy-start(s32[4,2,8]{2,1,0:T(2,128)} %param.9) | copy-start | bytes 772
  0.6 2.9 %copy-start.10 = (bf16[4,1024,128]{2,1,0:T(8,128)(2,1)S(1)}, bf16[4,1024,128]{2,1,0:T(8,128)(2,1)}, u32[]{:S(2)}) copy-start(bf16[4,1024,128]{2,1,0:T(8,128)(2,1)} %param.6) | copy-start | bytes 3145732
  0.7 2.9 %copy-start.11 = (bf16[4,1024,128]{2,1,0:T(8,128)(2,1)S(1)}, bf16[4,1024,128]{2,1,0:T(8,128)(2,1)}, u32[]{:S(2)}) copy-start(bf16[4,1024,128]{2,1,0:T(8,128)(2,1)} %param.7) | copy-start | bytes 3145732
  5.9 23.9 %collective-permute-start = (bf16[6,512,128]{2,1,0:T(8,128)(2,1)}, bf16[6,512,128]{2,1,0:T(8,128)(2,1)}, u32[]{:S(2)}, u32[]{:S(2)}) collective-permute-start(bf16[6,512,128]{2,1,0:T(8,128)(2,1)} %get-tuple-element.34), channel_id=1, source_target_pairs={{0,8},{8,16},{16,24},{24,0},{4,12},{12,20},{20,28},{28,4},{1,9},{9... | collective-permute-start | bytes 2359304 | tf_op jit(solution)/shard_map/ppermute | solution.py:161
  8.9 53.7 %collective-permute-start.1 = (bf16[6,512,128]{2,1,0:T(8,128)(2,1)}, bf16[6,512,128]{2,1,0:T(8,128)(2,1)}, u32[]{:S(2)}, u32[]{:S(2)}) collective-permute-start(bf16[6,512,128]{2,1,0:T(8,128)(2,1)} %get-tuple-element.33), channel_id=1, source_target_pairs={{0,16},{8,24},{16,0},{24,8},{4,20},{12,28},{20,4},{28,12},{1,17},{... | collective-permute-start | bytes 2359304 | tf_op jit(solution)/shard_map/ppermute | solution.py:161
  11.5 52.4 %collective-permute-start.2 = (bf16[6,512,128]{2,1,0:T(8,128)(2,1)}, bf16[6,512,128]{2,1,0:T(8,128)(2,1)}, u32[]{:S(2)}, u32[]{:S(2)}) collective-permute-start(bf16[6,512,128]{2,1,0:T(8,128)(2,1)} %get-tuple-element.32), channel_id=1, source_target_pairs={{0,24},{8,0},{16,8},{24,16},{4,28},{12,4},{20,12},{28,20},{1,25},{... | collective-permute-start | bytes 2359304 | tf_op jit(solution)/shard_map/ppermute | solution.py:161
  66.4 1.0 copy-start.4
  66.5 1.2 copy-start.5
  67.7 50.6 %collective-permute-start.6 = (bf16[4,2,512,128]{3,2,0,1:T(8,128)(2,1)S(1)}, bf16[4,2,512,128]{3,2,0,1:T(8,128)(2,1)S(1)}, u32[]{:S(2)}, u32[]{:S(2)}) collective-permute-start(bf16[4,2,512,128]{3,2,0,1:T(8,128)(2,1)S(1)} %fusion.5), channel_id=1, source_target_pairs={{0,4},{8,12},{16,20},{24,28},{4,0},{12,8},{20,16},{28,24},{1,5},{9... | collective-permute-start | bytes 3145736 | tf_op jit(solution)/shard_map/ppermute | solution.py:222
  70.3 41.8 %collective-permute-start.3 = (bf16[2,512,128]{2,1,0:T(8,128)(2,1)}, bf16[2,512,128]{2,1,0:T(8,128)(2,1)}, u32[]{:S(2)}, u32[]{:S(2)}) collective-permute-start(bf16[2,512,128]{2,1,0:T(8,128)(2,1)} %get-tuple-element.54), channel_id=1, source_target_pairs={{0,8},{8,16},{16,24},{24,0},{4,12},{12,20},{20,28},{28,4},{1,9},{9... | collective-permute-start | bytes 786440 | tf_op jit(solution)/shard_map/ppermute | solution.py:161
  86.4 28.6 %collective-permute-start.4 = (bf16[2,512,128]{2,1,0:T(8,128)(2,1)}, bf16[2,512,128]{2,1,0:T(8,128)(2,1)}, u32[]{:S(2)}, u32[]{:S(2)}) collective-permute-start(bf16[2,512,128]{2,1,0:T(8,128)(2,1)} %get-tuple-element.53), channel_id=1, source_target_pairs={{0,16},{8,24},{16,0},{24,8},{4,20},{12,28},{20,4},{28,12},{1,17},{... | collective-permute-start | bytes 786440 | tf_op jit(solution)/shard_map/ppermute | solution.py:161
  89.2 27.1 %collective-permute-start.5 = (bf16[2,512,128]{2,1,0:T(8,128)(2,1)}, bf16[2,512,128]{2,1,0:T(8,128)(2,1)}, u32[]{:S(2)}, u32[]{:S(2)}) collective-permute-start(bf16[2,512,128]{2,1,0:T(8,128)(2,1)} %get-tuple-element.52), channel_id=1, source_target_pairs={{0,24},{8,0},{16,8},{24,16},{4,28},{12,4},{20,12},{28,20},{1,25},{... | collective-permute-start | bytes 786440 | tf_op jit(solution)/shard_map/ppermute | solution.py:161
  110.6 57.1 %collective-permute-start.10 = (bf16[2,512,128]{2,1,0:T(8,128)(2,1)}, bf16[2,512,128]{2,1,0:T(8,128)(2,1)}, u32[]{:S(2)}, u32[]{:S(2)}) collective-permute-start(bf16[2,512,128]{2,1,0:T(8,128)(2,1)} %get-tuple-element.44), channel_id=1, source_target_pairs={{0,24},{8,0},{16,8},{24,16},{4,28},{12,4},{20,12},{28,20},{1,25},{... | collective-permute-start | bytes 786440 | tf_op jit(solution)/shard_map/ppermute | solution.py:176
  112.2 56.5 %collective-permute-start.11 = (bf16[2,512,128]{2,1,0:T(8,128)(2,1)}, bf16[2,512,128]{2,1,0:T(8,128)(2,1)}, u32[]{:S(2)}, u32[]{:S(2)}) collective-permute-start(bf16[2,512,128]{2,1,0:T(8,128)(2,1)} %get-tuple-element.43), channel_id=1, source_target_pairs={{0,16},{8,24},{16,0},{24,8},{4,20},{12,28},{20,4},{28,12},{1,17},{... | collective-permute-start | bytes 786440 | tf_op jit(solution)/shard_map/ppermute | solution.py:176
  115.1 72.8 %collective-permute-start.12 = (bf16[2,512,128]{2,1,0:T(8,128)(2,1)S(1)}, bf16[2,512,128]{2,1,0:T(8,128)(2,1)}, u32[]{:S(2)}, u32[]{:S(2)}) collective-permute-start(bf16[2,512,128]{2,1,0:T(8,128)(2,1)S(1)} %get-tuple-element.42), channel_id=1, source_target_pairs={{0,8},{8,16},{16,24},{24,0},{4,12},{12,20},{20,28},{28,4},{1,9},{9... | collective-permute-start | bytes 786440 | tf_op jit(solution)/shard_map/ppermute | solution.py:176
  138.7 2.0 copy-start.9
  138.7 6.0 %copy-start.2 = (f32[4,2,512,128]{3,2,1,0:T(8,128)S(1)}, f32[4,2,512,128]{3,2,1,0:T(8,128)}, u32[]{:S(2)}) copy-start(f32[4,2,512,128]{3,2,1,0:T(8,128)} %get-tuple-element.25) | copy-start | bytes 6291460
  140.7 46.1 %copy-start.8 = (f32[4,2,512,128]{3,2,1,0:T(8,128)S(1)}, f32[4,2,512,128]{3,2,1,0:T(8,128)}, u32[]{:S(2)}) copy-start(f32[4,2,512,128]{3,2,1,0:T(8,128)} %get-tuple-element.21) | copy-start | bytes 6291460
  140.8 10.6 %collective-permute-start.7 = (bf16[2,512,128]{2,1,0:T(8,128)(2,1)S(1)}, bf16[2,512,128]{2,1,0:T(8,128)(2,1)S(1)}, u32[]{:S(2)}, u32[]{:S(2)}) collective-permute-start(bf16[2,512,128]{2,1,0:T(8,128)(2,1)S(1)} %get-tuple-element.47), channel_id=1, source_target_pairs={{0,24},{8,0},{16,8},{24,16},{4,28},{12,4},{20,12},{28,20},{1,25},{... | collective-permute-start | bytes 786440 | tf_op jit(solution)/shard_map/ppermute | solution.py:176
  144.7 20.3 %collective-permute-start.8 = (bf16[2,512,128]{2,1,0:T(8,128)(2,1)S(1)}, bf16[2,512,128]{2,1,0:T(8,128)(2,1)S(1)}, u32[]{:S(2)}, u32[]{:S(2)}) collective-permute-start(bf16[2,512,128]{2,1,0:T(8,128)(2,1)S(1)} %get-tuple-element.46), channel_id=1, source_target_pairs={{0,16},{8,24},{16,0},{24,8},{4,20},{12,28},{20,4},{28,12},{1,17},{... | collective-permute-start | bytes 786440 | tf_op jit(solution)/shard_map/ppermute | solution.py:176
  144.7 42.2 %copy-start.6 = (f32[4,2,512,128]{3,2,1,0:T(8,128)S(1)}, f32[4,2,512,128]{3,2,1,0:T(8,128)}, u32[]{:S(2)}) copy-start(f32[4,2,512,128]{3,2,1,0:T(8,128)} %get-tuple-element.24) | copy-start | bytes 6291460
  144.7 42.2 %copy-start.7 = (f32[4,2,512,128]{3,2,1,0:T(8,128)S(1)}, f32[4,2,512,128]{3,2,1,0:T(8,128)}, u32[]{:S(2)}) copy-start(f32[4,2,512,128]{3,2,1,0:T(8,128)} %get-tuple-element.22) | copy-start | bytes 6291460
  144.8 42.0 %copy-start.3 = (f32[2,4,2,512,128]{4,3,2,1,0:T(8,128)S(1)}, f32[2,4,2,512,128]{4,3,2,1,0:T(8,128)}, u32[]{:S(2)}) copy-start(f32[2,4,2,512,128]{4,3,2,1,0:T(8,128)} %get-tuple-element.23) | copy-start | bytes 12582916
  151.4 15.2 %collective-permute-start.9 = (bf16[2,512,128]{2,1,0:T(8,128)(2,1)S(1)}, bf16[2,512,128]{2,1,0:T(8,128)(2,1)S(1)}, u32[]{:S(2)}, u32[]{:S(2)}) collective-permute-start(bf16[2,512,128]{2,1,0:T(8,128)(2,1)S(1)} %get-tuple-element.45), channel_id=1, source_target_pairs={{0,8},{8,16},{16,24},{24,0},{4,12},{12,20},{20,28},{28,4},{1,9},{9... | collective-permute-start | bytes 786440 | tf_op jit(solution)/shard_map/ppermute | solution.py:176
  165.0 21.9 %collective-permute-start.13 = (bf16[4,2,512,128]{3,2,0,1:T(8,128)(2,1)S(1)}, bf16[4,2,512,128]{3,2,0,1:T(8,128)(2,1)S(1)}, u32[]{:S(2)}, u32[]{:S(2)}) collective-permute-start(bf16[4,2,512,128]{3,2,0,1:T(8,128)(2,1)S(1)} %fusion.4), channel_id=1, source_target_pairs={{4,0},{12,8},{20,16},{28,24},{0,4},{8,12},{16,20},{24,28},{5,1},{1... | collective-permute-start | bytes 3145736 | tf_op jit(solution)/shard_map/ppermute | solution.py:244
  187.8 12.5 %collective-permute-start.14 = (bf16[4,512,128]{2,1,0:T(8,128)(2,1)S(1)}, bf16[4,512,128]{2,1,0:T(8,128)(2,1)S(1)}, u32[]{:S(2)}, u32[]{:S(2)}) collective-permute-start(bf16[4,512,128]{2,1,0:T(8,128)(2,1)S(1)} %get-tuple-element.38), channel_id=1, source_target_pairs={{0,24},{8,0},{16,8},{24,16},{4,28},{12,4},{20,12},{28,20},{1,25},{... | collective-permute-start | bytes 1572872 | tf_op jit(solution)/shard_map/ppermute | solution.py:176
  191.0 38.7 %collective-permute-start.15 = (bf16[4,512,128]{2,1,0:T(8,128)(2,1)S(1)}, bf16[4,512,128]{2,1,0:T(8,128)(2,1)S(1)}, u32[]{:S(2)}, u32[]{:S(2)}) collective-permute-start(bf16[4,512,128]{2,1,0:T(8,128)(2,1)S(1)} %get-tuple-element.39), channel_id=1, source_target_pairs={{0,16},{8,24},{16,0},{24,8},{4,20},{12,28},{20,4},{28,12},{1,17},{... | collective-permute-start | bytes 1572872 | tf_op jit(solution)/shard_map/ppermute | solution.py:176
  191.0 38.7 %collective-permute-start.16 = (bf16[4,512,128]{2,1,0:T(8,128)(2,1)S(1)}, bf16[4,512,128]{2,1,0:T(8,128)(2,1)S(1)}, u32[]{:S(2)}, u32[]{:S(2)}) collective-permute-start(bf16[4,512,128]{2,1,0:T(8,128)(2,1)S(1)} %get-tuple-element.36), channel_id=1, source_target_pairs={{0,8},{8,16},{16,24},{24,0},{4,12},{12,20},{20,28},{28,4},{1,9},{9... | collective-permute-start | bytes 1572872 | tf_op jit(solution)/shard_map/ppermute | solution.py:176
  229.8 2.3 copy-start.1

commit v15 on v14

--- a/solution.py
+++ b/solution.py
@@ -247,8 +247,10 @@
     partner_even = par_all[0]
     partner_odd = par_all[1]
     grads_even = (own_even + win_odd + partner_even).astype(jnp.bfloat16)
+    sent_grads = scatter_group(grads_even, within, nseg, group)
+    grads_even, own_odd, partner_odd = lax.optimization_barrier((grads_even, own_odd, partner_odd))
     grads_odd = (own_odd + window_back.astype(jnp.float32) + partner_odd).astype(jnp.bfloat16)
-    sent_last = scatter_group(jnp.concatenate([grads_even, grads_odd], axis=1), within, nseg, group)
+    sent_last = scatter_group(grads_odd, within, nseg, group)
 
     shape = (heads, row_count, width)
 
@@ -260,8 +262,8 @@
     return (
         assemble(column(sent_even, 0), column(sent_odd, 0), heads, shape),
         assemble(column(sent_even, 1), column(sent_odd, 1), heads, shape),
-        assemble(column(sent_last, 0), column(sent_last, 2), heads, shape),
-        assemble(column(sent_last, 1), column(sent_last, 3), heads, shape),
+        assemble(column(sent_grads, 0), column(sent_last, 0), heads, shape),
+        assemble(column(sent_grads, 1), column(sent_last, 1), heads, shape),
     )
 
 

time: 233 us -> 219 us (0.940)
  waiting for transfers between devices: 109 us -> 75.1 us
  starting transfers between devices: 48.8 us -> 67.5 us
    ppermute x9 -> x12, starting transfers between devices: 20.9 us -> 39.5 us  [scatter_group(): lax.ppermute(pick(y, (within - shift) % group), 'seq', group_pairs(nseg,...]
    ppermute x1, waiting for transfers between devices: 17.1 us -> 0.01 us  [body(): window_back = lax.ppermute(ret.astype(jnp.bfloat16), 'seq', back_pairs)]
    ppermute x9 -> x12, waiting for transfers between devices: 45.8 us -> 29.2 us  [scatter_group(): lax.ppermute(pick(y, (within - shift) % group), 'seq', group_pairs(nseg,...]
    unnamed x25 -> x31, local copies, waits for them, and re-layouts: 3.65 us -> 6.7 us
  transfers between devices with their start and end apart: 17 -> 20, of which waited for: 8 -> 7; matrix products, arithmetic and copies ran while one was open for 10% -> 10% of each run, Pallas kernels for 17% -> 18%
where the time goes in v15:
time: 219 us
  waiting for transfers between devices  75.1 us (34%)
  starting transfers between devices  67.5 us (31%)
  Pallas kernels  38.8 us (18%)
  local copies, waits for them, and re-layouts  33.3 us (15%)
  other arithmetic  2.63 us (1%)
    ppermute x6, waiting for transfers between devices, gather_group(): lax.ppermute(pick(x, (within + shift) % group), 'seq', group_pairs(nseg,...  46 us
    ppermute x12, starting transfers between devices, scatter_group(): lax.ppermute(pick(y, (within - shift) % group), 'seq', group_pairs(nseg,...  39.5 us
    pallas_call x2, Pallas kernels, fused_terms(): pl.pallas_call(attention_kernel, grid_spec=pltpu.PrefetchScalarGridSpec(n...  38.8 us
    ppermute x12, waiting for transfers between devices, scatter_group(): lax.ppermute(pick(y, (within - shift) % group), 'seq', group_pairs(nseg,...  29.2 us
    ppermute x6, starting transfers between devices, gather_group(): lax.ppermute(pick(x, (within + shift) % group), 'seq', group_pairs(nseg,...  25.9 us
    dynamic_update_slice x22, local copies, waits for them, and re-layouts, assemble(): lax.dynamic_update_slice(out, piece[None, None], (head, jnp.int32(column)...  6.72 us
    unnamed x31, local copies, waits for them, and re-layouts  6.7 us
    dynamic_update_slice x6, local copies, waits for them, and re-layouts, place(): lax.dynamic_update_index_in_dim(out, piece, (within - shift) % group, 0)  6.67 us
  transfers between devices with their start and end apart: 20, of which 7 were waited for; matrix products, arithmetic and copies ran while one was open for 10% of the time, Pallas kernels for 18%

profile of v15, /device:TPU:0, one launch (start us, length us, event | category | flops | bytes accessed | tf_op | source)
XLA Modules:
  0.0 218.5 jit_solution(9748447745223861037)
XLA Ops:
  0.8 2.8 %slice_bitcast_fusion.6 = (bf16[4,1,512,128]{3,2,0,1:T(8,128)(2,1)}, bf16[4,1,512,128]{3,2,0,1:T(8,128)(2,1)S(1)}, bf16[4,1,512,128]{3,2,0,1:T(8,128)(2,1)S(1)}, bf16[4,1,512,128]{3,2,0,1:T(8,128)(2,1)}) fusion(bf16[4,2,512,128]{3,2,1,0:T(8,128)(2,1)} %bitcast.229, bf16[4,2,512,128]{3,2,1,0:T(8,128)(2,1)} %bitcast.230), kind=kLoop, calls=%fused_computation.30 | loop fusion | bytes 4194304
  4.5 1.5 dynamic-slice_bitcast_fusion
  6.0 3.0 %collective-permute-start = (bf16[6,512,128]{2,1,0:T(8,128)(2,1)}, bf16[6,512,128]{2,1,0:T(8,128)(2,1)}, u32[]{:S(2)}, u32[]{:S(2)}) collective-permute-start(bf16[6,512,128]{2,1,0:T(8,128)(2,1)} %get-tuple-element.36), channel_id=1, source_target_pairs={{0,8},{8,16},{16,24},{24,0},{4,12},{12,20},{20,28},{28,4},{1,9},{9... | collective-permute-start | bytes 2359304 | tf_op jit(solution)/shard_map/ppermute | solution.py:161
  9.0 2.6 %collective-permute-start.1 = (bf16[6,512,128]{2,1,0:T(8,128)(2,1)}, bf16[6,512,128]{2,1,0:T(8,128)(2,1)}, u32[]{:S(2)}, u32[]{:S(2)}) collective-permute-start(bf16[6,512,128]{2,1,0:T(8,128)(2,1)} %get-tuple-element.35), channel_id=1, source_target_pairs={{0,16},{8,24},{16,0},{24,8},{4,20},{12,28},{20,4},{28,12},{1,17},{... | collective-permute-start | bytes 2359304 | tf_op jit(solution)/shard_map/ppermute | solution.py:161
  11.6 1.3 collective-permute-start.2
  14.2 1.3 pad_maximum_fusion.2
  15.5 14.3 %collective-permute-done = bf16[6,512,128]{2,1,0:T(8,128)(2,1)} collective-permute-done((bf16[6,512,128]{2,1,0:T(8,128)(2,1)}, bf16[6,512,128]{2,1,0:T(8,128)(2,1)}, u32[]{:S(2)}, u32[]{:S(2)}) %collective-permute-start) | collective-permute-done | bytes 786464 | tf_op jit(solution)/shard_map/ppermute | solution.py:161
  29.8 1.2 bitcast_dynamic-update-slice_fusion.2
  31.1 31.6 %collective-permute-done.1 = bf16[6,512,128]{2,1,0:T(8,128)(2,1)} collective-permute-done((bf16[6,512,128]{2,1,0:T(8,128)(2,1)}, bf16[6,512,128]{2,1,0:T(8,128)(2,1)}, u32[]{:S(2)}, u32[]{:S(2)}) %collective-permute-start.1) | collective-permute-done | bytes 786464 | tf_op jit(solution)/shard_map/ppermute | solution.py:161
  62.7 1.2 bitcast_dynamic-update-slice_fusion.1
  64.0 1.2 bitcast_dynamic-update-slice_fusion
  67.9 1.5 collective-permute-start.6
  70.4 16.1 %collective-permute-start.3 = (bf16[2,512,128]{2,1,0:T(8,128)(2,1)}, bf16[2,512,128]{2,1,0:T(8,128)(2,1)S(1)}, u32[]{:S(2)}, u32[]{:S(2)}) collective-permute-start(bf16[2,512,128]{2,1,0:T(8,128)(2,1)} %get-tuple-element.60), channel_id=1, source_target_pairs={{0,8},{8,16},{16,24},{24,0},{4,12},{12,20},{20,28},{28,4},{1,9},{9... | collective-permute-start | bytes 786440 | tf_op jit(solution)/shard_map/ppermute | solution.py:161
  86.5 2.8 %collective-permute-start.4 = (bf16[2,512,128]{2,1,0:T(8,128)(2,1)}, bf16[2,512,128]{2,1,0:T(8,128)(2,1)S(1)}, u32[]{:S(2)}, u32[]{:S(2)}) collective-permute-start(bf16[2,512,128]{2,1,0:T(8,128)(2,1)} %get-tuple-element.59), channel_id=1, source_target_pairs={{0,16},{8,24},{16,0},{24,8},{4,20},{12,28},{20,4},{28,12},{1,17},{... | collective-permute-start | bytes 786440 | tf_op jit(solution)/shard_map/ppermute | solution.py:161
  89.3 19.4 %shard_map.84 = (bf16[4,2,512,128]{3,2,1,0:T(8,128)(2,1)}, f32[4,2,512,128]{3,2,1,0:T(8,128)}, f32[4,2,512,128]{3,2,1,0:T(8,128)}, f32[2,4,2,512,128]{4,3,2,1,0:T(8,128)}) custom-call(s32[4]{0:T(128)} %slice.191.index_ref, s32[1]{0:T(128)} %constant.242.clone.1.flag_ref, bf16[4,512,128]{2,1,0:T(8,128)(2,1)} %get-tuple-element.18.q_ref, ...), custom_call_target="tpu_custom_call" | custom-call | flops 4831838208 | bytes 15728640 | tf_op jit(solution)/shard_map/pallas_call | solution.py:130
  108.7 1.2 dynamic-slice_bitcast_fusion.9
  109.9 1.6 collective-permute-start.10
  112.2 1.9 collective-permute-start.11
  118.9 2.3 %slice_bitcast_fusion.2 = (bf16[4,512,128]{2,1,0:T(8,128)(2,1)}, bf16[4,512,128]{2,1,0:T(8,128)(2,1)}) fusion(bf16[4,2,512,128]{3,2,0,1:T(8,128)(2,1)} %collective-permute-done.6), kind=kLoop, calls=%fused_computation.26 | loop fusion | bytes 2097152 | tf_op jit(solution)/shard_map/squeeze | solution.py:238
  121.1 19.4 %shard_map.85 = (bf16[4,2,512,128]{3,2,1,0:T(8,128)(2,1)}, f32[4,2,512,128]{3,2,1,0:T(8,128)}, f32[4,2,512,128]{3,2,1,0:T(8,128)}, f32[2,4,2,512,128]{4,3,2,1,0:T(8,128)}) custom-call(s32[4]{0:T(128)} %slice.174.index_ref, s32[1]{0:T(128)} %bitcast.1.flag_ref, bf16[4,512,128]{2,1,0:T(8,128)(2,1)} %get-tuple-element.57.q_ref, ...), custom_call_target="tpu_custom_call", output_to_operand_aliasing={{3}: (10, {})} | custom-call | flops 4831838208 | bytes 15728640 | tf_op jit(solution)/shard_map/pallas_call | solution.py:130
  140.6 1.9 copy.59
  144.6 3.8 %collective-permute-start.7 = (bf16[2,512,128]{2,1,0:T(8,128)(2,1)S(1)}, bf16[2,512,128]{2,1,0:T(8,128)(2,1)S(1)}, u32[]{:S(2)}, u32[]{:S(2)}) collective-permute-start(bf16[2,512,128]{2,1,0:T(8,128)(2,1)S(1)} %get-tuple-element.53), channel_id=1, source_target_pairs={{0,24},{8,0},{16,8},{24,16},{4,28},{12,4},{20,12},{28,20},{1,25},{... | collective-permute-start | bytes 786440 | tf_op jit(solution)/shard_map/ppermute | solution.py:176
  149.5 5.6 %collective-permute-done.7 = bf16[2,512,128]{2,1,0:T(8,128)(2,1)S(1)} collective-permute-done((bf16[2,512,128]{2,1,0:T(8,128)(2,1)S(1)}, bf16[2,512,128]{2,1,0:T(8,128)(2,1)S(1)}, u32[]{:S(2)}, u32[]{:S(2)}) %collective-permute-start.7) | collective-permute-done | bytes 262176 | tf_op jit(solution)/shard_map/ppermute | solution.py:176
  155.1 11.3 %collective-permute-start.9 = (bf16[2,512,128]{2,1,0:T(8,128)(2,1)S(1)}, bf16[2,512,128]{2,1,0:T(8,128)(2,1)S(1)}, u32[]{:S(2)}, u32[]{:S(2)}) collective-permute-start(bf16[2,512,128]{2,1,0:T(8,128)(2,1)S(1)} %get-tuple-element.51), channel_id=1, source_target_pairs={{0,8},{8,16},{16,24},{24,0},{4,12},{12,20},{20,28},{28,4},{1,9},{9... | collective-permute-start | bytes 786440 | tf_op jit(solution)/shard_map/ppermute | solution.py:176
  166.4 2.4 %collective-permute-done.8 = bf16[2,512,128]{2,1,0:T(8,128)(2,1)S(1)} collective-permute-done((bf16[2,512,128]{2,1,0:T(8,128)(2,1)S(1)}, bf16[2,512,128]{2,1,0:T(8,128)(2,1)S(1)}, u32[]{:S(2)}, u32[]{:S(2)}) %collective-permute-start.8) | collective-permute-done | bytes 262176 | tf_op jit(solution)/shard_map/ppermute | solution.py:176
  169.4 3.7 %collective-permute-done.9 = bf16[2,512,128]{2,1,0:T(8,128)(2,1)S(1)} collective-permute-done((bf16[2,512,128]{2,1,0:T(8,128)(2,1)S(1)}, bf16[2,512,128]{2,1,0:T(8,128)(2,1)S(1)}, u32[]{:S(2)}, u32[]{:S(2)}) %collective-permute-start.9) | collective-permute-done | bytes 262176 | tf_op jit(solution)/shard_map/ppermute | solution.py:176
  174.2 8.1 %collective-permute-start.14 = (bf16[2,512,128]{2,1,0:T(8,128)(2,1)S(1)}, bf16[2,512,128]{2,1,0:T(8,128)(2,1)S(1)}, u32[]{:S(2)}, u32[]{:S(2)}) collective-permute-start(bf16[2,512,128]{2,1,0:T(8,128)(2,1)S(1)} %get-tuple-element.44), channel_id=1, source_target_pairs={{0,16},{8,24},{16,0},{24,8},{4,20},{12,28},{20,4},{28,12},{1,17},{... | collective-permute-start | bytes 786440 | tf_op jit(solution)/shard_map/ppermute | solution.py:176
  183.2 2.1 collective-permute-start.15
  187.5 6.4 %collective-permute-done.14 = bf16[2,512,128]{2,1,0:T(8,128)(2,1)S(1)} collective-permute-done((bf16[2,512,128]{2,1,0:T(8,128)(2,1)S(1)}, bf16[2,512,128]{2,1,0:T(8,128)(2,1)S(1)}, u32[]{:S(2)}, u32[]{:S(2)}) %collective-permute-start.14) | collective-permute-done | bytes 262176 | tf_op jit(solution)/shard_map/ppermute | solution.py:176
  194.4 6.5 %collective-permute-start.17 = (bf16[2,512,128]{2,1,0:T(8,128)(2,1)S(1)}, bf16[2,512,128]{2,1,0:T(8,128)(2,1)S(1)}, u32[]{:S(2)}, u32[]{:S(2)}) collective-permute-start(bf16[2,512,128]{2,1,0:T(8,128)(2,1)S(1)} %get-tuple-element.42), channel_id=1, source_target_pairs={{0,24},{8,0},{16,8},{24,16},{4,28},{12,4},{20,12},{28,20},{1,25},{... | collective-permute-start | bytes 786440 | tf_op jit(solution)/shard_map/ppermute | solution.py:176
  200.9 4.3 %collective-permute-start.18 = (bf16[2,512,128]{2,1,0:T(8,128)(2,1)S(1)}, bf16[2,512,128]{2,1,0:T(8,128)(2,1)S(1)}, u32[]{:S(2)}, u32[]{:S(2)}) collective-permute-start(bf16[2,512,128]{2,1,0:T(8,128)(2,1)S(1)} %get-tuple-element.41), channel_id=1, source_target_pairs={{0,16},{8,24},{16,0},{24,8},{4,20},{12,28},{20,4},{28,12},{1,17},{... | collective-permute-start | bytes 786440 | tf_op jit(solution)/shard_map/ppermute | solution.py:176
  205.2 11.1 %collective-permute-done.18 = bf16[2,512,128]{2,1,0:T(8,128)(2,1)S(1)} collective-permute-done((bf16[2,512,128]{2,1,0:T(8,128)(2,1)S(1)}, bf16[2,512,128]{2,1,0:T(8,128)(2,1)S(1)}, u32[]{:S(2)}, u32[]{:S(2)}) %collective-permute-start.18) | collective-permute-done | bytes 262176 | tf_op jit(solution)/shard_map/ppermute | solution.py:176
  (105 shorter events, 22.0 us)
Async XLA Ops:
  0.6 12.3 %copy-start = (s32[4,2,8]{2,1,0:T(2,128)S(1)}, s32[4,2,8]{2,1,0:T(2,128)}, u32[]{:S(2)}) copy-start(s32[4,2,8]{2,1,0:T(2,128)} %param.9) | copy-start | bytes 772
  0.6 2.9 %copy-start.11 = (bf16[4,1024,128]{2,1,0:T(8,128)(2,1)S(1)}, bf16[4,1024,128]{2,1,0:T(8,128)(2,1)}, u32[]{:S(2)}) copy-start(bf16[4,1024,128]{2,1,0:T(8,128)(2,1)} %param.6) | copy-start | bytes 3145732
  0.7 2.9 %copy-start.12 = (bf16[4,1024,128]{2,1,0:T(8,128)(2,1)S(1)}, bf16[4,1024,128]{2,1,0:T(8,128)(2,1)}, u32[]{:S(2)}) copy-start(bf16[4,1024,128]{2,1,0:T(8,128)(2,1)} %param.7) | copy-start | bytes 3145732
  6.0 23.9 %collective-permute-start = (bf16[6,512,128]{2,1,0:T(8,128)(2,1)}, bf16[6,512,128]{2,1,0:T(8,128)(2,1)}, u32[]{:S(2)}, u32[]{:S(2)}) collective-permute-start(bf16[6,512,128]{2,1,0:T(8,128)(2,1)} %get-tuple-element.36), channel_id=1, source_target_pairs={{0,8},{8,16},{16,24},{24,0},{4,12},{12,20},{20,28},{28,4},{1,9},{9... | collective-permute-start | bytes 2359304 | tf_op jit(solution)/shard_map/ppermute | solution.py:161
  9.0 53.7 %collective-permute-start.1 = (bf16[6,512,128]{2,1,0:T(8,128)(2,1)}, bf16[6,512,128]{2,1,0:T(8,128)(2,1)}, u32[]{:S(2)}, u32[]{:S(2)}) collective-permute-start(bf16[6,512,128]{2,1,0:T(8,128)(2,1)} %get-tuple-element.35), channel_id=1, source_target_pairs={{0,16},{8,24},{16,0},{24,8},{4,20},{12,28},{20,4},{28,12},{1,17},{... | collective-permute-start | bytes 2359304 | tf_op jit(solution)/shard_map/ppermute | solution.py:161
  11.6 52.4 %collective-permute-start.2 = (bf16[6,512,128]{2,1,0:T(8,128)(2,1)}, bf16[6,512,128]{2,1,0:T(8,128)(2,1)}, u32[]{:S(2)}, u32[]{:S(2)}) collective-permute-start(bf16[6,512,128]{2,1,0:T(8,128)(2,1)} %get-tuple-element.34), channel_id=1, source_target_pairs={{0,24},{8,0},{16,8},{24,16},{4,28},{12,4},{20,12},{28,20},{1,25},{... | collective-permute-start | bytes 2359304 | tf_op jit(solution)/shard_map/ppermute | solution.py:161
  66.6 1.2 copy-start.6
  67.9 51.0 %collective-permute-start.6 = (bf16[4,2,512,128]{3,2,0,1:T(8,128)(2,1)S(1)}, bf16[4,2,512,128]{3,2,0,1:T(8,128)(2,1)}, u32[]{:S(2)}, u32[]{:S(2)}) collective-permute-start(bf16[4,2,512,128]{3,2,0,1:T(8,128)(2,1)S(1)} %fusion.5), channel_id=1, source_target_pairs={{0,4},{8,12},{16,20},{24,28},{4,0},{12,8},{20,16},{28,24},{1,5},{9... | collective-permute-start | bytes 3145736 | tf_op jit(solution)/shard_map/ppermute | solution.py:222
  70.4 41.1 %collective-permute-start.3 = (bf16[2,512,128]{2,1,0:T(8,128)(2,1)}, bf16[2,512,128]{2,1,0:T(8,128)(2,1)S(1)}, u32[]{:S(2)}, u32[]{:S(2)}) collective-permute-start(bf16[2,512,128]{2,1,0:T(8,128)(2,1)} %get-tuple-element.60), channel_id=1, source_target_pairs={{0,8},{8,16},{16,24},{24,0},{4,12},{12,20},{20,28},{28,4},{1,9},{9... | collective-permute-start | bytes 786440 | tf_op jit(solution)/shard_map/ppermute | solution.py:161
  86.5 28.6 %collective-permute-start.4 = (bf16[2,512,128]{2,1,0:T(8,128)(2,1)}, bf16[2,512,128]{2,1,0:T(8,128)(2,1)S(1)}, u32[]{:S(2)}, u32[]{:S(2)}) collective-permute-start(bf16[2,512,128]{2,1,0:T(8,128)(2,1)} %get-tuple-element.59), channel_id=1, source_target_pairs={{0,16},{8,24},{16,0},{24,8},{4,20},{12,28},{20,4},{28,12},{1,17},{... | collective-permute-start | bytes 786440 | tf_op jit(solution)/shard_map/ppermute | solution.py:161
  89.3 27.5 %collective-permute-start.5 = (bf16[2,512,128]{2,1,0:T(8,128)(2,1)}, bf16[2,512,128]{2,1,0:T(8,128)(2,1)}, u32[]{:S(2)}, u32[]{:S(2)}) collective-permute-start(bf16[2,512,128]{2,1,0:T(8,128)(2,1)} %get-tuple-element.58), channel_id=1, source_target_pairs={{0,24},{8,0},{16,8},{24,16},{4,28},{12,4},{20,12},{28,20},{1,25},{... | collective-permute-start | bytes 786440 | tf_op jit(solution)/shard_map/ppermute | solution.py:161
  109.9 64.3 %collective-permute-start.10 = (bf16[2,512,128]{2,1,0:T(8,128)(2,1)S(1)}, bf16[2,512,128]{2,1,0:T(8,128)(2,1)}, u32[]{:S(2)}, u32[]{:S(2)}) collective-permute-start(bf16[2,512,128]{2,1,0:T(8,128)(2,1)S(1)} %get-tuple-element.50), channel_id=1, source_target_pairs={{0,24},{8,0},{16,8},{24,16},{4,28},{12,4},{20,12},{28,20},{1,25},{... | collective-permute-start | bytes 786440 | tf_op jit(solution)/shard_map/ppermute | solution.py:176
  112.2 71.1 %collective-permute-start.11 = (bf16[2,512,128]{2,1,0:T(8,128)(2,1)S(1)}, bf16[2,512,128]{2,1,0:T(8,128)(2,1)S(1)}, u32[]{:S(2)}, u32[]{:S(2)}) collective-permute-start(bf16[2,512,128]{2,1,0:T(8,128)(2,1)S(1)} %get-tuple-element.49), channel_id=1, source_target_pairs={{0,16},{8,24},{16,0},{24,8},{4,20},{12,28},{20,4},{28,12},{1,17},{... | collective-permute-start | bytes 786440 | tf_op jit(solution)/shard_map/ppermute | solution.py:176
  115.8 69.5 %collective-permute-start.12 = (bf16[2,512,128]{2,1,0:T(8,128)(2,1)S(1)}, bf16[2,512,128]{2,1,0:T(8,128)(2,1)S(1)}, u32[]{:S(2)}, u32[]{:S(2)}) collective-permute-start(bf16[2,512,128]{2,1,0:T(8,128)(2,1)S(1)} %get-tuple-element.48), channel_id=1, source_target_pairs={{0,8},{8,16},{16,24},{24,0},{4,12},{12,20},{20,28},{28,4},{1,9},{9... | collective-permute-start | bytes 786440 | tf_op jit(solution)/shard_map/ppermute | solution.py:176
  140.5 2.8 %copy-start.3 = (f32[2,4,2,512,128]{4,3,2,1,0:T(8,128)S(1)}, f32[2,4,2,512,128]{4,3,2,1,0:T(8,128)}, u32[]{:S(2)}) copy-start(f32[2,4,2,512,128]{4,3,2,1,0:T(8,128)} %get-tuple-element.25) | copy-start | bytes 12582916
  142.5 1.8 copy-start.10
  143.4 5.0 %copy-start.2 = (f32[4,2,512,128]{3,2,1,0:T(8,128)S(1)}, f32[4,2,512,128]{3,2,1,0:T(8,128)}, u32[]{:S(2)}) copy-start(f32[4,2,512,128]{3,2,1,0:T(8,128)} %get-tuple-element.28) | copy-start | bytes 6291460
  144.3 4.1 %slice-start = ((bf16[4,2,512,128]{3,2,0,1:T(8,128)(2,1)}), bf16[3,2,512,128]{3,2,0,1:T(8,128)(2,1)S(1)}, s32[]{:S(2)}) async-start(bf16[4,2,512,128]{3,2,0,1:T(8,128)(2,1)} %copy-done.4), calls=%async_computation | async-start | bytes 1572864 | tf_op jit(solution)/shard_map/jit(_roll_static)/slice | solution.py:242
  144.4 4.2 %copy-start.8 = (f32[4,2,512,128]{3,2,1,0:T(8,128)S(1)}, f32[4,2,512,128]{3,2,1,0:T(8,128)}, u32[]{:S(2)}) copy-start(f32[4,2,512,128]{3,2,1,0:T(8,128)} %get-tuple-element.24) | copy-start | bytes 6291460
  144.4 4.2 %copy-start.9 = (f32[4,2,512,128]{3,2,1,0:T(8,128)S(1)}, f32[4,2,512,128]{3,2,1,0:T(8,128)}, u32[]{:S(2)}) copy-start(f32[4,2,512,128]{3,2,1,0:T(8,128)} %get-tuple-element.23) | copy-start | bytes 6291460
  144.6 10.6 %collective-permute-start.7 = (bf16[2,512,128]{2,1,0:T(8,128)(2,1)S(1)}, bf16[2,512,128]{2,1,0:T(8,128)(2,1)S(1)}, u32[]{:S(2)}, u32[]{:S(2)}) collective-permute-start(bf16[2,512,128]{2,1,0:T(8,128)(2,1)S(1)} %get-tuple-element.53), channel_id=1, source_target_pairs={{0,24},{8,0},{16,8},{24,16},{4,28},{12,4},{20,12},{28,20},{1,25},{... | collective-permute-start | bytes 786440 | tf_op jit(solution)/shard_map/ppermute | solution.py:176
  148.4 20.4 %collective-permute-start.8 = (bf16[2,512,128]{2,1,0:T(8,128)(2,1)S(1)}, bf16[2,512,128]{2,1,0:T(8,128)(2,1)S(1)}, u32[]{:S(2)}, u32[]{:S(2)}) collective-permute-start(bf16[2,512,128]{2,1,0:T(8,128)(2,1)S(1)} %get-tuple-element.52), channel_id=1, source_target_pairs={{0,16},{8,24},{16,0},{24,8},{4,20},{12,28},{20,4},{28,12},{1,17},{... | collective-permute-start | bytes 786440 | tf_op jit(solution)/shard_map/ppermute | solution.py:176
  155.1 18.0 %collective-permute-start.9 = (bf16[2,512,128]{2,1,0:T(8,128)(2,1)S(1)}, bf16[2,512,128]{2,1,0:T(8,128)(2,1)S(1)}, u32[]{:S(2)}, u32[]{:S(2)}) collective-permute-start(bf16[2,512,128]{2,1,0:T(8,128)(2,1)S(1)} %get-tuple-element.51), channel_id=1, source_target_pairs={{0,8},{8,16},{16,24},{24,0},{4,12},{12,20},{20,28},{28,4},{1,9},{9... | collective-permute-start | bytes 786440 | tf_op jit(solution)/shard_map/ppermute | solution.py:176
  168.8 25.2 %collective-permute-start.16 = (bf16[4,2,512,128]{3,2,0,1:T(8,128)(2,1)S(1)}, bf16[4,2,512,128]{3,2,0,1:T(8,128)(2,1)S(1)}, u32[]{:S(2)}, u32[]{:S(2)}) collective-permute-start(bf16[4,2,512,128]{3,2,0,1:T(8,128)(2,1)S(1)} %fusion.2), channel_id=1, source_target_pairs={{4,0},{12,8},{20,16},{28,24},{0,4},{8,12},{16,20},{24,28},{5,1},{1... | collective-permute-start | bytes 3145736 | tf_op jit(solution)/shard_map/ppermute | solution.py:244
  173.1 14.4 %collective-permute-start.13 = (bf16[2,512,128]{2,1,0:T(8,128)(2,1)S(1)}, bf16[2,512,128]{2,1,0:T(8,128)(2,1)S(1)}, u32[]{:S(2)}, u32[]{:S(2)}) collective-permute-start(bf16[2,512,128]{2,1,0:T(8,128)(2,1)S(1)} %get-tuple-element.45), channel_id=1, source_target_pairs={{0,24},{8,0},{16,8},{24,16},{4,28},{12,4},{20,12},{28,20},{1,25},{... | collective-permute-start | bytes 786440 | tf_op jit(solution)/shard_map/ppermute | solution.py:176
  174.2 19.8 %collective-permute-start.14 = (bf16[2,512,128]{2,1,0:T(8,128)(2,1)S(1)}, bf16[2,512,128]{2,1,0:T(8,128)(2,1)S(1)}, u32[]{:S(2)}, u32[]{:S(2)}) collective-permute-start(bf16[2,512,128]{2,1,0:T(8,128)(2,1)S(1)} %get-tuple-element.44), channel_id=1, source_target_pairs={{0,16},{8,24},{16,0},{24,8},{4,20},{12,28},{20,4},{28,12},{1,17},{... | collective-permute-start | bytes 786440 | tf_op jit(solution)/shard_map/ppermute | solution.py:176
  183.2 17.6 %collective-permute-start.15 = (bf16[2,512,128]{2,1,0:T(8,128)(2,1)S(1)}, bf16[2,512,128]{2,1,0:T(8,128)(2,1)S(1)}, u32[]{:S(2)}, u32[]{:S(2)}) collective-permute-start(bf16[2,512,128]{2,1,0:T(8,128)(2,1)S(1)} %get-tuple-element.43), channel_id=1, source_target_pairs={{0,8},{8,16},{16,24},{24,0},{4,12},{12,20},{20,28},{28,4},{1,9},{9... | collective-permute-start | bytes 786440 | tf_op jit(solution)/shard_map/ppermute | solution.py:176
  185.3 8.7 %copy-start.7 = (f32[4,2,512,128]{3,2,1,0:T(8,128)S(1)}, f32[4,2,512,128]{3,2,1,0:T(8,128)}, u32[]{:S(2)}) copy-start(f32[4,2,512,128]{3,2,1,0:T(8,128)} %get-tuple-element.27) | copy-start | bytes 6291460
  194.4 10.8 %collective-permute-start.17 = (bf16[2,512,128]{2,1,0:T(8,128)(2,1)S(1)}, bf16[2,512,128]{2,1,0:T(8,128)(2,1)S(1)}, u32[]{:S(2)}, u32[]{:S(2)}) collective-permute-start(bf16[2,512,128]{2,1,0:T(8,128)(2,1)S(1)} %get-tuple-element.42), channel_id=1, source_target_pairs={{0,24},{8,0},{16,8},{24,16},{4,28},{12,4},{20,12},{28,20},{1,25},{... | collective-permute-start | bytes 786440 | tf_op jit(solution)/shard_map/ppermute | solution.py:176
  200.9 15.5 %collective-permute-start.18 = (bf16[2,512,128]{2,1,0:T(8,128)(2,1)S(1)}, bf16[2,512,128]{2,1,0:T(8,128)(2,1)S(1)}, u32[]{:S(2)}, u32[]{:S(2)}) collective-permute-start(bf16[2,512,128]{2,1,0:T(8,128)(2,1)S(1)} %get-tuple-element.41), channel_id=1, source_target_pairs={{0,16},{8,24},{16,0},{24,8},{4,20},{12,28},{20,4},{28,12},{1,17},{... | collective-permute-start | bytes 786440 | tf_op jit(solution)/shard_map/ppermute | solution.py:176
  205.1 11.3 %collective-permute-start.19 = (bf16[2,512,128]{2,1,0:T(8,128)(2,1)S(1)}, bf16[2,512,128]{2,1,0:T(8,128)(2,1)S(1)}, u32[]{:S(2)}, u32[]{:S(2)}) collective-permute-start(bf16[2,512,128]{2,1,0:T(8,128)(2,1)S(1)} %get-tuple-element.40), channel_id=1, source_target_pairs={{0,8},{8,16},{16,24},{24,0},{4,12},{12,20},{20,28},{28,4},{1,9},{9... | collective-permute-start | bytes 786440 | tf_op jit(solution)/shard_map/ppermute | solution.py:176
  205.1 13.4 %copy-start.1 = (s32[4,2,8]{2,1,0:T(2,128)S(1)}, s32[4,2,8]{2,1,0:T(2,128)}, u32[]{:S(2)}) copy-start(s32[4,2,8]{2,1,0:T(2,128)} %param.9) | copy-start | bytes 772
  (4 other events, 3.4 us)
